TPU v7x, 512 devices: a whole 4x8x8 slice. The times are simulated.
512 devices in a mesh: panel: 16 (over y_hi, x), tile: 32 (over z, y_lo, core).
Axes of the slice: x: 4, y: 8 (y_hi: 4, y_lo: 2; y = y_hi * 2 + y_lo), z: 8, core: 2. Of those that a mesh axis runs over, the one named last changes fastest.
Arguments:
- tracer: bfloat16 [144, 768, 1152], P('panel', 'tile'), may hold values from 0.099609375 to 2
- moments: float32 [2, 144, 768, 4, 6], P(None, 'panel', 'tile'), may hold values from -0.9 to 0.9
- pieces: int32 [2, 144, 768, 4], P(None, 'panel', 'tile'), may hold values from 0 to 11
- cell_area: float32 [144, 768], P('panel', 'tile'), may hold values from 0.5 to 2
Outputs:
- updated: bfloat16 [144, 768, 1152], P('panel', 'tile')
Inputs may be any that keep to these rules, and one draw needn't show every extreme that they name: Codes of the cells that a face's swept pieces intersect.
All inputs are finite; a program needn't handle non-finite values.
Results may differ from a plain program's by a relative error of at most 0.0018.
Values may be sent and summed in bfloat16 or wider, within the bound.
No kernel may reach another device: no remote copies, remote signals or barrier semaphores. Data moves between devices by JAX's collectives and lax.ppermute only.
A program may use at most 64 MiB of HBM per device.

v0:
```python
import jax
import jax.numpy as jnp
import numpy as np
from jax import lax
from jax.sharding import PartitionSpec as P


def with_halo(value, sides, width, wrap):
    for axis, dim in sides:
        size, length = (lax.axis_size(axis), value.shape[dim])
        up = [(i, (i + 1) % size) for i in range(size if wrap else size - 1)]
        down = [(j, i) for i, j in up]
        last = lax.slice_in_dim(value, length - width, length, axis=dim)
        first = lax.slice_in_dim(value, 0, width, axis=dim)
        before = lax.ppermute(last, axis, up)
        after = lax.ppermute(first, axis, down)
        value = jnp.concatenate([before, value, after], axis=dim)
    return value


def shifted(value, axis, steps):
    count = lax.axis_size(axis)
    pairs = [(source, (source + steps) % count) for source in range(count)]
    return lax.ppermute(value, axis, pairs)


def passed_along(value, axis, by):
    size = lax.axis_size(axis)
    pairs = [(i, i + by) for i in range(size) if 0 <= i + by < size]
    return lax.ppermute(value, axis, pairs)


def stencil_table():
    stencil = np.zeros((6, 3, 3))
    stencil[0, 1, 1] = 7.0 / 6.0
    stencil[0, 1, 0] = -1.0 / 24.0
    stencil[0, 1, 2] = -1.0 / 24.0
    stencil[0, 0, 1] = -1.0 / 24.0
    stencil[0, 2, 1] = -1.0 / 24.0
    stencil[1, 1, 2] = 0.5
    stencil[1, 1, 0] = -0.5
    stencil[2, 2, 1] = 0.5
    stencil[2, 0, 1] = -0.5
    stencil[3, 1, 2] = 0.5
    stencil[3, 1, 0] = 0.5
    stencil[3, 1, 1] = -1.0
    stencil[4, 2, 2] = 0.25
    stencil[4, 2, 0] = -0.25
    stencil[4, 0, 2] = -0.25
    stencil[4, 0, 0] = 0.25
    stencil[5, 2, 1] = 0.5
    stencil[5, 0, 1] = 0.5
    stencil[5, 1, 1] = -1.0
    return stencil


def tap_tables():
    stencil = stencil_table()
    tables = np.zeros((2, 12, 6, 36))
    for direction in range(2):
        for code in range(12):
            if direction == 0:
                row_off = code // 4 - 1
                col_off = code % 4 - 1
            else:
                row_off = code % 4 - 1
                col_off = code // 4 - 1
            for tap_index in range(36):
                inner_row = tap_index // 6 - 2 - row_off
                inner_col = tap_index % 6 - 2 - col_off
                if abs(inner_row) <= 1 and abs(inner_col) <= 1:
                    tables[direction, code, :, tap_index] = stencil[:, inner_row + 1, inner_col + 1]
    return tables


def compose_taps(pieces, moments):
    codes = jnp.arange(12, dtype=jnp.int32)
    onehot = (pieces[..., None] == codes).astype(jnp.float32)
    summed = jnp.einsum("dijko,dijkm->dijom", onehot, moments, precision=lax.Precision.HIGHEST)
    tables = jnp.asarray(tap_tables(), dtype=jnp.float32)
    return jnp.einsum("dijom,domt->dijt", summed, tables, precision=lax.Precision.HIGHEST)


def apply_taps(weights, padded, row_start, col_start, nrow, ncol):
    width = padded.shape[2]
    total = jnp.zeros((nrow, ncol, width), jnp.float32)
    for tap_index in range(36):
        tap_row = row_start + tap_index // 6 - 2
        tap_col = col_start + tap_index % 6 - 2
        piece = lax.slice(padded, (tap_row, tap_col, 0), (tap_row + nrow, tap_col + ncol, width))
        total = total + weights[:, :, tap_index][:, :, None] * piece.astype(jnp.float32)
    return total


def local(tracer, moments, pieces, cell_area):
    rows = tracer.shape[0]
    cols = tracer.shape[1]
    weights = compose_taps(pieces, moments)
    is_top = lax.axis_index("panel") == lax.axis_size("panel") - 1
    last_row = jnp.arange(rows) == rows - 1
    row_mask = jnp.where(jnp.logical_and(last_row, is_top), 0.0, 1.0).astype(jnp.float32)
    east_weights = weights[0]
    north_weights = weights[1] * row_mask[:, None, None]
    wide = with_halo(tracer, (("tile", 1),), 3, True)
    padded = with_halo(wide, (("panel", 0),), 3, False)
    east = apply_taps(east_weights, padded, 3, 3, rows, cols)
    north = apply_taps(north_weights, padded, 3, 3, rows, cols)
    west_edge = shifted(east[:, cols - 1 :].astype(jnp.bfloat16), "tile", 1).astype(jnp.float32)
    south_edge = passed_along(north[rows - 1 :].astype(jnp.bfloat16), "panel", 1).astype(
        jnp.float32
    )
    west = jnp.concatenate([west_edge, east[:, : cols - 1]], axis=1)
    south = jnp.concatenate([south_edge, north[: rows - 1]], axis=0)
    change = (west - east + (south - north)) / cell_area[:, :, None]
    return (tracer.astype(jnp.float32) + change).astype(jnp.bfloat16)


def solution(mesh):
    in_specs = (
        P("panel", "tile", None),
        P(None, "panel", "tile", None, None),
        P(None, "panel", "tile", None),
        P("panel", "tile"),
    )
    out_specs = P("panel", "tile", None)
    return jax.shard_map(local, mesh=mesh, in_specs=in_specs, out_specs=out_specs, check_vma=False)
```

profile of v0, /device:TPU:20, one launch (start us, length us, event | category | flops | bytes accessed | tf_op | source)
XLA Modules:
  0.0 69.4 jit_solution(5953921788457804884)
XLA Ops:
  0.0 1.1 %fusion.82 = (bf16[9,3,1152]{2,1,0:T(4,128)(2,1)S(1)}, bf16[9,3,1152]{2,1,0:T(4,128)(2,1)S(1)}) fusion(bf16[9,24,1152]{2,1,0:T(8,128)(2,1)} %param.5), kind=kLoop, calls=%fused_computation.243 | loop fusion | bytes 248832 | tf_op jit(solution)/shard_map/slice | solution.py:14
  1.1 11.4 %collective-permute-start.1 = (bf16[9,3,1152]{2,1,0:T(4,128)(2,1)S(1)}, bf16[9,3,1152]{2,1,0:T(4,128)(2,1)S(1)}, u32[]{:S(2)}, u32[]{:S(2)}) collective-permute-start(bf16[9,3,1152]{2,1,0:T(4,128)(2,1)S(1)} %get-tuple-element.81), channel_id=1, source_target_pairs={{1,0},{2,1},{3,2},{4,3},{5,4},{6,5},{7,6},{8,7},{9,8},{10,9},{11,1... | collective-permute-start | bytes 186632 | tf_op jit(solution)/shard_map/ppermute | solution.py:16
  12.5 1.9 %collective-permute-start = (bf16[9,3,1152]{2,1,0:T(4,128)(2,1)S(1)}, bf16[9,3,1152]{2,1,0:T(4,128)(2,1)S(1)}, u32[]{:S(2)}, u32[]{:S(2)}) collective-permute-start(bf16[9,3,1152]{2,1,0:T(4,128)(2,1)S(1)} %get-tuple-element.82), channel_id=1, source_target_pairs={{0,1},{1,2},{2,3},{3,4},{4,5},{5,6},{6,7},{7,8},{8,9},{9,10},{10,1... | collective-permute-start | bytes 186632 | tf_op jit(solution)/shard_map/ppermute | solution.py:15
  14.4 1.1 %constant_dynamic-update-slice_fusion.1 = bf16[9,27,1152]{2,1,0:T(8,128)(2,1)S(1)} fusion(bf16[9,24,1152]{2,1,0:T(8,128)(2,1)} %param.5), kind=kLoop, calls=%fused_computation.241 | loop fusion | bytes 995328
  15.5 0.9 %copy.7 = s32[2,9,24,4]{3,2,1,0:T(8,128)S(1)} copy(s32[2,9,24,4]{2,3,1,0:T(4,128)} %param.7) | data formatting | bytes 13824 | tf_op args[2]
  16.4 1.4 %copy.8 = f32[2,9,24,4,6]{4,3,2,1,0:T(4,128)S(1)} copy(f32[2,9,24,4,6]{2,3,4,1,0:T(4,128)} %param.6) | data formatting | bytes 82944 | tf_op args[1]
  17.9 0.0 copy-start.1
  17.9 2.3 %fusion.78 = f32[2,9,24,12,6]{3,4,2,1,0:T(8,128)S(1)} fusion(f32[2,9,24,4,6]{4,3,2,1,0:T(4,128)S(1)} %copy.8, s32[2,9,24,4]{3,2,1,0:T(8,128)S(1)} %copy.7), kind=kOutput, calls=%fused_computation.154 | convolution fusion | flops 1513728 | bytes 172800 | tf_op jit(solution)/shard_map/dijko,dijkm->dijom/dot_general | solution.py:79
  20.2 0.0 copy-done.1
  20.2 1.3 %fusion.2 = f32[2,9,24,36]{3,2,1,0:T(8,128)S(1)} fusion(f32[2,12,6,36,1]{3,1,2,4,0:T(8,128)S(1)} %copy-done.1, f32[2,9,24,12,6]{3,4,2,1,0:T(8,128)S(1)} %fusion.78), kind=kOutput, calls=%fused_computation.75 | convolution fusion | flops 13436928 | bytes 207360 | tf_op jit(solution)/shard_map/dijom,domt->dijt/dot_general | solution.py:81
  21.5 1.1 %slice_reduce_fusion.70 = (f32[9,24]{1,0:T(8,128)S(1)}, f32[9,24]{1,0:T(8,128)S(1)}, f32[9,24]{1,0:T(8,128)S(1)}, f32[9,24]{1,0:T(8,128)S(1)}, f32[9,24]{1,0:T(8...) fusion(f32[9,24,36]{2,1,0:T(8,128)S(1)} %slice_bitcast_fusion.1), kind=kLoop, calls=%fused_computation.236 | loop fusion | bytes 29376 | tf_op jit(solution)/shard_map/slice | solution.py:91
  22.6 1.1 %slice_reduce_fusion.71 = (f32[9,24]{1,0:T(8,128)S(1)}, f32[9,24]{1,0:T(8,128)S(1)}, f32[9,24]{1,0:T(8,128)S(1)}, f32[9,24]{1,0:T(8,128)S(1)}, f32[9,24]{1,0:T(8...) fusion(f32[9,24,36]{2,1,0:T(8,128)S(1)} %slice_bitcast_fusion.1), kind=kLoop, calls=%fused_computation.237 | loop fusion | bytes 32832 | tf_op jit(solution)/shard_map/slice | solution.py:91
  23.8 0.1 fusion.81
  23.8 0.0 copy-start
  23.9 1.1 %slice_reduce_fusion.35 = (f32[9,24]{1,0:T(8,128)S(1)}, f32[9,24]{1,0:T(8,128)S(1)}, f32[9,24]{1,0:T(8,128)S(1)}, f32[9,24]{1,0:T(8,128)S(1)}, f32[9,24]{1,0:T(8...) fusion(f32[9,24,36]{2,1,0:T(8,128)S(1)} %fusion.81), kind=kLoop, calls=%fused_computation.199 | loop fusion | bytes 32832 | tf_op jit(solution)/shard_map/slice | solution.py:91
  25.0 1.1 %slice_reduce_fusion.34 = (f32[9,24]{1,0:T(8,128)S(1)}, f32[9,24]{1,0:T(8,128)S(1)}, f32[9,24]{1,0:T(8,128)S(1)}, f32[9,24]{1,0:T(8,128)S(1)}, f32[9,24]{1,0:T(8...) fusion(f32[9,24,36]{2,1,0:T(8,128)S(1)} %fusion.81), kind=kLoop, calls=%fused_computation.198 | loop fusion | bytes 29376 | tf_op jit(solution)/shard_map/slice | solution.py:91
  26.1 0.0 collective-permute-done.1
  26.1 0.0 collective-permute-done
  26.1 0.0 copy-done
  26.1 0.2 pad_maximum_fusion.4
  26.3 3.1 %collective-permute-start.2 = (bf16[3,30,1152]{2,1,0:T(8,128)(2,1)S(1)}, bf16[3,30,1152]{2,1,0:T(8,128)(2,1)S(1)}, u32[]{:S(2)}, u32[]{:S(2)}) collective-permute-start(bf16[3,30,1152]{2,1,0:T(8,128)(2,1)S(1)} %get-tuple-element.79), channel_id=1, source_target_pairs={{0,32},{32,64},{64,96},{96,128},{128,160},{160,192},{192,224},{224... | collective-permute-start | bytes 622088 | tf_op jit(solution)/shard_map/ppermute | solution.py:15
  29.4 2.7 %collective-permute-start.3 = (bf16[3,30,1152]{2,1,0:T(8,128)(2,1)S(1)}, bf16[3,30,1152]{2,1,0:T(8,128)(2,1)S(1)}, u32[]{:S(2)}, u32[]{:S(2)}) collective-permute-start(bf16[3,30,1152]{2,1,0:T(8,128)(2,1)S(1)} %get-tuple-element.80), channel_id=1, source_target_pairs={{32,0},{64,32},{96,64},{128,96},{160,128},{192,160},{224,192},{256... | collective-permute-start | bytes 622088 | tf_op jit(solution)/shard_map/ppermute | solution.py:16
  32.1 0.1 constant_dynamic-update-slice_fusion
  32.2 1.9 %collective-permute-done.2 = bf16[3,30,1152]{2,1,0:T(8,128)(2,1)S(1)} collective-permute-done((bf16[3,30,1152]{2,1,0:T(8,128)(2,1)S(1)}, bf16[3,30,1152]{2,1,0:T(8,128)(2,1)S(1)}, u32[]{:S(2)}, u32[]{:S(2)}) %collective-permute-start.2) | collective-permute-done | bytes 207392 | tf_op jit(solution)/shard_map/ppermute | solution.py:15
  34.1 3.9 %collective-permute-done.3 = bf16[3,30,1152]{2,1,0:T(8,128)(2,1)S(1)} collective-permute-done((bf16[3,30,1152]{2,1,0:T(8,128)(2,1)S(1)}, bf16[3,30,1152]{2,1,0:T(8,128)(2,1)S(1)}, u32[]{:S(2)}, u32[]{:S(2)}) %collective-permute-start.3) | collective-permute-done | bytes 207392 | tf_op jit(solution)/shard_map/ppermute | solution.py:16
  38.0 0.3 maximum_maximum_fusion
  38.3 5.4 %fusion.74 = f32[9,24,1152]{2,1,0:T(8,128)S(1)} fusion(bf16[9,24,1152]{2,1,0:T(8,128)(2,1)S(1)} %copy-done, bf16[9,3,1152]{2,1,0:T(4,128)(2,1)S(1)} %collective-permute-done, f32[9,24]{1,0:T(8,128)S(1)} %get-tuple-element.6, f32[9,24]{1,0:T(8,128)S(1)} %get-tuple-element.7, f32[9,24]{1,0:T(8,128)S(1)} %get-tuple-element.8, ...), kind=kLoop, calls=%fused_computation.145 | loop fusion | flops 28118016 | bytes 18009216 | tf_op jit(solution)/shard_map/add | solution.py:91
  43.7 8.3 %collective-permute-start.5 = (bf16[1,24,1152]{2,1,0:T(8,128)(2,1)S(1)}, bf16[1,24,1152]{2,1,0:T(8,128)(2,1)S(1)}, u32[]{:S(2)}, u32[]{:S(2)}) collective-permute-start(bf16[1,24,1152]{2,1,0:T(8,128)(2,1)S(1)} %slice.811), channel_id=1, source_target_pairs={{0,32},{32,64},{64,96},{96,128},{128,160},{160,192},{192,224},{224... | collective-permute-start | bytes 165896 | tf_op jit(solution)/shard_map/ppermute | solution.py:30
  52.0 5.4 %fusion.64 = f32[9,24,1152]{2,1,0:T(8,128)S(1)} fusion(bf16[9,24,1152]{2,1,0:T(8,128)(2,1)S(1)} %copy-done, bf16[9,3,1152]{2,1,0:T(4,128)(2,1)S(1)} %collective-permute-done, f32[9,24]{1,0:T(8,128)S(1)} %get-tuple-element.42, f32[9,24]{1,0:T(8,128)S(1)} %get-tuple-element.43, f32[9,24]{1,0:T(8,128)S(1)} %get-tuple-element.44, ...), kind=kLoop, calls=%fused_computation.135 | loop fusion | flops 28118016 | bytes 18009216 | tf_op jit(solution)/shard_map/add | solution.py:91
  57.4 0.0 copy-start.2
  57.5 1.9 %collective-permute-start.4 = (bf16[9,1,1152]{2,1,0:T(2,128)(2,1)S(1)}, bf16[9,1,1152]{2,1,0:T(2,128)(2,1)S(1)}, u32[]{:S(2)}, u32[]{:S(2)}) collective-permute-start(bf16[9,1,1152]{2,1,0:T(2,128)(2,1)S(1)} %slice.812), channel_id=1, source_target_pairs={{0,1},{1,2},{2,3},{3,4},{4,5},{5,6},{6,7},{7,8},{8,9},{9,10},{10,1... | collective-permute-start | bytes 62216 | tf_op jit(solution)/shard_map/ppermute | solution.py:24
  59.4 0.1 slice.652
  59.5 8.6 %collective-permute-done.4 = bf16[9,1,1152]{2,1,0:T(2,128)(2,1)S(1)} collective-permute-done((bf16[9,1,1152]{2,1,0:T(2,128)(2,1)S(1)}, bf16[9,1,1152]{2,1,0:T(2,128)(2,1)S(1)}, u32[]{:S(2)}, u32[]{:S(2)}) %collective-permute-start.4) | collective-permute-done | bytes 20768 | tf_op jit(solution)/shard_map/ppermute | solution.py:24
  68.1 0.0 collective-permute-done.5
  68.2 0.0 copy-done.2
  68.2 1.2 %fusion.75 = bf16[9,24,1152]{2,1,0:T(8,128)(2,1)} fusion(bf16[9,24,1152]{2,1,0:T(8,128)(2,1)S(1)} %copy-done, f32[9,24,1152]{2,1,0:T(8,128)S(1)} %fusion.64, f32[9,23,1152]{2,1,0:T(8,128)S(1)} %bitcast.15, f32[9,1,1152]{2,1,0:T(1,128)S(1)} %convert_element_type.193, f32[9,24,1152]{2,1,0:T(8,128)S(1)} %fusion.74, f32[8,24,1152]{2,1,0:T(8,128)S(1)} %slice.652, ...), kind=kLoop, calls=%fused_computation.146 | loop fusion | flops 2239488 | bytes 4977504 | tf_op jit(solution)/shard_map/convert_element_type | solution.py:115
  (6 shorter events, 0.1 us)
Async XLA Ops:
  1.1 25.0 %collective-permute-start.1 = (bf16[9,3,1152]{2,1,0:T(4,128)(2,1)S(1)}, bf16[9,3,1152]{2,1,0:T(4,128)(2,1)S(1)}, u32[]{:S(2)}, u32[]{:S(2)}) collective-permute-start(bf16[9,3,1152]{2,1,0:T(4,128)(2,1)S(1)} %get-tuple-element.81), channel_id=1, source_target_pairs={{1,0},{2,1},{3,2},{4,3},{5,4},{6,5},{7,6},{8,7},{9,8},{10,9},{11,1... | collective-permute-start | bytes 186632 | tf_op jit(solution)/shard_map/ppermute | solution.py:16
  12.5 13.6 %collective-permute-start = (bf16[9,3,1152]{2,1,0:T(4,128)(2,1)S(1)}, bf16[9,3,1152]{2,1,0:T(4,128)(2,1)S(1)}, u32[]{:S(2)}, u32[]{:S(2)}) collective-permute-start(bf16[9,3,1152]{2,1,0:T(4,128)(2,1)S(1)} %get-tuple-element.82), channel_id=1, source_target_pairs={{0,1},{1,2},{2,3},{3,4},{4,5},{5,6},{6,7},{7,8},{8,9},{9,10},{10,1... | collective-permute-start | bytes 186632 | tf_op jit(solution)/shard_map/ppermute | solution.py:15
  17.9 2.3 %copy-start.1 = (f32[2,12,6,36,1]{3,1,2,4,0:T(8,128)S(1)}, f32[2,12,6,36,1]{3,1,2,4,0:T(8,128)}, u32[]{:S(2)}) copy-start(f32[2,12,6,36,1]{3,1,2,4,0:T(8,128)} %constant.21) | copy-start | bytes 62212
  23.8 2.3 %copy-start = (bf16[9,24,1152]{2,1,0:T(8,128)(2,1)S(1)}, bf16[9,24,1152]{2,1,0:T(8,128)(2,1)}, u32[]{:S(2)}) copy-start(bf16[9,24,1152]{2,1,0:T(8,128)(2,1)} %param.5) | copy-start | bytes 1492996
  26.3 7.8 %collective-permute-start.2 = (bf16[3,30,1152]{2,1,0:T(8,128)(2,1)S(1)}, bf16[3,30,1152]{2,1,0:T(8,128)(2,1)S(1)}, u32[]{:S(2)}, u32[]{:S(2)}) collective-permute-start(bf16[3,30,1152]{2,1,0:T(8,128)(2,1)S(1)} %get-tuple-element.79), channel_id=1, source_target_pairs={{0,32},{32,64},{64,96},{96,128},{128,160},{160,192},{192,224},{224... | collective-permute-start | bytes 622088 | tf_op jit(solution)/shard_map/ppermute | solution.py:15
  29.4 8.6 %collective-permute-start.3 = (bf16[3,30,1152]{2,1,0:T(8,128)(2,1)S(1)}, bf16[3,30,1152]{2,1,0:T(8,128)(2,1)S(1)}, u32[]{:S(2)}, u32[]{:S(2)}) collective-permute-start(bf16[3,30,1152]{2,1,0:T(8,128)(2,1)S(1)} %get-tuple-element.80), channel_id=1, source_target_pairs={{32,0},{64,32},{96,64},{128,96},{160,128},{192,160},{224,192},{256... | collective-permute-start | bytes 622088 | tf_op jit(solution)/shard_map/ppermute | solution.py:16
  43.7 24.4 %collective-permute-start.5 = (bf16[1,24,1152]{2,1,0:T(8,128)(2,1)S(1)}, bf16[1,24,1152]{2,1,0:T(8,128)(2,1)S(1)}, u32[]{:S(2)}, u32[]{:S(2)}) collective-permute-start(bf16[1,24,1152]{2,1,0:T(8,128)(2,1)S(1)} %slice.811), channel_id=1, source_target_pairs={{0,32},{32,64},{64,96},{96,128},{128,160},{160,192},{192,224},{224... | collective-permute-start | bytes 165896 | tf_op jit(solution)/shard_map/ppermute | solution.py:30
  57.4 10.8 %copy-start.2 = (f32[9,24]{1,0:T(8,128)S(1)}, f32[9,24]{1,0:T(8,128)}, u32[]{:S(2)}) copy-start(f32[9,24]{1,0:T(8,128)} %param.8) | copy-start | bytes 2596
  57.5 10.6 %collective-permute-start.4 = (bf16[9,1,1152]{2,1,0:T(2,128)(2,1)S(1)}, bf16[9,1,1152]{2,1,0:T(2,128)(2,1)S(1)}, u32[]{:S(2)}, u32[]{:S(2)}) collective-permute-start(bf16[9,1,1152]{2,1,0:T(2,128)(2,1)S(1)} %slice.812), channel_id=1, source_target_pairs={{0,1},{1,2},{2,3},{3,4},{4,5},{5,6},{6,7},{7,8},{8,9},{9,10},{10,1... | collective-permute-start | bytes 62216 | tf_op jit(solution)/shard_map/ppermute | solution.py:24
where the time goes:
time: 69.8 us; the launch traced here: 69.4 us
  starting transfers between devices  29.4 us (42%)
  waiting for transfers between devices  14.4 us (21%)
  other arithmetic  12.6 us (18%)
  local copies, waits for them, and re-layouts  9.15 us (13%)
  matrix products  3.58 us (5%)
    ppermute x2, starting transfers between devices, with_halo(): after = lax.ppermute(first, axis, down)  14.1 us
    add x2, other arithmetic, apply_taps(): total + weights[:, :, tap_index][:, :, None] * piece.astype(jnp.float32)  10.7 us
    ppermute x1, waiting for transfers between devices, shifted(): return lax.ppermute(value, axis, pairs)  8.62 us
    ppermute x1, starting transfers between devices, passed_along(): return lax.ppermute(value, axis, pairs)  8.32 us
    ppermute x2, starting transfers between devices, with_halo(): before = lax.ppermute(last, axis, up)  5.02 us
    slice x4, local copies, waits for them, and re-layouts, apply_taps(): weights[:, :, tap_index][:, :, None] * piece.astype(jnp.float32)  4.43 us
    ppermute x2, waiting for transfers between devices, with_halo(): after = lax.ppermute(first, axis, down)  3.92 us
    unnamed x9, local copies, waits for them, and re-layouts  3.48 us
  transfers between devices with their start and end apart: 6, of which 3 were waited for; matrix products, arithmetic and copies ran while one was open for 25% of the time, Pallas kernels for 0%

commit v1 on v0

v1 whole, which is shorter than its diff:
```python
import jax
import jax.numpy as jnp
import numpy as np
from jax import lax
from jax.sharding import PartitionSpec as P


def from_prev(value, axis, wrap):
    size = lax.axis_size(axis)
    pairs = [(i, (i + 1) % size) for i in range(size if wrap else size - 1)]
    return lax.ppermute(value, axis, pairs)


def from_next(value, axis, wrap):
    size = lax.axis_size(axis)
    pairs = [((i + 1) % size, i) for i in range(size if wrap else size - 1)]
    return lax.ppermute(value, axis, pairs)


def stencil_table():
    stencil = np.zeros((6, 3, 3))
    stencil[0, 1, 1] = 7.0 / 6.0
    stencil[0, 1, 0] = -1.0 / 24.0
    stencil[0, 1, 2] = -1.0 / 24.0
    stencil[0, 0, 1] = -1.0 / 24.0
    stencil[0, 2, 1] = -1.0 / 24.0
    stencil[1, 1, 2] = 0.5
    stencil[1, 1, 0] = -0.5
    stencil[2, 2, 1] = 0.5
    stencil[2, 0, 1] = -0.5
    stencil[3, 1, 2] = 0.5
    stencil[3, 1, 0] = 0.5
    stencil[3, 1, 1] = -1.0
    stencil[4, 2, 2] = 0.25
    stencil[4, 2, 0] = -0.25
    stencil[4, 0, 2] = -0.25
    stencil[4, 0, 0] = 0.25
    stencil[5, 2, 1] = 0.5
    stencil[5, 0, 1] = 0.5
    stencil[5, 1, 1] = -1.0
    return stencil


def face_tables():
    stencil = stencil_table()
    tables = np.zeros((4, 12, 6, 7, 7))
    for face, (direction, shift_row, shift_col, sign) in enumerate(
        ((0, 0, -1, 1.0), (0, 0, 0, -1.0), (1, -1, 0, 1.0), (1, 0, 0, -1.0))
    ):
        for code in range(12):
            if direction == 0:
                row_off, col_off = code // 4 - 1, code % 4 - 1
            else:
                row_off, col_off = code % 4 - 1, code // 4 - 1
            for inner_row in range(-1, 2):
                for inner_col in range(-1, 2):
                    r = row_off + inner_row + shift_row + 3
                    c = col_off + inner_col + shift_col + 3
                    tables[face, code, :, r, c] += sign * stencil[:, inner_row + 1, inner_col + 1]
    tables = tables.reshape(4, 12, 6, 49)
    used = np.nonzero(np.abs(tables).sum(axis=(0, 1, 2)) > 0)[0]
    return tables[..., used], [(int(t) // 7 - 3, int(t) % 7 - 3) for t in used]


def summed_moments(pieces, moments):
    codes = jnp.arange(12, dtype=jnp.int32)
    onehot = (pieces[..., None] == codes).astype(jnp.float32)
    return jnp.einsum("ijko,ijkm->ijom", onehot, moments, precision=lax.Precision.HIGHEST)


def local(tracer, moments, pieces, cell_area):
    rows = tracer.shape[0]
    cols = tracer.shape[1]
    tables, offsets = face_tables()

    packed = jnp.concatenate([moments, pieces.astype(jnp.float32)[..., None]], axis=-1)
    west_col = from_prev(packed[0][:, cols - 1 :], "tile", True)
    south_row = from_prev(packed[1][rows - 1 :], "panel", False)

    wide = jnp.concatenate(
        [from_prev(tracer[:, cols - 3 :], "tile", True), tracer, from_next(tracer[:, :3], "tile", True)], axis=1
    )
    padded = jnp.concatenate(
        [from_prev(wide[rows - 3 :], "panel", False), wide, from_next(wide[:3], "panel", False)], axis=0
    )

    east_in = jnp.concatenate([west_col, packed[0]], axis=1)
    north_in = jnp.concatenate([south_row, packed[1]], axis=0)
    east_sum = summed_moments(east_in[..., 6].astype(jnp.int32), east_in[..., :6])
    north_sum = summed_moments(north_in[..., 6].astype(jnp.int32), north_in[..., :6])
    is_top = lax.axis_index("panel") == lax.axis_size("panel") - 1
    last_row = jnp.arange(rows + 1) == rows
    row_mask = jnp.where(jnp.logical_and(last_row, is_top), 0.0, 1.0).astype(jnp.float32)
    north_sum = north_sum * row_mask[:, None, None, None]

    faces = jnp.stack(
        [east_sum[:, :cols], east_sum[:, 1:], north_sum[:rows], north_sum[1:]], axis=2
    )
    weights = jnp.einsum(
        "ijfcm,fcmt->ijt", faces, jnp.asarray(tables, jnp.float32), precision=lax.Precision.HIGHEST
    )
    weights = weights / cell_area[:, :, None]

    total = tracer.astype(jnp.float32)
    for tap, (dr, dc) in enumerate(offsets):
        piece = lax.slice(padded, (3 + dr, 3 + dc, 0), (3 + dr + rows, 3 + dc + cols, padded.shape[2]))
        total = total + weights[:, :, tap][:, :, None] * piece.astype(jnp.float32)
    return total.astype(jnp.bfloat16)


def solution(mesh):
    in_specs = (
        P("panel", "tile", None),
        P(None, "panel", "tile", None, None),
        P(None, "panel", "tile", None),
        P("panel", "tile"),
    )
    out_specs = P("panel", "tile", None)
    return jax.shard_map(local, mesh=mesh, in_specs=in_specs, out_specs=out_specs, check_vma=False)
```

time: 69.8 us -> 58.1 us (0.83)
  the two profiles are of different devices: /device:TPU:20 before, /device:TPU:22 now
where the time goes in v1:
time: 58.1 us; the launch traced here: 57.8 us
  starting transfers between devices  25.5 us (44%)
  other arithmetic  11.5 us (20%)
  waiting for transfers between devices  9.54 us (16%)
  local copies, waits for them, and re-layouts  5.76 us (10%)
  matrix products  5.17 us (9%)
    ppermute x4, starting transfers between devices, from_prev(): return lax.ppermute(value, axis, pairs)  13.3 us
    ppermute x2, starting transfers between devices, from_next(): return lax.ppermute(value, axis, pairs)  12.2 us
    ppermute x2, waiting for transfers between devices, from_next(): return lax.ppermute(value, axis, pairs)  7.63 us
    convert_element_type x1, other arithmetic, local(): return total.astype(jnp.bfloat16)  7.54 us
    slice x3, local copies, waits for them, and re-layouts, local(): total = total + weights[:, :, tap][:, :, None] * piece.astype(jnp.float32)  2.84 us
    dot_general x2, matrix products, summed_moments(): jnp.einsum('ijko,ijkm->ijom', onehot, moments, precision=lax.Precision.HI...  2.67 us
    dot_general x1, matrix products, local(): jnp.einsum('ijfcm,fcmt->ijt', faces, jnp.asarray(tables, jnp.float32), pr...  2.5 us
    ppermute x4, waiting for transfers between devices, from_prev(): return lax.ppermute(value, axis, pairs)  1.91 us
  transfers between devices with their start and end apart: 6, of which 2 were waited for; matrix products, arithmetic and copies ran while one was open for 21% of the time, Pallas kernels for 0%

profile of v1, /device:TPU:22, one launch (start us, length us, event | category | flops | bytes accessed | tf_op | source)
XLA Modules:
  0.0 57.8 jit_solution(12092761995015278572)
XLA Ops:
  0.0 0.0 copy-start
  0.0 0.8 %convert_bitcast_fusion = f32[2,9,24,4,1]{2,3,4,1,0:T(4,128)S(1)} fusion(s32[2,9,24,4]{2,3,1,0:T(4,128)} %param.7), kind=kLoop, calls=%fused_computation.110 | loop fusion | flops 1728 | bytes 13824 | tf_op jit(solution)/shard_map/broadcast_in_dim | solution.py:76
  0.8 1.0 %fusion.39 = (f32[9,24,4,7]{1,2,3,0:T(4,128)S(1)}, f32[9,24,4,7]{1,2,3,0:T(4,128)S(1)}) fusion(f32[2,9,24,4,6]{2,3,4,1,0:T(4,128)} %param.6, f32[2,9,24,4,1]{2,3,4,1,0:T(4,128)S(1)} %convert_bitcast_fusion), kind=kLoop, calls=%fused_computation.60 | loop fusion | flops 12096 | bytes 96768 | tf_op jit(solution)/shard_map/squeeze | solution.py:77
  1.9 0.1 slice.473
  2.0 1.9 %collective-permute-start = (f32[9,1,4,7]{1,2,3,0:T(4,128)S(1)}, f32[9,1,4,7]{1,2,3,0:T(4,128)S(1)}, u32[]{:S(2)}, u32[]{:S(2)}) collective-permute-start(f32[9,1,4,7]{1,2,3,0:T(4,128)S(1)} %slice.473), channel_id=1, source_target_pairs={{0,1},{1,2},{2,3},{3,4},{4,5},{5,6},{6,7},{7,8},{8,9},{9,10},{10,1... | collective-permute-start | bytes 3032 | tf_op jit(solution)/shard_map/ppermute | solution.py:11
  3.9 0.7 %fusion.44 = f32[1,24,4,7]{1,2,3,0:T(4,128)S(1)} fusion(f32[2,9,24,4,1]{2,3,4,1,0:T(4,128)S(1)} %convert_bitcast_fusion, f32[2,9,24,4,6]{2,3,4,1,0:T(4,128)} %param.6), kind=kLoop, calls=%fused_computation.116 | loop fusion | flops 672 | bytes 51072 | tf_op jit(solution)/shard_map/slice | solution.py:78
  4.6 5.6 %collective-permute-start.1 = (f32[1,24,4,7]{1,2,3,0:T(4,128)S(1)}, f32[1,24,4,7]{1,2,3,0:T(4,128)S(1)}, u32[]{:S(2)}, u32[]{:S(2)}) collective-permute-start(f32[1,24,4,7]{1,2,3,0:T(4,128)S(1)} %fusion.44), channel_id=1, source_target_pairs={{0,32},{32,64},{64,96},{96,128},{128,160},{160,192},{192,224},{224... | collective-permute-start | bytes 8072 | tf_op jit(solution)/shard_map/ppermute | solution.py:11
  10.3 1.1 %fusion.45 = (bf16[9,3,1152]{2,1,0:T(4,128)(2,1)S(1)}, bf16[9,3,1152]{2,1,0:T(4,128)(2,1)S(1)}) fusion(bf16[9,24,1152]{2,1,0:T(8,128)(2,1)} %param.5), kind=kLoop, calls=%fused_computation.120 | loop fusion | bytes 248832 | tf_op jit(solution)/shard_map/slice | solution.py:81
  11.3 2.4 %collective-permute-start.2 = (bf16[9,3,1152]{2,1,0:T(4,128)(2,1)S(1)}, bf16[9,3,1152]{2,1,0:T(4,128)(2,1)S(1)}, u32[]{:S(2)}, u32[]{:S(2)}) collective-permute-start(bf16[9,3,1152]{2,1,0:T(4,128)(2,1)S(1)} %get-tuple-element.59), channel_id=1, source_target_pairs={{0,1},{1,2},{2,3},{3,4},{4,5},{5,6},{6,7},{7,8},{8,9},{9,10},{10,1... | collective-permute-start | bytes 186632 | tf_op jit(solution)/shard_map/ppermute | solution.py:11
  13.7 9.7 %collective-permute-start.3 = (bf16[9,3,1152]{2,1,0:T(4,128)(2,1)S(1)}, bf16[9,3,1152]{2,1,0:T(4,128)(2,1)S(1)}, u32[]{:S(2)}, u32[]{:S(2)}) collective-permute-start(bf16[9,3,1152]{2,1,0:T(4,128)(2,1)S(1)} %get-tuple-element.58), channel_id=1, source_target_pairs={{1,0},{2,1},{3,2},{4,3},{5,4},{6,5},{7,6},{8,7},{9,8},{10,9},{11,1... | collective-permute-start | bytes 186632 | tf_op jit(solution)/shard_map/ppermute | solution.py:17
  23.5 0.0 copy-done
  23.6 0.0 collective-permute-done
  23.6 0.1 pad_maximum_fusion.8
  23.7 0.3 copy.33
  24.0 0.1 fusion.42
  24.1 0.2 copy.27
  24.3 1.3 %fusion.35 = f32[9,25,12,6]{2,3,1,0:T(8,128)S(1)} fusion(f32[9,25,4,6]{3,2,1,0:T(4,128)S(1)} %copy.33, s32[9,25,4]{2,1,0:T(8,128)S(1)} %copy.27), kind=kOutput, calls=%fused_computation.49 | convolution fusion | flops 788400 | bytes 90000 | tf_op jit(solution)/shard_map/ijko,ijkm->ijom/dot_general | solution.py:68
  25.6 0.0 collective-permute-done.1
  25.6 0.3 copy.34
  26.0 0.1 copy.29
  26.1 1.4 %convolution_multiply_fusion = f32[10,24,12,6]{2,3,1,0:T(8,128)S(1)} fusion(f32[10,24,4,6]{3,2,1,0:T(4,128)S(1)} %copy.34, f32[10]{0:T(128)S(1)} %and_select_fusion, s32[10,24,4]{2,1,0:T(8,128)S(1)} %copy.29), kind=kOutput, calls=%fused_computation.3 | convolution fusion | flops 858240 | bytes 96040 | tf_op jit(solution)/shard_map/ijko,ijkm->ijom/dot_general | solution.py:68
  27.5 0.5 slice_bitcast_fusion.1
  28.0 0.0 copy-start.1
  28.0 0.0 copy-start.2
  28.0 0.7 %pad_maximum_fusion = f32[9,24,4,12,6]{3,4,1,0,2:T(8,128)S(1)} fusion(f32[9,24,1,12,6]{3,4,1,0,2:T(8,128)S(1)} %get-tuple-element.51, f32[9,24,1,12,6]{3,4,1,0,2:T(8,128)S(1)} %get-tuple-element.50, f32[9,24,1,12,6]{3,4,1,0,2:T(8,128)S(1)} %get-tuple-element.62, f32[9,24,1,12,6]{3,4,1,0,2:T(8,128)S(1)} %get-tuple-element.63), kind=kLoop, calls=%fused_computation | loop fusion | flops 186624 | bytes 497664 | tf_op jit(solution)/shard_map/stack | solution.py:96
  28.8 0.2 copy-done.1
  28.9 0.0 copy-done.2
  28.9 2.5 %fusion.5 = f32[9,24,45]{2,1,0:T(8,128)S(1)} fusion(f32[4,12,6,45,1]{3,1,2,0,4:T(8,128)S(1)} %copy-done.1, f32[9,24,4,12,6]{3,4,1,0,2:T(8,128)S(1)} %pad_maximum_fusion, f32[9,24]{1,0:T(8,128)S(1)} %copy-done.2), kind=kOutput, calls=%fused_computation.7 | convolution fusion | flops 33602040 | bytes 340416 | tf_op jit(solution)/shard_map/ijfcm,fcmt->ijt/dot_general | solution.py:99
  31.4 1.1 %slice_reduce_fusion.44 = (f32[9,24]{1,0:T(8,128)S(1)}, f32[9,24]{1,0:T(8,128)S(1)}, f32[9,24]{1,0:T(8,128)S(1)}, f32[9,24]{1,0:T(8,128)S(1)}, f32[9,24]{1,0:T(8...) fusion(f32[9,24,45]{2,1,0:T(8,128)S(1)} %fusion.5), kind=kLoop, calls=%fused_computation.108 | loop fusion | bytes 32832 | tf_op jit(solution)/shard_map/slice | solution.py:107
  32.6 1.2 %slice_reduce_fusion.43 = (f32[9,24]{1,0:T(8,128)S(1)}, f32[9,24]{1,0:T(8,128)S(1)}, f32[9,24]{1,0:T(8,128)S(1)}, f32[9,24]{1,0:T(8,128)S(1)}, f32[9,24]{1,0:T(8...) fusion(f32[9,24,45]{2,1,0:T(8,128)S(1)} %fusion.5), kind=kLoop, calls=%fused_computation.107 | loop fusion | bytes 32832 | tf_op jit(solution)/shard_map/slice | solution.py:107
  33.8 0.5 slice_reduce_fusion.42
  34.3 0.0 collective-permute-done.2
  34.3 0.0 collective-permute-done.3
  34.3 0.2 pad_maximum_fusion.5
  34.5 3.4 %collective-permute-start.4 = (bf16[3,30,1152]{2,1,0:T(8,128)(2,1)S(1)}, bf16[3,30,1152]{2,1,0:T(8,128)(2,1)S(1)}, u32[]{:S(2)}, u32[]{:S(2)}) collective-permute-start(bf16[3,30,1152]{2,1,0:T(8,128)(2,1)S(1)} %get-tuple-element.56), channel_id=1, source_target_pairs={{0,32},{32,64},{64,96},{96,128},{128,160},{160,192},{192,224},{224... | collective-permute-start | bytes 622088 | tf_op jit(solution)/shard_map/ppermute | solution.py:11
  37.9 2.4 %collective-permute-start.5 = (bf16[3,30,1152]{2,1,0:T(8,128)(2,1)S(1)}, bf16[3,30,1152]{2,1,0:T(8,128)(2,1)S(1)}, u32[]{:S(2)}, u32[]{:S(2)}) collective-permute-start(bf16[3,30,1152]{2,1,0:T(8,128)(2,1)S(1)} %get-tuple-element.57), channel_id=1, source_target_pairs={{32,0},{64,32},{96,64},{128,96},{160,128},{192,160},{224,192},{256... | collective-permute-start | bytes 622088 | tf_op jit(solution)/shard_map/ppermute | solution.py:17
  40.3 0.1 constant_dynamic-update-slice_fusion
  40.4 1.9 %collective-permute-done.4 = bf16[3,30,1152]{2,1,0:T(8,128)(2,1)S(1)} collective-permute-done((bf16[3,30,1152]{2,1,0:T(8,128)(2,1)S(1)}, bf16[3,30,1152]{2,1,0:T(8,128)(2,1)S(1)}, u32[]{:S(2)}, u32[]{:S(2)}) %collective-permute-start.4) | collective-permute-done | bytes 207392 | tf_op jit(solution)/shard_map/ppermute | solution.py:11
  42.3 7.6 %collective-permute-done.5 = bf16[3,30,1152]{2,1,0:T(8,128)(2,1)S(1)} collective-permute-done((bf16[3,30,1152]{2,1,0:T(8,128)(2,1)S(1)}, bf16[3,30,1152]{2,1,0:T(8,128)(2,1)S(1)}, u32[]{:S(2)}, u32[]{:S(2)}) %collective-permute-start.5) | collective-permute-done | bytes 207392 | tf_op jit(solution)/shard_map/ppermute | solution.py:17
  49.9 0.3 maximum_maximum_fusion
  50.2 7.5 %add_convert_fusion = bf16[9,24,1152]{2,1,0:T(8,128)(2,1)} fusion(bf16[9,24,1152]{2,1,0:T(8,128)(2,1)S(1)} %copy-done, bf16[9,3,1152]{2,1,0:T(4,128)(2,1)S(1)} %collective-permute-done.2, bf16[12,30,1152]{2,1,0:T(8,128)(2,1)S(1)} %get-tuple-element.55, bf16[9,27,1152]{2,1,0:T(8,128)(2,1)S(1)} %constant_dynamic-update-slice_fusion, ...), kind=kLoop, calls=%fused_computation.33 | loop fusion | flops 36080640 | bytes 21500640 | tf_op jit(solution)/shard_map/convert_element_type | solution.py:108
  (4 shorter events, 0.1 us)
Async XLA Ops:
  0.0 23.5 %copy-start = (bf16[9,24,1152]{2,1,0:T(8,128)(2,1)S(1)}, bf16[9,24,1152]{2,1,0:T(8,128)(2,1)}, u32[]{:S(2)}) copy-start(bf16[9,24,1152]{2,1,0:T(8,128)(2,1)} %param.5) | copy-start | bytes 1492996
  2.0 21.6 %collective-permute-start = (f32[9,1,4,7]{1,2,3,0:T(4,128)S(1)}, f32[9,1,4,7]{1,2,3,0:T(4,128)S(1)}, u32[]{:S(2)}, u32[]{:S(2)}) collective-permute-start(f32[9,1,4,7]{1,2,3,0:T(4,128)S(1)} %slice.473), channel_id=1, source_target_pairs={{0,1},{1,2},{2,3},{3,4},{4,5},{5,6},{6,7},{7,8},{8,9},{9,10},{10,1... | collective-permute-start | bytes 3032 | tf_op jit(solution)/shard_map/ppermute | solution.py:11
  4.6 20.9 %collective-permute-start.1 = (f32[1,24,4,7]{1,2,3,0:T(4,128)S(1)}, f32[1,24,4,7]{1,2,3,0:T(4,128)S(1)}, u32[]{:S(2)}, u32[]{:S(2)}) collective-permute-start(f32[1,24,4,7]{1,2,3,0:T(4,128)S(1)} %fusion.44), channel_id=1, source_target_pairs={{0,32},{32,64},{64,96},{96,128},{128,160},{160,192},{192,224},{224... | collective-permute-start | bytes 8072 | tf_op jit(solution)/shard_map/ppermute | solution.py:11
  11.3 23.0 %collective-permute-start.2 = (bf16[9,3,1152]{2,1,0:T(4,128)(2,1)S(1)}, bf16[9,3,1152]{2,1,0:T(4,128)(2,1)S(1)}, u32[]{:S(2)}, u32[]{:S(2)}) collective-permute-start(bf16[9,3,1152]{2,1,0:T(4,128)(2,1)S(1)} %get-tuple-element.59), channel_id=1, source_target_pairs={{0,1},{1,2},{2,3},{3,4},{4,5},{5,6},{6,7},{7,8},{8,9},{9,10},{10,1... | collective-permute-start | bytes 186632 | tf_op jit(solution)/shard_map/ppermute | solution.py:11
  13.7 20.6 %collective-permute-start.3 = (bf16[9,3,1152]{2,1,0:T(4,128)(2,1)S(1)}, bf16[9,3,1152]{2,1,0:T(4,128)(2,1)S(1)}, u32[]{:S(2)}, u32[]{:S(2)}) collective-permute-start(bf16[9,3,1152]{2,1,0:T(4,128)(2,1)S(1)} %get-tuple-element.58), channel_id=1, source_target_pairs={{1,0},{2,1},{3,2},{4,3},{5,4},{6,5},{7,6},{8,7},{9,8},{10,9},{11,1... | collective-permute-start | bytes 186632 | tf_op jit(solution)/shard_map/ppermute | solution.py:17
  28.0 0.9 %copy-start.1 = (f32[4,12,6,45,1]{3,1,2,0,4:T(8,128)S(1)}, f32[4,12,6,45,1]{3,1,2,0,4:T(8,128)}, u32[]{:S(2)}) copy-start(f32[4,12,6,45,1]{3,1,2,0,4:T(8,128)} %constant.21) | copy-start | bytes 155524
  28.0 0.9 %copy-start.2 = (f32[9,24]{1,0:T(8,128)S(1)}, f32[9,24]{1,0:T(8,128)}, u32[]{:S(2)}) copy-start(f32[9,24]{1,0:T(8,128)} %param.8) | copy-start | bytes 2596
  34.5 7.8 %collective-permute-start.4 = (bf16[3,30,1152]{2,1,0:T(8,128)(2,1)S(1)}, bf16[3,30,1152]{2,1,0:T(8,128)(2,1)S(1)}, u32[]{:S(2)}, u32[]{:S(2)}) collective-permute-start(bf16[3,30,1152]{2,1,0:T(8,128)(2,1)S(1)} %get-tuple-element.56), channel_id=1, source_target_pairs={{0,32},{32,64},{64,96},{96,128},{128,160},{160,192},{192,224},{224... | collective-permute-start | bytes 622088 | tf_op jit(solution)/shard_map/ppermute | solution.py:11
  37.9 12.0 %collective-permute-start.5 = (bf16[3,30,1152]{2,1,0:T(8,128)(2,1)S(1)}, bf16[3,30,1152]{2,1,0:T(8,128)(2,1)S(1)}, u32[]{:S(2)}, u32[]{:S(2)}) collective-permute-start(bf16[3,30,1152]{2,1,0:T(8,128)(2,1)S(1)} %get-tuple-element.57), channel_id=1, source_target_pairs={{32,0},{64,32},{96,64},{128,96},{160,128},{192,160},{224,192},{256... | collective-permute-start | bytes 622088 | tf_op jit(solution)/shard_map/ppermute | solution.py:17

commit v2 on v1

--- a/solution.py
+++ b/solution.py
@@ -68,26 +68,70 @@
     return jnp.einsum("ijko,ijkm->ijom", onehot, moments, precision=lax.Precision.HIGHEST)
 
 
+def split3(value):
+    hi = value.astype(jnp.bfloat16)
+    rest = value - hi.astype(jnp.float32)
+    mid = rest.astype(jnp.bfloat16)
+    lo = (rest - mid.astype(jnp.float32)).astype(jnp.bfloat16)
+    return jnp.concatenate([hi, mid, lo], axis=-1)
+
+
+def join3(value, count):
+    parts = [value[..., k * count : (k + 1) * count].astype(jnp.float32) for k in range(3)]
+    return (parts[0] + parts[1]) + parts[2]
+
+
+def pack_weights(moments, pieces, width):
+    lead = moments.shape[:-2]
+    flat = moments.reshape(lead + (moments.shape[-2] * moments.shape[-1],))
+    packed = jnp.concatenate([split3(flat), pieces.astype(jnp.bfloat16)], axis=-1)
+    return jnp.pad(packed, [(0, 0)] * len(lead) + [(0, width - packed.shape[-1])])
+
+
+def unpack_weights(packed, n_piece, n_moment):
+    count = n_piece * n_moment
+    lead = packed.shape[:-1]
+    moments = join3(packed[..., : 3 * count], count).reshape(lead + (n_piece, n_moment))
+    pieces = packed[..., 3 * count : 3 * count + n_piece].astype(jnp.int32)
+    return moments, pieces
+
+
 def local(tracer, moments, pieces, cell_area):
     rows = tracer.shape[0]
     cols = tracer.shape[1]
+    width = tracer.shape[2]
+    n_piece = moments.shape[3]
+    n_moment = moments.shape[4]
     tables, offsets = face_tables()
 
-    packed = jnp.concatenate([moments, pieces.astype(jnp.float32)[..., None]], axis=-1)
-    west_col = from_prev(packed[0][:, cols - 1 :], "tile", True)
-    south_row = from_prev(packed[1][rows - 1 :], "panel", False)
+    west_pack = pack_weights(moments[0][:, cols - 1], pieces[0][:, cols - 1], width)[:, None]
+    south_pack = pack_weights(moments[1][rows - 1], pieces[1][rows - 1], width)[None]
+    from_west = from_prev(jnp.concatenate([tracer[:, cols - 3 :], west_pack], axis=1), "tile", True)
+    from_east = from_next(tracer[:, :3], "tile", True)
+    from_south = from_prev(jnp.concatenate([tracer[rows - 3 :], south_pack], axis=0), "panel", False)
+    from_north = from_next(tracer[:3], "panel", False)
 
-    wide = jnp.concatenate(
-        [from_prev(tracer[:, cols - 3 :], "tile", True), tracer, from_next(tracer[:, :3], "tile", True)], axis=1
+    west_halo = from_west[:, :3]
+    corners_up = jnp.concatenate([west_halo[rows - 3 :], from_east[rows - 3 :]], axis=1)
+    corners_down = jnp.concatenate([west_halo[:3], from_east[:3]], axis=1)
+    south_corners = from_prev(corners_up, "panel", False)
+    north_corners = from_next(corners_down, "panel", False)
+
+    wide = jnp.concatenate([west_halo, tracer, from_east], axis=1)
+    south_rows = jnp.concatenate([south_corners[:, :3], from_south[:3], south_corners[:, 3:]], axis=1)
+    north_rows = jnp.concatenate([north_corners[:, :3], from_north, north_corners[:, 3:]], axis=1)
+    padded = jnp.concatenate([south_rows, wide, north_rows], axis=0)
+
+    west_m, west_p = unpack_weights(from_west[:, 3], n_piece, n_moment)
+    south_m, south_p = unpack_weights(from_south[3], n_piece, n_moment)
+    east_sum = summed_moments(
+        jnp.concatenate([west_p[:, None], pieces[0]], axis=1),
+        jnp.concatenate([west_m[:, None], moments[0]], axis=1),
     )
-    padded = jnp.concatenate(
-        [from_prev(wide[rows - 3 :], "panel", False), wide, from_next(wide[:3], "panel", False)], axis=0
+    north_sum = summed_moments(
+        jnp.concatenate([south_p[None], pieces[1]], axis=0),
+        jnp.concatenate([south_m[None], moments[1]], axis=0),
     )
-
-    east_in = jnp.concatenate([west_col, packed[0]], axis=1)
-    north_in = jnp.concatenate([south_row, packed[1]], axis=0)
-    east_sum = summed_moments(east_in[..., 6].astype(jnp.int32), east_in[..., :6])
-    north_sum = summed_moments(north_in[..., 6].astype(jnp.int32), north_in[..., :6])
     is_top = lax.axis_index("panel") == lax.axis_size("panel") - 1
     last_row = jnp.arange(rows + 1) == rows
     row_mask = jnp.where(jnp.logical_and(last_row, is_top), 0.0, 1.0).astype(jnp.float32)
@@ -103,7 +147,7 @@
 
     total = tracer.astype(jnp.float32)
     for tap, (dr, dc) in enumerate(offsets):
-        piece = lax.slice(padded, (3 + dr, 3 + dc, 0), (3 + dr + rows, 3 + dc + cols, padded.shape[2]))
+        piece = lax.slice(padded, (3 + dr, 3 + dc, 0), (3 + dr + rows, 3 + dc + cols, width))
         total = total + weights[:, :, tap][:, :, None] * piece.astype(jnp.float32)
     return total.astype(jnp.bfloat16)
 

time: 58.1 us -> 64.5 us (1.11)
  the two profiles are of different devices: /device:TPU:22 before, /device:TPU:233 now
where the time goes in v2:
time: 64.5 us; the launch traced here: 64 us
  starting transfers between devices  29.4 us (46%)
  other arithmetic  11.8 us (18%)
  local copies, waits for them, and re-layouts  11.4 us (18%)
  matrix products  6.06 us (9%)
  waiting for transfers between devices  4.97 us (8%)
    ppermute x3, starting transfers between devices, from_next(): return lax.ppermute(value, axis, pairs)  17.8 us
    ppermute x3, starting transfers between devices, from_prev(): return lax.ppermute(value, axis, pairs)  11.6 us
    convert_element_type x1, other arithmetic, local(): return total.astype(jnp.bfloat16)  7.53 us
    ppermute x3, waiting for transfers between devices, from_prev(): return lax.ppermute(value, axis, pairs)  4.96 us
    dot_general x2, matrix products, summed_moments(): jnp.einsum('ijko,ijkm->ijom', onehot, moments, precision=lax.Precision.HI...  3.56 us
    slice x3, local copies, waits for them, and re-layouts, local(): total = total + weights[:, :, tap][:, :, None] * piece.astype(jnp.float32)  2.84 us
    dot_general x1, matrix products, local(): jnp.einsum('ijfcm,fcmt->ijt', faces, jnp.asarray(tables, jnp.float32), pr...  2.5 us
    slice x3, local copies, waits for them, and re-layouts, local(): moments[1][rows - 1]  1.74 us
  transfers between devices with their start and end apart: 6, of which 1 were waited for; matrix products, arithmetic and copies ran while one was open for 26% of the time, Pallas kernels for 0%

profile of v2, /device:TPU:233, one launch (start us, length us, event | category | flops | bytes accessed | tf_op | source)
XLA Modules:
  0.0 64.0 jit_solution(1969137427892484087)
XLA Ops:
  0.0 1.0 %fusion.68 = (f32[1,9,24,4,6]{2,3,4,1,0:T(4,128)S(1)}, f32[1,9,24,4,6]{2,3,4,1,0:T(4,128)S(1)}) fusion(f32[2,9,24,4,6]{2,3,4,1,0:T(4,128)} %param.6), kind=kLoop, calls=%fused_computation.151 | loop fusion | bytes 82944 | tf_op jit(solution)/shard_map/slice | solution.py:108
  1.0 0.3 copy.152
  1.4 0.1 reshape_squeeze.6
  1.4 0.7 %slice_bitcast_fusion.4 = (s32[9,24,4]{1,2,0:T(4,128)S(1)}, s32[9,24,4]{1,2,0:T(4,128)S(1)}) fusion(s32[2,9,24,4]{2,3,1,0:T(4,128)} %param.7), kind=kLoop, calls=%fused_computation.129 | loop fusion | bytes 13824 | tf_op jit(solution)/shard_map/squeeze | solution.py:108
  2.2 0.1 slice_convert_fusion
  2.3 0.1 copy.133
  2.4 0.1 copy.134
  2.5 0.1 fusion.59
  2.6 1.1 %fusion.67 = (bf16[9,3,1152]{2,1,0:T(4,128)(2,1)S(1)}, bf16[9,3,1152]{2,1,0:T(4,128)(2,1)S(1)}) fusion(bf16[9,24,1152]{2,1,0:T(8,128)(2,1)} %param.5), kind=kLoop, calls=%fused_computation.150 | loop fusion | bytes 248832 | tf_op jit(solution)/shard_map/slice | solution.py:110
  3.7 0.1 pad_maximum_fusion.3
  3.8 6.6 %collective-permute-start = (bf16[9,4,1152]{2,1,0:T(4,128)(2,1)S(1)}, bf16[9,4,1152]{2,1,0:T(4,128)(2,1)S(1)}, u32[]{:S(2)}, u32[]{:S(2)}) collective-permute-start(bf16[9,4,1152]{2,1,0:T(4,128)(2,1)S(1)} %pad_maximum_fusion.3), channel_id=1, source_target_pairs={{0,1},{1,2},{2,3},{3,4},{4,5},{5,6},{6,7},{7,8},{8,9},{9,10},{10,1... | collective-permute-start | bytes 248840 | tf_op jit(solution)/shard_map/ppermute | solution.py:11
  10.4 0.7 %slice.452 = f32[1,1,24,4,6]{2,3,4,1,0:T(4,128)S(1)} slice(f32[2,9,24,4,6]{2,3,4,1,0:T(4,128)} %param.6), slice={[1:2], [8:9], [0:24], [0:4], [0:6]} | slice | bytes 4608 | tf_op jit(solution)/shard_map/slice | solution.py:108
  11.1 0.7 %fusion.62 = bf16[24,4]{0,1:T(4,128)(2,1)S(1)} fusion(s32[2,9,24,4]{2,3,1,0:T(4,128)} %param.7), kind=kLoop, calls=%fused_computation.144 | loop fusion | flops 96 | bytes 576 | tf_op jit(solution)/shard_map/convert_element_type | solution.py:87
  11.8 0.1 copy.142
  11.9 0.1 copy.143
  12.0 0.1 copy.144
  12.1 0.1 copy.145
  12.2 0.1 fusion.55
  12.3 0.7 %pad_maximum_fusion.2 = bf16[4,24,1152]{2,1,0:T(8,128)(2,1)} fusion(bf16[1,24,1152]{2,1,0:T(8,128)(2,1)S(1)} %fusion.55, bf16[3,24,1152]{2,1,0:T(8,128)(2,1)S(1)} %get-tuple-element.56), kind=kLoop, calls=%fused_computation.58 | loop fusion | flops 110592 | bytes 442368 | tf_op jit(solution)/shard_map/concatenate | solution.py:111
  13.0 3.1 %collective-permute-start.1 = (bf16[4,24,1152]{2,1,0:T(8,128)(2,1)}, bf16[4,24,1152]{2,1,0:T(8,128)(2,1)S(1)}, u32[]{:S(2)}, u32[]{:S(2)}) collective-permute-start(bf16[4,24,1152]{2,1,0:T(8,128)(2,1)} %pad_maximum_fusion.2), channel_id=1, source_target_pairs={{0,32},{32,64},{64,96},{96,128},{128,160},{160,192},{192,224},{224... | collective-permute-start | bytes 663560 | tf_op jit(solution)/shard_map/ppermute | solution.py:11
  16.1 1.9 %collective-permute-start.2 = (bf16[9,3,1152]{2,1,0:T(4,128)(2,1)S(1)}, bf16[9,3,1152]{2,1,0:T(4,128)(2,1)S(1)}, u32[]{:S(2)}, u32[]{:S(2)}) collective-permute-start(bf16[9,3,1152]{2,1,0:T(4,128)(2,1)S(1)} %get-tuple-element.58), channel_id=1, source_target_pairs={{1,0},{2,1},{3,2},{4,3},{5,4},{6,5},{7,6},{8,7},{9,8},{10,9},{11,1... | collective-permute-start | bytes 186632 | tf_op jit(solution)/shard_map/ppermute | solution.py:17
  18.0 6.4 %collective-permute-start.5 = (bf16[3,24,1152]{2,1,0:T(8,128)(2,1)S(1)}, bf16[3,24,1152]{2,1,0:T(8,128)(2,1)}, u32[]{:S(2)}, u32[]{:S(2)}) collective-permute-start(bf16[3,24,1152]{2,1,0:T(8,128)(2,1)S(1)} %get-tuple-element.57), channel_id=1, source_target_pairs={{32,0},{64,32},{96,64},{128,96},{160,128},{192,160},{224,192},{256... | collective-permute-start | bytes 497672 | tf_op jit(solution)/shard_map/ppermute | solution.py:17
  24.5 0.3 copy.156
  25.0 0.1 slice_convert_fusion.1
  25.1 0.1 convert_add_fusion.2
  25.2 0.1 copy.158
  25.2 0.1 copy.138
  25.4 0.1 pad_add_fusion.1
  25.4 0.8 %copy.139 = s32[9,25,4]{2,1,0:T(8,128)} copy(s32[9,25,4]{1,2,0:T(4,128)S(1)} %pad_add_fusion.1) | data formatting | bytes 7200 | tf_op jit(solution)/shard_map/concatenate | solution.py:128
  26.2 0.7 %broadcast_in_dim_reshape.6 = f32[9,1,4,6]{3,2,0,1:T(4,128)} reshape(f32[9,24]{1,0:T(8,128)S(1)} %convert_add_fusion.2) | data formatting | bytes 1728 | tf_op jit(solution)/shard_map/broadcast_in_dim;reshape | solution.py:129
  27.0 9.5 %collective-permute-start.4 = (bf16[3,6,1152]{2,1,0:T(8,128)(2,1)S(1)}, bf16[3,6,1152]{2,1,0:T(8,128)(2,1)S(1)}, u32[]{:S(2)}, u32[]{:S(2)}) collective-permute-start(bf16[3,6,1152]{2,1,0:T(8,128)(2,1)S(1)} %pad_maximum_fusion.5), channel_id=1, source_target_pairs={{32,0},{64,32},{96,64},{128,96},{160,128},{192,160},{224,192},{256... | collective-permute-start | bytes 124424 | tf_op jit(solution)/shard_map/ppermute | solution.py:17
  36.6 1.9 %collective-permute-start.3 = (bf16[3,6,1152]{2,1,0:T(8,128)(2,1)S(1)}, bf16[3,6,1152]{2,1,0:T(8,128)(2,1)S(1)}, u32[]{:S(2)}, u32[]{:S(2)}) collective-permute-start(bf16[3,6,1152]{2,1,0:T(8,128)(2,1)S(1)} %pad_maximum_fusion.4), channel_id=1, source_target_pairs={{0,32},{32,64},{64,96},{96,128},{128,160},{160,192},{192,224},{224... | collective-permute-start | bytes 124424 | tf_op jit(solution)/shard_map/ppermute | solution.py:11
  38.5 2.2 %fusion.38 = f32[9,25,12,6]{2,3,1,0:T(8,128)S(1)} fusion(f32[9,24,4,6]{3,2,1,0:T(4,128)S(1)} %bitcast.51, f32[9,1,4,6]{3,2,1,0:T(4,128)} %bitcast.57, s32[9,25,4]{2,1,0:T(8,128)} %copy.139), kind=kOutput, calls=%fused_computation.51 | convolution fusion | flops 793800 | bytes 90000 | tf_op jit(solution)/shard_map/ijko,ijkm->ijom/dot_general | solution.py:68
  40.7 5.0 %collective-permute-done.3 = bf16[3,6,1152]{2,1,0:T(8,128)(2,1)S(1)} collective-permute-done((bf16[3,6,1152]{2,1,0:T(8,128)(2,1)S(1)}, bf16[3,6,1152]{2,1,0:T(8,128)(2,1)S(1)}, u32[]{:S(2)}, u32[]{:S(2)}) %collective-permute-start.3) | collective-permute-done | bytes 41504 | tf_op jit(solution)/shard_map/ppermute | solution.py:11
  45.7 0.6 fusion.71
  46.3 0.2 copy.155
  46.6 0.1 copy.147
  46.7 0.1 copy.149
  46.9 1.4 %convolution_multiply_fusion = f32[10,24,12,6]{2,3,1,0:T(8,128)S(1)} fusion(f32[9,24,4,6]{3,2,1,0:T(4,128)S(1)} %bitcast.52, f32[1,24,4,6]{3,2,1,0:T(4,128)S(1)} %copy.149, f32[10]{0:T(128)S(1)} %and_select_fusion, s32[10,24,4]{2,1,0:T(8,128)S(1)} %copy.147), kind=kOutput, calls=%fused_computation.3 | convolution fusion | flops 864000 | bytes 96040 | tf_op jit(solution)/shard_map/ijko,ijkm->ijom/dot_general | solution.py:68
  48.2 0.5 slice_bitcast_fusion.1
  48.8 0.7 %pad_maximum_fusion = f32[9,24,4,12,6]{3,4,1,0,2:T(8,128)S(1)} fusion(f32[9,24,1,12,6]{3,4,1,0,2:T(8,128)S(1)} %get-tuple-element.51, f32[9,24,1,12,6]{3,4,1,0,2:T(8,128)S(1)} %get-tuple-element.50, f32[9,24,1,12,6]{3,4,1,0,2:T(8,128)S(1)} %get-tuple-element.78, f32[9,24,1,12,6]{3,4,1,0,2:T(8,128)S(1)} %get-tuple-element.79), kind=kLoop, calls=%fused_computation | loop fusion | flops 186624 | bytes 497664 | tf_op jit(solution)/shard_map/stack | solution.py:140
  49.5 0.2 copy-done.2
  49.7 2.5 %fusion.5 = f32[9,24,45]{2,1,0:T(8,128)S(1)} fusion(f32[4,12,6,45,1]{3,1,2,0,4:T(8,128)S(1)} %copy-done.2, f32[9,24,4,12,6]{3,4,1,0,2:T(8,128)S(1)} %pad_maximum_fusion, f32[9,24]{1,0:T(8,128)S(1)} %copy-done.4), kind=kOutput, calls=%fused_computation.7 | convolution fusion | flops 33602040 | bytes 340416 | tf_op jit(solution)/shard_map/ijfcm,fcmt->ijt/dot_general | solution.py:143
  52.2 1.1 %slice_reduce_fusion.44 = (f32[9,24]{1,0:T(8,128)S(1)}, f32[9,24]{1,0:T(8,128)S(1)}, f32[9,24]{1,0:T(8,128)S(1)}, f32[9,24]{1,0:T(8,128)S(1)}, f32[9,24]{1,0:T(8...) fusion(f32[9,24,45]{2,1,0:T(8,128)S(1)} %fusion.5), kind=kLoop, calls=%fused_computation.103 | loop fusion | bytes 32832 | tf_op jit(solution)/shard_map/slice | solution.py:151
  53.3 0.5 slice_reduce_fusion.42
  53.9 1.2 %slice_reduce_fusion.43 = (f32[9,24]{1,0:T(8,128)S(1)}, f32[9,24]{1,0:T(8,128)S(1)}, f32[9,24]{1,0:T(8,128)S(1)}, f32[9,24]{1,0:T(8,128)S(1)}, f32[9,24]{1,0:T(8...) fusion(f32[9,24,45]{2,1,0:T(8,128)S(1)} %fusion.5), kind=kLoop, calls=%fused_computation.102 | loop fusion | bytes 32832 | tf_op jit(solution)/shard_map/slice | solution.py:151
  55.1 1.4 %maximum_maximum_fusion = (bf16[12,30,1152]{2,1,0:T(8,128)(2,1)S(1)}, bf16[12,30,1152]{2,1,0:T(8,128)(2,1)S(1)}) fusion(bf16[9,3,1152]{2,1,0:T(4,128)(2,1)S(1)} %collective-permute-done.2, bf16[9,24,1152]{2,1,0:T(8,128)(2,1)S(1)} %copy-done, bf16[9,3,1152]{2,1,0:T(4,128)(2,1)S(1)} %bitcast.48, bf16[3,3,1152]{2,1,0:T(4,128)(2,1)S(1)} %copy-done.3, ...), kind=kLoop, calls=%fused_computation.38 | loop fusion | flops 9953280 | bytes 2695680 | tf_op jit(solution)/shard_map/concatenate | solution.py:123
  56.5 7.5 %add_convert_fusion = bf16[9,24,1152]{2,1,0:T(8,128)(2,1)} fusion(bf16[9,24,1152]{2,1,0:T(8,128)(2,1)S(1)} %copy-done, bf16[9,3,1152]{2,1,0:T(4,128)(2,1)S(1)} %bitcast.49, bf16[12,30,1152]{2,1,0:T(8,128)(2,1)S(1)} %get-tuple-element.55, bf16[9,27,1152]{2,1,0:T(8,128)(2,1)S(1)} %constant_dynamic-update-slice_fusion, ...), kind=kLoop, calls=%fused_computation.33 | loop fusion | flops 36080640 | bytes 21500640 | tf_op jit(solution)/shard_map/convert_element_type | solution.py:152
  (38 shorter events, 0.5 us)
Async XLA Ops:
  0.0 11.8 %copy-start = (bf16[9,24,1152]{2,1,0:T(8,128)(2,1)S(1)}, bf16[9,24,1152]{2,1,0:T(8,128)(2,1)}, u32[]{:S(2)}) copy-start(bf16[9,24,1152]{2,1,0:T(8,128)(2,1)} %param.5) | copy-start | bytes 1492996
  3.8 21.1 %collective-permute-start = (bf16[9,4,1152]{2,1,0:T(4,128)(2,1)S(1)}, bf16[9,4,1152]{2,1,0:T(4,128)(2,1)S(1)}, u32[]{:S(2)}, u32[]{:S(2)}) collective-permute-start(bf16[9,4,1152]{2,1,0:T(4,128)(2,1)S(1)} %pad_maximum_fusion.3), channel_id=1, source_target_pairs={{0,1},{1,2},{2,3},{3,4},{4,5},{5,6},{6,7},{7,8},{8,9},{9,10},{10,1... | collective-permute-start | bytes 248840 | tf_op jit(solution)/shard_map/ppermute | solution.py:11
  13.0 33.3 %collective-permute-start.1 = (bf16[4,24,1152]{2,1,0:T(8,128)(2,1)}, bf16[4,24,1152]{2,1,0:T(8,128)(2,1)S(1)}, u32[]{:S(2)}, u32[]{:S(2)}) collective-permute-start(bf16[4,24,1152]{2,1,0:T(8,128)(2,1)} %pad_maximum_fusion.2), channel_id=1, source_target_pairs={{0,32},{32,64},{64,96},{96,128},{128,160},{160,192},{192,224},{224... | collective-permute-start | bytes 663560 | tf_op jit(solution)/shard_map/ppermute | solution.py:11
  16.1 8.7 %collective-permute-start.2 = (bf16[9,3,1152]{2,1,0:T(4,128)(2,1)S(1)}, bf16[9,3,1152]{2,1,0:T(4,128)(2,1)S(1)}, u32[]{:S(2)}, u32[]{:S(2)}) collective-permute-start(bf16[9,3,1152]{2,1,0:T(4,128)(2,1)S(1)} %get-tuple-element.58), channel_id=1, source_target_pairs={{1,0},{2,1},{3,2},{4,3},{5,4},{6,5},{7,6},{8,7},{9,8},{10,9},{11,1... | collective-permute-start | bytes 186632 | tf_op jit(solution)/shard_map/ppermute | solution.py:17
  18.0 37.0 %collective-permute-start.5 = (bf16[3,24,1152]{2,1,0:T(8,128)(2,1)S(1)}, bf16[3,24,1152]{2,1,0:T(8,128)(2,1)}, u32[]{:S(2)}, u32[]{:S(2)}) collective-permute-start(bf16[3,24,1152]{2,1,0:T(8,128)(2,1)S(1)} %get-tuple-element.57), channel_id=1, source_target_pairs={{32,0},{64,32},{96,64},{128,96},{160,128},{192,160},{224,192},{256... | collective-permute-start | bytes 497672 | tf_op jit(solution)/shard_map/ppermute | solution.py:17
  27.0 13.7 %collective-permute-start.4 = (bf16[3,6,1152]{2,1,0:T(8,128)(2,1)S(1)}, bf16[3,6,1152]{2,1,0:T(8,128)(2,1)S(1)}, u32[]{:S(2)}, u32[]{:S(2)}) collective-permute-start(bf16[3,6,1152]{2,1,0:T(8,128)(2,1)S(1)} %pad_maximum_fusion.5), channel_id=1, source_target_pairs={{32,0},{64,32},{96,64},{128,96},{160,128},{192,160},{224,192},{256... | collective-permute-start | bytes 124424 | tf_op jit(solution)/shard_map/ppermute | solution.py:17
  36.6 9.1 %collective-permute-start.3 = (bf16[3,6,1152]{2,1,0:T(8,128)(2,1)S(1)}, bf16[3,6,1152]{2,1,0:T(8,128)(2,1)S(1)}, u32[]{:S(2)}, u32[]{:S(2)}) collective-permute-start(bf16[3,6,1152]{2,1,0:T(8,128)(2,1)S(1)} %pad_maximum_fusion.4), channel_id=1, source_target_pairs={{0,32},{32,64},{64,96},{96,128},{128,160},{160,192},{192,224},{224... | collective-permute-start | bytes 124424 | tf_op jit(solution)/shard_map/ppermute | solution.py:11
  46.3 7.5 %copy-start.1 = (bf16[4,24,1152]{2,1,0:T(8,128)(2,1)}, bf16[4,24,1152]{2,1,0:T(8,128)(2,1)S(1)}, u32[]{:S(2)}) copy-start(bf16[4,24,1152]{2,1,0:T(8,128)(2,1)S(1)} %collective-permute-done.1) | copy-start | bytes 663556
  48.7 0.9 %copy-start.2 = (f32[4,12,6,45,1]{3,1,2,0,4:T(8,128)S(1)}, f32[4,12,6,45,1]{3,1,2,0,4:T(8,128)}, u32[]{:S(2)}) copy-start(f32[4,12,6,45,1]{3,1,2,0,4:T(8,128)} %constant.28) | copy-start | bytes 155524
  48.7 0.9 %copy-start.4 = (f32[9,24]{1,0:T(8,128)S(1)}, f32[9,24]{1,0:T(8,128)}, u32[]{:S(2)}) copy-start(f32[9,24]{1,0:T(8,128)} %param.8) | copy-start | bytes 2596
  53.3 1.7 %copy-start.3 = (bf16[3,3,1152]{2,1,0:T(4,128)(2,1)S(1)}, bf16[3,3,1152]{2,1,0:T(4,128)(2,1)}, u32[]{:S(2)}) copy-start(bf16[3,3,1152]{2,1,0:T(4,128)(2,1)} %get-tuple-element.67) | copy-start | bytes 62212
  53.9 1.2 %slice-start = ((bf16[4,24,1152]{2,1,0:T(8,128)(2,1)}), bf16[3,24,1152]{2,1,0:T(8,128)(2,1)S(1)}, s32[]{:S(2)}) async-start(bf16[4,24,1152]{2,1,0:T(8,128)(2,1)} %copy-done.1), calls=%async_computation | async-start | bytes 331776 | tf_op jit(solution)/shard_map/slice | solution.py:121

commit v3 on v2

--- a/solution.py
+++ b/solution.py
@@ -65,7 +65,7 @@
 def summed_moments(pieces, moments):
     codes = jnp.arange(12, dtype=jnp.int32)
     onehot = (pieces[..., None] == codes).astype(jnp.float32)
-    return jnp.einsum("ijko,ijkm->ijom", onehot, moments, precision=lax.Precision.HIGHEST)
+    return jnp.einsum("...ko,...km->...om", onehot, moments, precision=lax.Precision.HIGHEST)
 
 
 def split3(value):
@@ -96,6 +96,18 @@
     return moments, pieces
 
 
+def from_corner(value, step_panel, step_tile):
+    n_panel = lax.axis_size("panel")
+    n_tile = lax.axis_size("tile")
+    pairs = []
+    for p in range(n_panel):
+        q = p + step_panel
+        if 0 <= q < n_panel:
+            for t in range(n_tile):
+                pairs.append((p * n_tile + t, q * n_tile + (t + step_tile) % n_tile))
+    return lax.ppermute(value, ("panel", "tile"), pairs)
+
+
 def local(tracer, moments, pieces, cell_area):
     rows = tracer.shape[0]
     cols = tracer.shape[1]
@@ -103,6 +115,7 @@
     n_piece = moments.shape[3]
     n_moment = moments.shape[4]
     tables, offsets = face_tables()
+    tables = jnp.asarray(tables, jnp.float32)
 
     west_pack = pack_weights(moments[0][:, cols - 1], pieces[0][:, cols - 1], width)[:, None]
     south_pack = pack_weights(moments[1][rows - 1], pieces[1][rows - 1], width)[None]
@@ -110,39 +123,42 @@
     from_east = from_next(tracer[:, :3], "tile", True)
     from_south = from_prev(jnp.concatenate([tracer[rows - 3 :], south_pack], axis=0), "panel", False)
     from_north = from_next(tracer[:3], "panel", False)
+    from_sw = from_corner(tracer[rows - 3 :, cols - 3 :], 1, 1)
+    from_se = from_corner(tracer[rows - 3 :, :3], 1, -1)
+    from_nw = from_corner(tracer[:3, cols - 3 :], -1, 1)
+    from_ne = from_corner(tracer[:3, :3], -1, -1)
 
-    west_halo = from_west[:, :3]
-    corners_up = jnp.concatenate([west_halo[rows - 3 :], from_east[rows - 3 :]], axis=1)
-    corners_down = jnp.concatenate([west_halo[:3], from_east[:3]], axis=1)
-    south_corners = from_prev(corners_up, "panel", False)
-    north_corners = from_next(corners_down, "panel", False)
+    south_rows = jnp.concatenate([from_sw, from_south[:3], from_se], axis=1)
+    wide = jnp.concatenate([from_west[:, :3], tracer, from_east], axis=1)
+    north_rows = jnp.concatenate([from_nw, from_north, from_ne], axis=1)
+    padded = jnp.concatenate([south_rows, wide, north_rows], axis=0)
 
-    wide = jnp.concatenate([west_halo, tracer, from_east], axis=1)
-    south_rows = jnp.concatenate([south_corners[:, :3], from_south[:3], south_corners[:, 3:]], axis=1)
-    north_rows = jnp.concatenate([north_corners[:, :3], from_north, north_corners[:, 3:]], axis=1)
-    padded = jnp.concatenate([south_rows, wide, north_rows], axis=0)
+    is_top = lax.axis_index("panel") == lax.axis_size("panel") - 1
+    last_row = jnp.arange(rows) == rows - 1
+    row_mask = jnp.where(jnp.logical_and(last_row, is_top), 0.0, 1.0).astype(jnp.float32)
+    east_sum = summed_moments(pieces[0], moments[0])
+    north_sum = summed_moments(pieces[1], moments[1]) * row_mask[:, None, None, None]
+    faces = jnp.stack(
+        [
+            jnp.pad(east_sum[:, : cols - 1], ((0, 0), (1, 0), (0, 0), (0, 0))),
+            east_sum,
+            jnp.pad(north_sum[: rows - 1], ((1, 0), (0, 0), (0, 0), (0, 0))),
+            north_sum,
+        ],
+        axis=2,
+    )
+    weights = jnp.einsum("ijfcm,fcmt->ijt", faces, tables, precision=lax.Precision.HIGHEST)
 
     west_m, west_p = unpack_weights(from_west[:, 3], n_piece, n_moment)
     south_m, south_p = unpack_weights(from_south[3], n_piece, n_moment)
-    east_sum = summed_moments(
-        jnp.concatenate([west_p[:, None], pieces[0]], axis=1),
-        jnp.concatenate([west_m[:, None], moments[0]], axis=1),
+    west_fix = jnp.einsum(
+        "icm,cmt->it", summed_moments(west_p, west_m), tables[0], precision=lax.Precision.HIGHEST
     )
-    north_sum = summed_moments(
-        jnp.concatenate([south_p[None], pieces[1]], axis=0),
-        jnp.concatenate([south_m[None], moments[1]], axis=0),
+    south_fix = jnp.einsum(
+        "jcm,cmt->jt", summed_moments(south_p, south_m), tables[2], precision=lax.Precision.HIGHEST
     )
-    is_top = lax.axis_index("panel") == lax.axis_size("panel") - 1
-    last_row = jnp.arange(rows + 1) == rows
-    row_mask = jnp.where(jnp.logical_and(last_row, is_top), 0.0, 1.0).astype(jnp.float32)
-    north_sum = north_sum * row_mask[:, None, None, None]
-
-    faces = jnp.stack(
-        [east_sum[:, :cols], east_sum[:, 1:], north_sum[:rows], north_sum[1:]], axis=2
-    )
-    weights = jnp.einsum(
-        "ijfcm,fcmt->ijt", faces, jnp.asarray(tables, jnp.float32), precision=lax.Precision.HIGHEST
-    )
+    weights = weights + jnp.pad(west_fix[:, None], ((0, 0), (0, cols - 1), (0, 0)))
+    weights = weights + jnp.pad(south_fix[None], ((0, rows - 1), (0, 0), (0, 0)))
     weights = weights / cell_area[:, :, None]
 
     total = tracer.astype(jnp.float32)

time: 64.5 us -> 83 us (1.29)
  the two profiles are of different devices: /device:TPU:233 before, /device:TPU:36 now
where the time goes in v3:
time: 83 us; the launch traced here: 81.6 us
  starting transfers between devices  36.5 us (44%)
  local copies, waits for them, and re-layouts  19.7 us (24%)
  other arithmetic  14.9 us (18%)
  matrix products  10.2 us (12%)
    ppermute x4, starting transfers between devices, from_corner(): return lax.ppermute(value, ('panel', 'tile'), pairs)  20.7 us
    ppermute x2, starting transfers between devices, from_next(): return lax.ppermute(value, axis, pairs)  10.8 us
    convert_element_type x1, other arithmetic, local(): return total.astype(jnp.bfloat16)  9.55 us
    ppermute x2, starting transfers between devices, from_prev(): return lax.ppermute(value, axis, pairs)  5 us
    dot_general x4, matrix products, summed_moments(): jnp.einsum('...ko,...km->...om', onehot, moments, precision=lax.Precision...  4.62 us
    dot_general x1, matrix products, local(): jnp.einsum('ijfcm,fcmt->ijt', faces, tables, precision=lax.Precision.HIGH...  3.45 us
    slice x3, local copies, waits for them, and re-layouts, local(): total = total + weights[:, :, tap][:, :, None] * piece.astype(jnp.float32)  2.84 us
    unnamed x14, local copies, waits for them, and re-layouts  2.44 us
  transfers between devices with their start and end apart: 8, of which 0 were waited for; matrix products, arithmetic and copies ran while one was open for 34% of the time, Pallas kernels for 0%

profile of v3, /device:TPU:36, one launch (start us, length us, event | category | flops | bytes accessed | tf_op | source)
XLA Modules:
  0.0 81.6 jit_solution(6311764568541510562)
XLA Ops:
  0.0 1.0 %fusion.74 = (f32[1,9,24,4,6]{2,3,4,1,0:T(4,128)S(1)}, f32[1,9,24,4,6]{2,3,4,1,0:T(4,128)S(1)}) fusion(f32[2,9,24,4,6]{2,3,4,1,0:T(4,128)} %param.6), kind=kLoop, calls=%fused_computation.152 | loop fusion | bytes 82944 | tf_op jit(solution)/shard_map/slice | solution.py:140
  1.0 0.3 copy.71
  1.4 0.7 slice_bitcast_fusion.2
  2.3 0.1 copy.57
  2.5 1.7 %fusion.73 = (bf16[9,3,1152]{2,1,0:T(4,128)(2,1)}, bf16[9,3,1152]{2,1,0:T(4,128)(2,1)S(1)}) fusion(bf16[9,24,1152]{2,1,0:T(8,128)(2,1)} %param.5), kind=kLoop, calls=%fused_computation.151 | loop fusion | bytes 248832 | tf_op jit(solution)/shard_map/slice | solution.py:123
  4.3 0.7 pad_maximum_fusion.3
  5.0 1.9 %collective-permute-start = (bf16[9,4,1152]{2,0,1:T(8,128)(2,1)}, bf16[9,4,1152]{2,0,1:T(8,128)(2,1)}, u32[]{:S(2)}, u32[]{:S(2)}) collective-permute-start(bf16[9,4,1152]{2,0,1:T(8,128)(2,1)} %pad_maximum_fusion.3), channel_id=1, source_target_pairs={{0,1},{1,2},{2,3},{3,4},{4,5},{5,6},{6,7},{7,8},{8,9},{9,10},{10,1... | collective-permute-start | bytes 248840 | tf_op jit(solution)/shard_map/ppermute | solution.py:11
  6.9 0.7 slice.441
  7.6 0.7 fusion.69
  8.3 0.7 fusion.72
  9.5 0.7 pad_maximum_fusion.2
  10.2 3.1 %collective-permute-start.1 = (bf16[4,24,1152]{2,1,0:T(8,128)(2,1)}, bf16[4,24,1152]{2,1,0:T(8,128)(2,1)}, u32[]{:S(2)}, u32[]{:S(2)}) collective-permute-start(bf16[4,24,1152]{2,1,0:T(8,128)(2,1)} %pad_maximum_fusion.2), channel_id=1, source_target_pairs={{0,32},{32,64},{64,96},{96,128},{128,160},{160,192},{192,224},{224... | collective-permute-start | bytes 663560 | tf_op jit(solution)/shard_map/ppermute | solution.py:11
  13.3 0.7 fusion.71
  14.0 2.7 %collective-permute-start.2 = (bf16[3,3,1152]{2,1,0:T(4,128)(2,1)}, bf16[3,3,1152]{2,1,0:T(4,128)(2,1)}, u32[]{:S(2)}, u32[]{:S(2)}) collective-permute-start(bf16[3,3,1152]{2,1,0:T(4,128)(2,1)} %get-tuple-element.52), channel_id=1, source_target_pairs={{0,33},{1,34},{2,35},{3,36},{4,37},{5,38},{6,39},{7,40},{8,41},{9,... | collective-permute-start | bytes 62216 | tf_op jit(solution)/shard_map/ppermute | solution.py:108
  16.7 9.6 %collective-permute-start.3 = (bf16[3,3,1152]{2,1,0:T(4,128)(2,1)}, bf16[3,3,1152]{2,1,0:T(4,128)(2,1)}, u32[]{:S(2)}, u32[]{:S(2)}) collective-permute-start(bf16[3,3,1152]{2,1,0:T(4,128)(2,1)} %get-tuple-element.54), channel_id=1, source_target_pairs={{0,63},{1,32},{2,33},{3,34},{4,35},{5,36},{6,37},{7,38},{8,39},{9,... | collective-permute-start | bytes 62216 | tf_op jit(solution)/shard_map/ppermute | solution.py:108
  26.2 3.7 %collective-permute-start.4 = (bf16[9,3,1152]{2,1,0:T(4,128)(2,1)}, bf16[9,3,1152]{2,1,0:T(4,128)(2,1)}, u32[]{:S(2)}, u32[]{:S(2)}) collective-permute-start(bf16[9,3,1152]{2,1,0:T(4,128)(2,1)} %get-tuple-element.58), channel_id=1, source_target_pairs={{1,0},{2,1},{3,2},{4,3},{5,4},{6,5},{7,6},{8,7},{9,8},{10,9},{11,1... | collective-permute-start | bytes 186632 | tf_op jit(solution)/shard_map/ppermute | solution.py:17
  29.9 0.1 copy.51
  30.1 0.8 %constant_dynamic-update-slice_fusion.1 = bf16[9,27,1152]{2,1,0:T(8,128)(2,1)} fusion(bf16[9,24,1152]{2,1,0:T(8,128)(2,1)S(1)} %copy-done), kind=kLoop, calls=%fused_computation.142 | loop fusion | bytes 995328
  30.9 1.2 %fusion.42 = f32[9,24,12,6]{2,3,1,0:T(8,128)S(1)} fusion(s32[9,24,4]{2,1,0:T(8,128)S(1)} %copy.51, f32[1,9,24,4,6]{4,3,2,1,0:T(4,128)S(1)} %copy.71), kind=kOutput, calls=%fused_computation.52 | convolution fusion | flops 756864 | bytes 86400 | tf_op jit(solution)/shard_map/...ko,...km->...om/dot_general | solution.py:68
  32.2 0.3 copy.72
  32.5 0.1 copy.53
  32.7 1.3 %convolution_multiply_fusion = f32[9,24,12,6]{2,3,1,0:T(8,128)S(1)} fusion(f32[1,9,24,4,6]{4,3,2,1,0:T(4,128)S(1)} %copy.72, f32[9]{0:T(128)S(1)} %and_select_fusion, s32[9,24,4]{2,1,0:T(8,128)S(1)} %copy.53), kind=kOutput, calls=%fused_computation.3 | convolution fusion | flops 772416 | bytes 86436 | tf_op jit(solution)/shard_map/...ko,...km->...om/dot_general | solution.py:68
  34.0 0.2 pad_bitcast_fusion
  34.2 0.9 %copy-done.3 = f32[9,24,12,6]{2,3,1,0:T(8,128)S(1)} copy-done((f32[9,24,12,6]{2,3,1,0:T(8,128)S(1)}, f32[9,24,12,6]{2,3,1,0:T(8,128)}, u32[]{:S(2)}) %copy-start.3) | copy-done | bytes 62232
  35.2 0.5 pad_maximum_fusion
  35.6 1.9 %collective-permute-start.5 = (bf16[3,3,1152]{2,1,0:T(4,128)(2,1)}, bf16[3,3,1152]{2,1,0:T(4,128)(2,1)}, u32[]{:S(2)}, u32[]{:S(2)}) collective-permute-start(bf16[3,3,1152]{2,1,0:T(4,128)(2,1)} %get-tuple-element.53), channel_id=1, source_target_pairs={{32,1},{33,2},{34,3},{35,4},{36,5},{37,6},{38,7},{39,8},{40,9},{41... | collective-permute-start | bytes 62216 | tf_op jit(solution)/shard_map/ppermute | solution.py:108
  37.6 1.6 %constant_dynamic-update-slice_fusion = bf16[9,27,1152]{2,1,0:T(8,128)(2,1)} fusion(bf16[9,27,1152]{2,1,0:T(8,128)(2,1)} %constant_dynamic-update-slice_fusion.1, bf16[9,3,1152]{2,1,0:T(4,128)(2,1)} %collective-permute-done.4), kind=kLoop, calls=%fused_computation.141 | loop fusion | bytes 165888 | tf_op jit(solution)/shard_map/concatenate | solution.py:132
  39.1 6.5 %collective-permute-start.7 = (bf16[3,3,1152]{2,1,0:T(4,128)(2,1)}, bf16[3,3,1152]{2,1,0:T(4,128)(2,1)}, u32[]{:S(2)}, u32[]{:S(2)}) collective-permute-start(bf16[3,3,1152]{2,1,0:T(4,128)(2,1)} %get-tuple-element.55), channel_id=1, source_target_pairs={{32,31},{33,0},{34,1},{35,2},{36,3},{37,4},{38,5},{39,6},{40,7},{4... | collective-permute-start | bytes 62216 | tf_op jit(solution)/shard_map/ppermute | solution.py:108
  45.6 0.8 slice_bitcast_fusion.1
  46.5 0.7 reshape.23
  47.2 1.0 %fusion.65 = f32[9,12,6]{1,2,0:T(8,128)S(1)} fusion(f32[9,4,6]{2,1,0:T(4,128)} %reshape.23, s32[9,4]{1,0:T(8,128)S(1)} %slice_convert_fusion.2), kind=kOutput, calls=%fused_computation.131 | convolution fusion | flops 31536 | bytes 3600 | tf_op jit(solution)/shard_map/...ko,...km->...om/dot_general | solution.py:68
  48.2 1.1 %convolution_bitcast_fusion.1 = f32[9,45]{1,0:T(8,128)S(1)} fusion(f32[12,6,45]{2,0,1:T(8,128)} %constant.38, f32[9,12,6]{1,2,0:T(8,128)S(1)} %fusion.65), kind=kOutput, calls=%fused_computation.11 | convolution fusion | flops 349920 | bytes 17172 | tf_op jit(solution)/shard_map/icm,cmt->it/dot_general | solution.py:154
  49.3 0.6 broadcast_in_dim.31
  49.9 0.9 %slice.563 = bf16[9,3,1152]{2,0,1:T(8,128)(2,1)S(1)} slice(bf16[9,4,1152]{2,0,1:T(8,128)(2,1)} %collective-permute-done), slice={[0:9], [0:3], [0:1152]} | slice | bytes 124416 | tf_op jit(solution)/shard_map/slice | solution.py:132
  50.8 0.7 copy.68
  51.4 7.1 %collective-permute-start.6 = (bf16[3,24,1152]{2,1,0:T(8,128)(2,1)}, bf16[3,24,1152]{2,1,0:T(8,128)(2,1)}, u32[]{:S(2)}, u32[]{:S(2)}) collective-permute-start(bf16[3,24,1152]{2,1,0:T(8,128)(2,1)} %get-tuple-element.57), channel_id=1, source_target_pairs={{32,0},{64,32},{96,64},{128,96},{160,128},{192,160},{224,192},{256... | collective-permute-start | bytes 497672 | tf_op jit(solution)/shard_map/ppermute | solution.py:17
  58.6 0.8 %slice_bitcast_fusion = bf16[24,1152]{1,0:T(8,128)(2,1)S(1)} fusion(bf16[4,24,1152]{2,1,0:T(8,128)(2,1)} %collective-permute-done.1), kind=kLoop, calls=%fused_computation.117 | loop fusion | bytes 110592 | tf_op jit(solution)/shard_map/squeeze | solution.py:153
  59.5 0.7 slice_convert_fusion.1
  60.2 0.7 reshape.29
  60.9 1.1 %fusion.59 = f32[24,12,6]{1,2,0:T(8,128)S(1)} fusion(f32[24,4,6]{2,1,0:T(4,128)} %reshape.29, s32[24,4]{1,0:T(8,128)} %slice_convert_fusion.1), kind=kOutput, calls=%fused_computation.120 | convolution fusion | flops 84096 | bytes 9600 | tf_op jit(solution)/shard_map/...ko,...km->...om/dot_general | solution.py:68
  62.0 1.1 %convolution_bitcast_fusion = f32[1,24,45]{2,1,0:T(8,128)S(1)} fusion(f32[12,6,45]{2,0,1:T(8,128)} %constant.40, f32[24,12,6]{1,2,0:T(8,128)S(1)} %fusion.59), kind=kOutput, calls=%fused_computation.10 | convolution fusion | flops 933120 | bytes 24192 | tf_op jit(solution)/shard_map/jcm,cmt->jt/dot_general | solution.py:157
  63.1 3.5 %fusion.11 = f32[9,24,45]{2,1,0:T(8,128)S(1)} fusion(f32[4,12,6,45,1]{3,1,2,0,4:T(8,128)} %constant.41, f32[9,24,4,12,6]{3,4,1,0,2:T(8,128)S(1)} %pad_maximum_fusion, f32[1,24,45]{2,1,0:T(8,128)S(1)} %convolution_bitcast_fusion, f32[9,1,45]{2,1,0:T(1,128)} %broadcast_in_dim.31, f32[9,24]{1,0:T(8,128)} %param.8), kind=kOutput, calls=%fused_computation.9 | convolution fusion | flops 33621480 | bytes 346356 | tf_op jit(solution)/shard_map/ijfcm,fcmt->ijt/dot_general | solution.py:150
  66.5 1.1 %slice_reduce_fusion.44 = (f32[9,24]{1,0:T(8,128)S(1)}, f32[9,24]{1,0:T(8,128)S(1)}, f32[9,24]{1,0:T(8,128)S(1)}, f32[9,24]{1,0:T(8,128)S(1)}, f32[9,24]{1,0:T(8...) fusion(f32[9,24,45]{2,1,0:T(8,128)S(1)} %fusion.11), kind=kLoop, calls=%fused_computation.101 | loop fusion | bytes 32832 | tf_op jit(solution)/shard_map/slice | solution.py:167
  67.7 1.2 %slice_reduce_fusion.43 = (f32[9,24]{1,0:T(8,128)S(1)}, f32[9,24]{1,0:T(8,128)S(1)}, f32[9,24]{1,0:T(8,128)S(1)}, f32[9,24]{1,0:T(8,128)S(1)}, f32[9,24]{1,0:T(8...) fusion(f32[9,24,45]{2,1,0:T(8,128)S(1)} %fusion.11), kind=kLoop, calls=%fused_computation.100 | loop fusion | bytes 32832 | tf_op jit(solution)/shard_map/slice | solution.py:167
  68.9 0.5 slice_reduce_fusion.42
  69.4 0.9 %slice.562 = bf16[3,24,1152]{2,1,0:T(8,128)(2,1)S(1)} slice(bf16[4,24,1152]{2,1,0:T(8,128)(2,1)} %collective-permute-done.1), slice={[0:3], [0:24], [0:1152]} | slice | bytes 331776 | tf_op jit(solution)/shard_map/slice | solution.py:131
  70.4 1.6 %maximum_maximum_fusion = (bf16[12,30,1152]{2,1,0:T(8,128)(2,1)S(1)}, bf16[12,30,1152]{2,1,0:T(8,128)(2,1)S(1)}) fusion(bf16[9,3,1152]{2,1,0:T(4,128)(2,1)} %collective-permute-done.4, bf16[9,24,1152]{2,1,0:T(8,128)(2,1)S(1)} %copy-done.1, bf16[9,3,1152]{2,1,0:T(4,128)(2,1)S(1)} %copy-done.4, bf16[3,3,1152]{2,1,0:T(4,128)(2,1)} %collective-permute-done.3, ...), kind=kLoop, calls=%fused_computation.38 | loop fusion | flops 9953280 | bytes 2695680 | tf_op jit(solution)/shard_map/concatenate | solution.py:134
  72.1 9.5 %add_convert_fusion = bf16[9,24,1152]{2,1,0:T(8,128)(2,1)} fusion(bf16[9,24,1152]{2,1,0:T(8,128)(2,1)S(1)} %copy-done.1, bf16[9,3,1152]{2,1,0:T(4,128)(2,1)S(1)} %copy-done.4, bf16[12,30,1152]{2,1,0:T(8,128)(2,1)S(1)} %get-tuple-element.51, bf16[9,27,1152]{2,1,0:T(8,128)(2,1)} %constant_dynamic-update-slice_fusion, ...), kind=kLoop, calls=%fused_computation.37 | loop fusion | flops 36080640 | bytes 21500640 | tf_op jit(solution)/shard_map/convert_element_type | solution.py:168
  (38 shorter events, 1.2 us)
Async XLA Ops:
  0.0 8.3 %copy-start = (bf16[9,24,1152]{2,1,0:T(8,128)(2,1)S(1)}, bf16[9,24,1152]{2,1,0:T(8,128)(2,1)}, u32[]{:S(2)}) copy-start(bf16[9,24,1152]{2,1,0:T(8,128)(2,1)} %param.5) | copy-start | bytes 1492996
  5.0 34.1 %collective-permute-start = (bf16[9,4,1152]{2,0,1:T(8,128)(2,1)}, bf16[9,4,1152]{2,0,1:T(8,128)(2,1)}, u32[]{:S(2)}, u32[]{:S(2)}) collective-permute-start(bf16[9,4,1152]{2,0,1:T(8,128)(2,1)} %pad_maximum_fusion.3), channel_id=1, source_target_pairs={{0,1},{1,2},{2,3},{3,4},{4,5},{5,6},{6,7},{7,8},{8,9},{9,10},{10,1... | collective-permute-start | bytes 248840 | tf_op jit(solution)/shard_map/ppermute | solution.py:11
  10.2 41.3 %collective-permute-start.1 = (bf16[4,24,1152]{2,1,0:T(8,128)(2,1)}, bf16[4,24,1152]{2,1,0:T(8,128)(2,1)}, u32[]{:S(2)}, u32[]{:S(2)}) collective-permute-start(bf16[4,24,1152]{2,1,0:T(8,128)(2,1)} %pad_maximum_fusion.2), channel_id=1, source_target_pairs={{0,32},{32,64},{64,96},{96,128},{128,160},{160,192},{192,224},{224... | collective-permute-start | bytes 663560 | tf_op jit(solution)/shard_map/ppermute | solution.py:11
  14.0 56.4 %collective-permute-start.2 = (bf16[3,3,1152]{2,1,0:T(4,128)(2,1)}, bf16[3,3,1152]{2,1,0:T(4,128)(2,1)}, u32[]{:S(2)}, u32[]{:S(2)}) collective-permute-start(bf16[3,3,1152]{2,1,0:T(4,128)(2,1)} %get-tuple-element.52), channel_id=1, source_target_pairs={{0,33},{1,34},{2,35},{3,36},{4,37},{5,38},{6,39},{7,40},{8,41},{9,... | collective-permute-start | bytes 62216 | tf_op jit(solution)/shard_map/ppermute | solution.py:108
  16.7 53.7 %collective-permute-start.3 = (bf16[3,3,1152]{2,1,0:T(4,128)(2,1)}, bf16[3,3,1152]{2,1,0:T(4,128)(2,1)}, u32[]{:S(2)}, u32[]{:S(2)}) collective-permute-start(bf16[3,3,1152]{2,1,0:T(4,128)(2,1)} %get-tuple-element.54), channel_id=1, source_target_pairs={{0,63},{1,32},{2,33},{3,34},{4,35},{5,36},{6,37},{7,38},{8,39},{9,... | collective-permute-start | bytes 62216 | tf_op jit(solution)/shard_map/ppermute | solution.py:108
  26.2 9.4 %collective-permute-start.4 = (bf16[9,3,1152]{2,1,0:T(4,128)(2,1)}, bf16[9,3,1152]{2,1,0:T(4,128)(2,1)}, u32[]{:S(2)}, u32[]{:S(2)}) collective-permute-start(bf16[9,3,1152]{2,1,0:T(4,128)(2,1)} %get-tuple-element.58), channel_id=1, source_target_pairs={{1,0},{2,1},{3,2},{4,3},{5,4},{6,5},{7,6},{8,7},{9,8},{10,9},{11,1... | collective-permute-start | bytes 186632 | tf_op jit(solution)/shard_map/ppermute | solution.py:17
  32.1 1.8 %copy-start.2 = (f32[9,24,12,6]{2,3,1,0:T(8,128)}, f32[9,24,12,6]{2,3,1,0:T(8,128)S(1)}, u32[]{:S(2)}) copy-start(f32[9,24,12,6]{2,3,1,0:T(8,128)S(1)} %fusion.42) | copy-start | bytes 186628
  34.0 1.2 %copy-start.3 = (f32[9,24,12,6]{2,3,1,0:T(8,128)S(1)}, f32[9,24,12,6]{2,3,1,0:T(8,128)}, u32[]{:S(2)}) copy-start(f32[9,24,12,6]{2,3,1,0:T(8,128)} %copy-done.2) | copy-start | bytes 186628
  35.6 34.7 %collective-permute-start.5 = (bf16[3,3,1152]{2,1,0:T(4,128)(2,1)}, bf16[3,3,1152]{2,1,0:T(4,128)(2,1)}, u32[]{:S(2)}, u32[]{:S(2)}) collective-permute-start(bf16[3,3,1152]{2,1,0:T(4,128)(2,1)} %get-tuple-element.53), channel_id=1, source_target_pairs={{32,1},{33,2},{34,3},{35,4},{36,5},{37,6},{38,7},{39,8},{40,9},{41... | collective-permute-start | bytes 62216 | tf_op jit(solution)/shard_map/ppermute | solution.py:108
  39.1 31.3 %collective-permute-start.7 = (bf16[3,3,1152]{2,1,0:T(4,128)(2,1)}, bf16[3,3,1152]{2,1,0:T(4,128)(2,1)}, u32[]{:S(2)}, u32[]{:S(2)}) collective-permute-start(bf16[3,3,1152]{2,1,0:T(4,128)(2,1)} %get-tuple-element.55), channel_id=1, source_target_pairs={{32,31},{33,0},{34,1},{35,2},{36,3},{37,4},{38,5},{39,6},{40,7},{4... | collective-permute-start | bytes 62216 | tf_op jit(solution)/shard_map/ppermute | solution.py:108
  51.4 18.9 %collective-permute-start.6 = (bf16[3,24,1152]{2,1,0:T(8,128)(2,1)}, bf16[3,24,1152]{2,1,0:T(8,128)(2,1)}, u32[]{:S(2)}, u32[]{:S(2)}) collective-permute-start(bf16[3,24,1152]{2,1,0:T(8,128)(2,1)} %get-tuple-element.57), channel_id=1, source_target_pairs={{32,0},{64,32},{96,64},{128,96},{160,128},{192,160},{224,192},{256... | collective-permute-start | bytes 497672 | tf_op jit(solution)/shard_map/ppermute | solution.py:17
  67.7 2.7 %copy-start.1 = (bf16[9,24,1152]{2,1,0:T(8,128)(2,1)S(1)}, bf16[9,24,1152]{2,1,0:T(8,128)(2,1)}, u32[]{:S(2)}) copy-start(bf16[9,24,1152]{2,1,0:T(8,128)(2,1)} %param.5) | copy-start | bytes 1492996
  67.7 2.7 %copy-start.4 = (bf16[9,3,1152]{2,1,0:T(4,128)(2,1)S(1)}, bf16[9,3,1152]{2,1,0:T(4,128)(2,1)}, u32[]{:S(2)}) copy-start(bf16[9,3,1152]{2,1,0:T(4,128)(2,1)} %copy.68) | copy-start | bytes 186628

commit v4 on v3

--- a/solution.py
+++ b/solution.py
@@ -69,11 +69,11 @@
 
 
 def split3(value):
-    hi = value.astype(jnp.bfloat16)
-    rest = value - hi.astype(jnp.float32)
-    mid = rest.astype(jnp.bfloat16)
-    lo = (rest - mid.astype(jnp.float32)).astype(jnp.bfloat16)
-    return jnp.concatenate([hi, mid, lo], axis=-1)
+    hi = lax.reduce_precision(value, exponent_bits=8, mantissa_bits=7)
+    rest = value - hi
+    mid = lax.reduce_precision(rest, exponent_bits=8, mantissa_bits=7)
+    lo = rest - mid
+    return jnp.concatenate([hi, mid, lo], axis=-1).astype(jnp.bfloat16)
 
 
 def join3(value, count):
@@ -96,16 +96,13 @@
     return moments, pieces
 
 
-def from_corner(value, step_panel, step_tile):
-    n_panel = lax.axis_size("panel")
-    n_tile = lax.axis_size("tile")
-    pairs = []
-    for p in range(n_panel):
-        q = p + step_panel
-        if 0 <= q < n_panel:
-            for t in range(n_tile):
-                pairs.append((p * n_tile + t, q * n_tile + (t + step_tile) % n_tile))
-    return lax.ppermute(value, ("panel", "tile"), pairs)
+def face_weights(moments, pieces, tables):
+    n_code = tables.shape[1]
+    onehot = (pieces[..., None] == jnp.arange(n_code, dtype=jnp.int32)).astype(jnp.float32)
+    spread = jnp.sum(onehot[..., :, None] * moments[..., None, :], axis=-3)
+    lead = spread.shape[:-3]
+    flat = spread.reshape(lead + (-1,))
+    return jnp.dot(flat, tables.reshape(-1, tables.shape[-1]), precision=lax.Precision.HIGHEST)
 
 
 def local(tracer, moments, pieces, cell_area):
@@ -118,45 +115,46 @@
     tables = jnp.asarray(tables, jnp.float32)
 
     west_pack = pack_weights(moments[0][:, cols - 1], pieces[0][:, cols - 1], width)[:, None]
-    south_pack = pack_weights(moments[1][rows - 1], pieces[1][rows - 1], width)[None]
     from_west = from_prev(jnp.concatenate([tracer[:, cols - 3 :], west_pack], axis=1), "tile", True)
     from_east = from_next(tracer[:, :3], "tile", True)
-    from_south = from_prev(jnp.concatenate([tracer[rows - 3 :], south_pack], axis=0), "panel", False)
-    from_north = from_next(tracer[:3], "panel", False)
-    from_sw = from_corner(tracer[rows - 3 :, cols - 3 :], 1, 1)
-    from_se = from_corner(tracer[rows - 3 :, :3], 1, -1)
-    from_nw = from_corner(tracer[:3, cols - 3 :], -1, 1)
-    from_ne = from_corner(tracer[:3, :3], -1, -1)
-
-    south_rows = jnp.concatenate([from_sw, from_south[:3], from_se], axis=1)
     wide = jnp.concatenate([from_west[:, :3], tracer, from_east], axis=1)
-    north_rows = jnp.concatenate([from_nw, from_north, from_ne], axis=1)
-    padded = jnp.concatenate([south_rows, wide, north_rows], axis=0)
+    south_pack = jnp.pad(
+        pack_weights(moments[1][rows - 1], pieces[1][rows - 1], width), ((3, 3), (0, 0))
+    )[None]
+    from_south = from_prev(jnp.concatenate([wide[rows - 3 :], south_pack], axis=0), "panel", False)
+    from_north = from_next(wide[:3], "panel", False)
+    padded = jnp.concatenate([from_south[:3], wide, from_north], axis=0)
 
     is_top = lax.axis_index("panel") == lax.axis_size("panel") - 1
     last_row = jnp.arange(rows) == rows - 1
     row_mask = jnp.where(jnp.logical_and(last_row, is_top), 0.0, 1.0).astype(jnp.float32)
-    east_sum = summed_moments(pieces[0], moments[0])
-    north_sum = summed_moments(pieces[1], moments[1]) * row_mask[:, None, None, None]
-    faces = jnp.stack(
+    north_m = moments[1] * row_mask[:, None, None, None]
+    zero_col = jnp.zeros_like(moments[0][:, :1])
+    zero_row = jnp.zeros_like(moments[1][:1])
+    face_m = jnp.stack(
         [
-            jnp.pad(east_sum[:, : cols - 1], ((0, 0), (1, 0), (0, 0), (0, 0))),
-            east_sum,
-            jnp.pad(north_sum[: rows - 1], ((1, 0), (0, 0), (0, 0), (0, 0))),
-            north_sum,
+            jnp.concatenate([zero_col, moments[0][:, : cols - 1]], axis=1),
+            moments[0],
+            jnp.concatenate([zero_row, north_m[: rows - 1]], axis=0),
+            north_m,
         ],
         axis=2,
     )
-    weights = jnp.einsum("ijfcm,fcmt->ijt", faces, tables, precision=lax.Precision.HIGHEST)
+    face_p = jnp.stack(
+        [
+            jnp.concatenate([pieces[0][:, :1], pieces[0][:, : cols - 1]], axis=1),
+            pieces[0],
+            jnp.concatenate([pieces[1][:1], pieces[1][: rows - 1]], axis=0),
+            pieces[1],
+        ],
+        axis=2,
+    )
+    weights = face_weights(face_m, face_p, tables)
 
     west_m, west_p = unpack_weights(from_west[:, 3], n_piece, n_moment)
-    south_m, south_p = unpack_weights(from_south[3], n_piece, n_moment)
-    west_fix = jnp.einsum(
-        "icm,cmt->it", summed_moments(west_p, west_m), tables[0], precision=lax.Precision.HIGHEST
-    )
-    south_fix = jnp.einsum(
-        "jcm,cmt->jt", summed_moments(south_p, south_m), tables[2], precision=lax.Precision.HIGHEST
-    )
+    south_m, south_p = unpack_weights(from_south[3, 3 : 3 + cols], n_piece, n_moment)
+    west_fix = face_weights(west_m[:, None], west_p[:, None], tables[:1])
+    south_fix = face_weights(south_m[:, None], south_p[:, None], tables[2:3])
     weights = weights + jnp.pad(west_fix[:, None], ((0, 0), (0, cols - 1), (0, 0)))
     weights = weights + jnp.pad(south_fix[None], ((0, rows - 1), (0, 0), (0, 0)))
     weights = weights / cell_area[:, :, None]

time: 83 us -> 57 us (0.69)
  the two profiles are of different devices: /device:TPU:36 before, /device:TPU:48 now
where the time goes in v4:
time: 57 us; the launch traced here: 56.6 us
  starting transfers between devices  21.4 us (38%)
  other arithmetic  18.2 us (32%)
  local copies, waits for them, and re-layouts  8.74 us (15%)
  matrix products  4.56 us (8%)
  waiting for transfers between devices  3.33 us (6%)
    ppermute x2, starting transfers between devices, from_next(): return lax.ppermute(value, axis, pairs)  16.1 us
    convert_element_type x1, other arithmetic, local(): return total.astype(jnp.bfloat16)  7.52 us
    ppermute x2, starting transfers between devices, from_prev(): return lax.ppermute(value, axis, pairs)  5.31 us
    reduce_sum x3, other arithmetic, face_weights(): spread = jnp.sum(onehot[..., :, None] * moments[..., None, :], axis=-3)  5.09 us
    dot_general x3, matrix products, face_weights(): jnp.dot(flat, tables.reshape(-1, tables.shape[-1]), precision=lax.Precisi...  4.56 us
    ppermute x2, waiting for transfers between devices, from_prev(): return lax.ppermute(value, axis, pairs)  3.33 us
    slice x3, local copies, waits for them, and re-layouts, local(): total = total + weights[:, :, tap][:, :, None] * piece.astype(jnp.float32)  2.84 us
    concatenate x1, other arithmetic, local(): padded = jnp.concatenate([from_south[:3], wide, from_north], axis=0)  1.21 us
  transfers between devices with their start and end apart: 4, of which 1 were waited for; matrix products, arithmetic and copies ran while one was open for 30% of the time, Pallas kernels for 0%

profile of v4, /device:TPU:48, one launch (start us, length us, event | category | flops | bytes accessed | tf_op | source)
XLA Modules:
  0.0 56.6 jit_solution(9672513881793563290)
XLA Ops:
  0.0 1.1 %slice_bitcast_fusion.1 = (f32[9,24,1,4,6]{1,3,4,0,2:T(4,128)S(1)}, f32[9,24,4,6]{1,2,3,0:T(4,128)S(1)}, f32[9,24,4,6]{1,2,3,0:T(4,128)S(1)}) fusion(f32[2,9,24,4,6]{2,3,4,1,0:T(4,128)} %param.6), kind=kLoop, calls=%fused_computation.109 | loop fusion | bytes 103680 | tf_op jit(solution)/shard_map/stack;squeeze | solution.py:134
  1.1 0.1 slice.566
  1.2 0.3 copy.86
  1.5 0.1 reshape_squeeze.6
  1.6 0.8 %slice_bitcast_fusion.5 = (s32[9,24,1,4]{1,3,0,2:T(4,128)S(1)}, s32[9,24,4]{1,2,0:T(4,128)S(1)}, s32[9,24,1,4]{1,3,0,2:T(4,128)S(1)}) fusion(s32[2,9,24,4]{2,3,1,0:T(4,128)} %param.7), kind=kLoop, calls=%fused_computation.141 | loop fusion | bytes 17280 | tf_op jit(solution)/shard_map/stack;squeeze | solution.py:143
  2.4 0.1 copy.87
  2.6 0.1 copy.88
  2.7 0.1 fusion.47
  2.8 1.1 %fusion.53 = (bf16[9,3,1152]{2,1,0:T(4,128)(2,1)S(1)}, bf16[9,3,1152]{2,1,0:T(4,128)(2,1)S(1)}) fusion(bf16[9,24,1152]{2,1,0:T(8,128)(2,1)} %param.5), kind=kLoop, calls=%fused_computation.159 | loop fusion | bytes 248832 | tf_op jit(solution)/shard_map/slice | solution.py:119
  3.9 0.1 pad_maximum_fusion.7
  4.0 1.9 %collective-permute-start = (bf16[9,4,1152]{2,1,0:T(4,128)(2,1)S(1)}, bf16[9,4,1152]{2,1,0:T(4,128)(2,1)S(1)}, u32[]{:S(2)}, u32[]{:S(2)}) collective-permute-start(bf16[9,4,1152]{2,1,0:T(4,128)(2,1)S(1)} %pad_maximum_fusion.7), channel_id=1, source_target_pairs={{0,1},{1,2},{2,3},{3,4},{4,5},{5,6},{6,7},{7,8},{8,9},{9,10},{10,1... | collective-permute-start | bytes 248840 | tf_op jit(solution)/shard_map/ppermute | solution.py:11
  5.9 10.5 %collective-permute-start.1 = (bf16[9,3,1152]{2,1,0:T(4,128)(2,1)S(1)}, bf16[9,3,1152]{2,1,0:T(4,128)(2,1)S(1)}, u32[]{:S(2)}, u32[]{:S(2)}) collective-permute-start(bf16[9,3,1152]{2,1,0:T(4,128)(2,1)S(1)} %get-tuple-element.54), channel_id=1, source_target_pairs={{1,0},{2,1},{3,2},{4,3},{5,4},{6,5},{7,6},{8,7},{9,8},{10,9},{11,1... | collective-permute-start | bytes 186632 | tf_op jit(solution)/shard_map/ppermute | solution.py:17
  16.6 0.1 copy.94
  16.7 0.1 copy.95
  16.7 0.1 copy.96
  16.8 0.1 copy.97
  16.9 0.1 bitcast_multiply_fusion
  17.0 0.1 slice_multiply_fusion
  17.1 0.1 pad_bitcast_fusion
  17.2 0.1 fusion.42
  17.3 0.1 add_bitcast_fusion
  17.4 0.2 fusion.28
  17.6 4.8 %multiply_reduce_fusion = f32[9,24,4,12,6]{1,4,3,2,0:T(8,128)S(1)} fusion(f32[9,24,4,4,12]{1,3,4,2,0:T(4,128)S(1)} %fusion.28, f32[9,24,1,4,6]{1,3,4,0,2:T(4,128)S(1)} %bitcast_multiply_fusion, f32[9,24,1,4,6]{1,3,4,0,2:T(4,128)S(1)} %get-tuple-element.72, f32[9,24,1,4,6]{1,3,4,0,2:T(4,128)S(1)} %get-tuple-element.56, f32[9,24,1,4,6]{1,3,4,0,2:T(4,128)S(1)} %get-tuple-element.73), kind=kLoop, calls=%fused_computation | loop fusion | flops 497664 | bytes 497664 | tf_op jit(solution)/shard_map/reduce_sum | solution.py:102
  22.5 0.1 copy.99
  22.7 0.8 %pad_maximum_fusion.6 = (bf16[3,30,1152]{2,1,0:T(8,128)(2,1)S(1)}, bf16[3,30,1152]{2,1,0:T(8,128)(2,1)}) fusion(bf16[9,3,1152]{2,1,0:T(4,128)(2,1)S(1)} %collective-permute-done.1, bf16[9,24,1152]{2,1,0:T(8,128)(2,1)S(1)} %copy-done, bf16[9,3,1152]{2,1,0:T(4,128)(2,1)S(1)} %bitcast.75), kind=kLoop, calls=%fused_computation.50 | loop fusion | flops 1244160 | bytes 1036800 | tf_op jit(solution)/shard_map/slice | solution.py:124
  23.6 0.1 copy.98
  23.7 1.0 %pad_maximum_fusion.3 = bf16[4,30,1152]{2,0,1:T(4,128)(2,1)} fusion(bf16[1,30,1152]{2,0,1:T(2,128)(2,1)S(1)} %copy.99, bf16[3,30,1152]{2,0,1:T(4,128)(2,1)S(1)} %copy.98), kind=kLoop, calls=%fused_computation.47 | loop fusion | flops 552960 | bytes 552960 | tf_op jit(solution)/shard_map/concatenate | solution.py:124
  24.7 3.4 %collective-permute-start.2 = (bf16[4,30,1152]{2,0,1:T(4,128)(2,1)}, bf16[4,30,1152]{2,0,1:T(4,128)(2,1)S(1)}, u32[]{:S(2)}, u32[]{:S(2)}) collective-permute-start(bf16[4,30,1152]{2,0,1:T(4,128)(2,1)} %pad_maximum_fusion.3), channel_id=1, source_target_pairs={{0,32},{32,64},{64,96},{96,128},{128,160},{160,192},{192,224},{224... | collective-permute-start | bytes 829448 | tf_op jit(solution)/shard_map/ppermute | solution.py:11
  28.2 0.1 slice_convert_fusion.1
  28.3 0.1 fusion.49
  28.4 0.1 mul.536
  28.5 0.1 copy.91
  28.6 0.1 multiply_reduce_fusion.2
  28.8 1.1 %convolution_bitcast_fusion.2 = f32[9,45]{1,0:T(8,128)S(1)} fusion(f32[12,6,45]{2,0,1:T(8,128)} %constant.42, f32[9,12,6]{1,2,0:T(8,128)S(1)} %multiply_reduce_fusion.2), kind=kOutput, calls=%fused_computation.8 | convolution fusion | flops 349920 | bytes 17172 | tf_op jit(solution)/shard_map/dot_general | solution.py:105
  29.9 5.6 %collective-permute-start.3 = (bf16[3,30,1152]{2,1,0:T(8,128)(2,1)}, bf16[3,30,1152]{2,1,0:T(8,128)(2,1)}, u32[]{:S(2)}, u32[]{:S(2)}) collective-permute-start(bf16[3,30,1152]{2,1,0:T(8,128)(2,1)} %get-tuple-element.53), channel_id=1, source_target_pairs={{32,0},{64,32},{96,64},{128,96},{160,128},{192,160},{224,192},{256... | collective-permute-start | bytes 622088 | tf_op jit(solution)/shard_map/ppermute | solution.py:17
  35.5 3.3 %collective-permute-done.2 = bf16[4,30,1152]{2,0,1:T(4,128)(2,1)S(1)} collective-permute-done((bf16[4,30,1152]{2,0,1:T(4,128)(2,1)}, bf16[4,30,1152]{2,0,1:T(4,128)(2,1)S(1)}, u32[]{:S(2)}, u32[]{:S(2)}) %collective-permute-start.2) | collective-permute-done | bytes 276512 | tf_op jit(solution)/shard_map/ppermute | solution.py:11
  38.8 0.1 slice.575
  39.0 0.9 %copy.106 = bf16[1,24,1152]{1,2,0:T(8,128)(2,1)} copy(bf16[1,24,1152]{2,0,1:T(2,128)(2,1)S(1)} %slice.575) | data formatting | bytes 110592
  39.9 0.7 %convert_add_fusion.1 = f32[24,24]{0,1:T(8,128)S(1)} fusion(bf16[24,1152]{0,1:T(8,128)(2,1)} %bitcast.80), kind=kLoop, calls=%fused_computation.144 | loop fusion | flops 2880 | bytes 5760 | tf_op jit(solution)/shard_map/add | solution.py:81
  40.6 0.7 %slice_convert_fusion.3 = s32[24,4]{0,1:T(4,128)S(1)} fusion(bf16[24,1152]{0,1:T(8,128)(2,1)} %bitcast.81), kind=kLoop, calls=%fused_computation.158 | loop fusion | flops 96 | bytes 576 | tf_op jit(solution)/shard_map/convert_element_type | solution.py:95
  41.3 0.1 multiply_reduce_fusion.1
  41.4 0.2 convolution_bitcast_fusion.1
  41.7 3.3 %fusion.2 = f32[9,24,45]{2,1,0:T(8,128)S(1)} fusion(f32[9,24,4,12,6]{1,4,3,2,0:T(8,128)S(1)} %multiply_reduce_fusion, f32[4,12,6,45,1]{3,2,1,4,0:T(8,128)} %constant.45, f32[1,24,45]{2,1,0:T(8,128)S(1)} %convolution_bitcast_fusion.1, f32[9,1,45]{2,1,0:T(1,128)S(1)} %broadcast_in_dim.19, f32[9,24]{1,0:T(8,128)} %param.8), kind=kOutput, calls=%fused_computation.6 | convolution fusion | flops 33621480 | bytes 346356 | tf_op jit(solution)/shard_map/dot_general | solution.py:105
  45.0 1.1 %slice_reduce_fusion.44 = (f32[9,24]{1,0:T(8,128)S(1)}, f32[9,24]{1,0:T(8,128)S(1)}, f32[9,24]{1,0:T(8,128)S(1)}, f32[9,24]{1,0:T(8,128)S(1)}, f32[9,24]{1,0:T(8...) fusion(f32[9,24,45]{2,1,0:T(8,128)S(1)} %fusion.2), kind=kLoop, calls=%fused_computation.97 | loop fusion | bytes 32832 | tf_op jit(solution)/shard_map/slice | solution.py:165
  46.1 0.5 slice_reduce_fusion.42
  46.7 1.2 %slice_reduce_fusion.43 = (f32[9,24]{1,0:T(8,128)S(1)}, f32[9,24]{1,0:T(8,128)S(1)}, f32[9,24]{1,0:T(8,128)S(1)}, f32[9,24]{1,0:T(8,128)S(1)}, f32[9,24]{1,0:T(8...) fusion(f32[9,24,45]{2,1,0:T(8,128)S(1)} %fusion.2), kind=kLoop, calls=%fused_computation.96 | loop fusion | bytes 32832 | tf_op jit(solution)/shard_map/slice | solution.py:165
  47.9 1.2 %maximum_maximum_fusion = (bf16[12,30,1152]{2,1,0:T(8,128)(2,1)S(1)}, bf16[12,30,1152]{2,1,0:T(8,128)(2,1)S(1)}) fusion(bf16[9,3,1152]{2,1,0:T(4,128)(2,1)S(1)} %collective-permute-done.1, bf16[9,24,1152]{2,1,0:T(8,128)(2,1)S(1)} %copy-done, bf16[9,3,1152]{2,1,0:T(4,128)(2,1)S(1)} %bitcast.76, bf16[3,30,1152]{2,1,0:T(8,128)(2,1)S(1)} %copy.102, ...), kind=kLoop, calls=%fused_computation.35 | loop fusion | flops 6635520 | bytes 2695680 | tf_op jit(solution)/shard_map/concatenate | solution.py:126
  49.1 7.5 %add_convert_fusion = bf16[9,24,1152]{2,1,0:T(8,128)(2,1)} fusion(bf16[9,24,1152]{2,1,0:T(8,128)(2,1)S(1)} %copy-done, bf16[9,3,1152]{2,1,0:T(4,128)(2,1)S(1)} %bitcast.77, bf16[12,30,1152]{2,1,0:T(8,128)(2,1)S(1)} %get-tuple-element.51, bf16[9,27,1152]{2,1,0:T(8,128)(2,1)S(1)} %constant_dynamic-update-slice_fusion, ...), kind=kLoop, calls=%fused_computation.34 | loop fusion | flops 36080640 | bytes 21500640 | tf_op jit(solution)/shard_map/convert_element_type | solution.py:166
  (32 shorter events, 0.5 us)
Async XLA Ops:
  0.0 16.4 %copy-start.1 = (f32[2,9,24,4,6]{2,3,4,1,0:T(4,128)S(1)}, f32[2,9,24,4,6]{2,3,4,1,0:T(4,128)}, u32[]{:S(2)}) copy-start(f32[2,9,24,4,6]{2,3,4,1,0:T(4,128)} %param.6) | copy-start | bytes 124420
  0.0 16.4 %copy-start.2 = (s32[2,9,24,4]{2,3,1,0:T(4,128)S(1)}, s32[2,9,24,4]{2,3,1,0:T(4,128)}, u32[]{:S(2)}) copy-start(s32[2,9,24,4]{2,3,1,0:T(4,128)} %param.7) | copy-start | bytes 20740
  0.0 16.5 %copy-start = (bf16[9,24,1152]{2,1,0:T(8,128)(2,1)S(1)}, bf16[9,24,1152]{2,1,0:T(8,128)(2,1)}, u32[]{:S(2)}) copy-start(bf16[9,24,1152]{2,1,0:T(8,128)(2,1)} %param.5) | copy-start | bytes 1492996
  4.0 18.7 %collective-permute-start = (bf16[9,4,1152]{2,1,0:T(4,128)(2,1)S(1)}, bf16[9,4,1152]{2,1,0:T(4,128)(2,1)S(1)}, u32[]{:S(2)}, u32[]{:S(2)}) collective-permute-start(bf16[9,4,1152]{2,1,0:T(4,128)(2,1)S(1)} %pad_maximum_fusion.7), channel_id=1, source_target_pairs={{0,1},{1,2},{2,3},{3,4},{4,5},{5,6},{6,7},{7,8},{8,9},{9,10},{10,1... | collective-permute-start | bytes 248840 | tf_op jit(solution)/shard_map/ppermute | solution.py:11
  5.9 16.7 %collective-permute-start.1 = (bf16[9,3,1152]{2,1,0:T(4,128)(2,1)S(1)}, bf16[9,3,1152]{2,1,0:T(4,128)(2,1)S(1)}, u32[]{:S(2)}, u32[]{:S(2)}) collective-permute-start(bf16[9,3,1152]{2,1,0:T(4,128)(2,1)S(1)} %get-tuple-element.54), channel_id=1, source_target_pairs={{1,0},{2,1},{3,2},{4,3},{5,4},{6,5},{7,6},{8,7},{9,8},{10,9},{11,1... | collective-permute-start | bytes 186632 | tf_op jit(solution)/shard_map/ppermute | solution.py:17
  22.7 18.7 %copy-start.3 = (f32[12,6,45]{2,1,0:T(8,128)S(1)}, f32[12,6,45]{2,1,0:T(8,128)}, u32[]{:S(2)}) copy-start(f32[12,6,45]{2,1,0:T(8,128)} %constant.44) | copy-start | bytes 38884
  24.7 14.1 %collective-permute-start.2 = (bf16[4,30,1152]{2,0,1:T(4,128)(2,1)}, bf16[4,30,1152]{2,0,1:T(4,128)(2,1)S(1)}, u32[]{:S(2)}, u32[]{:S(2)}) collective-permute-start(bf16[4,30,1152]{2,0,1:T(4,128)(2,1)} %pad_maximum_fusion.3), channel_id=1, source_target_pairs={{0,32},{32,64},{64,96},{96,128},{128,160},{160,192},{192,224},{224... | collective-permute-start | bytes 829448 | tf_op jit(solution)/shard_map/ppermute | solution.py:11
  29.9 18.0 %collective-permute-start.3 = (bf16[3,30,1152]{2,1,0:T(8,128)(2,1)}, bf16[3,30,1152]{2,1,0:T(8,128)(2,1)}, u32[]{:S(2)}, u32[]{:S(2)}) collective-permute-start(bf16[3,30,1152]{2,1,0:T(8,128)(2,1)} %get-tuple-element.53), channel_id=1, source_target_pairs={{32,0},{64,32},{96,64},{128,96},{160,128},{192,160},{224,192},{256... | collective-permute-start | bytes 622088 | tf_op jit(solution)/shard_map/ppermute | solution.py:17

commit v5 on v4

--- a/solution.py
+++ b/solution.py
@@ -105,25 +105,39 @@
     return jnp.dot(flat, tables.reshape(-1, tables.shape[-1]), precision=lax.Precision.HIGHEST)
 
 
+def tap_sum(weights, padded, row0, col0, nrow, ncol, offsets, taps):
+    total = None
+    for tap in taps:
+        dr, dc = offsets[tap]
+        piece = lax.slice(
+            padded, (3 + row0 + dr, 3 + col0 + dc, 0), (3 + row0 + dr + nrow, 3 + col0 + dc + ncol, padded.shape[2])
+        )
+        term = weights[:, :, tap][:, :, None] * piece.astype(jnp.float32)
+        total = term if total is None else total + term
+    return total
+
+
 def local(tracer, moments, pieces, cell_area):
     rows = tracer.shape[0]
     cols = tracer.shape[1]
     width = tracer.shape[2]
     n_piece = moments.shape[3]
     n_moment = moments.shape[4]
-    tables, offsets = face_tables()
-    tables = jnp.asarray(tables, jnp.float32)
+    np_tables, offsets = face_tables()
+    tables = jnp.asarray(np_tables, jnp.float32)
+    west_taps = [t for t in range(len(offsets)) if np.abs(np_tables[0, ..., t]).sum() > 0]
+    south_taps = [t for t in range(len(offsets)) if np.abs(np_tables[2, ..., t]).sum() > 0]
 
-    west_pack = pack_weights(moments[0][:, cols - 1], pieces[0][:, cols - 1], width)[:, None]
-    from_west = from_prev(jnp.concatenate([tracer[:, cols - 3 :], west_pack], axis=1), "tile", True)
-    from_east = from_next(tracer[:, :3], "tile", True)
-    wide = jnp.concatenate([from_west[:, :3], tracer, from_east], axis=1)
-    south_pack = jnp.pad(
-        pack_weights(moments[1][rows - 1], pieces[1][rows - 1], width), ((3, 3), (0, 0))
-    )[None]
-    from_south = from_prev(jnp.concatenate([wide[rows - 3 :], south_pack], axis=0), "panel", False)
-    from_north = from_next(wide[:3], "panel", False)
-    padded = jnp.concatenate([from_south[:3], wide, from_north], axis=0)
+    south_pack = pack_weights(moments[1][rows - 1], pieces[1][rows - 1], width)[None]
+    from_south = from_prev(jnp.concatenate([tracer[rows - 3 :], south_pack], axis=0), "panel", False)
+    from_north = from_next(tracer[:3], "panel", False)
+    tall = jnp.concatenate([from_south[:3], tracer, from_north], axis=0)
+    west_pack = jnp.pad(
+        pack_weights(moments[0][:, cols - 1], pieces[0][:, cols - 1], width), ((3, 3), (0, 0))
+    )[:, None]
+    from_west = from_prev(jnp.concatenate([tall[:, cols - 3 :], west_pack], axis=1), "tile", True)
+    from_east = from_next(tall[:, :3], "tile", True)
+    padded = jnp.concatenate([from_west[:, :3], tall, from_east], axis=1)
 
     is_top = lax.axis_index("panel") == lax.axis_size("panel") - 1
     last_row = jnp.arange(rows) == rows - 1
@@ -149,20 +163,18 @@
         ],
         axis=2,
     )
-    weights = face_weights(face_m, face_p, tables)
+    weights = face_weights(face_m, face_p, tables) / cell_area[:, :, None]
 
-    west_m, west_p = unpack_weights(from_west[:, 3], n_piece, n_moment)
-    south_m, south_p = unpack_weights(from_south[3, 3 : 3 + cols], n_piece, n_moment)
-    west_fix = face_weights(west_m[:, None], west_p[:, None], tables[:1])
-    south_fix = face_weights(south_m[:, None], south_p[:, None], tables[2:3])
-    weights = weights + jnp.pad(west_fix[:, None], ((0, 0), (0, cols - 1), (0, 0)))
-    weights = weights + jnp.pad(south_fix[None], ((0, rows - 1), (0, 0), (0, 0)))
-    weights = weights / cell_area[:, :, None]
+    west_m, west_p = unpack_weights(from_west[3 : 3 + rows, 3], n_piece, n_moment)
+    south_m, south_p = unpack_weights(from_south[3], n_piece, n_moment)
+    west_fix = face_weights(west_m[:, None], west_p[:, None], tables[:1]) / cell_area[:, :1]
+    south_fix = face_weights(south_m[:, None], south_p[:, None], tables[2:3]) / cell_area[0][:, None]
 
-    total = tracer.astype(jnp.float32)
-    for tap, (dr, dc) in enumerate(offsets):
-        piece = lax.slice(padded, (3 + dr, 3 + dc, 0), (3 + dr + rows, 3 + dc + cols, width))
-        total = total + weights[:, :, tap][:, :, None] * piece.astype(jnp.float32)
+    total = tracer.astype(jnp.float32) + tap_sum(weights, padded, 0, 0, rows, cols, offsets, range(len(offsets)))
+    west_add = tap_sum(west_fix[:, None], padded, 0, 0, rows, 1, offsets, west_taps)
+    south_add = tap_sum(south_fix[None], padded, 0, 0, 1, cols, offsets, south_taps)
+    total = total + jnp.pad(west_add, ((0, 0), (0, cols - 1), (0, 0)))
+    total = total + jnp.pad(south_add, ((0, rows - 1), (0, 0), (0, 0)))
     return total.astype(jnp.bfloat16)
 
 

time: 57 us -> 54.8 us (0.961)
  the two profiles are of different devices: /device:TPU:48 before, /device:TPU:22 now
where the time goes in v5:
time: 54.8 us; the launch traced here: 54.4 us
  starting transfers between devices  23 us (42%)
  other arithmetic  17.2 us (31%)
  local copies, waits for them, and re-layouts  11 us (20%)
  matrix products  2.79 us (5%)
    ppermute x2, starting transfers between devices, from_next(): return lax.ppermute(value, axis, pairs)  13.8 us
    ppermute x2, starting transfers between devices, from_prev(): return lax.ppermute(value, axis, pairs)  9.25 us
    convert_element_type x1, other arithmetic, local(): return total.astype(jnp.bfloat16)  7.94 us
    reduce_sum x3, other arithmetic, face_weights(): spread = jnp.sum(onehot[..., :, None] * moments[..., None, :], axis=-3)  4.89 us
    slice x7, local copies, waits for them, and re-layouts, tap_sum(): term = weights[:, :, tap][:, :, None] * piece.astype(jnp.float32)  4.64 us
    dot_general x3, matrix products, face_weights(): jnp.dot(flat, tables.reshape(-1, tables.shape[-1]), precision=lax.Precisi...  2.79 us
    add x2, other arithmetic, tap_sum(): total = term if total is None else total + term  1.77 us
    another operation x2, local copies, waits for them, and re-layouts, local(): jnp.stack([jnp.concatenate([zero_col, moments[0][:, :cols - 1]], axis=1),...  1.11 us
  transfers between devices with their start and end apart: 4, of which 0 were waited for; matrix products, arithmetic and copies ran while one was open for 35% of the time, Pallas kernels for 0%

profile of v5, /device:TPU:22, one launch (start us, length us, event | category | flops | bytes accessed | tf_op | source)
XLA Modules:
  0.0 54.4 jit_solution(7982089009319253397)
XLA Ops:
  0.0 1.1 %fusion.108 = (bf16[3,24,1152]{2,1,0:T(8,128)(2,1)S(1)}, bf16[3,24,1152]{2,1,0:T(8,128)(2,1)S(1)}) fusion(bf16[9,24,1152]{2,1,0:T(8,128)(2,1)} %param.5), kind=kLoop, calls=%fused_computation.310 | loop fusion | bytes 663552 | tf_op jit(solution)/shard_map/slice | solution.py:132
  1.1 2.7 %collective-permute-start.1 = (bf16[3,24,1152]{2,1,0:T(8,128)(2,1)S(1)}, bf16[3,24,1152]{2,1,0:T(8,128)(2,1)S(1)}, u32[]{:S(2)}, u32[]{:S(2)}) collective-permute-start(bf16[3,24,1152]{2,1,0:T(8,128)(2,1)S(1)} %get-tuple-element.113), channel_id=1, source_target_pairs={{32,0},{64,32},{96,64},{128,96},{160,128},{192,160},{224,192},{256... | collective-permute-start | bytes 497672 | tf_op jit(solution)/shard_map/ppermute | solution.py:17
  3.9 0.7 %slice_bitcast_fusion.8 = (s32[1,24,4]{1,2,0:T(4,128)S(1)}, bf16[24,4]{0,1:T(4,128)(2,1)S(1)}) fusion(s32[2,9,24,4]{2,3,1,0:T(4,128)} %param.7), kind=kLoop, calls=%fused_computation.306 | loop fusion | flops 96 | bytes 1344 | tf_op jit(solution)/shard_map/slice | solution.py:161
  4.6 0.1 copy.371
  4.7 0.7 %slice.872 = f32[1,1,24,4,6]{2,3,4,1,0:T(4,128)S(1)} slice(f32[2,9,24,4,6]{2,3,4,1,0:T(4,128)} %param.6), slice={[1:2], [8:9], [0:24], [0:4], [0:6]} | slice | bytes 4608 | tf_op jit(solution)/shard_map/slice | solution.py:131
  5.4 0.1 copy.368
  5.5 0.1 copy.370
  5.6 0.1 copy.369
  5.6 0.1 fusion.46
  5.8 7.3 %collective-permute-start = (bf16[4,24,1152]{2,1,0:T(8,128)(2,1)S(1)}, bf16[4,24,1152]{2,1,0:T(8,128)(2,1)S(1)}, u32[]{:S(2)}, u32[]{:S(2)}) collective-permute-start(bf16[4,24,1152]{2,1,0:T(8,128)(2,1)S(1)} %pad_maximum_fusion.2), channel_id=1, source_target_pairs={{0,32},{32,64},{64,96},{96,128},{128,160},{160,192},{192,224},{224... | collective-permute-start | bytes 663560 | tf_op jit(solution)/shard_map/ppermute | solution.py:11
  13.1 0.7 %slice_bitcast_fusion.5 = s32[8,24,4]{1,2,0:T(4,128)S(1)} fusion(s32[2,9,24,4]{2,3,1,0:T(4,128)} %param.7), kind=kLoop, calls=%fused_computation.230 | loop fusion | bytes 6144 | tf_op jit(solution)/shard_map/slice | solution.py:161
  13.8 0.7 %slice_bitcast_fusion.6 = (s32[9,24,1,4]{1,3,0,2:T(4,128)S(1)}, s32[9,24,4]{1,2,0:T(4,128)S(1)}, s32[9,24,1,4]{1,3,0,2:T(4,128)S(1)}) fusion(s32[2,9,24,4]{2,3,1,0:T(4,128)} %param.7), kind=kLoop, calls=%fused_computation.231 | loop fusion | bytes 17280 | tf_op jit(solution)/shard_map/stack;squeeze | solution.py:157
  14.6 1.0 %slice_bitcast_fusion.1 = (f32[9,24,1,4,6]{1,3,4,0,2:T(4,128)S(1)}, f32[9,24,4,6]{1,2,3,0:T(4,128)S(1)}, f32[9,24,4,6]{1,2,3,0:T(4,128)S(1)}) fusion(f32[2,9,24,4,6]{2,3,4,1,0:T(4,128)} %param.6), kind=kLoop, calls=%fused_computation.125 | loop fusion | bytes 103680 | tf_op jit(solution)/shard_map/stack;squeeze | solution.py:148
  15.8 0.1 bitcast_multiply_fusion
  15.8 0.1 slice.1111
  16.0 0.1 slice_multiply_fusion
  16.1 0.1 pad_bitcast_fusion
  16.2 0.1 add_bitcast_fusion
  16.3 0.2 fusion.29
  16.5 4.6 %multiply_reduce_fusion = f32[9,24,4,12,6]{1,4,3,2,0:T(8,128)S(1)} fusion(f32[9,24,4,4,12]{1,3,4,2,0:T(4,128)S(1)} %fusion.29, f32[9,24,1,4,6]{1,3,4,0,2:T(4,128)S(1)} %bitcast_multiply_fusion, f32[9,24,1,4,6]{1,3,4,0,2:T(4,128)S(1)} %get-tuple-element.130, f32[9,24,1,4,6]{1,3,4,0,2:T(4,128)S(1)} %get-tuple-element.114, ...), kind=kLoop, calls=%fused_computation | loop fusion | flops 497664 | bytes 497664 | tf_op jit(solution)/shard_map/reduce_sum | solution.py:102
  21.2 2.3 %fusion = f32[9,24,45]{2,1,0:T(8,128)S(1)} fusion(f32[9,24,4,12,6]{1,4,3,2,0:T(8,128)S(1)} %multiply_reduce_fusion, f32[4,12,6,45,1]{3,2,1,4,0:T(8,128)S(1)} %copy-done.5, f32[9,24]{1,0:T(8,128)S(1)} %copy-done.4), kind=kOutput, calls=%fused_computation.12 | convolution fusion | flops 33602040 | bytes 340416 | tf_op jit(solution)/shard_map/dot_general | solution.py:105
  23.5 0.5 slice_reduce_fusion.42
  24.0 1.2 %slice_reduce_fusion.43 = (f32[9,24]{1,0:T(8,128)S(1)}, f32[9,24]{1,0:T(8,128)S(1)}, f32[9,24]{1,0:T(8,128)S(1)}, f32[9,24]{1,0:T(8,128)S(1)}, f32[9,24]{1,0:T(8...) fusion(f32[9,24,45]{2,1,0:T(8,128)S(1)} %fusion), kind=kLoop, calls=%fused_computation.111 | loop fusion | bytes 32832 | tf_op jit(solution)/shard_map/slice | solution.py:115
  25.2 0.1 copy.373
  25.3 0.1 copy.374
  25.4 0.3 copy.372
  25.8 0.1 reshape_squeeze.7
  25.8 0.1 fusion.102
  26.0 0.1 slice_reduce_fusion.105
  26.2 1.1 %slice_reduce_fusion.44 = (f32[9,24]{1,0:T(8,128)S(1)}, f32[9,24]{1,0:T(8,128)S(1)}, f32[9,24]{1,0:T(8,128)S(1)}, f32[9,24]{1,0:T(8,128)S(1)}, f32[9,24]{1,0:T(8...) fusion(f32[9,24,45]{2,1,0:T(8,128)S(1)} %fusion), kind=kLoop, calls=%fused_computation.117 | loop fusion | bytes 32832 | tf_op jit(solution)/shard_map/slice | solution.py:115
  27.5 0.1 copy.384
  27.8 0.2 fusion.34
  27.9 1.9 %collective-permute-start.2 = (bf16[15,4,1152]{2,1,0:T(4,128)(2,1)S(1)}, bf16[15,4,1152]{2,1,0:T(4,128)(2,1)S(1)}, u32[]{:S(2)}, u32[]{:S(2)}) collective-permute-start(bf16[15,4,1152]{2,1,0:T(4,128)(2,1)S(1)} %fusion.34), channel_id=1, source_target_pairs={{0,1},{1,2},{2,3},{3,4},{4,5},{5,6},{6,7},{7,8},{8,9},{9,10},{10,1... | collective-permute-start | bytes 414728 | tf_op jit(solution)/shard_map/ppermute | solution.py:11
  29.9 0.1 multiply_reduce_fusion.1
  30.0 0.2 fusion.2
  30.3 0.4 slice_reduce_fusion.73
  30.7 11.0 %collective-permute-start.3 = (bf16[15,3,1152]{2,1,0:T(4,128)(2,1)S(1)}, bf16[15,3,1152]{2,1,0:T(4,128)(2,1)S(1)}, u32[]{:S(2)}, u32[]{:S(2)}) collective-permute-start(bf16[15,3,1152]{2,1,0:T(4,128)(2,1)S(1)} %pad_maximum_fusion.3), channel_id=1, source_target_pairs={{1,0},{2,1},{3,2},{4,3},{5,4},{6,5},{7,6},{8,7},{9,8},{10,9},{11,1... | collective-permute-start | bytes 311048 | tf_op jit(solution)/shard_map/ppermute | solution.py:17
  41.7 0.5 slice_reduce_fusion.74
  42.5 0.1 mul.1271
  42.6 0.1 copy.376
  42.7 0.1 multiply_reduce_fusion.2
  42.9 0.2 fusion.4
  43.2 0.5 slice_reduce_fusion.104
  43.7 0.4 slice_reduce_fusion.103
  44.1 0.6 %maximum_maximum_fusion = (bf16[15,27,1152]{2,1,0:T(8,128)(2,1)S(1)}, bf16[15,27,1152]{2,1,0:T(8,128)(2,1)S(1)}) fusion(bf16[3,24,1152]{2,1,0:T(8,128)(2,1)S(1)} %collective-permute-done.1, bf16[9,24,1152]{2,1,0:T(8,128)(2,1)S(1)} %copy-done, bf16[3,24,1152]{2,1,0:T(8,128)(2,1)S(1)} %slice.1110, bf16[15,3,1152]{2,1,0:T(4,128)(2,1)S(1)} %bitcast.84, ...), kind=kLoop, calls=%fused_computation.17 | loop fusion | flops 7464960 | bytes 2903040 | tf_op jit(solution)/shard_map/concatenate | solution.py:140
  44.6 1.2 %fusion.54 = f32[9,1,1152]{2,1,0:T(1,128)S(1)} fusion(bf16[12,24,1152]{2,1,0:T(8,128)(2,1)S(1)} %constant_dynamic-update-slice_fusion, bf16[15,4,1152]{2,1,0:T(4,128)(2,1)S(1)} %collective-permute-done.2, bf16[9,24,1152]{2,1,0:T(8,128)(2,1)S(1)} %copy-done, bf16[3,24,1152]{2,1,0:T(8,128)(2,1)S(1)} %slice.1110, f32[9]{0:T(128)S(1)} %get-tuple-element.81, ...), kind=kLoop, calls=%fused_computation.146 | loop fusion | flops 1109376 | bytes 1715712 | tf_op jit(solution)/shard_map/add | solution.py:116
  45.9 0.5 multiply_add_fusion
  46.4 7.9 %add_convert_fusion = bf16[9,24,1152]{2,1,0:T(8,128)(2,1)} fusion(f32[1,24,1152]{2,1,0:T(8,128)S(1)} %multiply_add_fusion, f32[9,1,1152]{2,1,0:T(1,128)S(1)} %fusion.54, bf16[9,24,1152]{2,1,0:T(8,128)(2,1)S(1)} %copy-done, bf16[3,24,1152]{2,1,0:T(8,128)(2,1)S(1)} %slice.1110, bf16[15,27,1152]{2,1,0:T(8,128)(2,1)S(1)} %get-tuple-element.111, ...), kind=kLoop, calls=%fused_computation.45 | loop fusion | flops 35085312 | bytes 21756384 | tf_op jit(solution)/shard_map/convert_element_type | solution.py:178
  (43 shorter events, 0.9 us)
Async XLA Ops:
  0.0 15.6 %copy-start = (bf16[9,24,1152]{2,1,0:T(8,128)(2,1)S(1)}, bf16[9,24,1152]{2,1,0:T(8,128)(2,1)}, u32[]{:S(2)}) copy-start(bf16[9,24,1152]{2,1,0:T(8,128)(2,1)} %param.5) | copy-start | bytes 1492996
  0.0 15.7 %copy-start.1 = (f32[2,9,24,4,6]{2,3,4,1,0:T(4,128)S(1)}, f32[2,9,24,4,6]{2,3,4,1,0:T(4,128)}, u32[]{:S(2)}) copy-start(f32[2,9,24,4,6]{2,3,4,1,0:T(4,128)} %param.6) | copy-start | bytes 124420
  0.0 15.6 %copy-start.4 = (f32[9,24]{1,0:T(8,128)S(1)}, f32[9,24]{1,0:T(8,128)}, u32[]{:S(2)}) copy-start(f32[9,24]{1,0:T(8,128)} %param.8) | copy-start | bytes 2596
  1.1 26.2 %collective-permute-start.1 = (bf16[3,24,1152]{2,1,0:T(8,128)(2,1)S(1)}, bf16[3,24,1152]{2,1,0:T(8,128)(2,1)S(1)}, u32[]{:S(2)}, u32[]{:S(2)}) collective-permute-start(bf16[3,24,1152]{2,1,0:T(8,128)(2,1)S(1)} %get-tuple-element.113), channel_id=1, source_target_pairs={{32,0},{64,32},{96,64},{128,96},{160,128},{192,160},{224,192},{256... | collective-permute-start | bytes 497672 | tf_op jit(solution)/shard_map/ppermute | solution.py:17
  5.8 21.6 %collective-permute-start = (bf16[4,24,1152]{2,1,0:T(8,128)(2,1)S(1)}, bf16[4,24,1152]{2,1,0:T(8,128)(2,1)S(1)}, u32[]{:S(2)}, u32[]{:S(2)}) collective-permute-start(bf16[4,24,1152]{2,1,0:T(8,128)(2,1)S(1)} %pad_maximum_fusion.2), channel_id=1, source_target_pairs={{0,32},{32,64},{64,96},{96,128},{128,160},{160,192},{192,224},{224... | collective-permute-start | bytes 663560 | tf_op jit(solution)/shard_map/ppermute | solution.py:11
  16.5 4.7 %copy-start.5 = (f32[4,12,6,45,1]{3,2,1,4,0:T(8,128)S(1)}, f32[4,12,6,45,1]{3,2,1,4,0:T(8,128)}, u32[]{:S(2)}) copy-start(f32[4,12,6,45,1]{3,2,1,4,0:T(8,128)} %constant.45) | copy-start | bytes 155524
  26.1 3.8 %copy-start.2 = (f32[12,6,45]{2,1,0:T(8,128)S(1)}, f32[12,6,45]{2,1,0:T(8,128)}, u32[]{:S(2)}) copy-start(f32[12,6,45]{2,1,0:T(8,128)} %constant.44) | copy-start | bytes 38884
  27.3 15.6 %copy-start.3 = (f32[12,6,45]{2,0,1:T(8,128)S(1)}, f32[12,6,45]{2,0,1:T(8,128)}, u32[]{:S(2)}) copy-start(f32[12,6,45]{2,0,1:T(8,128)} %constant.42) | copy-start | bytes 38884
  27.9 14.3 %collective-permute-start.2 = (bf16[15,4,1152]{2,1,0:T(4,128)(2,1)S(1)}, bf16[15,4,1152]{2,1,0:T(4,128)(2,1)S(1)}, u32[]{:S(2)}, u32[]{:S(2)}) collective-permute-start(bf16[15,4,1152]{2,1,0:T(4,128)(2,1)S(1)} %fusion.34), channel_id=1, source_target_pairs={{0,1},{1,2},{2,3},{3,4},{4,5},{5,6},{6,7},{7,8},{8,9},{9,10},{10,1... | collective-permute-start | bytes 414728 | tf_op jit(solution)/shard_map/ppermute | solution.py:11
  30.7 13.4 %collective-permute-start.3 = (bf16[15,3,1152]{2,1,0:T(4,128)(2,1)S(1)}, bf16[15,3,1152]{2,1,0:T(4,128)(2,1)S(1)}, u32[]{:S(2)}, u32[]{:S(2)}) collective-permute-start(bf16[15,3,1152]{2,1,0:T(4,128)(2,1)S(1)} %pad_maximum_fusion.3), channel_id=1, source_target_pairs={{1,0},{2,1},{3,2},{4,3},{5,4},{6,5},{7,6},{8,7},{9,8},{10,9},{11,1... | collective-permute-start | bytes 311048 | tf_op jit(solution)/shard_map/ppermute | solution.py:17

commit v6 on v5

--- a/solution.py
+++ b/solution.py
@@ -1,8 +1,16 @@
+import functools
+import math
+
 import jax
 import jax.numpy as jnp
 import numpy as np
 from jax import lax
+from jax.experimental import pallas as pl
+from jax.experimental.pallas import tpu as pltpu
 from jax.sharding import PartitionSpec as P
+
+
+INTERPRET = False
 
 
 def from_prev(value, axis, wrap):
@@ -115,6 +123,32 @@
         term = weights[:, :, tap][:, :, None] * piece.astype(jnp.float32)
         total = term if total is None else total + term
     return total
+
+
+def tap_kernel(offsets, chunk, w_ref, p_ref, t_ref, o_ref, s_ref):
+    s_ref[...] = p_ref[...].astype(jnp.float32)
+    rows, cols, width = t_ref.shape
+
+    def row(i, carry):
+        for start in range(0, width, chunk):
+            lanes = pl.ds(start, chunk)
+            acc = t_ref[i, :, lanes].astype(jnp.float32)
+            for tap, (dr, dc) in enumerate(offsets):
+                w = w_ref[i, :, tap : tap + 1]
+                acc = acc + w * s_ref[i + 3 + dr, pl.ds(3 + dc, cols), lanes]
+            o_ref[i, :, lanes] = acc.astype(o_ref.dtype)
+        return carry
+
+    lax.fori_loop(0, rows, row, 0)
+
+
+def apply_taps(weights, padded, tracer, offsets):
+    return pl.pallas_call(
+        functools.partial(tap_kernel, offsets, math.gcd(tracer.shape[2], 384)),
+        out_shape=jax.ShapeDtypeStruct(tracer.shape, jnp.bfloat16),
+        scratch_shapes=[pltpu.VMEM(padded.shape, jnp.float32)],
+        interpret=INTERPRET,
+    )(weights, padded, tracer)
 
 
 def local(tracer, moments, pieces, cell_area):
@@ -163,19 +197,17 @@
         ],
         axis=2,
     )
-    weights = face_weights(face_m, face_p, tables) / cell_area[:, :, None]
+    weights = face_weights(face_m, face_p, tables)
+    weights = lax.optimization_barrier(weights)
 
     west_m, west_p = unpack_weights(from_west[3 : 3 + rows, 3], n_piece, n_moment)
     south_m, south_p = unpack_weights(from_south[3], n_piece, n_moment)
-    west_fix = face_weights(west_m[:, None], west_p[:, None], tables[:1]) / cell_area[:, :1]
-    south_fix = face_weights(south_m[:, None], south_p[:, None], tables[2:3]) / cell_area[0][:, None]
-
-    total = tracer.astype(jnp.float32) + tap_sum(weights, padded, 0, 0, rows, cols, offsets, range(len(offsets)))
-    west_add = tap_sum(west_fix[:, None], padded, 0, 0, rows, 1, offsets, west_taps)
-    south_add = tap_sum(south_fix[None], padded, 0, 0, 1, cols, offsets, south_taps)
-    total = total + jnp.pad(west_add, ((0, 0), (0, cols - 1), (0, 0)))
-    total = total + jnp.pad(south_add, ((0, rows - 1), (0, 0), (0, 0)))
-    return total.astype(jnp.bfloat16)
+    west_fix = face_weights(west_m[:, None], west_p[:, None], tables[:1])
+    south_fix = face_weights(south_m[:, None], south_p[:, None], tables[2:3])
+    weights = weights + jnp.pad(west_fix[:, None], ((0, 0), (0, cols - 1), (0, 0)))
+    weights = weights + jnp.pad(south_fix[None], ((0, rows - 1), (0, 0), (0, 0)))
+    weights = weights / cell_area[:, :, None]
+    return apply_taps(weights, padded, tracer, offsets)
 
 
 def solution(mesh):

time: 54.8 us -> 51.4 us (0.938)
  the two profiles are of different devices: /device:TPU:22 before, /device:TPU:233 now
where the time goes in v6:
time: 51.4 us; the launch traced here: 51 us
  starting transfers between devices  18.5 us (36%)
  Pallas kernels  9.83 us (19%)
  other arithmetic  9.21 us (18%)
  local copies, waits for them, and re-layouts  5.82 us (11%)
  waiting for transfers between devices  4.48 us (9%)
  matrix products  2.8 us (5%)
    ppermute x2, starting transfers between devices, from_prev(): return lax.ppermute(value, axis, pairs)  10.2 us
    pallas_call x1, Pallas kernels, apply_taps(): pl.pallas_call(functools.partial(tap_kernel, offsets, math.gcd(tracer.sha...  9.83 us
    ppermute x2, starting transfers between devices, from_next(): return lax.ppermute(value, axis, pairs)  8.3 us
    reduce_sum x3, other arithmetic, face_weights(): spread = jnp.sum(onehot[..., :, None] * moments[..., None, :], axis=-3)  4.89 us
    ppermute x2, waiting for transfers between devices, from_next(): return lax.ppermute(value, axis, pairs)  3.36 us
    dot_general x3, matrix products, face_weights(): jnp.dot(flat, tables.reshape(-1, tables.shape[-1]), precision=lax.Precisi...  2.8 us
    concatenate x1, other arithmetic, local(): padded = jnp.concatenate([from_west[:, :3], tall, from_east], axis=1)  1.47 us
    ppermute x2, waiting for transfers between devices, from_prev(): return lax.ppermute(value, axis, pairs)  1.12 us
  transfers between devices with their start and end apart: 4, of which 2 were waited for; matrix products, arithmetic and copies ran while one was open for 26% of the time, Pallas kernels for 0%

profile of v6, /device:TPU:233, one launch (start us, length us, event | category | flops | bytes accessed | tf_op | source)
XLA Modules:
  0.0 51.0 jit_solution(154424526047954484)
XLA Ops:
  0.0 0.7 %slice_bitcast_fusion.8 = (s32[1,24,4]{1,2,0:T(4,128)S(1)}, bf16[24,4]{0,1:T(4,128)(2,1)S(1)}) fusion(s32[2,9,24,4]{2,3,1,0:T(4,128)} %param.7), kind=kLoop, calls=%fused_computation.73 | loop fusion | flops 96 | bytes 1344 | tf_op jit(solution)/shard_map/slice | solution.py:195
  0.7 0.1 copy.48
  0.8 0.7 %slice.140 = f32[1,1,24,4,6]{2,3,4,1,0:T(4,128)S(1)} slice(f32[2,9,24,4,6]{2,3,4,1,0:T(4,128)} %param.6), slice={[1:2], [8:9], [0:24], [0:4], [0:6]} | slice | bytes 4608 | tf_op jit(solution)/shard_map/slice | solution.py:165
  1.6 0.1 copy.46
  1.7 1.0 %fusion.24 = (bf16[3,24,1152]{2,1,0:T(8,128)(2,1)S(1)}, bf16[3,24,1152]{2,1,0:T(8,128)(2,1)S(1)}) fusion(bf16[9,24,1152]{2,1,0:T(8,128)(2,1)} %t_ref.1), kind=kLoop, calls=%fused_computation.76 | loop fusion | bytes 663552 | tf_op jit(solution)/shard_map/slice | solution.py:167
  2.7 0.1 fusion.14
  2.8 3.1 %collective-permute-start = (bf16[4,24,1152]{2,1,0:T(8,128)(2,1)S(1)}, bf16[4,24,1152]{2,1,0:T(8,128)(2,1)S(1)}, u32[]{:S(2)}, u32[]{:S(2)}) collective-permute-start(bf16[4,24,1152]{2,1,0:T(8,128)(2,1)S(1)} %pad_maximum_fusion.2), channel_id=1, source_target_pairs={{0,32},{32,64},{64,96},{96,128},{128,160},{160,192},{192,224},{224... | collective-permute-start | bytes 663560 | tf_op jit(solution)/shard_map/ppermute | solution.py:19
  5.9 6.4 %collective-permute-start.1 = (bf16[3,24,1152]{2,1,0:T(8,128)(2,1)S(1)}, bf16[3,24,1152]{2,1,0:T(8,128)(2,1)S(1)}, u32[]{:S(2)}, u32[]{:S(2)}) collective-permute-start(bf16[3,24,1152]{2,1,0:T(8,128)(2,1)S(1)} %get-tuple-element.5), channel_id=1, source_target_pairs={{32,0},{64,32},{96,64},{128,96},{160,128},{192,160},{224,192},{256... | collective-permute-start | bytes 497672 | tf_op jit(solution)/shard_map/ppermute | solution.py:25
  12.3 0.7 %slice_bitcast_fusion.7 = (s32[9,24,4]{1,2,0:T(4,128)S(1)}, s32[9,24,1,4]{1,3,0,2:T(4,128)S(1)}, s32[9,24,1,4]{1,3,0,2:T(4,128)S(1)}) fusion(s32[2,9,24,4]{2,3,1,0:T(4,128)} %param.7), kind=kLoop, calls=%fused_computation.61 | loop fusion | bytes 17280 | tf_op jit(solution)/shard_map/squeeze | solution.py:193
  13.1 0.7 %slice_bitcast_fusion.5 = s32[8,24,4]{1,2,0:T(4,128)S(1)} fusion(s32[2,9,24,4]{2,3,1,0:T(4,128)} %param.7), kind=kLoop, calls=%fused_computation.59 | loop fusion | bytes 6144 | tf_op jit(solution)/shard_map/slice | solution.py:195
  13.8 1.0 %slice_bitcast_fusion.2 = (f32[9,24,4,6]{1,2,3,0:T(4,128)S(1)}, f32[9,24,1,4,6]{1,3,4,0,2:T(4,128)S(1)}, f32[9,24,4,6]{1,2,3,0:T(4,128)S(1)}) fusion(f32[2,9,24,4,6]{2,3,4,1,0:T(4,128)} %param.6), kind=kLoop, calls=%fused_computation.29 | loop fusion | bytes 103680 | tf_op jit(solution)/shard_map/squeeze | solution.py:184
  14.8 0.1 slice_convert_fusion
  14.9 0.1 bitcast_multiply_fusion
  15.0 0.1 slice.168
  15.1 0.1 slice_multiply_fusion
  15.2 0.1 pad_bitcast_fusion
  15.3 0.1 add_bitcast_fusion
  15.4 0.2 fusion
  15.6 0.0 copy-start.5
  15.6 4.6 %multiply_reduce_fusion = f32[9,24,4,12,6]{1,4,3,2,0:T(8,128)S(1)} fusion(f32[9,24,4,4,12]{1,3,4,2,0:T(4,128)S(1)} %fusion, f32[9,24,1,4,6]{1,3,4,0,2:T(4,128)S(1)} %bitcast_multiply_fusion, f32[9,24,1,4,6]{1,3,4,0,2:T(4,128)S(1)} %get-tuple-element.23, f32[9,24,1,4,6]{1,3,4,0,2:T(4,128)S(1)} %get-tuple-element.8, f32[9,24,1,4,6]{1,3,4,0,2:T(4,128)S(1)} %get-tuple-element.24), kind=kLoop, calls=%fused_computation | loop fusion | flops 497664 | bytes 497664 | tf_op jit(solution)/shard_map/reduce_sum | solution.py:110
  20.3 2.3 %convolution_bitcast_fusion = f32[9,24,45]{2,1,0:T(8,128)S(1)} fusion(f32[9,24,4,12,6]{1,4,3,2,0:T(8,128)S(1)} %multiply_reduce_fusion, f32[4,12,6,45,1]{3,2,1,4,0:T(8,128)S(1)} %copy-done.5), kind=kOutput, calls=%fused_computation.1 | convolution fusion | flops 33592320 | bytes 339552 | tf_op jit(solution)/shard_map/dot_general | solution.py:113
  22.6 0.1 copy.50
  22.8 0.1 copy.51
  22.9 0.3 copy.49
  23.2 0.1 reshape_squeeze.7
  23.3 0.1 fusion.18
  23.4 0.1 copy.52
  23.5 0.1 convert_add_fusion
  23.6 0.1 slice_convert_fusion.1
  23.7 0.1 copy.56
  23.7 0.1 copy.55
  23.9 0.2 fusion.2
  24.1 7.1 %collective-permute-start.2 = (bf16[15,4,1152]{2,1,0:T(4,128)(2,1)S(1)}, bf16[15,4,1152]{2,1,0:T(4,128)(2,1)S(1)}, u32[]{:S(2)}, u32[]{:S(2)}) collective-permute-start(bf16[15,4,1152]{2,1,0:T(4,128)(2,1)S(1)} %fusion.2), channel_id=1, source_target_pairs={{0,1},{1,2},{2,3},{3,4},{4,5},{5,6},{6,7},{7,8},{8,9},{9,10},{10,1... | collective-permute-start | bytes 414728 | tf_op jit(solution)/shard_map/ppermute | solution.py:19
  31.2 1.9 %collective-permute-start.3 = (bf16[15,3,1152]{2,1,0:T(4,128)(2,1)S(1)}, bf16[15,3,1152]{2,1,0:T(4,128)(2,1)S(1)}, u32[]{:S(2)}, u32[]{:S(2)}) collective-permute-start(bf16[15,3,1152]{2,1,0:T(4,128)(2,1)S(1)} %pad_maximum_fusion.3), channel_id=1, source_target_pairs={{1,0},{2,1},{3,2},{4,3},{5,4},{6,5},{7,6},{8,7},{9,8},{10,9},{11,1... | collective-permute-start | bytes 311048 | tf_op jit(solution)/shard_map/ppermute | solution.py:25
  33.2 0.1 multiply_reduce_fusion.1
  33.3 0.2 convolution_bitcast_fusion.1
  33.5 1.1 %collective-permute-done.2 = bf16[15,4,1152]{2,1,0:T(4,128)(2,1)S(1)} collective-permute-done((bf16[15,4,1152]{2,1,0:T(4,128)(2,1)S(1)}, bf16[15,4,1152]{2,1,0:T(4,128)(2,1)S(1)}, u32[]{:S(2)}, u32[]{:S(2)}) %collective-permute-start.2) | collective-permute-done | bytes 138272 | tf_op jit(solution)/shard_map/ppermute | solution.py:19
  34.7 0.1 convert_add_fusion.1
  34.8 0.1 slice_convert_fusion.2
  34.8 0.1 mul.86
  34.9 0.1 copy.53
  35.1 0.1 fusion.20
  35.2 0.1 multiply_reduce_fusion.2
  35.3 0.3 convolution_bitcast_fusion.2
  35.6 0.7 %add_divide_fusion.w_ref = f32[9,24,45]{2,1,0:T(8,128)} fusion(f32[1,24,45]{2,1,0:T(8,128)S(1)} %convolution_bitcast_fusion.1, f32[9,24,45]{2,1,0:T(8,128)S(1)} %convolution_bitcast_fusion, f32[9,1,45]{2,1,0:T(1,128)S(1)} %broadcast_in_dim.36, f32[9,24]{1,0:T(8,128)S(1)} %copy-done.4), kind=kLoop, calls=%fused_computation.22 | loop fusion | flops 29160 | bytes 84564 | tf_op jit(solution)/shard_map/div | solution.py:209
  36.3 3.4 %collective-permute-done.3 = bf16[15,3,1152]{2,1,0:T(4,128)(2,1)S(1)} collective-permute-done((bf16[15,3,1152]{2,1,0:T(4,128)(2,1)S(1)}, bf16[15,3,1152]{2,1,0:T(4,128)(2,1)S(1)}, u32[]{:S(2)}, u32[]{:S(2)}) %collective-permute-start.3) | collective-permute-done | bytes 103712 | tf_op jit(solution)/shard_map/ppermute | solution.py:25
  39.7 1.5 %pad_maximum_fusion.p_ref = bf16[15,30,1152]{2,1,0:T(8,128)(2,1)} fusion(bf16[15,3,1152]{2,1,0:T(4,128)(2,1)S(1)} %collective-permute-done.3, bf16[3,24,1152]{2,1,0:T(8,128)(2,1)S(1)} %collective-permute-done.1, bf16[9,24,1152]{2,1,0:T(8,128)(2,1)S(1)} %copy-done, bf16[3,24,1152]{2,1,0:T(8,128)(2,1)S(1)} %slice.167, bf16[15,3,1152]{2,1,0:T(4,128)(2,1)S(1)} %bitcast.71), kind=kLoop, calls=%fused_computation.4 | loop fusion | flops 5184000 | bytes 2073600 | tf_op jit(solution)/shard_map/concatenate | solution.py:174
  41.2 9.8 %shard_map.55 = bf16[9,24,1152]{2,1,0:T(8,128)(2,1)} custom-call(f32[9,24,45]{2,1,0:T(8,128)} %add_divide_fusion.w_ref, bf16[15,30,1152]{2,1,0:T(8,128)(2,1)} %pad_maximum_fusion.p_ref, bf16[9,24,1152]{2,1,0:T(8,128)(2,1)} %t_ref.1), custom_call_target="tpu_custom_call" | custom-call | tf_op jit(solution)/shard_map/pallas_call | solution.py:146
  (29 shorter events, 0.3 us)
Async XLA Ops:
  0.0 14.9 %copy-start.1 = (f32[2,9,24,4,6]{2,3,4,1,0:T(4,128)S(1)}, f32[2,9,24,4,6]{2,3,4,1,0:T(4,128)}, u32[]{:S(2)}) copy-start(f32[2,9,24,4,6]{2,3,4,1,0:T(4,128)} %param.6) | copy-start | bytes 124420
  2.8 20.7 %collective-permute-start = (bf16[4,24,1152]{2,1,0:T(8,128)(2,1)S(1)}, bf16[4,24,1152]{2,1,0:T(8,128)(2,1)S(1)}, u32[]{:S(2)}, u32[]{:S(2)}) collective-permute-start(bf16[4,24,1152]{2,1,0:T(8,128)(2,1)S(1)} %pad_maximum_fusion.2), channel_id=1, source_target_pairs={{0,32},{32,64},{64,96},{96,128},{128,160},{160,192},{192,224},{224... | collective-permute-start | bytes 663560 | tf_op jit(solution)/shard_map/ppermute | solution.py:19
  5.9 17.9 %collective-permute-start.1 = (bf16[3,24,1152]{2,1,0:T(8,128)(2,1)S(1)}, bf16[3,24,1152]{2,1,0:T(8,128)(2,1)S(1)}, u32[]{:S(2)}, u32[]{:S(2)}) collective-permute-start(bf16[3,24,1152]{2,1,0:T(8,128)(2,1)S(1)} %get-tuple-element.5), channel_id=1, source_target_pairs={{32,0},{64,32},{96,64},{128,96},{160,128},{192,160},{224,192},{256... | collective-permute-start | bytes 497672 | tf_op jit(solution)/shard_map/ppermute | solution.py:25
  15.6 4.7 %copy-start.5 = (f32[4,12,6,45,1]{3,2,1,4,0:T(8,128)S(1)}, f32[4,12,6,45,1]{3,2,1,4,0:T(8,128)}, u32[]{:S(2)}) copy-start(f32[4,12,6,45,1]{3,2,1,4,0:T(8,128)} %constant.45) | copy-start | bytes 155524
  20.3 3.6 %copy-start = (bf16[9,24,1152]{2,1,0:T(8,128)(2,1)S(1)}, bf16[9,24,1152]{2,1,0:T(8,128)(2,1)}, u32[]{:S(2)}) copy-start(bf16[9,24,1152]{2,1,0:T(8,128)(2,1)} %t_ref.1) | copy-start | bytes 1492996
  22.6 10.6 %copy-start.2 = (f32[12,6,45]{2,1,0:T(8,128)S(1)}, f32[12,6,45]{2,1,0:T(8,128)}, u32[]{:S(2)}) copy-start(f32[12,6,45]{2,1,0:T(8,128)} %constant.44) | copy-start | bytes 38884
  23.2 12.1 %copy-start.3 = (f32[12,6,45]{2,0,1:T(8,128)S(1)}, f32[12,6,45]{2,0,1:T(8,128)}, u32[]{:S(2)}) copy-start(f32[12,6,45]{2,0,1:T(8,128)} %constant.42) | copy-start | bytes 38884
  23.3 12.3 %copy-start.4 = (f32[9,24]{1,0:T(8,128)S(1)}, f32[9,24]{1,0:T(8,128)}, u32[]{:S(2)}) copy-start(f32[9,24]{1,0:T(8,128)} %param.8) | copy-start | bytes 2596
  24.1 10.6 %collective-permute-start.2 = (bf16[15,4,1152]{2,1,0:T(4,128)(2,1)S(1)}, bf16[15,4,1152]{2,1,0:T(4,128)(2,1)S(1)}, u32[]{:S(2)}, u32[]{:S(2)}) collective-permute-start(bf16[15,4,1152]{2,1,0:T(4,128)(2,1)S(1)} %fusion.2), channel_id=1, source_target_pairs={{0,1},{1,2},{2,3},{3,4},{4,5},{5,6},{6,7},{7,8},{8,9},{9,10},{10,1... | collective-permute-start | bytes 414728 | tf_op jit(solution)/shard_map/ppermute | solution.py:19
  31.2 8.5 %collective-permute-start.3 = (bf16[15,3,1152]{2,1,0:T(4,128)(2,1)S(1)}, bf16[15,3,1152]{2,1,0:T(4,128)(2,1)S(1)}, u32[]{:S(2)}, u32[]{:S(2)}) collective-permute-start(bf16[15,3,1152]{2,1,0:T(4,128)(2,1)S(1)} %pad_maximum_fusion.3), channel_id=1, source_target_pairs={{1,0},{2,1},{3,2},{4,3},{5,4},{6,5},{7,6},{8,7},{9,8},{10,9},{11,1... | collective-permute-start | bytes 311048 | tf_op jit(solution)/shard_map/ppermute | solution.py:25

commit v7 on v6

--- a/solution.py
+++ b/solution.py
@@ -125,30 +125,43 @@
     return total
 
 
-def tap_kernel(offsets, chunk, w_ref, p_ref, t_ref, o_ref, s_ref):
-    s_ref[...] = p_ref[...].astype(jnp.float32)
+def tap_kernel(offsets, chunk, w_ref, south_ref, t_ref, north_ref, west_ref, east_ref, o_ref, s_ref, sh_ref):
     rows, cols, width = t_ref.shape
+    halo = south_ref.shape[0] - 1
+    f32 = jnp.float32
+    s_ref[0:halo, halo : halo + cols] = south_ref[0:halo].astype(f32)
+    s_ref[halo : halo + rows, halo : halo + cols] = t_ref[...].astype(f32)
+    s_ref[halo + rows :, halo : halo + cols] = north_ref[...].astype(f32)
+    s_ref[:, 0:halo] = west_ref[:, 0:halo].astype(f32)
+    s_ref[:, halo + cols :] = east_ref[...].astype(f32)
+    for shift in range(2 * halo + 1):
+        sh_ref[shift] = s_ref[:, pl.ds(shift, cols), :]
 
     def row(i, carry):
         for start in range(0, width, chunk):
             lanes = pl.ds(start, chunk)
-            acc = t_ref[i, :, lanes].astype(jnp.float32)
+            acc = s_ref[i + halo, pl.ds(halo, cols), lanes]
             for tap, (dr, dc) in enumerate(offsets):
                 w = w_ref[i, :, tap : tap + 1]
-                acc = acc + w * s_ref[i + 3 + dr, pl.ds(3 + dc, cols), lanes]
+                acc = acc + w * sh_ref[dc + halo, i + halo + dr, :, lanes]
             o_ref[i, :, lanes] = acc.astype(o_ref.dtype)
         return carry
 
     lax.fori_loop(0, rows, row, 0)
 
 
-def apply_taps(weights, padded, tracer, offsets):
+def apply_taps(weights, from_south, tracer, from_north, from_west, from_east, offsets):
+    rows, cols, width = tracer.shape
+    halo = from_north.shape[0]
     return pl.pallas_call(
-        functools.partial(tap_kernel, offsets, math.gcd(tracer.shape[2], 384)),
+        functools.partial(tap_kernel, offsets, math.gcd(width, 384)),
         out_shape=jax.ShapeDtypeStruct(tracer.shape, jnp.bfloat16),
-        scratch_shapes=[pltpu.VMEM(padded.shape, jnp.float32)],
+        scratch_shapes=[
+            pltpu.VMEM((rows + 2 * halo, cols + 2 * halo, width), jnp.float32),
+            pltpu.VMEM((2 * halo + 1, rows + 2 * halo, cols, width), jnp.float32),
+        ],
         interpret=INTERPRET,
-    )(weights, padded, tracer)
+    )(weights, from_south, tracer, from_north, from_west, from_east)
 
 
 def local(tracer, moments, pieces, cell_area):
@@ -171,7 +184,6 @@
     )[:, None]
     from_west = from_prev(jnp.concatenate([tall[:, cols - 3 :], west_pack], axis=1), "tile", True)
     from_east = from_next(tall[:, :3], "tile", True)
-    padded = jnp.concatenate([from_west[:, :3], tall, from_east], axis=1)
 
     is_top = lax.axis_index("panel") == lax.axis_size("panel") - 1
     last_row = jnp.arange(rows) == rows - 1
@@ -207,7 +219,7 @@
     weights = weights + jnp.pad(west_fix[:, None], ((0, 0), (0, cols - 1), (0, 0)))
     weights = weights + jnp.pad(south_fix[None], ((0, rows - 1), (0, 0), (0, 0)))
     weights = weights / cell_area[:, :, None]
-    return apply_taps(weights, padded, tracer, offsets)
+    return apply_taps(weights, from_south, tracer, from_north, from_west, from_east, offsets)
 
 
 def solution(mesh):

time: 51.4 us -> 52 us (1.012)
  other arithmetic: 9.21 us -> 7.76 us
  Pallas kernels: 9.83 us -> 11.2 us
  local copies, waits for them, and re-layouts: 5.82 us -> 6.49 us
    concatenate x1 -> x0, other arithmetic: 1.47 us -> none  [local(): padded = jnp.concatenate([from_west[:, :3], tall, from_east], axis=1)]
    pallas_call x1, Pallas kernels: 9.83 us -> 11.2 us  [apply_taps(): pl.pallas_call(functools.partial(tap_kernel, offsets, math.gcd(width, 384...]
    unnamed x13 -> x21, local copies, waits for them, and re-layouts: 0.04 us -> 0.72 us
where the time goes in v7:
time: 52 us; the launch traced here: 51.5 us
  starting transfers between devices  18.5 us (36%)
  Pallas kernels  11.2 us (22%)
  other arithmetic  7.76 us (15%)
  local copies, waits for them, and re-layouts  6.49 us (12%)
  waiting for transfers between devices  4.46 us (9%)
  matrix products  2.8 us (5%)
    pallas_call x1, Pallas kernels, apply_taps(): pl.pallas_call(functools.partial(tap_kernel, offsets, math.gcd(width, 384...  11.2 us
    ppermute x2, starting transfers between devices, from_prev(): return lax.ppermute(value, axis, pairs)  10.2 us
    ppermute x2, starting transfers between devices, from_next(): return lax.ppermute(value, axis, pairs)  8.3 us
    reduce_sum x3, other arithmetic, face_weights(): spread = jnp.sum(onehot[..., :, None] * moments[..., None, :], axis=-3)  4.89 us
    ppermute x2, waiting for transfers between devices, from_next(): return lax.ppermute(value, axis, pairs)  3.34 us
    dot_general x3, matrix products, face_weights(): jnp.dot(flat, tables.reshape(-1, tables.shape[-1]), precision=lax.Precisi...  2.8 us
    ppermute x2, waiting for transfers between devices, from_prev(): return lax.ppermute(value, axis, pairs)  1.12 us
  transfers between devices with their start and end apart: 4, of which 2 were waited for; matrix products, arithmetic and copies ran while one was open for 26% of the time, Pallas kernels for 0%

profile of v7, /device:TPU:233, one launch (start us, length us, event | category | flops | bytes accessed | tf_op | source)
XLA Modules:
  0.0 51.5 jit_solution(7370149786413392971)
XLA Ops:
  0.0 0.7 %slice_bitcast_fusion.8 = (s32[1,24,4]{1,2,0:T(4,128)S(1)}, bf16[24,4]{0,1:T(4,128)(2,1)S(1)}) fusion(s32[2,9,24,4]{2,3,1,0:T(4,128)} %param.7), kind=kLoop, calls=%fused_computation.72 | loop fusion | flops 96 | bytes 1344 | tf_op jit(solution)/shard_map/slice | solution.py:207
  0.7 0.1 copy.48
  0.8 0.7 %slice.137 = f32[1,1,24,4,6]{2,3,4,1,0:T(4,128)S(1)} slice(f32[2,9,24,4,6]{2,3,4,1,0:T(4,128)} %param.6), slice={[1:2], [8:9], [0:24], [0:4], [0:6]} | slice | bytes 4608 | tf_op jit(solution)/shard_map/slice | solution.py:178
  1.6 0.1 copy.46
  1.7 1.0 %fusion.24 = (bf16[3,24,1152]{2,1,0:T(8,128)(2,1)S(1)}, bf16[3,24,1152]{2,1,0:T(8,128)(2,1)S(1)}) fusion(bf16[9,24,1152]{2,1,0:T(8,128)(2,1)} %t_ref.1), kind=kLoop, calls=%fused_computation.75 | loop fusion | bytes 663552 | tf_op jit(solution)/shard_map/slice | solution.py:180
  2.7 0.1 fusion.14
  2.8 3.1 %collective-permute-start = (bf16[4,24,1152]{2,1,0:T(8,128)(2,1)S(1)}, bf16[4,24,1152]{2,1,0:T(8,128)(2,1)S(1)}, u32[]{:S(2)}, u32[]{:S(2)}) collective-permute-start(bf16[4,24,1152]{2,1,0:T(8,128)(2,1)S(1)} %pad_maximum_fusion.1), channel_id=1, source_target_pairs={{0,32},{32,64},{64,96},{96,128},{128,160},{160,192},{192,224},{224... | collective-permute-start | bytes 663560 | tf_op jit(solution)/shard_map/ppermute | solution.py:19
  5.9 6.4 %collective-permute-start.1 = (bf16[3,24,1152]{2,1,0:T(8,128)(2,1)S(1)}, bf16[3,24,1152]{2,1,0:T(8,128)(2,1)S(1)}, u32[]{:S(2)}, u32[]{:S(2)}) collective-permute-start(bf16[3,24,1152]{2,1,0:T(8,128)(2,1)S(1)} %get-tuple-element.5), channel_id=1, source_target_pairs={{32,0},{64,32},{96,64},{128,96},{160,128},{192,160},{224,192},{256... | collective-permute-start | bytes 497672 | tf_op jit(solution)/shard_map/ppermute | solution.py:25
  12.3 0.7 %slice_bitcast_fusion.7 = (s32[9,24,4]{1,2,0:T(4,128)S(1)}, s32[9,24,1,4]{1,3,0,2:T(4,128)S(1)}, s32[9,24,1,4]{1,3,0,2:T(4,128)S(1)}) fusion(s32[2,9,24,4]{2,3,1,0:T(4,128)} %param.7), kind=kLoop, calls=%fused_computation.60 | loop fusion | bytes 17280 | tf_op jit(solution)/shard_map/squeeze | solution.py:205
  13.1 0.7 %slice_bitcast_fusion.5 = s32[8,24,4]{1,2,0:T(4,128)S(1)} fusion(s32[2,9,24,4]{2,3,1,0:T(4,128)} %param.7), kind=kLoop, calls=%fused_computation.58 | loop fusion | bytes 6144 | tf_op jit(solution)/shard_map/slice | solution.py:207
  13.8 1.0 %slice_bitcast_fusion.2 = (f32[9,24,4,6]{1,2,3,0:T(4,128)S(1)}, f32[9,24,1,4,6]{1,3,4,0,2:T(4,128)S(1)}, f32[9,24,4,6]{1,2,3,0:T(4,128)S(1)}) fusion(f32[2,9,24,4,6]{2,3,4,1,0:T(4,128)} %param.6), kind=kLoop, calls=%fused_computation.28 | loop fusion | bytes 103680 | tf_op jit(solution)/shard_map/squeeze | solution.py:196
  14.8 0.1 slice_convert_fusion
  14.9 0.1 bitcast_multiply_fusion
  15.0 0.1 slice.164
  15.1 0.1 slice_multiply_fusion
  15.2 0.1 pad_bitcast_fusion
  15.3 0.1 add_bitcast_fusion
  15.4 0.2 fusion
  15.6 0.0 copy-start.9
  15.6 4.6 %multiply_reduce_fusion = f32[9,24,4,12,6]{1,4,3,2,0:T(8,128)S(1)} fusion(f32[9,24,4,4,12]{1,3,4,2,0:T(4,128)S(1)} %fusion, f32[9,24,1,4,6]{1,3,4,0,2:T(4,128)S(1)} %bitcast_multiply_fusion, f32[9,24,1,4,6]{1,3,4,0,2:T(4,128)S(1)} %get-tuple-element.23, f32[9,24,1,4,6]{1,3,4,0,2:T(4,128)S(1)} %get-tuple-element.8, f32[9,24,1,4,6]{1,3,4,0,2:T(4,128)S(1)} %get-tuple-element.24), kind=kLoop, calls=%fused_computation | loop fusion | flops 497664 | bytes 497664 | tf_op jit(solution)/shard_map/reduce_sum | solution.py:110
  20.3 2.3 %convolution_bitcast_fusion = f32[9,24,45]{2,1,0:T(8,128)S(1)} fusion(f32[9,24,4,12,6]{1,4,3,2,0:T(8,128)S(1)} %multiply_reduce_fusion, f32[4,12,6,45,1]{3,2,1,4,0:T(8,128)S(1)} %copy-done.9), kind=kOutput, calls=%fused_computation.1 | convolution fusion | flops 33592320 | bytes 339552 | tf_op jit(solution)/shard_map/dot_general | solution.py:113
  22.6 0.1 copy.50
  22.8 0.1 copy.51
  22.9 0.3 copy.49
  23.2 0.1 reshape_squeeze.7
  23.3 0.1 fusion.18
  23.4 0.1 copy.52
  23.5 0.1 convert_add_fusion
  23.6 0.1 slice_convert_fusion.1
  23.7 0.1 copy.56
  23.7 0.1 copy.55
  23.9 0.2 fusion.2
  24.1 7.1 %collective-permute-start.2 = (bf16[15,4,1152]{2,1,0:T(4,128)(2,1)S(1)}, bf16[15,4,1152]{2,1,0:T(4,128)(2,1)S(1)}, u32[]{:S(2)}, u32[]{:S(2)}) collective-permute-start(bf16[15,4,1152]{2,1,0:T(4,128)(2,1)S(1)} %fusion.2), channel_id=1, source_target_pairs={{0,1},{1,2},{2,3},{3,4},{4,5},{5,6},{6,7},{7,8},{8,9},{9,10},{10,1... | collective-permute-start | bytes 414728 | tf_op jit(solution)/shard_map/ppermute | solution.py:19
  31.2 1.9 %collective-permute-start.3 = (bf16[15,3,1152]{2,1,0:T(4,128)(2,1)S(1)}, bf16[15,3,1152]{2,1,0:T(4,128)(2,1)S(1)}, u32[]{:S(2)}, u32[]{:S(2)}) collective-permute-start(bf16[15,3,1152]{2,1,0:T(4,128)(2,1)S(1)} %pad_maximum_fusion.2), channel_id=1, source_target_pairs={{1,0},{2,1},{3,2},{4,3},{5,4},{6,5},{7,6},{8,7},{9,8},{10,9},{11,1... | collective-permute-start | bytes 311048 | tf_op jit(solution)/shard_map/ppermute | solution.py:25
  33.2 0.1 multiply_reduce_fusion.1
  33.3 0.2 convolution_bitcast_fusion.1
  33.5 1.1 %collective-permute-done.2.west_ref = bf16[15,4,1152]{2,1,0:T(4,128)(2,1)S(1)} collective-permute-done((bf16[15,4,1152]{2,1,0:T(4,128)(2,1)S(1)}, bf16[15,4,1152]{2,1,0:T(4,128)(2,1)S(1)}, u32[]{:S(2)}, u32[]{:S(2)}) %collective-permute-start.2) | collective-permute-done | bytes 138272 | tf_op jit(solution)/shard_map/ppermute | solution.py:19
  34.7 0.1 convert_add_fusion.1
  34.8 0.1 slice_convert_fusion.2
  34.9 0.1 mul.86
  34.9 0.1 copy.53
  35.1 0.1 fusion.20
  35.2 0.1 multiply_reduce_fusion.2
  35.3 0.3 convolution_bitcast_fusion.2
  35.6 0.8 %add_divide_fusion.w_ref = f32[9,24,45]{2,1,0:T(8,128)} fusion(f32[1,24,45]{2,1,0:T(8,128)S(1)} %convolution_bitcast_fusion.1, f32[9,24,45]{2,1,0:T(8,128)S(1)} %convolution_bitcast_fusion, f32[9,1,45]{2,1,0:T(1,128)S(1)} %broadcast_in_dim.36, f32[9,24]{1,0:T(8,128)S(1)} %copy-done.8), kind=kLoop, calls=%fused_computation.21 | loop fusion | flops 29160 | bytes 84564 | tf_op jit(solution)/shard_map/div | solution.py:221
  36.4 3.3 %collective-permute-done.3.east_ref = bf16[15,3,1152]{2,1,0:T(4,128)(2,1)S(1)} collective-permute-done((bf16[15,3,1152]{2,1,0:T(4,128)(2,1)S(1)}, bf16[15,3,1152]{2,1,0:T(4,128)(2,1)S(1)}, u32[]{:S(2)}, u32[]{:S(2)}) %collective-permute-start.3) | collective-permute-done | bytes 103712 | tf_op jit(solution)/shard_map/ppermute | solution.py:25
  39.7 0.7 %copy-done.5 = bf16[15,3,1152]{2,1,0:T(4,128)(2,1)} copy-done((bf16[15,3,1152]{2,1,0:T(4,128)(2,1)}, bf16[15,3,1152]{2,1,0:T(4,128)(2,1)S(1)}, u32[]{:S(2)}) %copy-start.5) | copy-done | bytes 103704
  40.4 11.2 %shard_map.55 = bf16[9,24,1152]{2,1,0:T(8,128)(2,1)} custom-call(f32[9,24,45]{2,1,0:T(8,128)} %add_divide_fusion.w_ref, bf16[4,24,1152]{2,1,0:T(8,128)(2,1)} %copy-done.2, bf16[9,24,1152]{2,1,0:T(8,128)(2,1)} %t_ref.1, bf16[3,24,1152]{2,1,0:T(8,128)(2,1)} %copy-done.1, bf16[15,4,1152]{2,1,0:T(4,128)(2,1)} %copy-done.4, bf16[15,3,1152]{2,1,0:T(4,128)(2,1)} %copy-done.5), custom_call_target="tpu_custom_call" | custom-call | tf_op jit(solution)/shard_map/pallas_call | solution.py:156
  (36 shorter events, 0.3 us)
Async XLA Ops:
  0.0 14.9 %copy-start.3 = (f32[2,9,24,4,6]{2,3,4,1,0:T(4,128)S(1)}, f32[2,9,24,4,6]{2,3,4,1,0:T(4,128)}, u32[]{:S(2)}) copy-start(f32[2,9,24,4,6]{2,3,4,1,0:T(4,128)} %param.6) | copy-start | bytes 124420
  2.8 20.7 %collective-permute-start = (bf16[4,24,1152]{2,1,0:T(8,128)(2,1)S(1)}, bf16[4,24,1152]{2,1,0:T(8,128)(2,1)S(1)}, u32[]{:S(2)}, u32[]{:S(2)}) collective-permute-start(bf16[4,24,1152]{2,1,0:T(8,128)(2,1)S(1)} %pad_maximum_fusion.1), channel_id=1, source_target_pairs={{0,32},{32,64},{64,96},{96,128},{128,160},{160,192},{192,224},{224... | collective-permute-start | bytes 663560 | tf_op jit(solution)/shard_map/ppermute | solution.py:19
  5.9 17.9 %collective-permute-start.1 = (bf16[3,24,1152]{2,1,0:T(8,128)(2,1)S(1)}, bf16[3,24,1152]{2,1,0:T(8,128)(2,1)S(1)}, u32[]{:S(2)}, u32[]{:S(2)}) collective-permute-start(bf16[3,24,1152]{2,1,0:T(8,128)(2,1)S(1)} %get-tuple-element.5), channel_id=1, source_target_pairs={{32,0},{64,32},{96,64},{128,96},{160,128},{192,160},{224,192},{256... | collective-permute-start | bytes 497672 | tf_op jit(solution)/shard_map/ppermute | solution.py:25
  15.6 4.7 %copy-start.9 = (f32[4,12,6,45,1]{3,2,1,4,0:T(8,128)S(1)}, f32[4,12,6,45,1]{3,2,1,4,0:T(8,128)}, u32[]{:S(2)}) copy-start(f32[4,12,6,45,1]{3,2,1,4,0:T(8,128)} %constant.45) | copy-start | bytes 155524
  20.3 3.6 %copy-start = (bf16[9,24,1152]{2,1,0:T(8,128)(2,1)S(1)}, bf16[9,24,1152]{2,1,0:T(8,128)(2,1)}, u32[]{:S(2)}) copy-start(bf16[9,24,1152]{2,1,0:T(8,128)(2,1)} %t_ref.1) | copy-start | bytes 1492996
  22.6 10.7 %copy-start.6 = (f32[12,6,45]{2,1,0:T(8,128)S(1)}, f32[12,6,45]{2,1,0:T(8,128)}, u32[]{:S(2)}) copy-start(f32[12,6,45]{2,1,0:T(8,128)} %constant.44) | copy-start | bytes 38884
  23.2 12.1 %copy-start.7 = (f32[12,6,45]{2,0,1:T(8,128)S(1)}, f32[12,6,45]{2,0,1:T(8,128)}, u32[]{:S(2)}) copy-start(f32[12,6,45]{2,0,1:T(8,128)} %constant.42) | copy-start | bytes 38884
  23.3 12.3 %copy-start.8 = (f32[9,24]{1,0:T(8,128)S(1)}, f32[9,24]{1,0:T(8,128)}, u32[]{:S(2)}) copy-start(f32[9,24]{1,0:T(8,128)} %param.8) | copy-start | bytes 2596
  23.5 12.9 %copy-start.2 = (bf16[4,24,1152]{2,1,0:T(8,128)(2,1)}, bf16[4,24,1152]{2,1,0:T(8,128)(2,1)S(1)}, u32[]{:S(2)}) copy-start(bf16[4,24,1152]{2,1,0:T(8,128)(2,1)S(1)} %collective-permute-done.south_ref) | copy-start | bytes 663556
  23.9 15.8 %copy-start.1 = (bf16[3,24,1152]{2,1,0:T(8,128)(2,1)}, bf16[3,24,1152]{2,1,0:T(8,128)(2,1)S(1)}, u32[]{:S(2)}) copy-start(bf16[3,24,1152]{2,1,0:T(8,128)(2,1)S(1)} %collective-permute-done.1.north_ref) | copy-start | bytes 497668
  24.1 10.6 %collective-permute-start.2 = (bf16[15,4,1152]{2,1,0:T(4,128)(2,1)S(1)}, bf16[15,4,1152]{2,1,0:T(4,128)(2,1)S(1)}, u32[]{:S(2)}, u32[]{:S(2)}) collective-permute-start(bf16[15,4,1152]{2,1,0:T(4,128)(2,1)S(1)} %fusion.2), channel_id=1, source_target_pairs={{0,1},{1,2},{2,3},{3,4},{4,5},{5,6},{6,7},{7,8},{8,9},{9,10},{10,1... | collective-permute-start | bytes 414728 | tf_op jit(solution)/shard_map/ppermute | solution.py:19
  31.2 8.5 %collective-permute-start.3 = (bf16[15,3,1152]{2,1,0:T(4,128)(2,1)S(1)}, bf16[15,3,1152]{2,1,0:T(4,128)(2,1)S(1)}, u32[]{:S(2)}, u32[]{:S(2)}) collective-permute-start(bf16[15,3,1152]{2,1,0:T(4,128)(2,1)S(1)} %pad_maximum_fusion.2), channel_id=1, source_target_pairs={{1,0},{2,1},{3,2},{4,3},{5,4},{6,5},{7,6},{8,7},{9,8},{10,9},{11,1... | collective-permute-start | bytes 311048 | tf_op jit(solution)/shard_map/ppermute | solution.py:25
  34.6 5.1 %copy-start.4 = (bf16[15,4,1152]{2,1,0:T(4,128)(2,1)}, bf16[15,4,1152]{2,1,0:T(4,128)(2,1)S(1)}, u32[]{:S(2)}) copy-start(bf16[15,4,1152]{2,1,0:T(4,128)(2,1)S(1)} %collective-permute-done.2.west_ref) | copy-start | bytes 414724
  39.7 0.7 %copy-start.5 = (bf16[15,3,1152]{2,1,0:T(4,128)(2,1)}, bf16[15,3,1152]{2,1,0:T(4,128)(2,1)S(1)}, u32[]{:S(2)}) copy-start(bf16[15,3,1152]{2,1,0:T(4,128)(2,1)S(1)} %collective-permute-done.3.east_ref) | copy-start | bytes 311044

commit v8 on v6

--- a/solution.py
+++ b/solution.py
@@ -123,6 +123,19 @@
         term = weights[:, :, tap][:, :, None] * piece.astype(jnp.float32)
         total = term if total is None else total + term
     return total
+
+
+def face_weights_t(moments, pieces, tables):
+    n_row, n_col = moments.shape[:2]
+    n_code = tables.shape[1]
+    m_t = jnp.transpose(moments, (2, 3, 4, 0, 1)).reshape(moments.shape[2:] + (n_row * n_col,))
+    p_t = jnp.transpose(pieces, (2, 3, 0, 1)).reshape(pieces.shape[2:] + (n_row * n_col,))
+    onehot = (p_t[:, :, None, :] == jnp.arange(n_code, dtype=jnp.int32)[None, None, :, None]).astype(jnp.float32)
+    spread = jnp.sum(onehot[:, :, :, None, :] * m_t[:, :, None, :, :], axis=1)
+    flat = spread.reshape(-1, n_row * n_col)
+    table_t = tables.reshape(-1, tables.shape[-1]).T
+    w_t = jnp.dot(table_t, flat, precision=lax.Precision.HIGHEST)
+    return w_t.T.reshape(n_row, n_col, tables.shape[-1])
 
 
 def tap_kernel(offsets, chunk, w_ref, p_ref, t_ref, o_ref, s_ref):
@@ -197,7 +210,7 @@
         ],
         axis=2,
     )
-    weights = face_weights(face_m, face_p, tables)
+    weights = face_weights_t(face_m, face_p, tables)
     weights = lax.optimization_barrier(weights)
 
     west_m, west_p = unpack_weights(from_west[3 : 3 + rows, 3], n_piece, n_moment)

time: 51.4 us -> 54.7 us (1.064)
  local copies, waits for them, and re-layouts: 5.82 us -> 9.54 us
  other arithmetic: 9.21 us -> 6.17 us
  matrix products: 2.8 us -> 4.96 us
    reduce_sum x3 -> x2, other arithmetic: 4.89 us -> 0.25 us  [face_weights(): spread = jnp.sum(onehot[..., :, None] * moments[..., None, :], axis=-3)]
    dot_general x0 -> x1, matrix products: none -> 4.49 us  [face_weights_t(): w_t = jnp.dot(table_t, flat, precision=lax.Precision.HIGHEST)]
    dot_general x3 -> x2, matrix products: 2.8 us -> 0.47 us  [face_weights(): jnp.dot(flat, tables.reshape(-1, tables.shape[-1]), precision=lax.Precisi...]
    slice x1, local copies, waits for them, and re-layouts: 0.02 us -> 0.94 us  [local(): tall = jnp.concatenate([from_south[:3], tracer, from_north], axis=0)]
    mul x2, other arithmetic: 0.17 us -> 1.06 us  [local(): north_m = moments[1] * row_mask[:, None, None, None]]
    dot_general x0 -> x1, local copies, waits for them, and re-layouts: none -> 0.84 us  [face_weights_t(): w_t = jnp.dot(table_t, flat, precision=lax.Precision.HIGHEST)]
    squeeze x1, local copies, waits for them, and re-layouts: 0.01 us -> 0.82 us  [local(): south_m, south_p = unpack_weights(from_south[3], n_piece, n_moment)]
    reduce_sum x0 -> x1, other arithmetic: none -> 0.8 us  [face_weights_t(): spread = jnp.sum(onehot[:, :, :, None, :] * m_t[:, :, None, :, :], axis=1)]
  transfers between devices with their start and end apart: 4 -> 4, of which waited for: 2 -> 2; matrix products, arithmetic and copies ran while one was open for 26% -> 29% of each run, Pallas kernels for 0% -> 0%
where the time goes in v8:
time: 54.7 us; the launch traced here: 54.1 us
  starting transfers between devices  18.5 us (34%)
  Pallas kernels  10.1 us (18%)
  local copies, waits for them, and re-layouts  9.54 us (17%)
  other arithmetic  6.17 us (11%)
  matrix products  4.96 us (9%)
  waiting for transfers between devices  4.49 us (8%)
    ppermute x2, starting transfers between devices, from_prev(): return lax.ppermute(value, axis, pairs)  10.2 us
    pallas_call x1, Pallas kernels, apply_taps(): pl.pallas_call(functools.partial(tap_kernel, offsets, math.gcd(tracer.sha...  10.1 us
    ppermute x2, starting transfers between devices, from_next(): return lax.ppermute(value, axis, pairs)  8.3 us
    dot_general x1, matrix products, face_weights_t(): w_t = jnp.dot(table_t, flat, precision=lax.Precision.HIGHEST)  4.49 us
    ppermute x2, waiting for transfers between devices, from_next(): return lax.ppermute(value, axis, pairs)  3.36 us
    slice x1, local copies, waits for them, and re-layouts, local(): from_north = from_next(tracer[:3], 'panel', False)  1.69 us
    concatenate x1, other arithmetic, local(): padded = jnp.concatenate([from_west[:, :3], tall, from_east], axis=1)  1.46 us
    ppermute x2, waiting for transfers between devices, from_prev(): return lax.ppermute(value, axis, pairs)  1.12 us
  transfers between devices with their start and end apart: 4, of which 2 were waited for; matrix products, arithmetic and copies ran while one was open for 29% of the time, Pallas kernels for 0%

profile of v8, /device:TPU:233, one launch (start us, length us, event | category | flops | bytes accessed | tf_op | source)
XLA Modules:
  0.0 54.1 jit_solution(16773386999883315967)
XLA Ops:
  0.0 0.7 %slice_bitcast_fusion.8 = (s32[1,24,4]{1,2,0:T(4,128)S(1)}, bf16[24,4]{0,1:T(4,128)(2,1)S(1)}) fusion(s32[2,9,24,4]{2,3,1,0:T(4,128)} %param.7), kind=kLoop, calls=%fused_computation.74 | loop fusion | flops 96 | bytes 1344 | tf_op jit(solution)/shard_map/slice | solution.py:208
  0.7 0.1 copy.50
  0.8 0.7 %slice.140 = f32[1,1,24,4,6]{2,3,4,1,0:T(4,128)S(1)} slice(f32[2,9,24,4,6]{2,3,4,1,0:T(4,128)} %param.6), slice={[1:2], [8:9], [0:24], [0:4], [0:6]} | slice | bytes 4608 | tf_op jit(solution)/shard_map/slice | solution.py:178
  1.6 1.7 %fusion.28 = (bf16[3,24,1152]{2,1,0:T(8,128)(2,1)}, bf16[3,24,1152]{2,1,0:T(8,128)(2,1)S(1)}) fusion(bf16[9,24,1152]{2,1,0:T(8,128)(2,1)} %t_ref.1), kind=kLoop, calls=%fused_computation.77 | loop fusion | bytes 663552 | tf_op jit(solution)/shard_map/slice | solution.py:180
  3.3 0.1 fusion.18
  3.4 3.1 %collective-permute-start = (bf16[4,24,1152]{2,1,0:T(8,128)(2,1)S(1)}, bf16[4,24,1152]{2,1,0:T(8,128)(2,1)}, u32[]{:S(2)}, u32[]{:S(2)}) collective-permute-start(bf16[4,24,1152]{2,1,0:T(8,128)(2,1)S(1)} %pad_maximum_fusion.1), channel_id=1, source_target_pairs={{0,32},{32,64},{64,96},{96,128},{128,160},{160,192},{192,224},{224... | collective-permute-start | bytes 663560 | tf_op jit(solution)/shard_map/ppermute | solution.py:19
  6.5 6.4 %collective-permute-start.1 = (bf16[3,24,1152]{2,1,0:T(8,128)(2,1)}, bf16[3,24,1152]{2,1,0:T(8,128)(2,1)S(1)}, u32[]{:S(2)}, u32[]{:S(2)}) collective-permute-start(bf16[3,24,1152]{2,1,0:T(8,128)(2,1)} %get-tuple-element.5), channel_id=1, source_target_pairs={{32,0},{64,32},{96,64},{128,96},{160,128},{192,160},{224,192},{256... | collective-permute-start | bytes 497672 | tf_op jit(solution)/shard_map/ppermute | solution.py:25
  12.9 1.0 %slice_bitcast_fusion.2 = (f32[9,24,4,6]{1,2,3,0:T(4,128)S(1)}, f32[9,24,1,4,6]{1,3,4,0,2:T(4,128)S(1)}, f32[9,24,4,6]{1,2,3,0:T(4,128)S(1)}) fusion(f32[2,9,24,4,6]{2,3,4,1,0:T(4,128)} %param.6), kind=kLoop, calls=%fused_computation.30 | loop fusion | bytes 103680 | tf_op jit(solution)/shard_map/squeeze | solution.py:197
  13.9 0.7 %slice_bitcast_fusion.7 = (s32[9,24,4]{1,2,0:T(4,128)S(1)}, s32[9,24,1,4]{1,3,0,2:T(4,128)S(1)}, s32[9,24,1,4]{1,3,0,2:T(4,128)S(1)}) fusion(s32[2,9,24,4]{2,3,1,0:T(4,128)} %param.7), kind=kLoop, calls=%fused_computation.62 | loop fusion | bytes 17280 | tf_op jit(solution)/shard_map/squeeze | solution.py:206
  14.7 0.7 %slice_bitcast_fusion.5 = s32[8,24,4]{1,2,0:T(4,128)S(1)} fusion(s32[2,9,24,4]{2,3,1,0:T(4,128)} %param.7), kind=kLoop, calls=%fused_computation.60 | loop fusion | bytes 6144 | tf_op jit(solution)/shard_map/slice | solution.py:208
  15.4 1.0 %bitcast_multiply_fusion = f32[9,24,1,4,6]{1,3,4,0,2:T(4,128)S(1)} fusion(f32[2,9,24,4,6]{2,3,4,1,0:T(4,128)} %param.6, f32[9]{0:T(128)S(1)} %and_select_fusion), kind=kLoop, calls=%fused_computation.22 | loop fusion | flops 5184 | bytes 41508 | tf_op jit(solution)/shard_map/mul | solution.py:192
  16.4 0.1 slice.168
  16.5 0.1 slice_multiply_fusion
  16.6 0.1 pad_bitcast_fusion
  16.7 0.1 maximum_bitcast_fusion
  16.8 0.1 copy.44
  17.0 0.2 mul.85
  17.2 0.1 slice_convert_fusion
  17.3 0.1 add_bitcast_fusion.1
  17.4 0.1 eq.67
  17.6 0.8 %multiply_reduce_fusion = f32[4,12,6,216]{3,2,1,0:T(8,128)S(1)} fusion(f32[4,4,6,216]{3,1,2,0:T(4,128)S(1)} %mul.85, f32[4,4,12,216]{3,1,2,0:T(4,128)S(1)} %fusion.5), kind=kLoop, calls=%fused_computation.2 | loop fusion | flops 435456 | bytes 497664 | tf_op jit(solution)/shard_map/reduce_sum | solution.py:134
  18.4 0.8 %reshape.95 = f32[9,24,4,12,6]{1,0,4,3,2:T(8,128)S(1)} reshape(f32[216,4,12,6]{0,3,2,1:T(8,128)S(1)} %bitcast.71) | data formatting | bytes 497664 | tf_op jit(solution)/shard_map/dot_general | solution.py:137
  19.3 4.5 %fusion.2 = f32[9,24,45]{2,1,0:T(8,128)S(1)} fusion(f32[4,12,6,45,1]{3,1,2,0,4:T(8,128)} %constant.45, f32[9,24,4,12,6]{1,0,4,3,2:T(8,128)S(1)} %reshape.95), kind=kOutput, calls=%fused_computation.3 | convolution fusion | flops 33592320 | bytes 339552 | tf_op jit(solution)/shard_map/dot_general | solution.py:137
  23.8 0.1 copy.52
  23.9 0.1 copy.53
  24.0 0.3 copy.51
  24.3 0.1 reshape_squeeze.7
  24.4 0.1 fusion.22
  24.6 0.8 %slice_bitcast_fusion.3 = bf16[24,1152]{1,0:T(8,128)(2,1)S(1)} fusion(bf16[4,24,1152]{2,1,0:T(8,128)(2,1)} %collective-permute-done), kind=kLoop, calls=%fused_computation.41 | loop fusion | bytes 110592 | tf_op jit(solution)/shard_map/squeeze | solution.py:217
  25.5 0.1 slice_convert_fusion.1
  25.7 0.1 copy.57
  25.8 0.9 %slice.167 = bf16[3,24,1152]{2,1,0:T(8,128)(2,1)S(1)} slice(bf16[4,24,1152]{2,1,0:T(8,128)(2,1)} %collective-permute-done), slice={[0:3], [0:24], [0:1152]} | slice | bytes 331776 | tf_op jit(solution)/shard_map/slice | solution.py:181
  26.7 0.2 fusion.6
  26.9 7.1 %collective-permute-start.2 = (bf16[15,4,1152]{2,1,0:T(4,128)(2,1)S(1)}, bf16[15,4,1152]{2,1,0:T(4,128)(2,1)S(1)}, u32[]{:S(2)}, u32[]{:S(2)}) collective-permute-start(bf16[15,4,1152]{2,1,0:T(4,128)(2,1)S(1)} %fusion.6), channel_id=1, source_target_pairs={{0,1},{1,2},{2,3},{3,4},{4,5},{5,6},{6,7},{7,8},{8,9},{9,10},{10,1... | collective-permute-start | bytes 414728 | tf_op jit(solution)/shard_map/ppermute | solution.py:19
  34.1 1.9 %collective-permute-start.3 = (bf16[15,3,1152]{2,1,0:T(4,128)(2,1)S(1)}, bf16[15,3,1152]{2,1,0:T(4,128)(2,1)S(1)}, u32[]{:S(2)}, u32[]{:S(2)}) collective-permute-start(bf16[15,3,1152]{2,1,0:T(4,128)(2,1)S(1)} %pad_maximum_fusion.2), channel_id=1, source_target_pairs={{1,0},{2,1},{3,2},{4,3},{5,4},{6,5},{7,6},{8,7},{9,8},{10,9},{11,1... | collective-permute-start | bytes 311048 | tf_op jit(solution)/shard_map/ppermute | solution.py:25
  36.0 0.1 multiply_reduce_fusion.1
  36.1 0.2 convolution_bitcast_fusion
  36.4 1.1 %collective-permute-done.2 = bf16[15,4,1152]{2,1,0:T(4,128)(2,1)S(1)} collective-permute-done((bf16[15,4,1152]{2,1,0:T(4,128)(2,1)S(1)}, bf16[15,4,1152]{2,1,0:T(4,128)(2,1)S(1)}, u32[]{:S(2)}, u32[]{:S(2)}) %collective-permute-start.2) | collective-permute-done | bytes 138272 | tf_op jit(solution)/shard_map/ppermute | solution.py:19
  37.6 0.1 slice_convert_fusion.2
  37.7 0.1 mul.89
  37.8 0.1 copy.55
  37.9 0.1 fusion.24
  38.0 0.1 multiply_reduce_fusion.2
  38.2 0.3 convolution_bitcast_fusion.1
  38.5 0.7 %add_divide_fusion.w_ref = f32[9,24,45]{2,1,0:T(8,128)} fusion(f32[1,24,45]{2,1,0:T(8,128)S(1)} %convolution_bitcast_fusion, f32[9,24,45]{2,1,0:T(8,128)S(1)} %fusion.2, f32[9,1,45]{2,1,0:T(1,128)S(1)} %broadcast_in_dim.34, f32[9,24]{1,0:T(8,128)S(1)} %copy-done.3), kind=kLoop, calls=%fused_computation.23 | loop fusion | flops 29160 | bytes 84564 | tf_op jit(solution)/shard_map/div | solution.py:222
  39.2 3.4 %collective-permute-done.3 = bf16[15,3,1152]{2,1,0:T(4,128)(2,1)S(1)} collective-permute-done((bf16[15,3,1152]{2,1,0:T(4,128)(2,1)S(1)}, bf16[15,3,1152]{2,1,0:T(4,128)(2,1)S(1)}, u32[]{:S(2)}, u32[]{:S(2)}) %collective-permute-start.3) | collective-permute-done | bytes 103712 | tf_op jit(solution)/shard_map/ppermute | solution.py:25
  42.6 1.5 %pad_maximum_fusion.p_ref = bf16[15,30,1152]{2,1,0:T(8,128)(2,1)} fusion(bf16[15,3,1152]{2,1,0:T(4,128)(2,1)S(1)} %collective-permute-done.3, bf16[3,24,1152]{2,1,0:T(8,128)(2,1)S(1)} %collective-permute-done.1, bf16[9,24,1152]{2,1,0:T(8,128)(2,1)S(1)} %copy-done, bf16[3,24,1152]{2,1,0:T(8,128)(2,1)S(1)} %slice.167, bf16[15,3,1152]{2,1,0:T(4,128)(2,1)S(1)} %bitcast.74), kind=kLoop, calls=%fused_computation.6 | loop fusion | flops 5184000 | bytes 2073600 | tf_op jit(solution)/shard_map/concatenate | solution.py:187
  44.0 10.1 %shard_map.55 = bf16[9,24,1152]{2,1,0:T(8,128)(2,1)} custom-call(f32[9,24,45]{2,1,0:T(8,128)} %add_divide_fusion.w_ref, bf16[15,30,1152]{2,1,0:T(8,128)(2,1)} %pad_maximum_fusion.p_ref, bf16[9,24,1152]{2,1,0:T(8,128)(2,1)} %t_ref.1), custom_call_target="tpu_custom_call" | custom-call | tf_op jit(solution)/shard_map/pallas_call | solution.py:159
  (32 shorter events, 0.7 us)
Async XLA Ops:
  3.4 21.2 %collective-permute-start = (bf16[4,24,1152]{2,1,0:T(8,128)(2,1)S(1)}, bf16[4,24,1152]{2,1,0:T(8,128)(2,1)}, u32[]{:S(2)}, u32[]{:S(2)}) collective-permute-start(bf16[4,24,1152]{2,1,0:T(8,128)(2,1)S(1)} %pad_maximum_fusion.1), channel_id=1, source_target_pairs={{0,32},{32,64},{64,96},{96,128},{128,160},{160,192},{192,224},{224... | collective-permute-start | bytes 663560 | tf_op jit(solution)/shard_map/ppermute | solution.py:19
  6.5 20.2 %collective-permute-start.1 = (bf16[3,24,1152]{2,1,0:T(8,128)(2,1)}, bf16[3,24,1152]{2,1,0:T(8,128)(2,1)S(1)}, u32[]{:S(2)}, u32[]{:S(2)}) collective-permute-start(bf16[3,24,1152]{2,1,0:T(8,128)(2,1)} %get-tuple-element.5), channel_id=1, source_target_pairs={{32,0},{64,32},{96,64},{128,96},{160,128},{192,160},{224,192},{256... | collective-permute-start | bytes 497672 | tf_op jit(solution)/shard_map/ppermute | solution.py:25
  19.2 7.5 %copy-start = (bf16[9,24,1152]{2,1,0:T(8,128)(2,1)S(1)}, bf16[9,24,1152]{2,1,0:T(8,128)(2,1)}, u32[]{:S(2)}) copy-start(bf16[9,24,1152]{2,1,0:T(8,128)(2,1)} %t_ref.1) | copy-start | bytes 1492996
  19.3 16.9 %copy-start.1 = (f32[12,6,45]{2,1,0:T(8,128)S(1)}, f32[12,6,45]{2,1,0:T(8,128)}, u32[]{:S(2)}) copy-start(f32[12,6,45]{2,1,0:T(8,128)} %constant.44) | copy-start | bytes 38884
  23.8 14.4 %copy-start.2 = (f32[12,6,45]{2,0,1:T(8,128)S(1)}, f32[12,6,45]{2,0,1:T(8,128)}, u32[]{:S(2)}) copy-start(f32[12,6,45]{2,0,1:T(8,128)} %constant.42) | copy-start | bytes 38884
  23.8 14.7 %copy-start.3 = (f32[9,24]{1,0:T(8,128)S(1)}, f32[9,24]{1,0:T(8,128)}, u32[]{:S(2)}) copy-start(f32[9,24]{1,0:T(8,128)} %param.8) | copy-start | bytes 2596
  26.9 10.6 %collective-permute-start.2 = (bf16[15,4,1152]{2,1,0:T(4,128)(2,1)S(1)}, bf16[15,4,1152]{2,1,0:T(4,128)(2,1)S(1)}, u32[]{:S(2)}, u32[]{:S(2)}) collective-permute-start(bf16[15,4,1152]{2,1,0:T(4,128)(2,1)S(1)} %fusion.6), channel_id=1, source_target_pairs={{0,1},{1,2},{2,3},{3,4},{4,5},{5,6},{6,7},{7,8},{8,9},{9,10},{10,1... | collective-permute-start | bytes 414728 | tf_op jit(solution)/shard_map/ppermute | solution.py:19
  34.1 8.5 %collective-permute-start.3 = (bf16[15,3,1152]{2,1,0:T(4,128)(2,1)S(1)}, bf16[15,3,1152]{2,1,0:T(4,128)(2,1)S(1)}, u32[]{:S(2)}, u32[]{:S(2)}) collective-permute-start(bf16[15,3,1152]{2,1,0:T(4,128)(2,1)S(1)} %pad_maximum_fusion.2), channel_id=1, source_target_pairs={{1,0},{2,1},{3,2},{4,3},{5,4},{6,5},{7,6},{8,7},{9,8},{10,9},{11,1... | collective-permute-start | bytes 311048 | tf_op jit(solution)/shard_map/ppermute | solution.py:25

commit v9 on v6

--- a/solution.py
+++ b/solution.py
@@ -67,7 +67,7 @@
                     tables[face, code, :, r, c] += sign * stencil[:, inner_row + 1, inner_col + 1]
     tables = tables.reshape(4, 12, 6, 49)
     used = np.nonzero(np.abs(tables).sum(axis=(0, 1, 2)) > 0)[0]
-    return tables[..., used], [(int(t) // 7 - 3, int(t) % 7 - 3) for t in used]
+    return tables[..., used], [(int(t) // 7 - 3, int(t) % 7 - 3) for t in used], tables
 
 
 def summed_moments(pieces, moments):
@@ -157,10 +157,8 @@
     width = tracer.shape[2]
     n_piece = moments.shape[3]
     n_moment = moments.shape[4]
-    np_tables, offsets = face_tables()
-    tables = jnp.asarray(np_tables, jnp.float32)
-    west_taps = [t for t in range(len(offsets)) if np.abs(np_tables[0, ..., t]).sum() > 0]
-    south_taps = [t for t in range(len(offsets)) if np.abs(np_tables[2, ..., t]).sum() > 0]
+    _, _, np_full = face_tables()
+    tables_full = jnp.asarray(np_full, jnp.float32)
 
     south_pack = pack_weights(moments[1][rows - 1], pieces[1][rows - 1], width)[None]
     from_south = from_prev(jnp.concatenate([tracer[rows - 3 :], south_pack], axis=0), "panel", False)
@@ -197,17 +195,39 @@
         ],
         axis=2,
     )
-    weights = face_weights(face_m, face_p, tables)
+    weights = face_weights(face_m, face_p, tables_full)
     weights = lax.optimization_barrier(weights)
 
     west_m, west_p = unpack_weights(from_west[3 : 3 + rows, 3], n_piece, n_moment)
     south_m, south_p = unpack_weights(from_south[3], n_piece, n_moment)
-    west_fix = face_weights(west_m[:, None], west_p[:, None], tables[:1])
-    south_fix = face_weights(south_m[:, None], south_p[:, None], tables[2:3])
+    west_fix = face_weights(west_m[:, None], west_p[:, None], tables_full[:1])
+    south_fix = face_weights(south_m[:, None], south_p[:, None], tables_full[2:3])
     weights = weights + jnp.pad(west_fix[:, None], ((0, 0), (0, cols - 1), (0, 0)))
     weights = weights + jnp.pad(south_fix[None], ((0, rows - 1), (0, 0), (0, 0)))
     weights = weights / cell_area[:, :, None]
-    return apply_taps(weights, padded, tracer, offsets)
+
+    span = 7
+    wide_cols = cols + 8
+    grid = jnp.transpose(weights.reshape(rows, cols, span, span), (0, 2, 1, 3))
+    grid = jnp.pad(grid, ((0, 0), (0, 0), (0, 0), (0, wide_cols + 1 - span)))
+    grid = grid.reshape(rows, span, cols * (wide_cols + 1))[:, :, : cols * wide_cols]
+    grid = grid.reshape(rows, span, cols, wide_cols)
+    banded = jnp.stack(
+        [jnp.pad(grid[i], ((i, rows - 1 - i), (0, 0), (0, 0))) for i in range(rows)], axis=0
+    )
+    banded = jnp.transpose(banded, (0, 2, 1, 3)).reshape(rows * cols, (rows + 6) * wide_cols)
+    hi = lax.reduce_precision(banded, exponent_bits=8, mantissa_bits=7)
+    rest = banded - hi
+    mid = lax.reduce_precision(rest, exponent_bits=8, mantissa_bits=7)
+    lo = rest - mid
+
+    source = jnp.pad(padded, ((0, 0), (0, wide_cols - cols - 6), (0, 0))).reshape(-1, width)
+    change = None
+    for part in (hi, mid, lo):
+        term = jnp.dot(part.astype(jnp.bfloat16), source, preferred_element_type=jnp.float32)
+        change = term if change is None else change + term
+    total = tracer.astype(jnp.float32) + change.reshape(rows, cols, width)
+    return total.astype(jnp.bfloat16)
 
 
 def solution(mesh):

time: 51.4 us -> 55.9 us (1.088)
  the two profiles are of different devices: /device:TPU:233 before, /device:TPU:22 now
where the time goes in v9:
time: 55.9 us; the launch traced here: 55.4 us
  starting transfers between devices  15.1 us (27%)
  waiting for transfers between devices  14.4 us (26%)
  local copies, waits for them, and re-layouts  11.1 us (20%)
  other arithmetic  10 us (18%)
  matrix products  4.15 us (7%)
  between operations  0.61 us (1%)
    ppermute x2, waiting for transfers between devices, from_prev(): return lax.ppermute(value, axis, pairs)  8.67 us
    ppermute x2, starting transfers between devices, from_prev(): return lax.ppermute(value, axis, pairs)  7.72 us
    ppermute x2, starting transfers between devices, from_next(): return lax.ppermute(value, axis, pairs)  7.4 us
    ppermute x2, waiting for transfers between devices, from_next(): return lax.ppermute(value, axis, pairs)  5.76 us
    reduce_sum x3, other arithmetic, face_weights(): spread = jnp.sum(onehot[..., :, None] * moments[..., None, :], axis=-3)  4.9 us
    convert_element_type x6, local copies, waits for them, and re-layouts, local(): part.astype(jnp.bfloat16)  4.1 us
    dot_general x3, matrix products, face_weights(): jnp.dot(flat, tables.reshape(-1, tables.shape[-1]), precision=lax.Precisi...  2.8 us
    unnamed x27, local copies, waits for them, and re-layouts  2.7 us
  transfers between devices with their start and end apart: 4, of which 2 were waited for; matrix products, arithmetic and copies ran while one was open for 17% of the time, Pallas kernels for 0%

profile of v9, /device:TPU:22, one launch (start us, length us, event | category | flops | bytes accessed | tf_op | source)
XLA Modules:
  0.0 55.4 jit_solution(15139115749132180217)
XLA Ops:
  0.0 0.8 %slice_bitcast_fusion.8 = (s32[1,24,4]{1,2,0:T(4,128)S(1)}, bf16[24,4]{0,1:T(4,128)(2,1)S(1)}) fusion(s32[2,9,24,4]{2,3,1,0:T(4,128)} %param.7), kind=kLoop, calls=%fused_computation.89 | loop fusion | flops 96 | bytes 1344 | tf_op jit(solution)/shard_map/slice | solution.py:193
  0.8 0.1 copy.124
  0.9 0.7 %slice.186 = f32[1,1,24,4,6]{2,3,4,1,0:T(4,128)S(1)} slice(f32[2,9,24,4,6]{2,3,4,1,0:T(4,128)} %param.6), slice={[1:2], [8:9], [0:24], [0:4], [0:6]} | slice | bytes 4608 | tf_op jit(solution)/shard_map/slice | solution.py:163
  1.8 0.1 fusion.15
  2.0 1.1 %copy.119 = bf16[9,24,1152]{2,0,1:T(8,128)(2,1)S(1)} copy(bf16[9,24,1152]{2,1,0:T(8,128)(2,1)} %param.5) | data formatting | bytes 995328 | tf_op args[0]
  3.2 0.2 fusion.25
  3.4 0.2 pad_maximum_fusion.2
  3.6 5.6 %collective-permute-start = (bf16[4,24,1152]{2,0,1:T(4,128)(2,1)S(1)}, bf16[4,24,1152]{2,0,1:T(4,128)(2,1)S(1)}, u32[]{:S(2)}, u32[]{:S(2)}) collective-permute-start(bf16[4,24,1152]{2,0,1:T(4,128)(2,1)S(1)} %pad_maximum_fusion.2), channel_id=1, source_target_pairs={{0,32},{32,64},{64,96},{96,128},{128,160},{160,192},{192,224},{224... | collective-permute-start | bytes 663560 | tf_op jit(solution)/shard_map/ppermute | solution.py:19
  9.2 1.9 %collective-permute-start.1 = (bf16[3,24,1152]{2,0,1:T(4,128)(2,1)S(1)}, bf16[3,24,1152]{2,0,1:T(4,128)(2,1)S(1)}, u32[]{:S(2)}, u32[]{:S(2)}) collective-permute-start(bf16[3,24,1152]{2,0,1:T(4,128)(2,1)S(1)} %get-tuple-element.8), channel_id=1, source_target_pairs={{32,0},{64,32},{96,64},{128,96},{160,128},{192,160},{224,192},{256... | collective-permute-start | bytes 497672 | tf_op jit(solution)/shard_map/ppermute | solution.py:25
  11.4 0.1 copy.129
  11.5 0.1 copy.130
  11.6 0.1 bitcast_multiply_fusion
  11.7 0.1 slice.225
  11.8 0.3 copy.128
  12.3 0.1 pad_bitcast_fusion
  12.5 0.2 fusion.1
  12.8 4.6 %multiply_reduce_fusion = f32[9,24,4,12,6]{1,4,3,2,0:T(8,128)S(1)} fusion(f32[9,24,4,4,12]{1,3,4,2,0:T(4,128)S(1)} %fusion.1, f32[9,24,1,4,6]{1,3,4,0,2:T(4,128)S(1)} %bitcast_multiply_fusion, f32[9,24,1,4,6]{1,3,4,0,2:T(4,128)S(1)} %get-tuple-element.35, f32[9,24,1,4,6]{1,3,4,0,2:T(4,128)S(1)} %get-tuple-element.20, f32[9,24,1,4,6]{1,3,4,0,2:T(4,128)S(1)} %get-tuple-element.36), kind=kLoop, calls=%fused_computation | loop fusion | flops 497664 | bytes 497664 | tf_op jit(solution)/shard_map/reduce_sum | solution.py:110
  17.4 2.3 %convolution_bitcast_fusion = f32[9,24,49]{2,1,0:T(8,128)S(1)} fusion(f32[9,24,4,12,6]{1,4,3,2,0:T(8,128)S(1)} %multiply_reduce_fusion, f32[4,12,6,49,1]{3,2,1,4,0:T(8,128)S(1)} %copy-done.6), kind=kOutput, calls=%fused_computation.8 | convolution fusion | flops 36578304 | bytes 347616 | tf_op jit(solution)/shard_map/dot_general | solution.py:113
  19.9 0.1 slice.232
  20.4 5.8 %collective-permute-done.1 = bf16[3,24,1152]{2,0,1:T(4,128)(2,1)S(1)} collective-permute-done((bf16[3,24,1152]{2,0,1:T(4,128)(2,1)S(1)}, bf16[3,24,1152]{2,0,1:T(4,128)(2,1)S(1)}, u32[]{:S(2)}, u32[]{:S(2)}) %collective-permute-start.1) | collective-permute-done | bytes 165920 | tf_op jit(solution)/shard_map/ppermute | solution.py:25
  26.2 5.5 %collective-permute-start.3 = (bf16[15,3,1152]{2,0,1:T(8,128)(2,1)S(1)}, bf16[15,3,1152]{2,0,1:T(8,128)(2,1)S(1)}, u32[]{:S(2)}, u32[]{:S(2)}) collective-permute-start(bf16[15,3,1152]{2,0,1:T(8,128)(2,1)S(1)} %pad_maximum_fusion.5), channel_id=1, source_target_pairs={{1,0},{2,1},{3,2},{4,3},{5,4},{6,5},{7,6},{8,7},{9,8},{10,9},{11,1... | collective-permute-start | bytes 311048 | tf_op jit(solution)/shard_map/ppermute | solution.py:25
  31.8 2.1 %collective-permute-start.2 = (bf16[15,4,1152]{2,0,1:T(8,128)(2,1)S(1)}, bf16[15,4,1152]{2,0,1:T(8,128)(2,1)S(1)}, u32[]{:S(2)}, u32[]{:S(2)}) collective-permute-start(bf16[15,4,1152]{2,0,1:T(8,128)(2,1)S(1)} %fusion.3), channel_id=1, source_target_pairs={{0,1},{1,2},{2,3},{3,4},{4,5},{5,6},{6,7},{7,8},{8,9},{9,10},{10,1... | collective-permute-start | bytes 414728 | tf_op jit(solution)/shard_map/ppermute | solution.py:19
  33.9 0.1 multiply_reduce_fusion.1
  34.0 0.2 convolution_bitcast_fusion.1
  34.2 8.7 %collective-permute-done.2 = bf16[15,4,1152]{2,0,1:T(8,128)(2,1)S(1)} collective-permute-done((bf16[15,4,1152]{2,0,1:T(8,128)(2,1)S(1)}, bf16[15,4,1152]{2,0,1:T(8,128)(2,1)S(1)}, u32[]{:S(2)}, u32[]{:S(2)}) %collective-permute-start.2) | collective-permute-done | bytes 138272 | tf_op jit(solution)/shard_map/ppermute | solution.py:19
  43.1 0.6 %pad_maximum_fusion = bf16[15,30,1152]{2,0,1:T(8,128)(2,1)S(1)} fusion(bf16[15,3,1152]{2,0,1:T(8,128)(2,1)S(1)} %collective-permute-done.3, bf16[3,24,1152]{2,0,1:T(4,128)(2,1)S(1)} %collective-permute-done.1, bf16[9,24,1152]{2,0,1:T(8,128)(2,1)S(1)} %copy.119, bf16[3,24,1152]{2,0,1:T(4,128)(2,1)S(1)} %bitcast.114, bf16[15,3,1152]{2,0,1:T(8,128)(2,1)S(1)} %slice.246), kind=kLoop, calls=%fused_computation.11 | loop fusion | flops 5184000 | bytes 2073600 | tf_op jit(solution)/shard_map/concatenate | solution.py:172
  43.7 0.2 copy.147
  44.1 0.1 copy.131
  44.2 0.1 multiply_reduce_fusion.2
  44.4 0.1 copy-done.4
  44.5 0.2 convolution_bitcast_fusion.2
  44.8 0.1 add_divide_fusion
  44.9 0.2 copy.136
  45.1 0.4 copy.146
  45.6 0.3 reshape.125
  47.0 1.3 %fusion = (bf16[9,24,15,32]{3,1,2,0:T(8,128)(2,1)S(1)}, bf16[9,24,15,32]{3,1,2,0:T(8,128)(2,1)}, bf16[9,24,15,32]{3,1,2,0:T(8,128)(2,1)S(1)}) fusion(f32[9,15,24,32]{3,2,1,0:T(8,128)S(1)} %bitcast_dynamic-update-slice_fusion), kind=kLoop, calls=%fused_computation.7 | loop fusion | flops 725760 | bytes 1036800 | tf_op jit(solution)/shard_map/convert_element_type | solution.py:227
  48.3 0.2 copy.141
  48.5 0.8 %convert_element_type.134 = bf16[216,480]{1,0:T(8,128)(2,1)S(1)} reshape(bf16[9,24,15,32]{3,2,1,0:T(8,128)(2,1)S(1)} %copy.141) | data formatting | bytes 414720 | tf_op jit(solution)/shard_map/convert_element_type | solution.py:227
  49.3 1.3 %copy.140 = bf16[9,24,15,32]{3,2,1,0:T(8,128)(2,1)S(1)} copy(bf16[9,24,15,32]{3,1,2,0:T(8,128)(2,1)} %get-tuple-element.6) | data formatting | bytes 414720 | tf_op jit(solution)/shard_map/convert_element_type | solution.py:227
  50.7 0.8 %convert_element_type.132 = bf16[216,480]{1,0:T(8,128)(2,1)S(1)} reshape(bf16[9,24,15,32]{3,2,1,0:T(8,128)(2,1)S(1)} %copy.140) | data formatting | bytes 414720 | tf_op jit(solution)/shard_map/convert_element_type | solution.py:227
  51.5 0.2 copy.138
  51.6 0.8 %convert_element_type.130 = bf16[216,480]{1,0:T(8,128)(2,1)S(1)} reshape(bf16[9,24,15,32]{3,2,1,0:T(8,128)(2,1)S(1)} %copy.138) | data formatting | bytes 414720 | tf_op jit(solution)/shard_map/convert_element_type | solution.py:227
  52.5 0.1 pad.81.clone
  52.6 0.5 fusion.27
  53.0 0.5 convolution_add_fusion.1
  53.5 0.5 convolution_add_fusion
  54.0 0.6 %copy-done = bf16[9,24,1152]{2,1,0:T(8,128)(2,1)S(1)} copy-done((bf16[9,24,1152]{2,1,0:T(8,128)(2,1)S(1)}, bf16[9,24,1152]{2,1,0:T(8,128)(2,1)}, u32[]{:S(2)}) %copy-start) | copy-done | bytes 497688
  54.5 0.9 %add_convert_fusion = bf16[9,24,1152]{2,1,0:T(8,128)(2,1)} fusion(f32[9,24,1152]{2,1,0:T(8,128)S(1)} %bitcast.111, bf16[9,24,1152]{2,1,0:T(8,128)(2,1)S(1)} %copy-done), kind=kLoop, calls=%fused_computation.12 | loop fusion | flops 746496 | bytes 1990656 | tf_op jit(solution)/shard_map/convert_element_type | solution.py:230
  (71 shorter events, 2.7 us)
Async XLA Ops:
  0.0 11.2 %copy-start.2 = (s32[2,9,24,4]{2,3,1,0:T(4,128)S(1)}, s32[2,9,24,4]{2,3,1,0:T(4,128)}, u32[]{:S(2)}) copy-start(s32[2,9,24,4]{2,3,1,0:T(4,128)} %param.7) | copy-start | bytes 20740
  1.6 9.6 %copy-start.1 = (f32[2,9,24,4,6]{2,3,4,1,0:T(4,128)S(1)}, f32[2,9,24,4,6]{2,3,4,1,0:T(4,128)}, u32[]{:S(2)}) copy-start(f32[2,9,24,4,6]{2,3,4,1,0:T(4,128)} %param.6) | copy-start | bytes 124420
  3.6 16.3 %collective-permute-start = (bf16[4,24,1152]{2,0,1:T(4,128)(2,1)S(1)}, bf16[4,24,1152]{2,0,1:T(4,128)(2,1)S(1)}, u32[]{:S(2)}, u32[]{:S(2)}) collective-permute-start(bf16[4,24,1152]{2,0,1:T(4,128)(2,1)S(1)} %pad_maximum_fusion.2), channel_id=1, source_target_pairs={{0,32},{32,64},{64,96},{96,128},{128,160},{160,192},{192,224},{224... | collective-permute-start | bytes 663560 | tf_op jit(solution)/shard_map/ppermute | solution.py:19
  9.2 16.9 %collective-permute-start.1 = (bf16[3,24,1152]{2,0,1:T(4,128)(2,1)S(1)}, bf16[3,24,1152]{2,0,1:T(4,128)(2,1)S(1)}, u32[]{:S(2)}, u32[]{:S(2)}) collective-permute-start(bf16[3,24,1152]{2,0,1:T(4,128)(2,1)S(1)} %get-tuple-element.8), channel_id=1, source_target_pairs={{32,0},{64,32},{96,64},{128,96},{160,128},{192,160},{224,192},{256... | collective-permute-start | bytes 497672 | tf_op jit(solution)/shard_map/ppermute | solution.py:25
  12.8 4.7 %copy-start.6 = (f32[4,12,6,49,1]{3,2,1,4,0:T(8,128)S(1)}, f32[4,12,6,49,1]{3,2,1,4,0:T(8,128)}, u32[]{:S(2)}) copy-start(f32[4,12,6,49,1]{3,2,1,4,0:T(8,128)} %constant.67) | copy-start | bytes 169348
  20.0 14.0 %copy-start.3 = (f32[12,6,49]{2,1,0:T(8,128)S(1)}, f32[12,6,49]{2,1,0:T(8,128)}, u32[]{:S(2)}) copy-start(f32[12,6,49]{2,1,0:T(8,128)} %constant.66) | copy-start | bytes 42340
  26.2 16.9 %collective-permute-start.3 = (bf16[15,3,1152]{2,0,1:T(8,128)(2,1)S(1)}, bf16[15,3,1152]{2,0,1:T(8,128)(2,1)S(1)}, u32[]{:S(2)}, u32[]{:S(2)}) collective-permute-start(bf16[15,3,1152]{2,0,1:T(8,128)(2,1)S(1)} %pad_maximum_fusion.5), channel_id=1, source_target_pairs={{1,0},{2,1},{3,2},{4,3},{5,4},{6,5},{7,6},{8,7},{9,8},{10,9},{11,1... | collective-permute-start | bytes 311048 | tf_op jit(solution)/shard_map/ppermute | solution.py:25
  31.8 11.1 %collective-permute-start.2 = (bf16[15,4,1152]{2,0,1:T(8,128)(2,1)S(1)}, bf16[15,4,1152]{2,0,1:T(8,128)(2,1)S(1)}, u32[]{:S(2)}, u32[]{:S(2)}) collective-permute-start(bf16[15,4,1152]{2,0,1:T(8,128)(2,1)S(1)} %fusion.3), channel_id=1, source_target_pairs={{0,1},{1,2},{2,3},{3,4},{4,5},{5,6},{6,7},{7,8},{8,9},{9,10},{10,1... | collective-permute-start | bytes 414728 | tf_op jit(solution)/shard_map/ppermute | solution.py:19
  43.7 0.8 %copy-start.4 = (f32[12,6,49]{2,0,1:T(8,128)S(1)}, f32[12,6,49]{2,0,1:T(8,128)}, u32[]{:S(2)}) copy-start(f32[12,6,49]{2,0,1:T(8,128)} %constant.64) | copy-start | bytes 42340
  43.7 1.1 %copy-start.5 = (f32[9,24]{1,0:T(8,128)S(1)}, f32[9,24]{1,0:T(8,128)}, u32[]{:S(2)}) copy-start(f32[9,24]{1,0:T(8,128)} %param.8) | copy-start | bytes 2596
  53.5 1.0 %copy-start = (bf16[9,24,1152]{2,1,0:T(8,128)(2,1)S(1)}, bf16[9,24,1152]{2,1,0:T(8,128)(2,1)}, u32[]{:S(2)}) copy-start(bf16[9,24,1152]{2,1,0:T(8,128)(2,1)} %param.5) | copy-start | bytes 1492996

commit v10 on v9

--- a/solution.py
+++ b/solution.py
@@ -157,8 +157,11 @@
     width = tracer.shape[2]
     n_piece = moments.shape[3]
     n_moment = moments.shape[4]
-    _, _, np_full = face_tables()
+    np_tables, offsets, np_full = face_tables()
+    tables = jnp.asarray(np_tables, jnp.float32)
     tables_full = jnp.asarray(np_full, jnp.float32)
+    west_taps = [t for t in range(len(offsets)) if np.abs(np_tables[0, ..., t]).sum() > 0]
+    south_taps = [t for t in range(len(offsets)) if np.abs(np_tables[2, ..., t]).sum() > 0]
 
     south_pack = pack_weights(moments[1][rows - 1], pieces[1][rows - 1], width)[None]
     from_south = from_prev(jnp.concatenate([tracer[rows - 3 :], south_pack], axis=0), "panel", False)
@@ -195,16 +198,7 @@
         ],
         axis=2,
     )
-    weights = face_weights(face_m, face_p, tables_full)
-    weights = lax.optimization_barrier(weights)
-
-    west_m, west_p = unpack_weights(from_west[3 : 3 + rows, 3], n_piece, n_moment)
-    south_m, south_p = unpack_weights(from_south[3], n_piece, n_moment)
-    west_fix = face_weights(west_m[:, None], west_p[:, None], tables_full[:1])
-    south_fix = face_weights(south_m[:, None], south_p[:, None], tables_full[2:3])
-    weights = weights + jnp.pad(west_fix[:, None], ((0, 0), (0, cols - 1), (0, 0)))
-    weights = weights + jnp.pad(south_fix[None], ((0, rows - 1), (0, 0), (0, 0)))
-    weights = weights / cell_area[:, :, None]
+    weights = face_weights(face_m, face_p, tables_full) / cell_area[:, :, None]
 
     span = 7
     wide_cols = cols + 8
@@ -219,14 +213,24 @@
     hi = lax.reduce_precision(banded, exponent_bits=8, mantissa_bits=7)
     rest = banded - hi
     mid = lax.reduce_precision(rest, exponent_bits=8, mantissa_bits=7)
-    lo = rest - mid
+    parts = jnp.stack([hi, mid, rest - mid]).astype(jnp.bfloat16)
+    parts = lax.optimization_barrier(parts)
+
+    west_m, west_p = unpack_weights(from_west[3 : 3 + rows, 3], n_piece, n_moment)
+    south_m, south_p = unpack_weights(from_south[3], n_piece, n_moment)
+    west_fix = face_weights(west_m[:, None], west_p[:, None], tables[:1]) / cell_area[:, :1]
+    south_fix = face_weights(south_m[:, None], south_p[:, None], tables[2:3]) / cell_area[0][:, None]
 
     source = jnp.pad(padded, ((0, 0), (0, wide_cols - cols - 6), (0, 0))).reshape(-1, width)
     change = None
-    for part in (hi, mid, lo):
-        term = jnp.dot(part.astype(jnp.bfloat16), source, preferred_element_type=jnp.float32)
+    for k in range(3):
+        term = jnp.dot(parts[k], source, preferred_element_type=jnp.float32)
         change = term if change is None else change + term
     total = tracer.astype(jnp.float32) + change.reshape(rows, cols, width)
+    west_add = tap_sum(west_fix[:, None], padded, 0, 0, rows, 1, offsets, west_taps)
+    south_add = tap_sum(south_fix[None], padded, 0, 0, 1, cols, offsets, south_taps)
+    total = total + jnp.pad(west_add, ((0, 0), (0, cols - 1), (0, 0)))
+    total = total + jnp.pad(south_add, ((0, rows - 1), (0, 0), (0, 0)))
     return total.astype(jnp.bfloat16)
 
 

time: 55.9 us -> 60.7 us (1.086)
  the two profiles are of different devices: /device:TPU:22 before, /device:TPU:32 now
where the time goes in v10:
time: 60.7 us; the launch traced here: 60.1 us
  starting transfers between devices  22.1 us (36%)
  local copies, waits for them, and re-layouts  21.1 us (35%)
  other arithmetic  12.2 us (20%)
  matrix products  4.18 us (7%)
    ppermute x2, starting transfers between devices, from_next(): return lax.ppermute(value, axis, pairs)  16.8 us
    ppermute x2, starting transfers between devices, from_prev(): return lax.ppermute(value, axis, pairs)  5.31 us
    reduce_sum x3, other arithmetic, face_weights(): spread = jnp.sum(onehot[..., :, None] * moments[..., None, :], axis=-3)  5.08 us
    unnamed x30, local copies, waits for them, and re-layouts  3.7 us
    dot_general x3, matrix products, face_weights(): jnp.dot(flat, tables.reshape(-1, tables.shape[-1]), precision=lax.Precisi...  2.81 us
    add x2, other arithmetic, tap_sum(): total = term if total is None else total + term  2.71 us
    squeeze x9, local copies, waits for them, and re-layouts, local(): grid[i]  2.01 us
    slice x2, local copies, waits for them, and re-layouts, local(): moments[0][:, cols - 1]  1.99 us
  transfers between devices with their start and end apart: 4, of which 0 were waited for; matrix products, arithmetic and copies ran while one was open for 40% of the time, Pallas kernels for 0%

profile of v10, /device:TPU:32, one launch (start us, length us, event | category | flops | bytes accessed | tf_op | source)
XLA Modules:
  0.0 60.1 jit_solution(8441202945775603738)
XLA Ops:
  0.0 0.8 %slice_bitcast_fusion.14 = (s32[1,24,4]{1,2,0:T(4,128)S(1)}, bf16[24,4]{0,1:T(4,128)(2,1)S(1)}) fusion(s32[2,9,24,4]{2,3,1,0:T(4,128)} %param.8), kind=kLoop, calls=%fused_computation.259 | loop fusion | flops 96 | bytes 1344 | tf_op jit(solution)/shard_map/slice | solution.py:196
  0.8 0.7 %slice.625 = f32[1,1,24,4,6]{2,3,4,1,0:T(4,128)S(1)} slice(f32[2,9,24,4,6]{2,3,4,1,0:T(4,128)} %param.7), slice={[1:2], [8:9], [0:24], [0:4], [0:6]} | slice | bytes 4608 | tf_op jit(solution)/shard_map/slice | solution.py:166
  1.9 1.7 %fusion.95 = (bf16[3,24,1152]{2,1,0:T(8,128)(2,1)S(1)}, bf16[3,24,1152]{2,1,0:T(8,128)(2,1)}) fusion(bf16[9,24,1152]{2,1,0:T(8,128)(2,1)} %param.6), kind=kLoop, calls=%fused_computation.263 | loop fusion | bytes 663552 | tf_op jit(solution)/shard_map/slice | solution.py:167
  3.7 0.7 %pad_maximum_fusion.2 = bf16[4,24,1152]{2,1,0:T(8,128)(2,1)} fusion(bf16[1,24,1152]{2,1,0:T(8,128)(2,1)S(1)} %fusion.30, bf16[3,24,1152]{2,1,0:T(8,128)(2,1)S(1)} %get-tuple-element.65), kind=kLoop, calls=%fused_computation.35 | loop fusion | flops 110592 | bytes 442368 | tf_op jit(solution)/shard_map/concatenate | solution.py:167
  4.4 3.4 %collective-permute-start = (bf16[4,24,1152]{2,1,0:T(8,128)(2,1)}, bf16[4,24,1152]{2,1,0:T(8,128)(2,1)}, u32[]{:S(2)}, u32[]{:S(2)}) collective-permute-start(bf16[4,24,1152]{2,1,0:T(8,128)(2,1)} %pad_maximum_fusion.2), channel_id=1, source_target_pairs={{0,32},{32,64},{64,96},{96,128},{128,160},{160,192},{192,224},{224... | collective-permute-start | bytes 663560 | tf_op jit(solution)/shard_map/ppermute | solution.py:19
  7.8 6.7 %collective-permute-start.1 = (bf16[3,24,1152]{2,1,0:T(8,128)(2,1)}, bf16[3,24,1152]{2,1,0:T(8,128)(2,1)S(1)}, u32[]{:S(2)}, u32[]{:S(2)}) collective-permute-start(bf16[3,24,1152]{2,1,0:T(8,128)(2,1)} %get-tuple-element.66), channel_id=1, source_target_pairs={{32,0},{64,32},{96,64},{128,96},{160,128},{192,160},{224,192},{256... | collective-permute-start | bytes 497672 | tf_op jit(solution)/shard_map/ppermute | solution.py:25
  14.4 0.7 %slice_bitcast_fusion.12 = (s32[9,24,1,4]{1,3,0,2:T(4,128)S(1)}, s32[9,24,4]{1,2,0:T(4,128)S(1)}, s32[9,24,1,4]{1,3,0,2:T(4,128)S(1)}) fusion(s32[2,9,24,4]{2,3,1,0:T(4,128)} %param.8), kind=kLoop, calls=%fused_computation.186 | loop fusion | bytes 17280 | tf_op jit(solution)/shard_map/stack;squeeze | solution.py:192
  15.2 0.7 %slice_bitcast_fusion.11 = s32[8,24,4]{1,2,0:T(4,128)S(1)} fusion(s32[2,9,24,4]{2,3,1,0:T(4,128)} %param.8), kind=kLoop, calls=%fused_computation.185 | loop fusion | bytes 6144 | tf_op jit(solution)/shard_map/slice | solution.py:196
  15.9 1.0 %slice_bitcast_fusion.7 = (f32[9,24,1,4,6]{1,3,4,0,2:T(4,128)S(1)}, f32[9,24,4,6]{1,2,3,0:T(4,128)S(1)}, f32[9,24,4,6]{1,2,3,0:T(4,128)S(1)}) fusion(f32[2,9,24,4,6]{2,3,4,1,0:T(4,128)} %param.7), kind=kLoop, calls=%fused_computation.64 | loop fusion | bytes 103680 | tf_op jit(solution)/shard_map/stack;squeeze | solution.py:183
  17.1 0.8 %slice.787 = f32[9,1,4,6]{1,2,3,0:T(4,128)} slice(f32[9,24,4,6]{1,2,3,0:T(4,128)S(1)} %get-tuple-element.80), slice={[0:9], [23:24], [0:4], [0:6]} | slice | bytes 1728 | tf_op jit(solution)/shard_map/slice | solution.py:171
  17.9 0.5 slice_bitcast_fusion.15
  18.5 0.1 pad_bitcast_fusion
  18.7 0.2 fusion.14
  19.0 4.8 %multiply_reduce_fusion = f32[9,24,4,12,6]{1,4,3,2,0:T(8,128)S(1)} fusion(f32[9,24,4,4,12]{1,3,4,2,0:T(4,128)S(1)} %fusion.14, f32[9,24,1,4,6]{1,3,4,0,2:T(4,128)S(1)} %bitcast_multiply_fusion, f32[9,24,1,4,6]{1,3,4,0,2:T(4,128)S(1)} %get-tuple-element.95, f32[9,24,1,4,6]{1,3,4,0,2:T(4,128)S(1)} %get-tuple-element.79, f32[9,24,1,4,6]{1,3,4,0,2:T(4,128)S(1)} %get-tuple-element.96), kind=kLoop, calls=%fused_computation | loop fusion | flops 497664 | bytes 497664 | tf_op jit(solution)/shard_map/reduce_sum | solution.py:110
  23.8 2.3 %fusion.5 = f32[9,24,49]{2,1,0:T(8,128)S(1)} fusion(f32[9,24,4,12,6]{1,4,3,2,0:T(8,128)S(1)} %multiply_reduce_fusion, f32[4,12,6,49,1]{3,2,1,4,0:T(8,128)S(1)} %copy-done.8, f32[9,24]{1,0:T(8,128)S(1)} %copy-done.5), kind=kOutput, calls=%fused_computation.10 | convolution fusion | flops 36588888 | bytes 348480 | tf_op jit(solution)/shard_map/dot_general | solution.py:113
  26.2 0.2 copy.93
  26.4 0.5 copy.114
  26.9 0.3 reshape.279
  27.4 0.7 %squeeze.67 = f32[7,24,32]{2,1,0:T(8,128)} reshape(f32[1,7,768]{2,1,0:T(8,128)S(1)} %get-tuple-element.77) | data formatting | bytes 43008 | tf_op jit(solution)/shard_map/squeeze | solution.py:210
  28.1 0.7 %squeeze.68 = f32[7,24,32]{2,1,0:T(8,128)} reshape(f32[1,7,768]{2,1,0:T(8,128)S(1)} %get-tuple-element.76) | data formatting | bytes 43008 | tf_op jit(solution)/shard_map/squeeze | solution.py:210
  29.3 0.9 %bitcast_dynamic-update-slice_fusion.7 = f32[9,15,24,32]{3,2,1,0:T(8,128)S(1)} fusion(f32[9,15,24,32]{3,2,1,0:T(8,128)S(1)} %bitcast_dynamic-update-slice_fusion.8, f32[7,24,32]{2,1,0:T(8,128)} %squeeze.67), kind=kLoop, calls=%fused_computation.44 | loop fusion | bytes 205824
  30.3 0.9 %bitcast_dynamic-update-slice_fusion.6 = f32[9,15,24,32]{3,2,1,0:T(8,128)S(1)} fusion(f32[9,15,24,32]{3,2,1,0:T(8,128)S(1)} %bitcast_dynamic-update-slice_fusion.7, f32[7,24,32]{2,1,0:T(8,128)} %squeeze.68), kind=kLoop, calls=%fused_computation.43 | loop fusion | bytes 205824
  31.3 1.2 %copy-done.1 = f32[9,15,24,32]{3,2,1,0:T(8,128)} copy-done((f32[9,15,24,32]{3,2,1,0:T(8,128)}, f32[9,15,24,32]{3,2,1,0:T(8,128)S(1)}, u32[]{:S(2)}) %copy-start.1) | copy-done | bytes 414744
  32.5 1.7 %copy.95 = f32[9,24,15,32]{3,2,1,0:T(8,128)S(1)} copy(f32[9,24,15,32]{3,1,2,0:T(8,128)} %bitcast.128) | data formatting | bytes 829440 | tf_op jit(solution)/shard_map/transpose | solution.py:212
  34.2 0.6 %reshape.280 = f32[1,216,480]{2,1,0:T(8,128)S(1)} reshape(f32[9,24,15,32]{3,2,1,0:T(8,128)S(1)} %copy.95) | data formatting | bytes 829440 | tf_op jit(solution)/shard_map/reshape | solution.py:212
  35.0 1.2 %copy.101 = f32[9,1,4,6]{3,2,0,1:T(4,128)S(1)} copy(f32[9,1,4,6]{1,2,3,0:T(4,128)} %slice.787) | data formatting | bytes 1728 | tf_op jit(solution)/shard_map/slice | solution.py:171
  36.3 0.1 copy.102
  36.8 0.1 slice_reduce_fusion.60
  37.0 0.8 %slice_bitcast_fusion.9 = bf16[24,1152]{1,0:T(8,128)(2,1)S(1)} fusion(bf16[4,24,1152]{2,1,0:T(8,128)(2,1)} %collective-permute-done), kind=kLoop, calls=%fused_computation.82 | loop fusion | bytes 110592 | tf_op jit(solution)/shard_map/squeeze | solution.py:220
  38.0 0.9 %slice.786 = bf16[3,24,1152]{2,1,0:T(8,128)(2,1)S(1)} slice(bf16[4,24,1152]{2,1,0:T(8,128)(2,1)} %collective-permute-done), slice={[0:3], [0:24], [0:1152]} | slice | bytes 331776 | tf_op jit(solution)/shard_map/slice | solution.py:169
  38.9 0.2 fusion.18
  39.1 1.9 %collective-permute-start.2 = (bf16[15,4,1152]{2,1,0:T(4,128)(2,1)S(1)}, bf16[15,4,1152]{2,1,0:T(4,128)(2,1)S(1)}, u32[]{:S(2)}, u32[]{:S(2)}) collective-permute-start(bf16[15,4,1152]{2,1,0:T(4,128)(2,1)S(1)} %fusion.18), channel_id=1, source_target_pairs={{0,1},{1,2},{2,3},{3,4},{4,5},{5,6},{6,7},{7,8},{8,9},{9,10},{10,1... | collective-permute-start | bytes 414728 | tf_op jit(solution)/shard_map/ppermute | solution.py:19
  41.1 10.1 %collective-permute-start.3 = (bf16[15,3,1152]{2,1,0:T(4,128)(2,1)S(1)}, bf16[15,3,1152]{2,1,0:T(4,128)(2,1)S(1)}, u32[]{:S(2)}, u32[]{:S(2)}) collective-permute-start(bf16[15,3,1152]{2,1,0:T(4,128)(2,1)S(1)} %pad_maximum_fusion.3), channel_id=1, source_target_pairs={{1,0},{2,1},{3,2},{4,3},{5,4},{6,5},{7,6},{8,7},{9,8},{10,9},{11,1... | collective-permute-start | bytes 311048 | tf_op jit(solution)/shard_map/ppermute | solution.py:25
  51.5 0.2 fusion.7
  51.7 0.4 slice_reduce_fusion.28
  52.1 0.5 slice_reduce_fusion.29
  53.0 0.1 copy.105
  53.2 0.1 multiply_reduce_fusion.2
  53.4 0.2 fusion.13
  53.6 0.5 slice_reduce_fusion.59
  54.2 0.4 slice_reduce_fusion.58
  54.5 0.6 fusion.9
  55.1 0.5 fusion.16
  55.6 0.5 convolution_add_fusion.1
  56.0 0.5 convolution_add_fusion
  56.5 1.5 %multiply_add_fusion = f32[1,24,1152]{2,1,0:T(8,128)S(1)} fusion(bf16[15,3,1152]{2,1,0:T(4,128)(2,1)S(1)} %collective-permute-done.3, bf16[3,24,1152]{2,1,0:T(8,128)(2,1)S(1)} %collective-permute-done.1, bf16[9,24,1152]{2,1,0:T(8,128)(2,1)S(1)} %copy-done, bf16[3,24,1152]{2,1,0:T(8,128)(2,1)S(1)} %slice.786, bf16[15,3,1152]{2,1,0:T(4,128)(2,1)S(1)} %bitcast.126, ...), kind=kLoop, calls=%fused_computation.58 | loop fusion | flops 7105536 | bytes 1563648 | tf_op jit(solution)/shard_map/add | solution.py:124
  58.0 1.2 %fusion.33 = f32[9,1,1152]{2,1,0:T(1,128)S(1)} fusion(bf16[12,24,1152]{2,1,0:T(8,128)(2,1)S(1)} %constant_dynamic-update-slice_fusion, bf16[15,4,1152]{2,1,0:T(4,128)(2,1)S(1)} %collective-permute-done.2, bf16[9,24,1152]{2,1,0:T(8,128)(2,1)S(1)} %copy-done, bf16[3,24,1152]{2,1,0:T(8,128)(2,1)S(1)} %slice.786, f32[9]{0:T(128)S(1)} %get-tuple-element.36, ...), kind=kLoop, calls=%fused_computation.86 | loop fusion | flops 1109376 | bytes 1715712 | tf_op jit(solution)/shard_map/add | solution.py:124
  59.2 0.9 %add_convert_fusion = bf16[9,24,1152]{2,1,0:T(8,128)(2,1)} fusion(f32[1,24,1152]{2,1,0:T(8,128)S(1)} %multiply_add_fusion, f32[9,1,1152]{2,1,0:T(1,128)S(1)} %fusion.33, f32[9,24,1152]{2,1,0:T(8,128)S(1)} %bitcast.127, bf16[9,24,1152]{2,1,0:T(8,128)(2,1)S(1)} %copy-done), kind=kLoop, calls=%fused_computation.21 | loop fusion | flops 1244160 | bytes 2142720 | tf_op jit(solution)/shard_map/convert_element_type | solution.py:234
  (77 shorter events, 3.1 us)
Async XLA Ops:
  0.0 17.0 %copy-start.2 = (f32[2,9,24,4,6]{2,3,4,1,0:T(4,128)S(1)}, f32[2,9,24,4,6]{2,3,4,1,0:T(4,128)}, u32[]{:S(2)}) copy-start(f32[2,9,24,4,6]{2,3,4,1,0:T(4,128)} %param.7) | copy-start | bytes 124420
  0.0 16.9 %copy-start = (bf16[9,24,1152]{2,1,0:T(8,128)(2,1)S(1)}, bf16[9,24,1152]{2,1,0:T(8,128)(2,1)}, u32[]{:S(2)}) copy-start(bf16[9,24,1152]{2,1,0:T(8,128)(2,1)} %param.6) | copy-start | bytes 1492996
  1.9 16.1 %copy-start.5 = (f32[9,24]{1,0:T(8,128)S(1)}, f32[9,24]{1,0:T(8,128)}, u32[]{:S(2)}) copy-start(f32[9,24]{1,0:T(8,128)} %param.9) | copy-start | bytes 2596
  4.4 32.6 %collective-permute-start = (bf16[4,24,1152]{2,1,0:T(8,128)(2,1)}, bf16[4,24,1152]{2,1,0:T(8,128)(2,1)}, u32[]{:S(2)}, u32[]{:S(2)}) collective-permute-start(bf16[4,24,1152]{2,1,0:T(8,128)(2,1)} %pad_maximum_fusion.2), channel_id=1, source_target_pairs={{0,32},{32,64},{64,96},{96,128},{128,160},{160,192},{192,224},{224... | collective-permute-start | bytes 663560 | tf_op jit(solution)/shard_map/ppermute | solution.py:19
  7.8 29.2 %collective-permute-start.1 = (bf16[3,24,1152]{2,1,0:T(8,128)(2,1)}, bf16[3,24,1152]{2,1,0:T(8,128)(2,1)S(1)}, u32[]{:S(2)}, u32[]{:S(2)}) collective-permute-start(bf16[3,24,1152]{2,1,0:T(8,128)(2,1)} %get-tuple-element.66), channel_id=1, source_target_pairs={{32,0},{64,32},{96,64},{128,96},{160,128},{192,160},{224,192},{256... | collective-permute-start | bytes 497672 | tf_op jit(solution)/shard_map/ppermute | solution.py:25
  19.0 4.8 %copy-start.8 = (f32[4,12,6,49,1]{3,2,1,4,0:T(8,128)S(1)}, f32[4,12,6,49,1]{3,2,1,4,0:T(8,128)}, u32[]{:S(2)}) copy-start(f32[4,12,6,49,1]{3,2,1,4,0:T(8,128)} %constant.70) | copy-start | bytes 169348
  31.3 1.2 %copy-start.1 = (f32[9,15,24,32]{3,2,1,0:T(8,128)}, f32[9,15,24,32]{3,2,1,0:T(8,128)S(1)}, u32[]{:S(2)}) copy-start(f32[9,15,24,32]{3,2,1,0:T(8,128)S(1)} %bitcast_dynamic-update-slice_fusion) | copy-start | bytes 1244164
  34.9 1.9 %copy-start.6 = (f32[9,24]{1,0:T(8,128)S(1)}, f32[9,24]{1,0:T(8,128)}, u32[]{:S(2)}) copy-start(f32[9,24]{1,0:T(8,128)} %param.9) | copy-start | bytes 2596
  36.7 14.8 %copy-start.3 = (f32[12,6,45]{2,1,0:T(8,128)S(1)}, f32[12,6,45]{2,1,0:T(8,128)}, u32[]{:S(2)}) copy-start(f32[12,6,45]{2,1,0:T(8,128)} %constant.69) | copy-start | bytes 38884
  36.8 14.8 %copy-start.7 = (f32[24]{0:T(128)S(1)}, f32[24]{0:T(128)}, u32[]{:S(2)}) copy-start(f32[24]{0:T(128)} %slice_bitcast_fusion.15) | copy-start | bytes 292
  38.0 15.4 %copy-start.4 = (f32[12,6,45]{2,0,1:T(8,128)S(1)}, f32[12,6,45]{2,0,1:T(8,128)}, u32[]{:S(2)}) copy-start(f32[12,6,45]{2,0,1:T(8,128)} %constant.67) | copy-start | bytes 38884
  39.1 13.6 %collective-permute-start.2 = (bf16[15,4,1152]{2,1,0:T(4,128)(2,1)S(1)}, bf16[15,4,1152]{2,1,0:T(4,128)(2,1)S(1)}, u32[]{:S(2)}, u32[]{:S(2)}) collective-permute-start(bf16[15,4,1152]{2,1,0:T(4,128)(2,1)S(1)} %fusion.18), channel_id=1, source_target_pairs={{0,1},{1,2},{2,3},{3,4},{4,5},{5,6},{6,7},{7,8},{8,9},{9,10},{10,1... | collective-permute-start | bytes 414728 | tf_op jit(solution)/shard_map/ppermute | solution.py:19
  41.1 13.5 %collective-permute-start.3 = (bf16[15,3,1152]{2,1,0:T(4,128)(2,1)S(1)}, bf16[15,3,1152]{2,1,0:T(4,128)(2,1)S(1)}, u32[]{:S(2)}, u32[]{:S(2)}) collective-permute-start(bf16[15,3,1152]{2,1,0:T(4,128)(2,1)S(1)} %pad_maximum_fusion.3), channel_id=1, source_target_pairs={{1,0},{2,1},{3,2},{4,3},{5,4},{6,5},{7,6},{8,7},{9,8},{10,9},{11,1... | collective-permute-start | bytes 311048 | tf_op jit(solution)/shard_map/ppermute | solution.py:25

commit v11 on v6

--- a/solution.py
+++ b/solution.py
@@ -144,7 +144,7 @@
 
 def apply_taps(weights, padded, tracer, offsets):
     return pl.pallas_call(
-        functools.partial(tap_kernel, offsets, math.gcd(tracer.shape[2], 384)),
+        functools.partial(tap_kernel, offsets, tracer.shape[2]),
         out_shape=jax.ShapeDtypeStruct(tracer.shape, jnp.bfloat16),
         scratch_shapes=[pltpu.VMEM(padded.shape, jnp.float32)],
         interpret=INTERPRET,

time: 51.4 us -> 51 us (level)
  no operation moved by 1% of the time
where the time goes in v11:
time: 51 us; the launch traced here: 50.6 us
  starting transfers between devices  18.5 us (36%)
  Pallas kernels  9.4 us (18%)
  other arithmetic  9.21 us (18%)
  local copies, waits for them, and re-layouts  5.82 us (11%)
  waiting for transfers between devices  4.48 us (9%)
  matrix products  2.8 us (5%)
    ppermute x2, starting transfers between devices, from_prev(): return lax.ppermute(value, axis, pairs)  10.2 us
    pallas_call x1, Pallas kernels, apply_taps(): pl.pallas_call(functools.partial(tap_kernel, offsets, tracer.shape[2]), o...  9.4 us
    ppermute x2, starting transfers between devices, from_next(): return lax.ppermute(value, axis, pairs)  8.3 us
    reduce_sum x3, other arithmetic, face_weights(): spread = jnp.sum(onehot[..., :, None] * moments[..., None, :], axis=-3)  4.89 us
    ppermute x2, waiting for transfers between devices, from_next(): return lax.ppermute(value, axis, pairs)  3.36 us
    dot_general x3, matrix products, face_weights(): jnp.dot(flat, tables.reshape(-1, tables.shape[-1]), precision=lax.Precisi...  2.8 us
    concatenate x1, other arithmetic, local(): padded = jnp.concatenate([from_west[:, :3], tall, from_east], axis=1)  1.47 us
    ppermute x2, waiting for transfers between devices, from_prev(): return lax.ppermute(value, axis, pairs)  1.12 us
  transfers between devices with their start and end apart: 4, of which 2 were waited for; matrix products, arithmetic and copies ran while one was open for 26% of the time, Pallas kernels for 0%

profile of v11, /device:TPU:233, one launch (start us, length us, event | category | flops | bytes accessed | tf_op | source)
XLA Modules:
  0.0 50.6 jit_solution(2687460553775310425)
XLA Ops:
  0.0 0.7 %slice_bitcast_fusion.8 = (s32[1,24,4]{1,2,0:T(4,128)S(1)}, bf16[24,4]{0,1:T(4,128)(2,1)S(1)}) fusion(s32[2,9,24,4]{2,3,1,0:T(4,128)} %param.7), kind=kLoop, calls=%fused_computation.73 | loop fusion | flops 96 | bytes 1344 | tf_op jit(solution)/shard_map/slice | solution.py:195
  0.7 0.1 copy.48
  0.8 0.7 %slice.140 = f32[1,1,24,4,6]{2,3,4,1,0:T(4,128)S(1)} slice(f32[2,9,24,4,6]{2,3,4,1,0:T(4,128)} %param.6), slice={[1:2], [8:9], [0:24], [0:4], [0:6]} | slice | bytes 4608 | tf_op jit(solution)/shard_map/slice | solution.py:165
  1.6 0.1 copy.46
  1.7 1.0 %fusion.24 = (bf16[3,24,1152]{2,1,0:T(8,128)(2,1)S(1)}, bf16[3,24,1152]{2,1,0:T(8,128)(2,1)S(1)}) fusion(bf16[9,24,1152]{2,1,0:T(8,128)(2,1)} %t_ref.1), kind=kLoop, calls=%fused_computation.76 | loop fusion | bytes 663552 | tf_op jit(solution)/shard_map/slice | solution.py:167
  2.7 0.1 fusion.14
  2.8 3.1 %collective-permute-start = (bf16[4,24,1152]{2,1,0:T(8,128)(2,1)S(1)}, bf16[4,24,1152]{2,1,0:T(8,128)(2,1)S(1)}, u32[]{:S(2)}, u32[]{:S(2)}) collective-permute-start(bf16[4,24,1152]{2,1,0:T(8,128)(2,1)S(1)} %pad_maximum_fusion.2), channel_id=1, source_target_pairs={{0,32},{32,64},{64,96},{96,128},{128,160},{160,192},{192,224},{224... | collective-permute-start | bytes 663560 | tf_op jit(solution)/shard_map/ppermute | solution.py:19
  5.9 6.4 %collective-permute-start.1 = (bf16[3,24,1152]{2,1,0:T(8,128)(2,1)S(1)}, bf16[3,24,1152]{2,1,0:T(8,128)(2,1)S(1)}, u32[]{:S(2)}, u32[]{:S(2)}) collective-permute-start(bf16[3,24,1152]{2,1,0:T(8,128)(2,1)S(1)} %get-tuple-element.5), channel_id=1, source_target_pairs={{32,0},{64,32},{96,64},{128,96},{160,128},{192,160},{224,192},{256... | collective-permute-start | bytes 497672 | tf_op jit(solution)/shard_map/ppermute | solution.py:25
  12.3 0.7 %slice_bitcast_fusion.7 = (s32[9,24,4]{1,2,0:T(4,128)S(1)}, s32[9,24,1,4]{1,3,0,2:T(4,128)S(1)}, s32[9,24,1,4]{1,3,0,2:T(4,128)S(1)}) fusion(s32[2,9,24,4]{2,3,1,0:T(4,128)} %param.7), kind=kLoop, calls=%fused_computation.61 | loop fusion | bytes 17280 | tf_op jit(solution)/shard_map/squeeze | solution.py:193
  13.1 0.7 %slice_bitcast_fusion.5 = s32[8,24,4]{1,2,0:T(4,128)S(1)} fusion(s32[2,9,24,4]{2,3,1,0:T(4,128)} %param.7), kind=kLoop, calls=%fused_computation.59 | loop fusion | bytes 6144 | tf_op jit(solution)/shard_map/slice | solution.py:195
  13.8 1.0 %slice_bitcast_fusion.2 = (f32[9,24,4,6]{1,2,3,0:T(4,128)S(1)}, f32[9,24,1,4,6]{1,3,4,0,2:T(4,128)S(1)}, f32[9,24,4,6]{1,2,3,0:T(4,128)S(1)}) fusion(f32[2,9,24,4,6]{2,3,4,1,0:T(4,128)} %param.6), kind=kLoop, calls=%fused_computation.29 | loop fusion | bytes 103680 | tf_op jit(solution)/shard_map/squeeze | solution.py:184
  14.8 0.1 slice_convert_fusion
  14.9 0.1 bitcast_multiply_fusion
  15.0 0.1 slice.168
  15.1 0.1 slice_multiply_fusion
  15.2 0.1 pad_bitcast_fusion
  15.3 0.1 add_bitcast_fusion
  15.4 0.2 fusion
  15.6 0.0 copy-start.5
  15.6 4.6 %multiply_reduce_fusion = f32[9,24,4,12,6]{1,4,3,2,0:T(8,128)S(1)} fusion(f32[9,24,4,4,12]{1,3,4,2,0:T(4,128)S(1)} %fusion, f32[9,24,1,4,6]{1,3,4,0,2:T(4,128)S(1)} %bitcast_multiply_fusion, f32[9,24,1,4,6]{1,3,4,0,2:T(4,128)S(1)} %get-tuple-element.23, f32[9,24,1,4,6]{1,3,4,0,2:T(4,128)S(1)} %get-tuple-element.8, f32[9,24,1,4,6]{1,3,4,0,2:T(4,128)S(1)} %get-tuple-element.24), kind=kLoop, calls=%fused_computation | loop fusion | flops 497664 | bytes 497664 | tf_op jit(solution)/shard_map/reduce_sum | solution.py:110
  20.3 2.3 %convolution_bitcast_fusion = f32[9,24,45]{2,1,0:T(8,128)S(1)} fusion(f32[9,24,4,12,6]{1,4,3,2,0:T(8,128)S(1)} %multiply_reduce_fusion, f32[4,12,6,45,1]{3,2,1,4,0:T(8,128)S(1)} %copy-done.5), kind=kOutput, calls=%fused_computation.1 | convolution fusion | flops 33592320 | bytes 339552 | tf_op jit(solution)/shard_map/dot_general | solution.py:113
  22.6 0.1 copy.50
  22.8 0.1 copy.51
  22.9 0.3 copy.49
  23.2 0.1 reshape_squeeze.7
  23.3 0.1 fusion.18
  23.4 0.1 copy.52
  23.5 0.1 convert_add_fusion
  23.6 0.1 slice_convert_fusion.1
  23.7 0.1 copy.56
  23.7 0.1 copy.55
  23.9 0.2 fusion.2
  24.1 7.1 %collective-permute-start.2 = (bf16[15,4,1152]{2,1,0:T(4,128)(2,1)S(1)}, bf16[15,4,1152]{2,1,0:T(4,128)(2,1)S(1)}, u32[]{:S(2)}, u32[]{:S(2)}) collective-permute-start(bf16[15,4,1152]{2,1,0:T(4,128)(2,1)S(1)} %fusion.2), channel_id=1, source_target_pairs={{0,1},{1,2},{2,3},{3,4},{4,5},{5,6},{6,7},{7,8},{8,9},{9,10},{10,1... | collective-permute-start | bytes 414728 | tf_op jit(solution)/shard_map/ppermute | solution.py:19
  31.2 1.9 %collective-permute-start.3 = (bf16[15,3,1152]{2,1,0:T(4,128)(2,1)S(1)}, bf16[15,3,1152]{2,1,0:T(4,128)(2,1)S(1)}, u32[]{:S(2)}, u32[]{:S(2)}) collective-permute-start(bf16[15,3,1152]{2,1,0:T(4,128)(2,1)S(1)} %pad_maximum_fusion.3), channel_id=1, source_target_pairs={{1,0},{2,1},{3,2},{4,3},{5,4},{6,5},{7,6},{8,7},{9,8},{10,9},{11,1... | collective-permute-start | bytes 311048 | tf_op jit(solution)/shard_map/ppermute | solution.py:25
  33.2 0.1 multiply_reduce_fusion.1
  33.3 0.2 convolution_bitcast_fusion.1
  33.5 1.1 %collective-permute-done.2 = bf16[15,4,1152]{2,1,0:T(4,128)(2,1)S(1)} collective-permute-done((bf16[15,4,1152]{2,1,0:T(4,128)(2,1)S(1)}, bf16[15,4,1152]{2,1,0:T(4,128)(2,1)S(1)}, u32[]{:S(2)}, u32[]{:S(2)}) %collective-permute-start.2) | collective-permute-done | bytes 138272 | tf_op jit(solution)/shard_map/ppermute | solution.py:19
  34.7 0.1 convert_add_fusion.1
  34.8 0.1 slice_convert_fusion.2
  34.8 0.1 mul.86
  34.9 0.1 copy.53
  35.1 0.1 fusion.20
  35.2 0.1 multiply_reduce_fusion.2
  35.3 0.3 convolution_bitcast_fusion.2
  35.6 0.7 %add_divide_fusion.w_ref = f32[9,24,45]{2,1,0:T(8,128)} fusion(f32[1,24,45]{2,1,0:T(8,128)S(1)} %convolution_bitcast_fusion.1, f32[9,24,45]{2,1,0:T(8,128)S(1)} %convolution_bitcast_fusion, f32[9,1,45]{2,1,0:T(1,128)S(1)} %broadcast_in_dim.36, f32[9,24]{1,0:T(8,128)S(1)} %copy-done.4), kind=kLoop, calls=%fused_computation.22 | loop fusion | flops 29160 | bytes 84564 | tf_op jit(solution)/shard_map/div | solution.py:209
  36.3 3.4 %collective-permute-done.3 = bf16[15,3,1152]{2,1,0:T(4,128)(2,1)S(1)} collective-permute-done((bf16[15,3,1152]{2,1,0:T(4,128)(2,1)S(1)}, bf16[15,3,1152]{2,1,0:T(4,128)(2,1)S(1)}, u32[]{:S(2)}, u32[]{:S(2)}) %collective-permute-start.3) | collective-permute-done | bytes 103712 | tf_op jit(solution)/shard_map/ppermute | solution.py:25
  39.7 1.5 %pad_maximum_fusion.p_ref = bf16[15,30,1152]{2,1,0:T(8,128)(2,1)} fusion(bf16[15,3,1152]{2,1,0:T(4,128)(2,1)S(1)} %collective-permute-done.3, bf16[3,24,1152]{2,1,0:T(8,128)(2,1)S(1)} %collective-permute-done.1, bf16[9,24,1152]{2,1,0:T(8,128)(2,1)S(1)} %copy-done, bf16[3,24,1152]{2,1,0:T(8,128)(2,1)S(1)} %slice.167, bf16[15,3,1152]{2,1,0:T(4,128)(2,1)S(1)} %bitcast.71), kind=kLoop, calls=%fused_computation.4 | loop fusion | flops 5184000 | bytes 2073600 | tf_op jit(solution)/shard_map/concatenate | solution.py:174
  41.2 9.4 %shard_map.55 = bf16[9,24,1152]{2,1,0:T(8,128)(2,1)} custom-call(f32[9,24,45]{2,1,0:T(8,128)} %add_divide_fusion.w_ref, bf16[15,30,1152]{2,1,0:T(8,128)(2,1)} %pad_maximum_fusion.p_ref, bf16[9,24,1152]{2,1,0:T(8,128)(2,1)} %t_ref.1), custom_call_target="tpu_custom_call" | custom-call | tf_op jit(solution)/shard_map/pallas_call | solution.py:146
  (29 shorter events, 0.3 us)
Async XLA Ops:
  0.0 14.9 %copy-start.1 = (f32[2,9,24,4,6]{2,3,4,1,0:T(4,128)S(1)}, f32[2,9,24,4,6]{2,3,4,1,0:T(4,128)}, u32[]{:S(2)}) copy-start(f32[2,9,24,4,6]{2,3,4,1,0:T(4,128)} %param.6) | copy-start | bytes 124420
  2.8 20.7 %collective-permute-start = (bf16[4,24,1152]{2,1,0:T(8,128)(2,1)S(1)}, bf16[4,24,1152]{2,1,0:T(8,128)(2,1)S(1)}, u32[]{:S(2)}, u32[]{:S(2)}) collective-permute-start(bf16[4,24,1152]{2,1,0:T(8,128)(2,1)S(1)} %pad_maximum_fusion.2), channel_id=1, source_target_pairs={{0,32},{32,64},{64,96},{96,128},{128,160},{160,192},{192,224},{224... | collective-permute-start | bytes 663560 | tf_op jit(solution)/shard_map/ppermute | solution.py:19
  5.9 17.9 %collective-permute-start.1 = (bf16[3,24,1152]{2,1,0:T(8,128)(2,1)S(1)}, bf16[3,24,1152]{2,1,0:T(8,128)(2,1)S(1)}, u32[]{:S(2)}, u32[]{:S(2)}) collective-permute-start(bf16[3,24,1152]{2,1,0:T(8,128)(2,1)S(1)} %get-tuple-element.5), channel_id=1, source_target_pairs={{32,0},{64,32},{96,64},{128,96},{160,128},{192,160},{224,192},{256... | collective-permute-start | bytes 497672 | tf_op jit(solution)/shard_map/ppermute | solution.py:25
  15.6 4.7 %copy-start.5 = (f32[4,12,6,45,1]{3,2,1,4,0:T(8,128)S(1)}, f32[4,12,6,45,1]{3,2,1,4,0:T(8,128)}, u32[]{:S(2)}) copy-start(f32[4,12,6,45,1]{3,2,1,4,0:T(8,128)} %constant.45) | copy-start | bytes 155524
  20.3 3.6 %copy-start = (bf16[9,24,1152]{2,1,0:T(8,128)(2,1)S(1)}, bf16[9,24,1152]{2,1,0:T(8,128)(2,1)}, u32[]{:S(2)}) copy-start(bf16[9,24,1152]{2,1,0:T(8,128)(2,1)} %t_ref.1) | copy-start | bytes 1492996
  22.6 10.6 %copy-start.2 = (f32[12,6,45]{2,1,0:T(8,128)S(1)}, f32[12,6,45]{2,1,0:T(8,128)}, u32[]{:S(2)}) copy-start(f32[12,6,45]{2,1,0:T(8,128)} %constant.44) | copy-start | bytes 38884
  23.2 12.1 %copy-start.3 = (f32[12,6,45]{2,0,1:T(8,128)S(1)}, f32[12,6,45]{2,0,1:T(8,128)}, u32[]{:S(2)}) copy-start(f32[12,6,45]{2,0,1:T(8,128)} %constant.42) | copy-start | bytes 38884
  23.3 12.3 %copy-start.4 = (f32[9,24]{1,0:T(8,128)S(1)}, f32[9,24]{1,0:T(8,128)}, u32[]{:S(2)}) copy-start(f32[9,24]{1,0:T(8,128)} %param.8) | copy-start | bytes 2596
  24.1 10.6 %collective-permute-start.2 = (bf16[15,4,1152]{2,1,0:T(4,128)(2,1)S(1)}, bf16[15,4,1152]{2,1,0:T(4,128)(2,1)S(1)}, u32[]{:S(2)}, u32[]{:S(2)}) collective-permute-start(bf16[15,4,1152]{2,1,0:T(4,128)(2,1)S(1)} %fusion.2), channel_id=1, source_target_pairs={{0,1},{1,2},{2,3},{3,4},{4,5},{5,6},{6,7},{7,8},{8,9},{9,10},{10,1... | collective-permute-start | bytes 414728 | tf_op jit(solution)/shard_map/ppermute | solution.py:19
  31.2 8.5 %collective-permute-start.3 = (bf16[15,3,1152]{2,1,0:T(4,128)(2,1)S(1)}, bf16[15,3,1152]{2,1,0:T(4,128)(2,1)S(1)}, u32[]{:S(2)}, u32[]{:S(2)}) collective-permute-start(bf16[15,3,1152]{2,1,0:T(4,128)(2,1)S(1)} %pad_maximum_fusion.3), channel_id=1, source_target_pairs={{1,0},{2,1},{3,2},{4,3},{5,4},{6,5},{7,6},{8,7},{9,8},{10,9},{11,1... | collective-permute-start | bytes 311048 | tf_op jit(solution)/shard_map/ppermute | solution.py:25

commit v12 on v11

--- a/solution.py
+++ b/solution.py
@@ -123,6 +123,19 @@
         term = weights[:, :, tap][:, :, None] * piece.astype(jnp.float32)
         total = term if total is None else total + term
     return total
+
+
+def face_weights_cells(moments, pieces, tables):
+    n_row, n_col = moments.shape[:2]
+    n_code = tables.shape[1]
+    m_t = jnp.transpose(moments, (2, 3, 4, 0, 1)).reshape(moments.shape[2:] + (n_row * n_col,))
+    p_t = jnp.transpose(pieces, (2, 3, 0, 1)).reshape(pieces.shape[2:] + (n_row * n_col,))
+    onehot = (p_t[:, :, None, :] == jnp.arange(n_code, dtype=jnp.int32)[None, None, :, None]).astype(jnp.float32)
+    spread = jnp.sum(onehot[:, :, :, None, :] * m_t[:, :, None, :, :], axis=1)
+    flat = spread.reshape(-1, n_row * n_col).T
+    scaled = jnp.round(tables * 24.0).reshape(-1, tables.shape[-1])
+    weights = jnp.dot(flat, scaled, precision=lax.Precision.HIGH) / 24.0
+    return weights.reshape(n_row, n_col, tables.shape[-1])
 
 
 def tap_kernel(offsets, chunk, w_ref, p_ref, t_ref, o_ref, s_ref):
@@ -197,7 +210,7 @@
         ],
         axis=2,
     )
-    weights = face_weights(face_m, face_p, tables)
+    weights = face_weights_cells(face_m, face_p, tables)
     weights = lax.optimization_barrier(weights)
 
     west_m, west_p = unpack_weights(from_west[3 : 3 + rows, 3], n_piece, n_moment)

time: 51 us -> 48.5 us (0.951)
  the two profiles are of different devices: /device:TPU:233 before, /device:TPU:223 now
where the time goes in v12:
time: 48.5 us; the launch traced here: 48.2 us
  starting transfers between devices  18.7 us (39%)
  waiting for transfers between devices  9.62 us (20%)
  Pallas kernels  9.4 us (19%)
  other arithmetic  5.35 us (11%)
  local copies, waits for them, and re-layouts  4.02 us (8%)
  matrix products  0.8 us (2%)
    ppermute x2, starting transfers between devices, from_prev(): return lax.ppermute(value, axis, pairs)  14.8 us
    pallas_call x1, Pallas kernels, apply_taps(): pl.pallas_call(functools.partial(tap_kernel, offsets, tracer.shape[2]), o...  9.4 us
    ppermute x2, waiting for transfers between devices, from_next(): return lax.ppermute(value, axis, pairs)  6.74 us
    ppermute x2, starting transfers between devices, from_next(): return lax.ppermute(value, axis, pairs)  3.84 us
    ppermute x2, waiting for transfers between devices, from_prev(): return lax.ppermute(value, axis, pairs)  2.88 us
    concatenate x1, other arithmetic, local(): padded = jnp.concatenate([from_west[:, :3], tall, from_east], axis=1)  1.47 us
    slice x1, local copies, waits for them, and re-layouts, local(): from_north = from_next(tracer[:3], 'panel', False)  1.02 us
  transfers between devices with their start and end apart: 4, of which 4 were waited for; matrix products, arithmetic and copies ran while one was open for 12% of the time, Pallas kernels for 0%

profile of v12, /device:TPU:223, one launch (start us, length us, event | category | flops | bytes accessed | tf_op | source)
XLA Modules:
  0.0 48.2 jit_solution(6989913025847752513)
XLA Ops:
  0.0 0.8 %slice_bitcast_fusion.8 = (s32[1,24,4]{1,2,0:T(4,128)S(1)}, bf16[24,4]{0,1:T(4,128)(2,1)S(1)}) fusion(s32[2,9,24,4]{2,3,1,0:T(4,128)} %param.7), kind=kLoop, calls=%fused_computation.73 | loop fusion | flops 96 | bytes 1344 | tf_op jit(solution)/shard_map/slice | solution.py:208
  0.8 0.1 copy.50
  0.9 0.7 %slice.140 = f32[1,1,24,4,6]{2,3,4,1,0:T(4,128)S(1)} slice(f32[2,9,24,4,6]{2,3,4,1,0:T(4,128)} %param.6), slice={[1:2], [8:9], [0:24], [0:4], [0:6]} | slice | bytes 4608 | tf_op jit(solution)/shard_map/slice | solution.py:178
  1.6 0.1 copy.48
  1.7 1.0 %fusion.24 = (bf16[3,24,1152]{2,1,0:T(8,128)(2,1)S(1)}, bf16[3,24,1152]{2,1,0:T(8,128)(2,1)S(1)}) fusion(bf16[9,24,1152]{2,1,0:T(8,128)(2,1)} %t_ref.1), kind=kLoop, calls=%fused_computation.76 | loop fusion | bytes 663552 | tf_op jit(solution)/shard_map/slice | solution.py:180
  2.7 0.1 fusion.14
  2.8 4.4 %collective-permute-start = (bf16[4,24,1152]{2,1,0:T(8,128)(2,1)S(1)}, bf16[4,24,1152]{2,1,0:T(8,128)(2,1)S(1)}, u32[]{:S(2)}, u32[]{:S(2)}) collective-permute-start(bf16[4,24,1152]{2,1,0:T(8,128)(2,1)S(1)} %pad_maximum_fusion.1), channel_id=1, source_target_pairs={{0,32},{32,64},{64,96},{96,128},{128,160},{160,192},{192,224},{224... | collective-permute-start | bytes 663560 | tf_op jit(solution)/shard_map/ppermute | solution.py:19
  7.3 1.9 %collective-permute-start.1 = (bf16[3,24,1152]{2,1,0:T(8,128)(2,1)S(1)}, bf16[3,24,1152]{2,1,0:T(8,128)(2,1)S(1)}, u32[]{:S(2)}, u32[]{:S(2)}) collective-permute-start(bf16[3,24,1152]{2,1,0:T(8,128)(2,1)S(1)} %get-tuple-element.5), channel_id=1, source_target_pairs={{32,0},{64,32},{96,64},{128,96},{160,128},{192,160},{224,192},{256... | collective-permute-start | bytes 497672 | tf_op jit(solution)/shard_map/ppermute | solution.py:25
  9.3 0.1 bitcast_multiply_fusion
  9.4 0.1 slice.168
  9.5 0.1 slice_multiply_fusion
  9.6 0.1 pad_bitcast_fusion
  9.7 0.1 maximum_bitcast_fusion
  9.9 0.1 copy.45
  10.0 0.2 mul.91
  10.3 0.1 slice_convert_fusion
  10.3 0.1 add_bitcast_fusion.1
  10.5 0.1 eq.67
  10.6 0.8 %multiply_reduce_fusion = f32[4,12,6,216]{3,2,1,0:T(8,128)S(1)} fusion(f32[4,4,6,216]{3,1,2,0:T(4,128)S(1)} %mul.91, f32[4,4,12,216]{3,1,2,0:T(4,128)S(1)} %fusion.1), kind=kLoop, calls=%fused_computation | loop fusion | flops 435456 | bytes 497664 | tf_op jit(solution)/shard_map/reduce_sum | solution.py:134
  11.4 0.3 fusion
  11.8 0.1 copy.46
  11.9 0.1 copy.52
  12.0 0.1 copy.53
  12.1 0.3 copy.51
  12.4 0.1 reshape_squeeze.7
  12.5 0.1 fusion.18
  12.7 2.3 %collective-permute-done = bf16[4,24,1152]{2,1,0:T(8,128)(2,1)S(1)} collective-permute-done((bf16[4,24,1152]{2,1,0:T(8,128)(2,1)S(1)}, bf16[4,24,1152]{2,1,0:T(8,128)(2,1)S(1)}, u32[]{:S(2)}, u32[]{:S(2)}) %collective-permute-start) | collective-permute-done | bytes 221216 | tf_op jit(solution)/shard_map/ppermute | solution.py:19
  15.0 0.1 convert_add_fusion
  15.1 0.1 slice_convert_fusion.1
  15.3 0.1 copy.57
  15.4 2.8 %collective-permute-done.1 = bf16[3,24,1152]{2,1,0:T(8,128)(2,1)S(1)} collective-permute-done((bf16[3,24,1152]{2,1,0:T(8,128)(2,1)S(1)}, bf16[3,24,1152]{2,1,0:T(8,128)(2,1)S(1)}, u32[]{:S(2)}, u32[]{:S(2)}) %collective-permute-start.1) | collective-permute-done | bytes 165920 | tf_op jit(solution)/shard_map/ppermute | solution.py:25
  18.3 0.2 fusion.2
  18.4 10.4 %collective-permute-start.2 = (bf16[15,4,1152]{2,1,0:T(4,128)(2,1)S(1)}, bf16[15,4,1152]{2,1,0:T(4,128)(2,1)S(1)}, u32[]{:S(2)}, u32[]{:S(2)}) collective-permute-start(bf16[15,4,1152]{2,1,0:T(4,128)(2,1)S(1)} %fusion.2), channel_id=1, source_target_pairs={{0,1},{1,2},{2,3},{3,4},{4,5},{5,6},{6,7},{7,8},{8,9},{9,10},{10,1... | collective-permute-start | bytes 414728 | tf_op jit(solution)/shard_map/ppermute | solution.py:19
  28.9 1.9 %collective-permute-start.3 = (bf16[15,3,1152]{2,1,0:T(4,128)(2,1)S(1)}, bf16[15,3,1152]{2,1,0:T(4,128)(2,1)S(1)}, u32[]{:S(2)}, u32[]{:S(2)}) collective-permute-start(bf16[15,3,1152]{2,1,0:T(4,128)(2,1)S(1)} %pad_maximum_fusion.2), channel_id=1, source_target_pairs={{1,0},{2,1},{3,2},{4,3},{5,4},{6,5},{7,6},{8,7},{9,8},{10,9},{11,1... | collective-permute-start | bytes 311048 | tf_op jit(solution)/shard_map/ppermute | solution.py:25
  30.8 0.1 multiply_reduce_fusion.1
  30.9 0.2 convolution_bitcast_fusion.1
  31.2 0.6 %collective-permute-done.2 = bf16[15,4,1152]{2,1,0:T(4,128)(2,1)S(1)} collective-permute-done((bf16[15,4,1152]{2,1,0:T(4,128)(2,1)S(1)}, bf16[15,4,1152]{2,1,0:T(4,128)(2,1)S(1)}, u32[]{:S(2)}, u32[]{:S(2)}) %collective-permute-start.2) | collective-permute-done | bytes 138272 | tf_op jit(solution)/shard_map/ppermute | solution.py:19
  31.8 0.1 convert_add_fusion.1
  31.9 0.1 slice_convert_fusion.2
  31.9 0.1 mul.97
  32.0 0.1 copy.55
  32.2 0.1 fusion.20
  32.2 0.1 multiply_reduce_fusion.2
  32.4 0.3 convolution_bitcast_fusion.2
  32.7 0.7 %add_divide_fusion.w_ref = f32[9,24,45]{2,1,0:T(8,128)} fusion(f32[1,24,45]{2,1,0:T(8,128)S(1)} %convolution_bitcast_fusion.1, f32[9,24,45]{2,1,0:T(8,128)S(1)} %bitcast.72, f32[9,1,45]{2,1,0:T(1,128)S(1)} %broadcast_in_dim.34, f32[9,24]{1,0:T(8,128)S(1)} %copy-done.6), kind=kLoop, calls=%fused_computation.22 | loop fusion | flops 29160 | bytes 84564 | tf_op jit(solution)/shard_map/div | solution.py:222
  33.4 3.9 %collective-permute-done.3 = bf16[15,3,1152]{2,1,0:T(4,128)(2,1)S(1)} collective-permute-done((bf16[15,3,1152]{2,1,0:T(4,128)(2,1)S(1)}, bf16[15,3,1152]{2,1,0:T(4,128)(2,1)S(1)}, u32[]{:S(2)}, u32[]{:S(2)}) %collective-permute-start.3) | collective-permute-done | bytes 103712 | tf_op jit(solution)/shard_map/ppermute | solution.py:25
  37.4 1.5 %pad_maximum_fusion.p_ref = bf16[15,30,1152]{2,1,0:T(8,128)(2,1)} fusion(bf16[15,3,1152]{2,1,0:T(4,128)(2,1)S(1)} %collective-permute-done.3, bf16[3,24,1152]{2,1,0:T(8,128)(2,1)S(1)} %collective-permute-done.1, bf16[9,24,1152]{2,1,0:T(8,128)(2,1)S(1)} %copy-done, bf16[3,24,1152]{2,1,0:T(8,128)(2,1)S(1)} %slice.167, bf16[15,3,1152]{2,1,0:T(4,128)(2,1)S(1)} %bitcast.74), kind=kLoop, calls=%fused_computation.5 | loop fusion | flops 5184000 | bytes 2073600 | tf_op jit(solution)/shard_map/concatenate | solution.py:187
  38.8 9.4 %shard_map.55 = bf16[9,24,1152]{2,1,0:T(8,128)(2,1)} custom-call(f32[9,24,45]{2,1,0:T(8,128)} %add_divide_fusion.w_ref, bf16[15,30,1152]{2,1,0:T(8,128)(2,1)} %pad_maximum_fusion.p_ref, bf16[9,24,1152]{2,1,0:T(8,128)(2,1)} %t_ref.1), custom_call_target="tpu_custom_call" | custom-call | tf_op jit(solution)/shard_map/pallas_call | solution.py:159
  (38 shorter events, 0.5 us)
Async XLA Ops:
  0.0 9.3 %copy-start.3 = (s32[2,9,24,4]{2,3,1,0:T(4,128)S(1)}, s32[2,9,24,4]{2,3,1,0:T(4,128)}, u32[]{:S(2)}) copy-start(s32[2,9,24,4]{2,3,1,0:T(4,128)} %param.7) | copy-start | bytes 20740
  0.0 9.2 %copy-start.1 = (f32[2,9,24,4,6]{2,3,4,1,0:T(4,128)S(1)}, f32[2,9,24,4,6]{2,3,4,1,0:T(4,128)}, u32[]{:S(2)}) copy-start(f32[2,9,24,4,6]{2,3,4,1,0:T(4,128)} %param.6) | copy-start | bytes 124420
  2.8 12.2 %collective-permute-start = (bf16[4,24,1152]{2,1,0:T(8,128)(2,1)S(1)}, bf16[4,24,1152]{2,1,0:T(8,128)(2,1)S(1)}, u32[]{:S(2)}, u32[]{:S(2)}) collective-permute-start(bf16[4,24,1152]{2,1,0:T(8,128)(2,1)S(1)} %pad_maximum_fusion.1), channel_id=1, source_target_pairs={{0,32},{32,64},{64,96},{96,128},{128,160},{160,192},{192,224},{224... | collective-permute-start | bytes 663560 | tf_op jit(solution)/shard_map/ppermute | solution.py:19
  7.3 11.0 %collective-permute-start.1 = (bf16[3,24,1152]{2,1,0:T(8,128)(2,1)S(1)}, bf16[3,24,1152]{2,1,0:T(8,128)(2,1)S(1)}, u32[]{:S(2)}, u32[]{:S(2)}) collective-permute-start(bf16[3,24,1152]{2,1,0:T(8,128)(2,1)S(1)} %get-tuple-element.5), channel_id=1, source_target_pairs={{32,0},{64,32},{96,64},{128,96},{160,128},{192,160},{224,192},{256... | collective-permute-start | bytes 497672 | tf_op jit(solution)/shard_map/ppermute | solution.py:25
  10.0 1.4 %copy-start.2 = (f32[4,12,6,45]{3,2,1,0:T(8,128)S(1)}, f32[4,12,6,45]{3,2,1,0:T(8,128)}, u32[]{:S(2)}) copy-start(f32[4,12,6,45]{3,2,1,0:T(8,128)} %constant.47) | copy-start | bytes 155524
  10.6 7.6 %copy-start = (bf16[9,24,1152]{2,1,0:T(8,128)(2,1)S(1)}, bf16[9,24,1152]{2,1,0:T(8,128)(2,1)}, u32[]{:S(2)}) copy-start(bf16[9,24,1152]{2,1,0:T(8,128)(2,1)} %t_ref.1) | copy-start | bytes 1492996
  15.4 15.5 %copy-start.4 = (f32[12,6,45]{2,1,0:T(8,128)S(1)}, f32[12,6,45]{2,1,0:T(8,128)}, u32[]{:S(2)}) copy-start(f32[12,6,45]{2,1,0:T(8,128)} %constant.51) | copy-start | bytes 38884
  15.4 17.0 %copy-start.5 = (f32[12,6,45]{2,0,1:T(8,128)S(1)}, f32[12,6,45]{2,0,1:T(8,128)}, u32[]{:S(2)}) copy-start(f32[12,6,45]{2,0,1:T(8,128)} %constant.49) | copy-start | bytes 38884
  15.4 17.3 %copy-start.6 = (f32[9,24]{1,0:T(8,128)S(1)}, f32[9,24]{1,0:T(8,128)}, u32[]{:S(2)}) copy-start(f32[9,24]{1,0:T(8,128)} %param.8) | copy-start | bytes 2596
  18.4 13.3 %collective-permute-start.2 = (bf16[15,4,1152]{2,1,0:T(4,128)(2,1)S(1)}, bf16[15,4,1152]{2,1,0:T(4,128)(2,1)S(1)}, u32[]{:S(2)}, u32[]{:S(2)}) collective-permute-start(bf16[15,4,1152]{2,1,0:T(4,128)(2,1)S(1)} %fusion.2), channel_id=1, source_target_pairs={{0,1},{1,2},{2,3},{3,4},{4,5},{5,6},{6,7},{7,8},{8,9},{9,10},{10,1... | collective-permute-start | bytes 414728 | tf_op jit(solution)/shard_map/ppermute | solution.py:19
  28.9 8.5 %collective-permute-start.3 = (bf16[15,3,1152]{2,1,0:T(4,128)(2,1)S(1)}, bf16[15,3,1152]{2,1,0:T(4,128)(2,1)S(1)}, u32[]{:S(2)}, u32[]{:S(2)}) collective-permute-start(bf16[15,3,1152]{2,1,0:T(4,128)(2,1)S(1)} %pad_maximum_fusion.2), channel_id=1, source_target_pairs={{1,0},{2,1},{3,2},{4,3},{5,4},{6,5},{7,6},{8,7},{9,8},{10,9},{11,1... | collective-permute-start | bytes 311048 | tf_op jit(solution)/shard_map/ppermute | solution.py:25

commit v13 on v12

--- a/solution.py
+++ b/solution.py
@@ -138,30 +138,38 @@
     return weights.reshape(n_row, n_col, tables.shape[-1])
 
 
-def tap_kernel(offsets, chunk, w_ref, p_ref, t_ref, o_ref, s_ref):
-    s_ref[...] = p_ref[...].astype(jnp.float32)
+def tap_kernel(offsets, chunk, w_ref, south_ref, t_ref, north_ref, west_ref, east_ref, o_ref, s_ref):
     rows, cols, width = t_ref.shape
+    halo = north_ref.shape[0]
+    f32 = jnp.float32
+    s_ref[0:halo, halo : halo + cols] = south_ref[0:halo].astype(f32)
+    s_ref[halo : halo + rows, halo : halo + cols] = t_ref[...].astype(f32)
+    s_ref[halo + rows :, halo : halo + cols] = north_ref[...].astype(f32)
+    s_ref[:, 0:halo] = west_ref[:, 0:halo].astype(f32)
+    s_ref[:, halo + cols :] = east_ref[...].astype(f32)
 
     def row(i, carry):
         for start in range(0, width, chunk):
             lanes = pl.ds(start, chunk)
-            acc = t_ref[i, :, lanes].astype(jnp.float32)
+            acc = s_ref[i + halo, pl.ds(halo, cols), lanes]
             for tap, (dr, dc) in enumerate(offsets):
                 w = w_ref[i, :, tap : tap + 1]
-                acc = acc + w * s_ref[i + 3 + dr, pl.ds(3 + dc, cols), lanes]
+                acc = acc + w * s_ref[i + halo + dr, pl.ds(halo + dc, cols), lanes]
             o_ref[i, :, lanes] = acc.astype(o_ref.dtype)
         return carry
 
     lax.fori_loop(0, rows, row, 0)
 
 
-def apply_taps(weights, padded, tracer, offsets):
+def apply_taps(weights, from_south, tracer, from_north, from_west, from_east, offsets):
+    rows, cols, width = tracer.shape
+    halo = from_north.shape[0]
     return pl.pallas_call(
-        functools.partial(tap_kernel, offsets, tracer.shape[2]),
+        functools.partial(tap_kernel, offsets, width),
         out_shape=jax.ShapeDtypeStruct(tracer.shape, jnp.bfloat16),
-        scratch_shapes=[pltpu.VMEM(padded.shape, jnp.float32)],
+        scratch_shapes=[pltpu.VMEM((rows + 2 * halo, cols + 2 * halo, width), jnp.float32)],
         interpret=INTERPRET,
-    )(weights, padded, tracer)
+    )(weights, from_south, tracer, from_north, from_west, from_east)
 
 
 def local(tracer, moments, pieces, cell_area):
@@ -184,7 +192,6 @@
     )[:, None]
     from_west = from_prev(jnp.concatenate([tall[:, cols - 3 :], west_pack], axis=1), "tile", True)
     from_east = from_next(tall[:, :3], "tile", True)
-    padded = jnp.concatenate([from_west[:, :3], tall, from_east], axis=1)
 
     is_top = lax.axis_index("panel") == lax.axis_size("panel") - 1
     last_row = jnp.arange(rows) == rows - 1
@@ -220,7 +227,7 @@
     weights = weights + jnp.pad(west_fix[:, None], ((0, 0), (0, cols - 1), (0, 0)))
     weights = weights + jnp.pad(south_fix[None], ((0, rows - 1), (0, 0), (0, 0)))
     weights = weights / cell_area[:, :, None]
-    return apply_taps(weights, padded, tracer, offsets)
+    return apply_taps(weights, from_south, tracer, from_north, from_west, from_east, offsets)
 
 
 def solution(mesh):

time: 48.5 us -> 51.5 us (1.062)
  Pallas kernels: 9.4 us -> 12.9 us
  other arithmetic: 5.35 us -> 3.88 us
  local copies, waits for them, and re-layouts: 4.02 us -> 4.68 us
    pallas_call x1, Pallas kernels: 9.4 us -> 12.9 us  [apply_taps(): pl.pallas_call(functools.partial(tap_kernel, offsets, width), out_shape=j...]
    concatenate x1 -> x0, other arithmetic: 1.47 us -> none  [local(): padded = jnp.concatenate([from_west[:, :3], tall, from_east], axis=1)]
    unnamed x15 -> x23, local copies, waits for them, and re-layouts: 0.05 us -> 0.71 us
  transfers between devices with their start and end apart: 4 -> 4, of which waited for: 4 -> 4; matrix products, arithmetic and copies ran while one was open for 12% -> 11% of each run, Pallas kernels for 0% -> 0%
where the time goes in v13:
time: 51.5 us; the launch traced here: 51.1 us
  starting transfers between devices  18.8 us (37%)
  Pallas kernels  12.9 us (25%)
  waiting for transfers between devices  9.64 us (19%)
  local copies, waits for them, and re-layouts  4.68 us (9%)
  other arithmetic  3.88 us (8%)
  matrix products  0.8 us (2%)
    ppermute x2, starting transfers between devices, from_prev(): return lax.ppermute(value, axis, pairs)  15 us
    pallas_call x1, Pallas kernels, apply_taps(): pl.pallas_call(functools.partial(tap_kernel, offsets, width), out_shape=j...  12.9 us
    ppermute x2, waiting for transfers between devices, from_next(): return lax.ppermute(value, axis, pairs)  6.77 us
    ppermute x2, starting transfers between devices, from_next(): return lax.ppermute(value, axis, pairs)  3.84 us
    ppermute x2, waiting for transfers between devices, from_prev(): return lax.ppermute(value, axis, pairs)  2.86 us
  transfers between devices with their start and end apart: 4, of which 4 were waited for; matrix products, arithmetic and copies ran while one was open for 11% of the time, Pallas kernels for 0%

profile of v13, /device:TPU:223, one launch (start us, length us, event | category | flops | bytes accessed | tf_op | source)
XLA Modules:
  0.0 51.1 jit_solution(9916662609976385568)
XLA Ops:
  0.0 0.7 %slice_bitcast_fusion.8 = (s32[1,24,4]{1,2,0:T(4,128)S(1)}, bf16[24,4]{0,1:T(4,128)(2,1)S(1)}) fusion(s32[2,9,24,4]{2,3,1,0:T(4,128)} %param.7), kind=kLoop, calls=%fused_computation.72 | loop fusion | flops 96 | bytes 1344 | tf_op jit(solution)/shard_map/slice | solution.py:215
  0.7 0.1 copy.50
  0.8 0.7 %slice.137 = f32[1,1,24,4,6]{2,3,4,1,0:T(4,128)S(1)} slice(f32[2,9,24,4,6]{2,3,4,1,0:T(4,128)} %param.6), slice={[1:2], [8:9], [0:24], [0:4], [0:6]} | slice | bytes 4608 | tf_op jit(solution)/shard_map/slice | solution.py:186
  1.6 0.1 copy.48
  1.7 1.0 %fusion.24 = (bf16[3,24,1152]{2,1,0:T(8,128)(2,1)S(1)}, bf16[3,24,1152]{2,1,0:T(8,128)(2,1)S(1)}) fusion(bf16[9,24,1152]{2,1,0:T(8,128)(2,1)} %t_ref.1), kind=kLoop, calls=%fused_computation.75 | loop fusion | bytes 663552 | tf_op jit(solution)/shard_map/slice | solution.py:188
  2.7 0.1 fusion.14
  2.8 4.4 %collective-permute-start = (bf16[4,24,1152]{2,1,0:T(8,128)(2,1)S(1)}, bf16[4,24,1152]{2,1,0:T(8,128)(2,1)S(1)}, u32[]{:S(2)}, u32[]{:S(2)}) collective-permute-start(bf16[4,24,1152]{2,1,0:T(8,128)(2,1)S(1)} %pad_maximum_fusion), channel_id=1, source_target_pairs={{0,32},{32,64},{64,96},{96,128},{128,160},{160,192},{192,224},{224... | collective-permute-start | bytes 663560 | tf_op jit(solution)/shard_map/ppermute | solution.py:19
  7.3 1.9 %collective-permute-start.1 = (bf16[3,24,1152]{2,1,0:T(8,128)(2,1)S(1)}, bf16[3,24,1152]{2,1,0:T(8,128)(2,1)S(1)}, u32[]{:S(2)}, u32[]{:S(2)}) collective-permute-start(bf16[3,24,1152]{2,1,0:T(8,128)(2,1)S(1)} %get-tuple-element.5), channel_id=1, source_target_pairs={{32,0},{64,32},{96,64},{128,96},{160,128},{192,160},{224,192},{256... | collective-permute-start | bytes 497672 | tf_op jit(solution)/shard_map/ppermute | solution.py:25
  9.3 0.1 bitcast_multiply_fusion
  9.4 0.1 slice.164
  9.5 0.1 slice_multiply_fusion
  9.6 0.1 pad_bitcast_fusion
  9.7 0.1 maximum_bitcast_fusion
  9.9 0.1 copy.45
  10.0 0.2 mul.91
  10.2 0.1 slice_convert_fusion
  10.3 0.1 add_bitcast_fusion.1
  10.5 0.1 eq.67
  10.6 0.8 %multiply_reduce_fusion = f32[4,12,6,216]{3,2,1,0:T(8,128)S(1)} fusion(f32[4,4,6,216]{3,1,2,0:T(4,128)S(1)} %mul.91, f32[4,4,12,216]{3,1,2,0:T(4,128)S(1)} %fusion.1), kind=kLoop, calls=%fused_computation | loop fusion | flops 435456 | bytes 497664 | tf_op jit(solution)/shard_map/reduce_sum | solution.py:134
  11.4 0.3 fusion
  11.8 0.1 copy.46
  11.9 0.1 copy.52
  12.0 0.1 copy.53
  12.1 0.3 copy.51
  12.4 0.1 reshape_squeeze.7
  12.5 0.1 fusion.18
  12.7 2.3 %collective-permute-done.south_ref = bf16[4,24,1152]{2,1,0:T(8,128)(2,1)S(1)} collective-permute-done((bf16[4,24,1152]{2,1,0:T(8,128)(2,1)S(1)}, bf16[4,24,1152]{2,1,0:T(8,128)(2,1)S(1)}, u32[]{:S(2)}, u32[]{:S(2)}) %collective-permute-start) | collective-permute-done | bytes 221216 | tf_op jit(solution)/shard_map/ppermute | solution.py:19
  15.0 0.1 convert_add_fusion
  15.1 0.1 slice_convert_fusion.1
  15.3 0.1 copy.57
  15.4 2.8 %collective-permute-done.1.north_ref = bf16[3,24,1152]{2,1,0:T(8,128)(2,1)S(1)} collective-permute-done((bf16[3,24,1152]{2,1,0:T(8,128)(2,1)S(1)}, bf16[3,24,1152]{2,1,0:T(8,128)(2,1)S(1)}, u32[]{:S(2)}, u32[]{:S(2)}) %collective-permute-start.1) | collective-permute-done | bytes 165920 | tf_op jit(solution)/shard_map/ppermute | solution.py:25
  18.3 0.2 fusion.2
  18.5 10.5 %collective-permute-start.2 = (bf16[15,4,1152]{2,1,0:T(4,128)(2,1)S(1)}, bf16[15,4,1152]{2,1,0:T(4,128)(2,1)S(1)}, u32[]{:S(2)}, u32[]{:S(2)}) collective-permute-start(bf16[15,4,1152]{2,1,0:T(4,128)(2,1)S(1)} %fusion.2), channel_id=1, source_target_pairs={{0,1},{1,2},{2,3},{3,4},{4,5},{5,6},{6,7},{7,8},{8,9},{9,10},{10,1... | collective-permute-start | bytes 414728 | tf_op jit(solution)/shard_map/ppermute | solution.py:19
  29.1 1.9 %collective-permute-start.3 = (bf16[15,3,1152]{2,1,0:T(4,128)(2,1)S(1)}, bf16[15,3,1152]{2,1,0:T(4,128)(2,1)S(1)}, u32[]{:S(2)}, u32[]{:S(2)}) collective-permute-start(bf16[15,3,1152]{2,1,0:T(4,128)(2,1)S(1)} %pad_maximum_fusion.1), channel_id=1, source_target_pairs={{1,0},{2,1},{3,2},{4,3},{5,4},{6,5},{7,6},{8,7},{9,8},{10,9},{11,1... | collective-permute-start | bytes 311048 | tf_op jit(solution)/shard_map/ppermute | solution.py:25
  31.0 0.1 multiply_reduce_fusion.1
  31.1 0.2 convolution_bitcast_fusion.1
  31.3 0.5 %collective-permute-done.2.west_ref = bf16[15,4,1152]{2,1,0:T(4,128)(2,1)S(1)} collective-permute-done((bf16[15,4,1152]{2,1,0:T(4,128)(2,1)S(1)}, bf16[15,4,1152]{2,1,0:T(4,128)(2,1)S(1)}, u32[]{:S(2)}, u32[]{:S(2)}) %collective-permute-start.2) | collective-permute-done | bytes 138272 | tf_op jit(solution)/shard_map/ppermute | solution.py:19
  31.9 0.1 convert_add_fusion.1
  32.0 0.1 slice_convert_fusion.2
  32.1 0.1 mul.97
  32.2 0.1 copy.55
  32.3 0.1 fusion.20
  32.4 0.1 multiply_reduce_fusion.2
  32.6 0.3 convolution_bitcast_fusion.2
  32.8 0.8 %add_divide_fusion.w_ref = f32[9,24,45]{2,1,0:T(8,128)} fusion(f32[1,24,45]{2,1,0:T(8,128)S(1)} %convolution_bitcast_fusion.1, f32[9,24,45]{2,1,0:T(8,128)S(1)} %bitcast.71, f32[9,1,45]{2,1,0:T(1,128)S(1)} %broadcast_in_dim.34, f32[9,24]{1,0:T(8,128)S(1)} %copy-done.10), kind=kLoop, calls=%fused_computation.21 | loop fusion | flops 29160 | bytes 84564 | tf_op jit(solution)/shard_map/div | solution.py:229
  33.6 3.9 %collective-permute-done.3.east_ref = bf16[15,3,1152]{2,1,0:T(4,128)(2,1)S(1)} collective-permute-done((bf16[15,3,1152]{2,1,0:T(4,128)(2,1)S(1)}, bf16[15,3,1152]{2,1,0:T(4,128)(2,1)S(1)}, u32[]{:S(2)}, u32[]{:S(2)}) %collective-permute-start.3) | collective-permute-done | bytes 103712 | tf_op jit(solution)/shard_map/ppermute | solution.py:25
  37.5 0.6 %copy-done.6 = bf16[15,3,1152]{2,1,0:T(4,128)(2,1)} copy-done((bf16[15,3,1152]{2,1,0:T(4,128)(2,1)}, bf16[15,3,1152]{2,1,0:T(4,128)(2,1)S(1)}, u32[]{:S(2)}) %copy-start.6) | copy-done | bytes 103704
  38.2 12.9 %shard_map.55 = bf16[9,24,1152]{2,1,0:T(8,128)(2,1)} custom-call(f32[9,24,45]{2,1,0:T(8,128)} %add_divide_fusion.w_ref, bf16[4,24,1152]{2,1,0:T(8,128)(2,1)} %copy-done.2, bf16[9,24,1152]{2,1,0:T(8,128)(2,1)} %t_ref.1, bf16[3,24,1152]{2,1,0:T(8,128)(2,1)} %copy-done.1, bf16[15,4,1152]{2,1,0:T(4,128)(2,1)} %copy-done.4, bf16[15,3,1152]{2,1,0:T(4,128)(2,1)} %copy-done.6), custom_call_target="tpu_custom_call" | custom-call | tf_op jit(solution)/shard_map/pallas_call | solution.py:167
  (45 shorter events, 0.5 us)
Async XLA Ops:
  0.0 9.2 %copy-start.3 = (f32[2,9,24,4,6]{2,3,4,1,0:T(4,128)S(1)}, f32[2,9,24,4,6]{2,3,4,1,0:T(4,128)}, u32[]{:S(2)}) copy-start(f32[2,9,24,4,6]{2,3,4,1,0:T(4,128)} %param.6) | copy-start | bytes 124420
  1.7 7.6 %copy-start.7 = (s32[2,9,24,4]{2,3,1,0:T(4,128)S(1)}, s32[2,9,24,4]{2,3,1,0:T(4,128)}, u32[]{:S(2)}) copy-start(s32[2,9,24,4]{2,3,1,0:T(4,128)} %param.7) | copy-start | bytes 20740
  2.8 12.2 %collective-permute-start = (bf16[4,24,1152]{2,1,0:T(8,128)(2,1)S(1)}, bf16[4,24,1152]{2,1,0:T(8,128)(2,1)S(1)}, u32[]{:S(2)}, u32[]{:S(2)}) collective-permute-start(bf16[4,24,1152]{2,1,0:T(8,128)(2,1)S(1)} %pad_maximum_fusion), channel_id=1, source_target_pairs={{0,32},{32,64},{64,96},{96,128},{128,160},{160,192},{192,224},{224... | collective-permute-start | bytes 663560 | tf_op jit(solution)/shard_map/ppermute | solution.py:19
  7.3 11.0 %collective-permute-start.1 = (bf16[3,24,1152]{2,1,0:T(8,128)(2,1)S(1)}, bf16[3,24,1152]{2,1,0:T(8,128)(2,1)S(1)}, u32[]{:S(2)}, u32[]{:S(2)}) collective-permute-start(bf16[3,24,1152]{2,1,0:T(8,128)(2,1)S(1)} %get-tuple-element.5), channel_id=1, source_target_pairs={{32,0},{64,32},{96,64},{128,96},{160,128},{192,160},{224,192},{256... | collective-permute-start | bytes 497672 | tf_op jit(solution)/shard_map/ppermute | solution.py:25
  10.2 1.2 %copy-start.5 = (f32[4,12,6,45]{3,2,1,0:T(8,128)S(1)}, f32[4,12,6,45]{3,2,1,0:T(8,128)}, u32[]{:S(2)}) copy-start(f32[4,12,6,45]{3,2,1,0:T(8,128)} %constant.47) | copy-start | bytes 155524
  11.4 6.8 %copy-start = (bf16[9,24,1152]{2,1,0:T(8,128)(2,1)S(1)}, bf16[9,24,1152]{2,1,0:T(8,128)(2,1)}, u32[]{:S(2)}) copy-start(bf16[9,24,1152]{2,1,0:T(8,128)(2,1)} %t_ref.1) | copy-start | bytes 1492996
  15.0 3.4 %copy-start.2 = (bf16[4,24,1152]{2,1,0:T(8,128)(2,1)}, bf16[4,24,1152]{2,1,0:T(8,128)(2,1)S(1)}, u32[]{:S(2)}) copy-start(bf16[4,24,1152]{2,1,0:T(8,128)(2,1)S(1)} %collective-permute-done.south_ref) | copy-start | bytes 663556
  15.4 15.7 %copy-start.8 = (f32[12,6,45]{2,1,0:T(8,128)S(1)}, f32[12,6,45]{2,1,0:T(8,128)}, u32[]{:S(2)}) copy-start(f32[12,6,45]{2,1,0:T(8,128)} %constant.51) | copy-start | bytes 38884
  18.3 10.8 %copy-start.1 = (bf16[3,24,1152]{2,1,0:T(8,128)(2,1)}, bf16[3,24,1152]{2,1,0:T(8,128)(2,1)S(1)}, u32[]{:S(2)}) copy-start(bf16[3,24,1152]{2,1,0:T(8,128)(2,1)S(1)} %collective-permute-done.1.north_ref) | copy-start | bytes 497668
  18.4 14.1 %copy-start.9 = (f32[12,6,45]{2,0,1:T(8,128)S(1)}, f32[12,6,45]{2,0,1:T(8,128)}, u32[]{:S(2)}) copy-start(f32[12,6,45]{2,0,1:T(8,128)} %constant.49) | copy-start | bytes 38884
  18.5 14.4 %copy-start.10 = (f32[9,24]{1,0:T(8,128)S(1)}, f32[9,24]{1,0:T(8,128)}, u32[]{:S(2)}) copy-start(f32[9,24]{1,0:T(8,128)} %param.8) | copy-start | bytes 2596
  18.5 13.4 %collective-permute-start.2 = (bf16[15,4,1152]{2,1,0:T(4,128)(2,1)S(1)}, bf16[15,4,1152]{2,1,0:T(4,128)(2,1)S(1)}, u32[]{:S(2)}, u32[]{:S(2)}) collective-permute-start(bf16[15,4,1152]{2,1,0:T(4,128)(2,1)S(1)} %fusion.2), channel_id=1, source_target_pairs={{0,1},{1,2},{2,3},{3,4},{4,5},{5,6},{6,7},{7,8},{8,9},{9,10},{10,1... | collective-permute-start | bytes 414728 | tf_op jit(solution)/shard_map/ppermute | solution.py:19
  29.1 8.5 %collective-permute-start.3 = (bf16[15,3,1152]{2,1,0:T(4,128)(2,1)S(1)}, bf16[15,3,1152]{2,1,0:T(4,128)(2,1)S(1)}, u32[]{:S(2)}, u32[]{:S(2)}) collective-permute-start(bf16[15,3,1152]{2,1,0:T(4,128)(2,1)S(1)} %pad_maximum_fusion.1), channel_id=1, source_target_pairs={{1,0},{2,1},{3,2},{4,3},{5,4},{6,5},{7,6},{8,7},{9,8},{10,9},{11,1... | collective-permute-start | bytes 311048 | tf_op jit(solution)/shard_map/ppermute | solution.py:25
  31.9 5.7 %copy-start.4 = (bf16[15,4,1152]{2,1,0:T(4,128)(2,1)}, bf16[15,4,1152]{2,1,0:T(4,128)(2,1)S(1)}, u32[]{:S(2)}) copy-start(bf16[15,4,1152]{2,1,0:T(4,128)(2,1)S(1)} %collective-permute-done.2.west_ref) | copy-start | bytes 414724
  37.5 0.7 %copy-start.6 = (bf16[15,3,1152]{2,1,0:T(4,128)(2,1)}, bf16[15,3,1152]{2,1,0:T(4,128)(2,1)S(1)}, u32[]{:S(2)}) copy-start(bf16[15,3,1152]{2,1,0:T(4,128)(2,1)S(1)} %collective-permute-done.3.east_ref) | copy-start | bytes 311044

commit v14 on v12

--- a/solution.py
+++ b/solution.py
@@ -175,16 +175,16 @@
     west_taps = [t for t in range(len(offsets)) if np.abs(np_tables[0, ..., t]).sum() > 0]
     south_taps = [t for t in range(len(offsets)) if np.abs(np_tables[2, ..., t]).sum() > 0]
 
-    south_pack = pack_weights(moments[1][rows - 1], pieces[1][rows - 1], width)[None]
-    from_south = from_prev(jnp.concatenate([tracer[rows - 3 :], south_pack], axis=0), "panel", False)
-    from_north = from_next(tracer[:3], "panel", False)
-    tall = jnp.concatenate([from_south[:3], tracer, from_north], axis=0)
-    west_pack = jnp.pad(
-        pack_weights(moments[0][:, cols - 1], pieces[0][:, cols - 1], width), ((3, 3), (0, 0))
-    )[:, None]
-    from_west = from_prev(jnp.concatenate([tall[:, cols - 3 :], west_pack], axis=1), "tile", True)
-    from_east = from_next(tall[:, :3], "tile", True)
-    padded = jnp.concatenate([from_west[:, :3], tall, from_east], axis=1)
+    west_pack = pack_weights(moments[0][:, cols - 1], pieces[0][:, cols - 1], width)[:, None]
+    from_west = from_prev(jnp.concatenate([tracer[:, cols - 3 :], west_pack], axis=1), "tile", True)
+    from_east = from_next(tracer[:, :3], "tile", True)
+    wide = jnp.concatenate([from_west[:, :3], tracer, from_east], axis=1)
+    south_pack = jnp.pad(
+        pack_weights(moments[1][rows - 1], pieces[1][rows - 1], width), ((3, 3), (0, 0))
+    )[None]
+    from_south = from_prev(jnp.concatenate([wide[rows - 3 :], south_pack], axis=0), "panel", False)
+    from_north = from_next(wide[:3], "panel", False)
+    padded = jnp.concatenate([from_south[:3], wide, from_north], axis=0)
 
     is_top = lax.axis_index("panel") == lax.axis_size("panel") - 1
     last_row = jnp.arange(rows) == rows - 1
@@ -213,8 +213,8 @@
     weights = face_weights_cells(face_m, face_p, tables)
     weights = lax.optimization_barrier(weights)
 
-    west_m, west_p = unpack_weights(from_west[3 : 3 + rows, 3], n_piece, n_moment)
-    south_m, south_p = unpack_weights(from_south[3], n_piece, n_moment)
+    west_m, west_p = unpack_weights(from_west[:, 3], n_piece, n_moment)
+    south_m, south_p = unpack_weights(from_south[3, 3 : 3 + cols], n_piece, n_moment)
     west_fix = face_weights(west_m[:, None], west_p[:, None], tables[:1])
     south_fix = face_weights(south_m[:, None], south_p[:, None], tables[2:3])
     weights = weights + jnp.pad(west_fix[:, None], ((0, 0), (0, cols - 1), (0, 0)))

time: 48.5 us -> 52.2 us (1.076)
  the two profiles are of different devices: /device:TPU:223 before, /device:TPU:22 now
where the time goes in v14:
time: 52.2 us; the launch traced here: 51.8 us
  starting transfers between devices  20 us (38%)
  waiting for transfers between devices  11.8 us (23%)
  Pallas kernels  9.4 us (18%)
  local copies, waits for them, and re-layouts  5.09 us (10%)
  other arithmetic  4.42 us (8%)
  matrix products  0.8 us (2%)
    ppermute x2, starting transfers between devices, from_next(): return lax.ppermute(value, axis, pairs)  13.3 us
    pallas_call x1, Pallas kernels, apply_taps(): pl.pallas_call(functools.partial(tap_kernel, offsets, tracer.shape[2]), o...  9.4 us
    ppermute x2, waiting for transfers between devices, from_next(): return lax.ppermute(value, axis, pairs)  7.16 us
    ppermute x2, starting transfers between devices, from_prev(): return lax.ppermute(value, axis, pairs)  6.64 us
    ppermute x2, waiting for transfers between devices, from_prev(): return lax.ppermute(value, axis, pairs)  4.65 us
    concatenate x1, other arithmetic, local(): padded = jnp.concatenate([from_south[:3], wide, from_north], axis=0)  1.26 us
    another operation x2, local copies, waits for them, and re-layouts, local(): jnp.stack([jnp.concatenate([zero_col, moments[0][:, :cols - 1]], axis=1),...  1.13 us
    slice x1, local copies, waits for them, and re-layouts, local(): tracer[:, cols - 3:]  1.1 us
  transfers between devices with their start and end apart: 4, of which 3 were waited for; matrix products, arithmetic and copies ran while one was open for 15% of the time, Pallas kernels for 0%

profile of v14, /device:TPU:22, one launch (start us, length us, event | category | flops | bytes accessed | tf_op | source)
XLA Modules:
  0.0 51.8 jit_solution(9370543516339965184)
XLA Ops:
  0.0 1.1 %fusion.24 = (bf16[9,3,1152]{2,1,0:T(4,128)(2,1)S(1)}, bf16[9,3,1152]{2,1,0:T(4,128)(2,1)S(1)}) fusion(bf16[9,24,1152]{2,1,0:T(8,128)(2,1)} %t_ref.1), kind=kLoop, calls=%fused_computation.76 | loop fusion | bytes 248832 | tf_op jit(solution)/shard_map/slice | solution.py:179
  1.1 11.4 %collective-permute-start.1 = (bf16[9,3,1152]{2,1,0:T(4,128)(2,1)S(1)}, bf16[9,3,1152]{2,1,0:T(4,128)(2,1)S(1)}, u32[]{:S(2)}, u32[]{:S(2)}) collective-permute-start(bf16[9,3,1152]{2,1,0:T(4,128)(2,1)S(1)} %get-tuple-element.6), channel_id=1, source_target_pairs={{1,0},{2,1},{3,2},{4,3},{5,4},{6,5},{7,6},{8,7},{9,8},{10,9},{11,1... | collective-permute-start | bytes 186632 | tf_op jit(solution)/shard_map/ppermute | solution.py:25
  12.5 0.7 %slice_bitcast_fusion.6 = (s32[9,24,1,4]{1,3,0,2:T(4,128)S(1)}, s32[9,24,4]{1,2,0:T(4,128)S(1)}, s32[9,24,1,4]{1,3,0,2:T(4,128)S(1)}) fusion(s32[2,9,24,4]{2,3,1,0:T(4,128)} %param.7), kind=kLoop, calls=%fused_computation.60 | loop fusion | bytes 17280 | tf_op jit(solution)/shard_map/stack;squeeze | solution.py:204
  13.3 0.1 fusion.25
  13.3 0.1 copy.48
  13.5 0.1 copy.49
  13.6 1.0 %slice_bitcast_fusion.1 = (f32[9,24,1,4,6]{1,3,4,0,2:T(4,128)S(1)}, f32[9,24,4,6]{1,2,3,0:T(4,128)S(1)}, f32[9,24,4,6]{1,2,3,0:T(4,128)S(1)}) fusion(f32[2,9,24,4,6]{2,3,4,1,0:T(4,128)} %param.6), kind=kLoop, calls=%fused_computation.27 | loop fusion | bytes 103680 | tf_op jit(solution)/shard_map/stack;squeeze | solution.py:195
  14.6 0.1 slice.166
  14.7 0.3 copy.47
  15.0 0.1 reshape_squeeze.6
  15.1 0.1 fusion.18
  15.3 0.1 pad_maximum_fusion.5
  15.4 1.9 %collective-permute-start = (bf16[9,4,1152]{2,1,0:T(4,128)(2,1)S(1)}, bf16[9,4,1152]{2,1,0:T(4,128)(2,1)S(1)}, u32[]{:S(2)}, u32[]{:S(2)}) collective-permute-start(bf16[9,4,1152]{2,1,0:T(4,128)(2,1)S(1)} %pad_maximum_fusion.5), channel_id=1, source_target_pairs={{0,1},{1,2},{2,3},{3,4},{4,5},{5,6},{6,7},{7,8},{8,9},{9,10},{10,1... | collective-permute-start | bytes 248840 | tf_op jit(solution)/shard_map/ppermute | solution.py:19
  17.3 0.1 copy.56
  17.6 0.1 bitcast_multiply_fusion
  17.6 0.1 slice_multiply_fusion
  17.7 0.1 pad_bitcast_fusion
  17.9 0.1 maximum_bitcast_fusion
  18.0 0.1 copy.45
  18.1 0.2 mul.91
  18.4 0.1 add_bitcast_fusion.1
  18.5 0.1 eq.67
  18.7 0.8 %multiply_reduce_fusion = f32[4,12,6,216]{3,2,1,0:T(8,128)S(1)} fusion(f32[4,4,6,216]{3,1,2,0:T(4,128)S(1)} %mul.91, f32[4,4,12,216]{3,1,2,0:T(4,128)S(1)} %fusion.2), kind=kLoop, calls=%fused_computation | loop fusion | flops 435456 | bytes 497664 | tf_op jit(solution)/shard_map/reduce_sum | solution.py:134
  19.5 0.3 fusion
  19.8 0.1 fusion.13
  19.9 0.1 copy.46
  20.0 3.2 %collective-permute-done = bf16[9,4,1152]{2,1,0:T(4,128)(2,1)S(1)} collective-permute-done((bf16[9,4,1152]{2,1,0:T(4,128)(2,1)S(1)}, bf16[9,4,1152]{2,1,0:T(4,128)(2,1)S(1)}, u32[]{:S(2)}, u32[]{:S(2)}) %collective-permute-start) | collective-permute-done | bytes 82976 | tf_op jit(solution)/shard_map/ppermute | solution.py:19
  23.3 0.1 convert_add_fusion.1
  23.4 0.1 slice_convert_fusion.2
  23.5 0.1 fusion.1
  23.6 4.7 %collective-permute-start.2 = (bf16[4,30,1152]{2,1,0:T(8,128)(2,1)S(1)}, bf16[4,30,1152]{2,1,0:T(8,128)(2,1)S(1)}, u32[]{:S(2)}, u32[]{:S(2)}) collective-permute-start(bf16[4,30,1152]{2,1,0:T(8,128)(2,1)S(1)} %fusion.1), channel_id=1, source_target_pairs={{0,32},{32,64},{64,96},{96,128},{128,160},{160,192},{192,224},{224... | collective-permute-start | bytes 829448 | tf_op jit(solution)/shard_map/ppermute | solution.py:19
  28.3 0.1 mul.97
  28.4 0.1 copy.51
  28.5 0.1 fusion.20
  28.6 0.1 multiply_reduce_fusion.2
  28.8 0.3 convolution_bitcast_fusion.2
  29.0 0.1 pad_maximum_fusion.3
  29.1 1.9 %collective-permute-start.3 = (bf16[3,30,1152]{2,1,0:T(8,128)(2,1)S(1)}, bf16[3,30,1152]{2,1,0:T(8,128)(2,1)S(1)}, u32[]{:S(2)}, u32[]{:S(2)}) collective-permute-start(bf16[3,30,1152]{2,1,0:T(8,128)(2,1)S(1)} %pad_maximum_fusion.3), channel_id=1, source_target_pairs={{32,0},{64,32},{96,64},{128,96},{160,128},{192,160},{224,192},{256... | collective-permute-start | bytes 622088 | tf_op jit(solution)/shard_map/ppermute | solution.py:25
  31.1 1.5 %collective-permute-done.2 = bf16[4,30,1152]{2,1,0:T(8,128)(2,1)S(1)} collective-permute-done((bf16[4,30,1152]{2,1,0:T(8,128)(2,1)S(1)}, bf16[4,30,1152]{2,1,0:T(8,128)(2,1)S(1)}, u32[]{:S(2)}, u32[]{:S(2)}) %collective-permute-start.2) | collective-permute-done | bytes 276512 | tf_op jit(solution)/shard_map/ppermute | solution.py:19
  32.5 0.1 convert_add_fusion
  32.6 0.1 slice_convert_fusion.1
  32.8 0.1 copy.57
  32.9 0.1 multiply_reduce_fusion.1
  33.0 0.2 convolution_bitcast_fusion.1
  33.3 0.8 %add_divide_fusion.w_ref = f32[9,24,45]{2,1,0:T(8,128)} fusion(f32[1,24,45]{2,1,0:T(8,128)S(1)} %convolution_bitcast_fusion.1, f32[9,24,45]{2,1,0:T(8,128)S(1)} %bitcast.75, f32[9,1,45]{2,1,0:T(1,128)S(1)} %broadcast_in_dim.33, f32[9,24]{1,0:T(8,128)S(1)} %copy-done.6), kind=kLoop, calls=%fused_computation.21 | loop fusion | flops 29160 | bytes 84564 | tf_op jit(solution)/shard_map/div | solution.py:222
  34.0 7.2 %collective-permute-done.3 = bf16[3,30,1152]{2,1,0:T(8,128)(2,1)S(1)} collective-permute-done((bf16[3,30,1152]{2,1,0:T(8,128)(2,1)S(1)}, bf16[3,30,1152]{2,1,0:T(8,128)(2,1)S(1)}, u32[]{:S(2)}, u32[]{:S(2)}) %collective-permute-start.3) | collective-permute-done | bytes 207392 | tf_op jit(solution)/shard_map/ppermute | solution.py:25
  41.2 1.3 %pad_maximum_fusion.p_ref = bf16[15,30,1152]{2,1,0:T(8,128)(2,1)} fusion(bf16[3,30,1152]{2,1,0:T(8,128)(2,1)S(1)} %collective-permute-done.3, bf16[9,3,1152]{2,1,0:T(4,128)(2,1)S(1)} %collective-permute-done.1, bf16[9,24,1152]{2,1,0:T(8,128)(2,1)S(1)} %copy-done, bf16[9,3,1152]{2,1,0:T(4,128)(2,1)S(1)} %bitcast.73, bf16[3,30,1152]{2,1,0:T(8,128)(2,1)S(1)} %slice.180), kind=kLoop, calls=%fused_computation.5 | loop fusion | flops 5184000 | bytes 2073600 | tf_op jit(solution)/shard_map/concatenate | solution.py:187
  42.5 9.4 %shard_map.55 = bf16[9,24,1152]{2,1,0:T(8,128)(2,1)} custom-call(f32[9,24,45]{2,1,0:T(8,128)} %add_divide_fusion.w_ref, bf16[15,30,1152]{2,1,0:T(8,128)(2,1)} %pad_maximum_fusion.p_ref, bf16[9,24,1152]{2,1,0:T(8,128)(2,1)} %t_ref.1), custom_call_target="tpu_custom_call" | custom-call | tf_op jit(solution)/shard_map/pallas_call | solution.py:159
  (38 shorter events, 0.5 us)
Async XLA Ops:
  0.0 17.3 %copy-start.3 = (s32[2,9,24,4]{2,3,1,0:T(4,128)S(1)}, s32[2,9,24,4]{2,3,1,0:T(4,128)}, u32[]{:S(2)}) copy-start(s32[2,9,24,4]{2,3,1,0:T(4,128)} %param.7) | copy-start | bytes 20740
  0.0 17.3 %copy-start.1 = (f32[2,9,24,4,6]{2,3,4,1,0:T(4,128)S(1)}, f32[2,9,24,4,6]{2,3,4,1,0:T(4,128)}, u32[]{:S(2)}) copy-start(f32[2,9,24,4,6]{2,3,4,1,0:T(4,128)} %param.6) | copy-start | bytes 124420
  1.1 22.3 %collective-permute-start.1 = (bf16[9,3,1152]{2,1,0:T(4,128)(2,1)S(1)}, bf16[9,3,1152]{2,1,0:T(4,128)(2,1)S(1)}, u32[]{:S(2)}, u32[]{:S(2)}) collective-permute-start(bf16[9,3,1152]{2,1,0:T(4,128)(2,1)S(1)} %get-tuple-element.6), channel_id=1, source_target_pairs={{1,0},{2,1},{3,2},{4,3},{5,4},{6,5},{7,6},{8,7},{9,8},{10,9},{11,1... | collective-permute-start | bytes 186632 | tf_op jit(solution)/shard_map/ppermute | solution.py:25
  15.4 7.9 %collective-permute-start = (bf16[9,4,1152]{2,1,0:T(4,128)(2,1)S(1)}, bf16[9,4,1152]{2,1,0:T(4,128)(2,1)S(1)}, u32[]{:S(2)}, u32[]{:S(2)}) collective-permute-start(bf16[9,4,1152]{2,1,0:T(4,128)(2,1)S(1)} %pad_maximum_fusion.5), channel_id=1, source_target_pairs={{0,1},{1,2},{2,3},{3,4},{4,5},{5,6},{6,7},{7,8},{8,9},{9,10},{10,1... | collective-permute-start | bytes 248840 | tf_op jit(solution)/shard_map/ppermute | solution.py:19
  18.1 1.4 %copy-start.2 = (f32[4,12,6,45]{3,2,1,0:T(8,128)S(1)}, f32[4,12,6,45]{3,2,1,0:T(8,128)}, u32[]{:S(2)}) copy-start(f32[4,12,6,45]{3,2,1,0:T(8,128)} %constant.47) | copy-start | bytes 155524
  18.5 5.0 %copy-start = (bf16[9,24,1152]{2,1,0:T(8,128)(2,1)S(1)}, bf16[9,24,1152]{2,1,0:T(8,128)(2,1)}, u32[]{:S(2)}) copy-start(bf16[9,24,1152]{2,1,0:T(8,128)(2,1)} %t_ref.1) | copy-start | bytes 1492996
  19.5 9.3 %copy-start.5 = (f32[12,6,45]{2,0,1:T(8,128)S(1)}, f32[12,6,45]{2,0,1:T(8,128)}, u32[]{:S(2)}) copy-start(f32[12,6,45]{2,0,1:T(8,128)} %constant.49) | copy-start | bytes 38884
  23.5 9.5 %copy-start.4 = (f32[12,6,45]{2,1,0:T(8,128)S(1)}, f32[12,6,45]{2,1,0:T(8,128)}, u32[]{:S(2)}) copy-start(f32[12,6,45]{2,1,0:T(8,128)} %constant.51) | copy-start | bytes 38884
  23.6 9.7 %copy-start.6 = (f32[9,24]{1,0:T(8,128)S(1)}, f32[9,24]{1,0:T(8,128)}, u32[]{:S(2)}) copy-start(f32[9,24]{1,0:T(8,128)} %param.8) | copy-start | bytes 2596
  23.6 9.0 %collective-permute-start.2 = (bf16[4,30,1152]{2,1,0:T(8,128)(2,1)S(1)}, bf16[4,30,1152]{2,1,0:T(8,128)(2,1)S(1)}, u32[]{:S(2)}, u32[]{:S(2)}) collective-permute-start(bf16[4,30,1152]{2,1,0:T(8,128)(2,1)S(1)} %fusion.1), channel_id=1, source_target_pairs={{0,32},{32,64},{64,96},{96,128},{128,160},{160,192},{192,224},{224... | collective-permute-start | bytes 829448 | tf_op jit(solution)/shard_map/ppermute | solution.py:19
  29.1 12.0 %collective-permute-start.3 = (bf16[3,30,1152]{2,1,0:T(8,128)(2,1)S(1)}, bf16[3,30,1152]{2,1,0:T(8,128)(2,1)S(1)}, u32[]{:S(2)}, u32[]{:S(2)}) collective-permute-start(bf16[3,30,1152]{2,1,0:T(8,128)(2,1)S(1)} %pad_maximum_fusion.3), channel_id=1, source_target_pairs={{32,0},{64,32},{96,64},{128,96},{160,128},{192,160},{224,192},{256... | collective-permute-start | bytes 622088 | tf_op jit(solution)/shard_map/ppermute | solution.py:25

commit v15 on v13

--- a/solution.py
+++ b/solution.py
@@ -138,24 +138,22 @@
     return weights.reshape(n_row, n_col, tables.shape[-1])
 
 
-def tap_kernel(offsets, chunk, w_ref, south_ref, t_ref, north_ref, west_ref, east_ref, o_ref, s_ref):
+def tap_kernel(offsets, base, w_ref, south_ref, t_ref, north_ref, west_ref, east_ref, o_ref, s_ref):
     rows, cols, width = t_ref.shape
     halo = north_ref.shape[0]
     f32 = jnp.float32
-    s_ref[0:halo, halo : halo + cols] = south_ref[0:halo].astype(f32)
-    s_ref[halo : halo + rows, halo : halo + cols] = t_ref[...].astype(f32)
-    s_ref[halo + rows :, halo : halo + cols] = north_ref[...].astype(f32)
-    s_ref[:, 0:halo] = west_ref[:, 0:halo].astype(f32)
-    s_ref[:, halo + cols :] = east_ref[...].astype(f32)
+    s_ref[0:halo, base : base + cols] = south_ref[0:halo].astype(f32)
+    s_ref[halo : halo + rows, base : base + cols] = t_ref[...].astype(f32)
+    s_ref[halo + rows :, base : base + cols] = north_ref[...].astype(f32)
+    s_ref[:, base - halo : base] = west_ref[:, 0:halo].astype(f32)
+    s_ref[:, base + cols : base + cols + halo] = east_ref[...].astype(f32)
 
     def row(i, carry):
-        for start in range(0, width, chunk):
-            lanes = pl.ds(start, chunk)
-            acc = s_ref[i + halo, pl.ds(halo, cols), lanes]
-            for tap, (dr, dc) in enumerate(offsets):
-                w = w_ref[i, :, tap : tap + 1]
-                acc = acc + w * s_ref[i + halo + dr, pl.ds(halo + dc, cols), lanes]
-            o_ref[i, :, lanes] = acc.astype(o_ref.dtype)
+        acc = s_ref[i + halo, pl.ds(base, cols), :]
+        for tap, (dr, dc) in enumerate(offsets):
+            w = w_ref[i, :, tap : tap + 1]
+            acc = acc + w * s_ref[i + halo + dr, pl.ds(base + dc, cols), :]
+        o_ref[i] = acc.astype(o_ref.dtype)
         return carry
 
     lax.fori_loop(0, rows, row, 0)
@@ -164,10 +162,11 @@
 def apply_taps(weights, from_south, tracer, from_north, from_west, from_east, offsets):
     rows, cols, width = tracer.shape
     halo = from_north.shape[0]
+    base = 8
     return pl.pallas_call(
-        functools.partial(tap_kernel, offsets, width),
+        functools.partial(tap_kernel, offsets, base),
         out_shape=jax.ShapeDtypeStruct(tracer.shape, jnp.bfloat16),
-        scratch_shapes=[pltpu.VMEM((rows + 2 * halo, cols + 2 * halo, width), jnp.float32)],
+        scratch_shapes=[pltpu.VMEM((rows + 2 * halo, base + cols + 8, width), jnp.float32)],
         interpret=INTERPRET,
     )(weights, from_south, tracer, from_north, from_west, from_east)
 

time: 51.5 us -> 47.9 us (0.930)
  Pallas kernels: 12.9 us -> 9.33 us
    pallas_call x1, Pallas kernels: 12.9 us -> 9.33 us  [apply_taps(): pl.pallas_call(functools.partial(tap_kernel, offsets, base), out_shape=ja...]
  transfers between devices with their start and end apart: 4 -> 4, of which waited for: 4 -> 4; matrix products, arithmetic and copies ran while one was open for 11% -> 12% of each run, Pallas kernels for 0% -> 0%
where the time goes in v15:
time: 47.9 us; the launch traced here: 47.5 us
  starting transfers between devices  18.8 us (39%)
  waiting for transfers between devices  9.64 us (20%)
  Pallas kernels  9.33 us (19%)
  local copies, waits for them, and re-layouts  4.68 us (10%)
  other arithmetic  3.88 us (8%)
  matrix products  0.8 us (2%)
    ppermute x2, starting transfers between devices, from_prev(): return lax.ppermute(value, axis, pairs)  15 us
    pallas_call x1, Pallas kernels, apply_taps(): pl.pallas_call(functools.partial(tap_kernel, offsets, base), out_shape=ja...  9.33 us
    ppermute x2, waiting for transfers between devices, from_next(): return lax.ppermute(value, axis, pairs)  6.77 us
    ppermute x2, starting transfers between devices, from_next(): return lax.ppermute(value, axis, pairs)  3.84 us
    ppermute x2, waiting for transfers between devices, from_prev(): return lax.ppermute(value, axis, pairs)  2.86 us
    slice x1, local copies, waits for them, and re-layouts, local(): from_north = from_next(tracer[:3], 'panel', False)  1.03 us
  transfers between devices with their start and end apart: 4, of which 4 were waited for; matrix products, arithmetic and copies ran while one was open for 12% of the time, Pallas kernels for 0%

profile of v15, /device:TPU:223, one launch (start us, length us, event | category | flops | bytes accessed | tf_op | source)
XLA Modules:
  0.0 47.5 jit_solution(8253385941153390963)
XLA Ops:
  0.0 0.7 %slice_bitcast_fusion.8 = (s32[1,24,4]{1,2,0:T(4,128)S(1)}, bf16[24,4]{0,1:T(4,128)(2,1)S(1)}) fusion(s32[2,9,24,4]{2,3,1,0:T(4,128)} %param.7), kind=kLoop, calls=%fused_computation.72 | loop fusion | flops 96 | bytes 1344 | tf_op jit(solution)/shard_map/slice | solution.py:214
  0.7 0.1 copy.50
  0.8 0.7 %slice.137 = f32[1,1,24,4,6]{2,3,4,1,0:T(4,128)S(1)} slice(f32[2,9,24,4,6]{2,3,4,1,0:T(4,128)} %param.6), slice={[1:2], [8:9], [0:24], [0:4], [0:6]} | slice | bytes 4608 | tf_op jit(solution)/shard_map/slice | solution.py:185
  1.6 0.1 copy.48
  1.7 1.0 %fusion.24 = (bf16[3,24,1152]{2,1,0:T(8,128)(2,1)S(1)}, bf16[3,24,1152]{2,1,0:T(8,128)(2,1)S(1)}) fusion(bf16[9,24,1152]{2,1,0:T(8,128)(2,1)} %t_ref.1), kind=kLoop, calls=%fused_computation.75 | loop fusion | bytes 663552 | tf_op jit(solution)/shard_map/slice | solution.py:187
  2.7 0.1 fusion.14
  2.8 4.4 %collective-permute-start = (bf16[4,24,1152]{2,1,0:T(8,128)(2,1)S(1)}, bf16[4,24,1152]{2,1,0:T(8,128)(2,1)S(1)}, u32[]{:S(2)}, u32[]{:S(2)}) collective-permute-start(bf16[4,24,1152]{2,1,0:T(8,128)(2,1)S(1)} %pad_maximum_fusion), channel_id=1, source_target_pairs={{0,32},{32,64},{64,96},{96,128},{128,160},{160,192},{192,224},{224... | collective-permute-start | bytes 663560 | tf_op jit(solution)/shard_map/ppermute | solution.py:19
  7.3 1.9 %collective-permute-start.1 = (bf16[3,24,1152]{2,1,0:T(8,128)(2,1)S(1)}, bf16[3,24,1152]{2,1,0:T(8,128)(2,1)S(1)}, u32[]{:S(2)}, u32[]{:S(2)}) collective-permute-start(bf16[3,24,1152]{2,1,0:T(8,128)(2,1)S(1)} %get-tuple-element.5), channel_id=1, source_target_pairs={{32,0},{64,32},{96,64},{128,96},{160,128},{192,160},{224,192},{256... | collective-permute-start | bytes 497672 | tf_op jit(solution)/shard_map/ppermute | solution.py:25
  9.3 0.1 bitcast_multiply_fusion
  9.4 0.1 slice.164
  9.5 0.1 slice_multiply_fusion
  9.6 0.1 pad_bitcast_fusion
  9.7 0.1 maximum_bitcast_fusion
  9.9 0.1 copy.45
  10.0 0.2 mul.91
  10.2 0.1 slice_convert_fusion
  10.3 0.1 add_bitcast_fusion.1
  10.5 0.1 eq.67
  10.6 0.8 %multiply_reduce_fusion = f32[4,12,6,216]{3,2,1,0:T(8,128)S(1)} fusion(f32[4,4,6,216]{3,1,2,0:T(4,128)S(1)} %mul.91, f32[4,4,12,216]{3,1,2,0:T(4,128)S(1)} %fusion.1), kind=kLoop, calls=%fused_computation | loop fusion | flops 435456 | bytes 497664 | tf_op jit(solution)/shard_map/reduce_sum | solution.py:134
  11.4 0.3 fusion
  11.8 0.1 copy.46
  11.9 0.1 copy.52
  12.0 0.1 copy.53
  12.1 0.3 copy.51
  12.4 0.1 reshape_squeeze.7
  12.5 0.1 fusion.18
  12.7 2.3 %collective-permute-done.south_ref = bf16[4,24,1152]{2,1,0:T(8,128)(2,1)S(1)} collective-permute-done((bf16[4,24,1152]{2,1,0:T(8,128)(2,1)S(1)}, bf16[4,24,1152]{2,1,0:T(8,128)(2,1)S(1)}, u32[]{:S(2)}, u32[]{:S(2)}) %collective-permute-start) | collective-permute-done | bytes 221216 | tf_op jit(solution)/shard_map/ppermute | solution.py:19
  15.0 0.1 convert_add_fusion
  15.1 0.1 slice_convert_fusion.1
  15.3 0.1 copy.57
  15.4 2.8 %collective-permute-done.1.north_ref = bf16[3,24,1152]{2,1,0:T(8,128)(2,1)S(1)} collective-permute-done((bf16[3,24,1152]{2,1,0:T(8,128)(2,1)S(1)}, bf16[3,24,1152]{2,1,0:T(8,128)(2,1)S(1)}, u32[]{:S(2)}, u32[]{:S(2)}) %collective-permute-start.1) | collective-permute-done | bytes 165920 | tf_op jit(solution)/shard_map/ppermute | solution.py:25
  18.3 0.2 fusion.2
  18.5 10.5 %collective-permute-start.2 = (bf16[15,4,1152]{2,1,0:T(4,128)(2,1)S(1)}, bf16[15,4,1152]{2,1,0:T(4,128)(2,1)S(1)}, u32[]{:S(2)}, u32[]{:S(2)}) collective-permute-start(bf16[15,4,1152]{2,1,0:T(4,128)(2,1)S(1)} %fusion.2), channel_id=1, source_target_pairs={{0,1},{1,2},{2,3},{3,4},{4,5},{5,6},{6,7},{7,8},{8,9},{9,10},{10,1... | collective-permute-start | bytes 414728 | tf_op jit(solution)/shard_map/ppermute | solution.py:19
  29.1 1.9 %collective-permute-start.3 = (bf16[15,3,1152]{2,1,0:T(4,128)(2,1)S(1)}, bf16[15,3,1152]{2,1,0:T(4,128)(2,1)S(1)}, u32[]{:S(2)}, u32[]{:S(2)}) collective-permute-start(bf16[15,3,1152]{2,1,0:T(4,128)(2,1)S(1)} %pad_maximum_fusion.1), channel_id=1, source_target_pairs={{1,0},{2,1},{3,2},{4,3},{5,4},{6,5},{7,6},{8,7},{9,8},{10,9},{11,1... | collective-permute-start | bytes 311048 | tf_op jit(solution)/shard_map/ppermute | solution.py:25
  31.0 0.1 multiply_reduce_fusion.1
  31.1 0.2 convolution_bitcast_fusion.1
  31.3 0.5 %collective-permute-done.2.west_ref = bf16[15,4,1152]{2,1,0:T(4,128)(2,1)S(1)} collective-permute-done((bf16[15,4,1152]{2,1,0:T(4,128)(2,1)S(1)}, bf16[15,4,1152]{2,1,0:T(4,128)(2,1)S(1)}, u32[]{:S(2)}, u32[]{:S(2)}) %collective-permute-start.2) | collective-permute-done | bytes 138272 | tf_op jit(solution)/shard_map/ppermute | solution.py:19
  31.9 0.1 convert_add_fusion.1
  32.0 0.1 slice_convert_fusion.2
  32.1 0.1 mul.97
  32.2 0.1 copy.55
  32.3 0.1 fusion.20
  32.4 0.1 multiply_reduce_fusion.2
  32.6 0.3 convolution_bitcast_fusion.2
  32.8 0.8 %add_divide_fusion.w_ref = f32[9,24,45]{2,1,0:T(8,128)} fusion(f32[1,24,45]{2,1,0:T(8,128)S(1)} %convolution_bitcast_fusion.1, f32[9,24,45]{2,1,0:T(8,128)S(1)} %bitcast.71, f32[9,1,45]{2,1,0:T(1,128)S(1)} %broadcast_in_dim.34, f32[9,24]{1,0:T(8,128)S(1)} %copy-done.10), kind=kLoop, calls=%fused_computation.21 | loop fusion | flops 29160 | bytes 84564 | tf_op jit(solution)/shard_map/div | solution.py:228
  33.6 3.9 %collective-permute-done.3.east_ref = bf16[15,3,1152]{2,1,0:T(4,128)(2,1)S(1)} collective-permute-done((bf16[15,3,1152]{2,1,0:T(4,128)(2,1)S(1)}, bf16[15,3,1152]{2,1,0:T(4,128)(2,1)S(1)}, u32[]{:S(2)}, u32[]{:S(2)}) %collective-permute-start.3) | collective-permute-done | bytes 103712 | tf_op jit(solution)/shard_map/ppermute | solution.py:25
  37.5 0.6 %copy-done.6 = bf16[15,3,1152]{2,1,0:T(4,128)(2,1)} copy-done((bf16[15,3,1152]{2,1,0:T(4,128)(2,1)}, bf16[15,3,1152]{2,1,0:T(4,128)(2,1)S(1)}, u32[]{:S(2)}) %copy-start.6) | copy-done | bytes 103704
  38.2 9.3 %shard_map.55 = bf16[9,24,1152]{2,1,0:T(8,128)(2,1)} custom-call(f32[9,24,45]{2,1,0:T(8,128)} %add_divide_fusion.w_ref, bf16[4,24,1152]{2,1,0:T(8,128)(2,1)} %copy-done.2, bf16[9,24,1152]{2,1,0:T(8,128)(2,1)} %t_ref.1, bf16[3,24,1152]{2,1,0:T(8,128)(2,1)} %copy-done.1, bf16[15,4,1152]{2,1,0:T(4,128)(2,1)} %copy-done.4, bf16[15,3,1152]{2,1,0:T(4,128)(2,1)} %copy-done.6), custom_call_target="tpu_custom_call" | custom-call | tf_op jit(solution)/shard_map/pallas_call | solution.py:166
  (45 shorter events, 0.5 us)
Async XLA Ops:
  0.0 9.2 %copy-start.3 = (f32[2,9,24,4,6]{2,3,4,1,0:T(4,128)S(1)}, f32[2,9,24,4,6]{2,3,4,1,0:T(4,128)}, u32[]{:S(2)}) copy-start(f32[2,9,24,4,6]{2,3,4,1,0:T(4,128)} %param.6) | copy-start | bytes 124420
  1.7 7.6 %copy-start.7 = (s32[2,9,24,4]{2,3,1,0:T(4,128)S(1)}, s32[2,9,24,4]{2,3,1,0:T(4,128)}, u32[]{:S(2)}) copy-start(s32[2,9,24,4]{2,3,1,0:T(4,128)} %param.7) | copy-start | bytes 20740
  2.8 12.2 %collective-permute-start = (bf16[4,24,1152]{2,1,0:T(8,128)(2,1)S(1)}, bf16[4,24,1152]{2,1,0:T(8,128)(2,1)S(1)}, u32[]{:S(2)}, u32[]{:S(2)}) collective-permute-start(bf16[4,24,1152]{2,1,0:T(8,128)(2,1)S(1)} %pad_maximum_fusion), channel_id=1, source_target_pairs={{0,32},{32,64},{64,96},{96,128},{128,160},{160,192},{192,224},{224... | collective-permute-start | bytes 663560 | tf_op jit(solution)/shard_map/ppermute | solution.py:19
  7.3 11.0 %collective-permute-start.1 = (bf16[3,24,1152]{2,1,0:T(8,128)(2,1)S(1)}, bf16[3,24,1152]{2,1,0:T(8,128)(2,1)S(1)}, u32[]{:S(2)}, u32[]{:S(2)}) collective-permute-start(bf16[3,24,1152]{2,1,0:T(8,128)(2,1)S(1)} %get-tuple-element.5), channel_id=1, source_target_pairs={{32,0},{64,32},{96,64},{128,96},{160,128},{192,160},{224,192},{256... | collective-permute-start | bytes 497672 | tf_op jit(solution)/shard_map/ppermute | solution.py:25
  10.2 1.2 %copy-start.5 = (f32[4,12,6,45]{3,2,1,0:T(8,128)S(1)}, f32[4,12,6,45]{3,2,1,0:T(8,128)}, u32[]{:S(2)}) copy-start(f32[4,12,6,45]{3,2,1,0:T(8,128)} %constant.47) | copy-start | bytes 155524
  11.4 6.8 %copy-start = (bf16[9,24,1152]{2,1,0:T(8,128)(2,1)S(1)}, bf16[9,24,1152]{2,1,0:T(8,128)(2,1)}, u32[]{:S(2)}) copy-start(bf16[9,24,1152]{2,1,0:T(8,128)(2,1)} %t_ref.1) | copy-start | bytes 1492996
  15.0 3.4 %copy-start.2 = (bf16[4,24,1152]{2,1,0:T(8,128)(2,1)}, bf16[4,24,1152]{2,1,0:T(8,128)(2,1)S(1)}, u32[]{:S(2)}) copy-start(bf16[4,24,1152]{2,1,0:T(8,128)(2,1)S(1)} %collective-permute-done.south_ref) | copy-start | bytes 663556
  15.4 15.7 %copy-start.8 = (f32[12,6,45]{2,1,0:T(8,128)S(1)}, f32[12,6,45]{2,1,0:T(8,128)}, u32[]{:S(2)}) copy-start(f32[12,6,45]{2,1,0:T(8,128)} %constant.51) | copy-start | bytes 38884
  18.3 10.8 %copy-start.1 = (bf16[3,24,1152]{2,1,0:T(8,128)(2,1)}, bf16[3,24,1152]{2,1,0:T(8,128)(2,1)S(1)}, u32[]{:S(2)}) copy-start(bf16[3,24,1152]{2,1,0:T(8,128)(2,1)S(1)} %collective-permute-done.1.north_ref) | copy-start | bytes 497668
  18.4 14.1 %copy-start.9 = (f32[12,6,45]{2,0,1:T(8,128)S(1)}, f32[12,6,45]{2,0,1:T(8,128)}, u32[]{:S(2)}) copy-start(f32[12,6,45]{2,0,1:T(8,128)} %constant.49) | copy-start | bytes 38884
  18.5 14.4 %copy-start.10 = (f32[9,24]{1,0:T(8,128)S(1)}, f32[9,24]{1,0:T(8,128)}, u32[]{:S(2)}) copy-start(f32[9,24]{1,0:T(8,128)} %param.8) | copy-start | bytes 2596
  18.5 13.4 %collective-permute-start.2 = (bf16[15,4,1152]{2,1,0:T(4,128)(2,1)S(1)}, bf16[15,4,1152]{2,1,0:T(4,128)(2,1)S(1)}, u32[]{:S(2)}, u32[]{:S(2)}) collective-permute-start(bf16[15,4,1152]{2,1,0:T(4,128)(2,1)S(1)} %fusion.2), channel_id=1, source_target_pairs={{0,1},{1,2},{2,3},{3,4},{4,5},{5,6},{6,7},{7,8},{8,9},{9,10},{10,1... | collective-permute-start | bytes 414728 | tf_op jit(solution)/shard_map/ppermute | solution.py:19
  29.1 8.5 %collective-permute-start.3 = (bf16[15,3,1152]{2,1,0:T(4,128)(2,1)S(1)}, bf16[15,3,1152]{2,1,0:T(4,128)(2,1)S(1)}, u32[]{:S(2)}, u32[]{:S(2)}) collective-permute-start(bf16[15,3,1152]{2,1,0:T(4,128)(2,1)S(1)} %pad_maximum_fusion.1), channel_id=1, source_target_pairs={{1,0},{2,1},{3,2},{4,3},{5,4},{6,5},{7,6},{8,7},{9,8},{10,9},{11,1... | collective-permute-start | bytes 311048 | tf_op jit(solution)/shard_map/ppermute | solution.py:25
  31.9 5.7 %copy-start.4 = (bf16[15,4,1152]{2,1,0:T(4,128)(2,1)}, bf16[15,4,1152]{2,1,0:T(4,128)(2,1)S(1)}, u32[]{:S(2)}) copy-start(bf16[15,4,1152]{2,1,0:T(4,128)(2,1)S(1)} %collective-permute-done.2.west_ref) | copy-start | bytes 414724
  37.5 0.7 %copy-start.6 = (bf16[15,3,1152]{2,1,0:T(4,128)(2,1)}, bf16[15,3,1152]{2,1,0:T(4,128)(2,1)S(1)}, u32[]{:S(2)}) copy-start(bf16[15,3,1152]{2,1,0:T(4,128)(2,1)S(1)} %collective-permute-done.3.east_ref) | copy-start | bytes 311044

commit v16 on v15

--- a/solution.py
+++ b/solution.py
@@ -157,6 +157,41 @@
         return carry
 
     lax.fori_loop(0, rows, row, 0)
+
+
+def edge_kernel(offsets, base, w_ref, south_ref, t_ref, north_ref, west_ref, east_ref, left_ref, right_ref, s_ref):
+    rows, cols, width = t_ref.shape
+    halo = north_ref.shape[0]
+    f32 = jnp.float32
+    s_ref[0:halo, base : base + cols] = south_ref[0:halo].astype(f32)
+    s_ref[halo : halo + rows, base : base + cols] = t_ref[...].astype(f32)
+    s_ref[halo + rows :, base : base + cols] = north_ref[...].astype(f32)
+    s_ref[:, base - halo : base] = west_ref[:, 0:halo].astype(f32)
+    s_ref[:, base + cols : base + cols + halo] = east_ref[...].astype(f32)
+
+    def row(i, carry):
+        for first, out_ref in ((0, left_ref), (cols - halo, right_ref)):
+            acc = s_ref[i + halo, pl.ds(base + first, halo), :]
+            for tap, (dr, dc) in enumerate(offsets):
+                w = w_ref[i, first : first + halo, tap : tap + 1]
+                acc = acc + w * s_ref[i + halo + dr, pl.ds(base + first + dc, halo), :]
+            out_ref[i] = acc.astype(out_ref.dtype)
+        return carry
+
+    lax.fori_loop(0, rows, row, 0)
+
+
+def edge_taps(weights, from_south, tracer, from_north, from_west, from_east, offsets):
+    rows, cols, width = tracer.shape
+    halo = from_north.shape[0]
+    base = 8
+    side = jax.ShapeDtypeStruct((rows, halo, width), jnp.bfloat16)
+    return pl.pallas_call(
+        functools.partial(edge_kernel, offsets, base),
+        out_shape=(side, side),
+        scratch_shapes=[pltpu.VMEM((rows + 2 * halo, base + cols + 8, width), jnp.float32)],
+        interpret=INTERPRET,
+    )(weights, from_south, tracer, from_north, from_west, from_east)
 
 
 def apply_taps(weights, from_south, tracer, from_north, from_west, from_east, offsets):
@@ -223,10 +258,15 @@
     south_m, south_p = unpack_weights(from_south[3], n_piece, n_moment)
     west_fix = face_weights(west_m[:, None], west_p[:, None], tables[:1])
     south_fix = face_weights(south_m[:, None], south_p[:, None], tables[2:3])
+    weights = weights + jnp.pad(south_fix[None], ((0, rows - 1), (0, 0), (0, 0)))
+    inner_weights = weights / cell_area[:, :, None]
     weights = weights + jnp.pad(west_fix[:, None], ((0, 0), (0, cols - 1), (0, 0)))
-    weights = weights + jnp.pad(south_fix[None], ((0, rows - 1), (0, 0), (0, 0)))
     weights = weights / cell_area[:, :, None]
-    return apply_taps(weights, from_south, tracer, from_north, from_west, from_east, offsets)
+    no_west = jnp.zeros_like(from_west)
+    no_east = jnp.zeros_like(from_east)
+    inner = apply_taps(inner_weights, from_south, tracer, from_north, no_west, no_east, offsets)
+    left, right = edge_taps(weights, from_south, tracer, from_north, from_west, from_east, offsets)
+    return jnp.concatenate([left, inner[:, 3 : cols - 3], right], axis=1)
 
 
 def solution(mesh):

time: 47.9 us -> 58.4 us (1.22)
  the two profiles are of different devices: /device:TPU:223 before, /device:TPU:16 now
where the time goes in v16:
time: 58.4 us; the launch traced here: 57.9 us
  starting transfers between devices  24.1 us (41%)
  Pallas kernels  16.3 us (28%)
  local copies, waits for them, and re-layouts  7.21 us (12%)
  other arithmetic  5.87 us (10%)
  waiting for transfers between devices  3.2 us (5%)
  matrix products  0.8 us (1%)
    ppermute x2, starting transfers between devices, from_next(): return lax.ppermute(value, axis, pairs)  18.6 us
    pallas_call x1, Pallas kernels, apply_taps(): pl.pallas_call(functools.partial(tap_kernel, offsets, base), out_shape=ja...  9.38 us
    pallas_call x1, Pallas kernels, edge_taps(): pl.pallas_call(functools.partial(edge_kernel, offsets, base), out_shape=(...  6.97 us
    ppermute x2, starting transfers between devices, from_prev(): return lax.ppermute(value, axis, pairs)  5.45 us
    ppermute x2, waiting for transfers between devices, from_next(): return lax.ppermute(value, axis, pairs)  2.82 us
    concatenate x1, other arithmetic, local(): return jnp.concatenate([left, inner[:, 3:cols - 3], right], axis=1)  1.93 us
  transfers between devices with their start and end apart: 4, of which 2 were waited for; matrix products, arithmetic and copies ran while one was open for 14% of the time, Pallas kernels for 16%

profile of v16, /device:TPU:16, one launch (start us, length us, event | category | flops | bytes accessed | tf_op | source)
XLA Modules:
  0.0 57.9 jit_solution(18174593557275878022)
XLA Ops:
  0.0 0.7 %slice_bitcast_fusion.8 = (s32[1,24,4]{1,2,0:T(4,128)S(1)}, bf16[24,4]{0,1:T(4,128)(2,1)S(1)}) fusion(s32[2,9,24,4]{2,3,1,0:T(4,128)} %param.7), kind=kLoop, calls=%fused_computation.75 | loop fusion | flops 96 | bytes 1344 | tf_op jit(solution)/shard_map/slice | solution.py:249
  0.7 0.1 copy.50
  0.8 0.7 %slice.140 = f32[1,1,24,4,6]{2,3,4,1,0:T(4,128)S(1)} slice(f32[2,9,24,4,6]{2,3,4,1,0:T(4,128)} %param.6), slice={[1:2], [8:9], [0:24], [0:4], [0:6]} | slice | bytes 4608 | tf_op jit(solution)/shard_map/slice | solution.py:220
  1.7 1.0 %fusion.25 = (bf16[3,24,1152]{2,1,0:T(8,128)(2,1)S(1)}, bf16[3,24,1152]{2,1,0:T(8,128)(2,1)S(1)}) fusion(bf16[9,24,1152]{2,1,0:T(8,128)(2,1)} %t_ref.3), kind=kLoop, calls=%fused_computation.78 | loop fusion | bytes 663552 | tf_op jit(solution)/shard_map/slice | solution.py:221
  2.7 0.1 fusion.15
  2.8 3.4 %collective-permute-start = (bf16[4,24,1152]{2,1,0:T(8,128)(2,1)S(1)}, bf16[4,24,1152]{2,1,0:T(8,128)(2,1)S(1)}, u32[]{:S(2)}, u32[]{:S(2)}) collective-permute-start(bf16[4,24,1152]{2,1,0:T(8,128)(2,1)S(1)} %pad_maximum_fusion.1), channel_id=1, source_target_pairs={{0,32},{32,64},{64,96},{96,128},{128,160},{160,192},{192,224},{224... | collective-permute-start | bytes 663560 | tf_op jit(solution)/shard_map/ppermute | solution.py:19
  6.2 5.5 %collective-permute-start.1 = (bf16[3,24,1152]{2,1,0:T(8,128)(2,1)S(1)}, bf16[3,24,1152]{2,1,0:T(8,128)(2,1)S(1)}, u32[]{:S(2)}, u32[]{:S(2)}) collective-permute-start(bf16[3,24,1152]{2,1,0:T(8,128)(2,1)S(1)} %get-tuple-element.10), channel_id=1, source_target_pairs={{32,0},{64,32},{96,64},{128,96},{160,128},{192,160},{224,192},{256... | collective-permute-start | bytes 497672 | tf_op jit(solution)/shard_map/ppermute | solution.py:25
  11.8 0.1 bitcast_multiply_fusion
  11.9 0.1 slice.173
  12.0 0.1 slice_multiply_fusion
  12.1 0.1 pad_bitcast_fusion
  12.2 0.1 maximum_bitcast_fusion
  12.3 0.1 copy.45
  12.5 0.2 mul.91
  12.7 0.1 fusion.26
  12.8 0.1 add_bitcast_fusion.1
  13.0 0.1 eq.67
  13.1 0.8 %multiply_reduce_fusion = f32[4,12,6,216]{3,2,1,0:T(8,128)S(1)} fusion(f32[4,4,6,216]{3,1,2,0:T(4,128)S(1)} %mul.91, f32[4,4,12,216]{3,1,2,0:T(4,128)S(1)} %fusion.1), kind=kLoop, calls=%fused_computation | loop fusion | flops 435456 | bytes 497664 | tf_op jit(solution)/shard_map/reduce_sum | solution.py:134
  13.9 0.3 fusion
  14.3 0.1 copy.46
  14.4 0.1 copy.55
  14.5 0.1 copy.56
  14.6 0.3 copy.54
  14.9 0.1 reshape_squeeze.7
  15.0 0.1 fusion.19
  15.3 0.1 convert_add_fusion
  15.5 0.1 copy.51
  15.6 2.8 %collective-permute-done.1.north_ref = bf16[3,24,1152]{2,1,0:T(8,128)(2,1)S(1)} collective-permute-done((bf16[3,24,1152]{2,1,0:T(8,128)(2,1)S(1)}, bf16[3,24,1152]{2,1,0:T(8,128)(2,1)S(1)}, u32[]{:S(2)}, u32[]{:S(2)}) %collective-permute-start.1) | collective-permute-done | bytes 165920 | tf_op jit(solution)/shard_map/ppermute | solution.py:25
  18.4 0.2 fusion.2
  18.6 2.1 %collective-permute-start.2 = (bf16[15,4,1152]{2,1,0:T(4,128)(2,1)S(1)}, bf16[15,4,1152]{2,1,0:T(4,128)(2,1)S(1)}, u32[]{:S(2)}, u32[]{:S(2)}) collective-permute-start(bf16[15,4,1152]{2,1,0:T(4,128)(2,1)S(1)} %fusion.2), channel_id=1, source_target_pairs={{0,1},{1,2},{2,3},{3,4},{4,5},{5,6},{6,7},{7,8},{8,9},{9,10},{10,1... | collective-permute-start | bytes 414728 | tf_op jit(solution)/shard_map/ppermute | solution.py:19
  20.8 13.2 %collective-permute-start.3 = (bf16[15,3,1152]{2,1,0:T(4,128)(2,1)S(1)}, bf16[15,3,1152]{2,1,0:T(4,128)(2,1)S(1)}, u32[]{:S(2)}, u32[]{:S(2)}) collective-permute-start(bf16[15,3,1152]{2,1,0:T(4,128)(2,1)S(1)} %pad_maximum_fusion.2), channel_id=1, source_target_pairs={{1,0},{2,1},{3,2},{4,3},{5,4},{6,5},{7,6},{8,7},{9,8},{10,9},{11,1... | collective-permute-start | bytes 311048 | tf_op jit(solution)/shard_map/ppermute | solution.py:25
  33.9 0.1 multiply_reduce_fusion.1
  34.1 0.2 convolution_bitcast_fusion.1
  34.3 0.4 collective-permute-done.2.west_ref
  34.8 0.1 slice_convert_fusion.2
  34.9 0.1 mul.101
  35.0 0.1 copy.58
  35.1 0.1 fusion.21
  35.2 0.1 multiply_reduce_fusion.2
  35.4 0.3 convolution_bitcast_fusion.2
  35.7 0.8 %fusion.7 = (f32[9,24,45]{2,1,0:T(8,128)}, f32[9,24,45]{2,1,0:T(8,128)}) fusion(f32[9,24,45]{2,1,0:T(8,128)S(1)} %bitcast.71, f32[1,24,45]{2,1,0:T(8,128)S(1)} %convolution_bitcast_fusion.1, f32[9,24]{1,0:T(8,128)S(1)} %copy-done.10, f32[9,1,45]{2,1,0:T(1,128)S(1)} %broadcast_in_dim.42), kind=kLoop, calls=%fused_computation.31 | loop fusion | flops 38880 | bytes 123444 | tf_op jit(solution)/shard_map/div | solution.py:262
  36.4 0.7 %broadcast_in_dim.43.west_ref = bf16[15,4,1152]{2,1,0:T(4,128)(2,1)} broadcast(bf16[]{:T(256)} %constant.28.clone.1), dimensions={} | broadcast | bytes 138242 | tf_op jit(solution)/shard_map/broadcast_in_dim | solution.py:265
  37.1 0.7 %broadcast_in_dim.44.east_ref = bf16[15,3,1152]{2,1,0:T(4,128)(2,1)} broadcast(bf16[]{:T(256)} %constant.28.clone.1), dimensions={} | broadcast | bytes 103682 | tf_op jit(solution)/shard_map/broadcast_in_dim | solution.py:266
  37.8 9.4 %shard_map.56 = bf16[9,24,1152]{2,1,0:T(8,128)(2,1)} custom-call(f32[9,24,45]{2,1,0:T(8,128)} %get-tuple-element.14.w_ref, bf16[4,24,1152]{2,1,0:T(8,128)(2,1)} %copy-done.2, bf16[9,24,1152]{2,1,0:T(8,128)(2,1)} %t_ref.3, bf16[3,24,1152]{2,1,0:T(8,128)(2,1)} %copy-done.1, bf16[15,4,1152]{2,1,0:T(4,128)(2,1)} %broadcast_in_dim.43.west_ref, ...), custom_call_target="tpu_custom_call" | custom-call | tf_op jit(solution)/shard_map/pallas_call | solution.py:201
  47.2 1.1 %slice.180 = bf16[9,18,1152]{2,1,0:T(8,128)(2,1)S(1)} slice(bf16[9,24,1152]{2,1,0:T(8,128)(2,1)} %shard_map.56), slice={[0:9], [3:21], [0:1152]} | slice | bytes 746496 | tf_op jit(solution)/shard_map/slice | solution.py:269
  48.4 0.6 %copy-done.6 = bf16[15,3,1152]{2,1,0:T(4,128)(2,1)} copy-done((bf16[15,3,1152]{2,1,0:T(4,128)(2,1)}, bf16[15,3,1152]{2,1,0:T(4,128)(2,1)S(1)}, u32[]{:S(2)}) %copy-start.6) | copy-done | bytes 103704
  49.0 7.0 %shard_map.55 = (bf16[9,3,1152]{2,1,0:T(4,128)(2,1)}, bf16[9,3,1152]{2,1,0:T(4,128)(2,1)}) custom-call(f32[9,24,45]{2,1,0:T(8,128)} %get-tuple-element.15.w_ref, bf16[4,24,1152]{2,1,0:T(8,128)(2,1)} %copy-done.2, bf16[9,24,1152]{2,1,0:T(8,128)(2,1)} %t_ref.3, bf16[3,24,1152]{2,1,0:T(8,128)(2,1)} %copy-done.1, bf16[15,4,1152]{2,1,0:T(4,128)(2,1)} %copy-done.4, ...), custom_call_target="tpu_custom_call" | custom-call | tf_op jit(solution)/shard_map/pallas_call | solution.py:189
  56.0 1.9 %pad_maximum_fusion = bf16[9,24,1152]{2,1,0:T(8,128)(2,1)} fusion(bf16[9,3,1152]{2,1,0:T(4,128)(2,1)} %get-tuple-element.8, bf16[9,18,1152]{2,1,0:T(8,128)(2,1)S(1)} %slice.180, bf16[9,3,1152]{2,1,0:T(4,128)(2,1)} %get-tuple-element.7), kind=kLoop, calls=%fused_computation.5 | loop fusion | flops 1492992 | bytes 995328 | tf_op jit(solution)/shard_map/concatenate | solution.py:269
  (50 shorter events, 0.8 us)
Async XLA Ops:
  0.0 11.7 %copy-start.3 = (f32[2,9,24,4,6]{2,3,4,1,0:T(4,128)S(1)}, f32[2,9,24,4,6]{2,3,4,1,0:T(4,128)}, u32[]{:S(2)}) copy-start(f32[2,9,24,4,6]{2,3,4,1,0:T(4,128)} %param.6) | copy-start | bytes 124420
  1.7 10.1 %copy-start.7 = (s32[2,9,24,4]{2,3,1,0:T(4,128)S(1)}, s32[2,9,24,4]{2,3,1,0:T(4,128)}, u32[]{:S(2)}) copy-start(s32[2,9,24,4]{2,3,1,0:T(4,128)} %param.7) | copy-start | bytes 20740
  2.8 12.4 %collective-permute-start = (bf16[4,24,1152]{2,1,0:T(8,128)(2,1)S(1)}, bf16[4,24,1152]{2,1,0:T(8,128)(2,1)S(1)}, u32[]{:S(2)}, u32[]{:S(2)}) collective-permute-start(bf16[4,24,1152]{2,1,0:T(8,128)(2,1)S(1)} %pad_maximum_fusion.1), channel_id=1, source_target_pairs={{0,32},{32,64},{64,96},{96,128},{128,160},{160,192},{192,224},{224... | collective-permute-start | bytes 663560 | tf_op jit(solution)/shard_map/ppermute | solution.py:19
  6.2 12.2 %collective-permute-start.1 = (bf16[3,24,1152]{2,1,0:T(8,128)(2,1)S(1)}, bf16[3,24,1152]{2,1,0:T(8,128)(2,1)S(1)}, u32[]{:S(2)}, u32[]{:S(2)}) collective-permute-start(bf16[3,24,1152]{2,1,0:T(8,128)(2,1)S(1)} %get-tuple-element.10), channel_id=1, source_target_pairs={{32,0},{64,32},{96,64},{128,96},{160,128},{192,160},{224,192},{256... | collective-permute-start | bytes 497672 | tf_op jit(solution)/shard_map/ppermute | solution.py:25
  12.7 1.2 %copy-start.5 = (f32[4,12,6,45]{3,2,1,0:T(8,128)S(1)}, f32[4,12,6,45]{3,2,1,0:T(8,128)}, u32[]{:S(2)}) copy-start(f32[4,12,6,45]{3,2,1,0:T(8,128)} %constant.49) | copy-start | bytes 155524
  13.9 4.5 %copy-start = (bf16[9,24,1152]{2,1,0:T(8,128)(2,1)S(1)}, bf16[9,24,1152]{2,1,0:T(8,128)(2,1)}, u32[]{:S(2)}) copy-start(bf16[9,24,1152]{2,1,0:T(8,128)(2,1)} %t_ref.3) | copy-start | bytes 1492996
  15.2 3.4 %copy-start.2 = (bf16[4,24,1152]{2,1,0:T(8,128)(2,1)}, bf16[4,24,1152]{2,1,0:T(8,128)(2,1)S(1)}, u32[]{:S(2)}) copy-start(bf16[4,24,1152]{2,1,0:T(8,128)(2,1)S(1)} %collective-permute-done.south_ref) | copy-start | bytes 663556
  15.6 18.5 %copy-start.8 = (f32[12,6,45]{2,1,0:T(8,128)S(1)}, f32[12,6,45]{2,1,0:T(8,128)}, u32[]{:S(2)}) copy-start(f32[12,6,45]{2,1,0:T(8,128)} %constant.51) | copy-start | bytes 38884
  18.4 2.3 %copy-start.1 = (bf16[3,24,1152]{2,1,0:T(8,128)(2,1)}, bf16[3,24,1152]{2,1,0:T(8,128)(2,1)S(1)}, u32[]{:S(2)}) copy-start(bf16[3,24,1152]{2,1,0:T(8,128)(2,1)S(1)} %collective-permute-done.1.north_ref) | copy-start | bytes 497668
  18.6 16.7 %copy-start.9 = (f32[12,6,45]{2,0,1:T(8,128)S(1)}, f32[12,6,45]{2,0,1:T(8,128)}, u32[]{:S(2)}) copy-start(f32[12,6,45]{2,0,1:T(8,128)} %constant.53) | copy-start | bytes 38884
  18.6 17.0 %copy-start.10 = (f32[9,24]{1,0:T(8,128)S(1)}, f32[9,24]{1,0:T(8,128)}, u32[]{:S(2)}) copy-start(f32[9,24]{1,0:T(8,128)} %param.8) | copy-start | bytes 2596
  18.6 16.0 %collective-permute-start.2 = (bf16[15,4,1152]{2,1,0:T(4,128)(2,1)S(1)}, bf16[15,4,1152]{2,1,0:T(4,128)(2,1)S(1)}, u32[]{:S(2)}, u32[]{:S(2)}) collective-permute-start(bf16[15,4,1152]{2,1,0:T(4,128)(2,1)S(1)} %fusion.2), channel_id=1, source_target_pairs={{0,1},{1,2},{2,3},{3,4},{4,5},{5,6},{6,7},{7,8},{8,9},{9,10},{10,1... | collective-permute-start | bytes 414728 | tf_op jit(solution)/shard_map/ppermute | solution.py:19
  20.8 27.6 %collective-permute-start.3 = (bf16[15,3,1152]{2,1,0:T(4,128)(2,1)S(1)}, bf16[15,3,1152]{2,1,0:T(4,128)(2,1)S(1)}, u32[]{:S(2)}, u32[]{:S(2)}) collective-permute-start(bf16[15,3,1152]{2,1,0:T(4,128)(2,1)S(1)} %pad_maximum_fusion.2), channel_id=1, source_target_pairs={{1,0},{2,1},{3,2},{4,3},{5,4},{6,5},{7,6},{8,7},{9,8},{10,9},{11,1... | collective-permute-start | bytes 311048 | tf_op jit(solution)/shard_map/ppermute | solution.py:25
  34.7 12.5 %copy-start.4 = (bf16[15,4,1152]{2,1,0:T(4,128)(2,1)}, bf16[15,4,1152]{2,1,0:T(4,128)(2,1)S(1)}, u32[]{:S(2)}) copy-start(bf16[15,4,1152]{2,1,0:T(4,128)(2,1)S(1)} %collective-permute-done.2.west_ref) | copy-start | bytes 414724
  48.4 0.7 %copy-start.6 = (bf16[15,3,1152]{2,1,0:T(4,128)(2,1)}, bf16[15,3,1152]{2,1,0:T(4,128)(2,1)S(1)}, u32[]{:S(2)}) copy-start(bf16[15,3,1152]{2,1,0:T(4,128)(2,1)S(1)} %collective-permute-done.3.east_ref) | copy-start | bytes 311044

commit v17 on v15

--- a/solution.py
+++ b/solution.py
@@ -148,15 +148,12 @@
     s_ref[:, base - halo : base] = west_ref[:, 0:halo].astype(f32)
     s_ref[:, base + cols : base + cols + halo] = east_ref[...].astype(f32)
 
-    def row(i, carry):
+    for i in range(rows):
         acc = s_ref[i + halo, pl.ds(base, cols), :]
         for tap, (dr, dc) in enumerate(offsets):
             w = w_ref[i, :, tap : tap + 1]
             acc = acc + w * s_ref[i + halo + dr, pl.ds(base + dc, cols), :]
         o_ref[i] = acc.astype(o_ref.dtype)
-        return carry
-
-    lax.fori_loop(0, rows, row, 0)
 
 
 def apply_taps(weights, from_south, tracer, from_north, from_west, from_east, offsets):

time: 47.9 us -> 47.6 us (level)
  no operation moved by 1% of the time
where the time goes in v17:
time: 47.6 us; the launch traced here: 47.3 us
  starting transfers between devices  18.8 us (39%)
  waiting for transfers between devices  9.64 us (20%)
  Pallas kernels  9.07 us (19%)
  local copies, waits for them, and re-layouts  4.68 us (10%)
  other arithmetic  3.88 us (8%)
  matrix products  0.8 us (2%)
    ppermute x2, starting transfers between devices, from_prev(): return lax.ppermute(value, axis, pairs)  15 us
    pallas_call x1, Pallas kernels, apply_taps(): pl.pallas_call(functools.partial(tap_kernel, offsets, base), out_shape=ja...  9.07 us
    ppermute x2, waiting for transfers between devices, from_next(): return lax.ppermute(value, axis, pairs)  6.77 us
    ppermute x2, starting transfers between devices, from_next(): return lax.ppermute(value, axis, pairs)  3.84 us
    ppermute x2, waiting for transfers between devices, from_prev(): return lax.ppermute(value, axis, pairs)  2.86 us
    slice x1, local copies, waits for them, and re-layouts, local(): from_north = from_next(tracer[:3], 'panel', False)  1.03 us
  transfers between devices with their start and end apart: 4, of which 4 were waited for; matrix products, arithmetic and copies ran while one was open for 12% of the time, Pallas kernels for 0%

profile of v17, /device:TPU:223, one launch (start us, length us, event | category | flops | bytes accessed | tf_op | source)
XLA Modules:
  0.0 47.3 jit_solution(7019707677291458627)
XLA Ops:
  0.0 0.7 %slice_bitcast_fusion.8 = (s32[1,24,4]{1,2,0:T(4,128)S(1)}, bf16[24,4]{0,1:T(4,128)(2,1)S(1)}) fusion(s32[2,9,24,4]{2,3,1,0:T(4,128)} %param.7), kind=kLoop, calls=%fused_computation.72 | loop fusion | flops 96 | bytes 1344 | tf_op jit(solution)/shard_map/slice | solution.py:211
  0.7 0.1 copy.50
  0.8 0.7 %slice.137 = f32[1,1,24,4,6]{2,3,4,1,0:T(4,128)S(1)} slice(f32[2,9,24,4,6]{2,3,4,1,0:T(4,128)} %param.6), slice={[1:2], [8:9], [0:24], [0:4], [0:6]} | slice | bytes 4608 | tf_op jit(solution)/shard_map/slice | solution.py:182
  1.6 0.1 copy.48
  1.7 1.0 %fusion.24 = (bf16[3,24,1152]{2,1,0:T(8,128)(2,1)S(1)}, bf16[3,24,1152]{2,1,0:T(8,128)(2,1)S(1)}) fusion(bf16[9,24,1152]{2,1,0:T(8,128)(2,1)} %t_ref.1), kind=kLoop, calls=%fused_computation.75 | loop fusion | bytes 663552 | tf_op jit(solution)/shard_map/slice | solution.py:184
  2.7 0.1 fusion.14
  2.8 4.4 %collective-permute-start = (bf16[4,24,1152]{2,1,0:T(8,128)(2,1)S(1)}, bf16[4,24,1152]{2,1,0:T(8,128)(2,1)S(1)}, u32[]{:S(2)}, u32[]{:S(2)}) collective-permute-start(bf16[4,24,1152]{2,1,0:T(8,128)(2,1)S(1)} %pad_maximum_fusion), channel_id=1, source_target_pairs={{0,32},{32,64},{64,96},{96,128},{128,160},{160,192},{192,224},{224... | collective-permute-start | bytes 663560 | tf_op jit(solution)/shard_map/ppermute | solution.py:19
  7.3 1.9 %collective-permute-start.1 = (bf16[3,24,1152]{2,1,0:T(8,128)(2,1)S(1)}, bf16[3,24,1152]{2,1,0:T(8,128)(2,1)S(1)}, u32[]{:S(2)}, u32[]{:S(2)}) collective-permute-start(bf16[3,24,1152]{2,1,0:T(8,128)(2,1)S(1)} %get-tuple-element.5), channel_id=1, source_target_pairs={{32,0},{64,32},{96,64},{128,96},{160,128},{192,160},{224,192},{256... | collective-permute-start | bytes 497672 | tf_op jit(solution)/shard_map/ppermute | solution.py:25
  9.3 0.1 bitcast_multiply_fusion
  9.4 0.1 slice.164
  9.5 0.1 slice_multiply_fusion
  9.6 0.1 pad_bitcast_fusion
  9.7 0.1 maximum_bitcast_fusion
  9.9 0.1 copy.45
  10.0 0.2 mul.91
  10.2 0.1 slice_convert_fusion
  10.3 0.1 add_bitcast_fusion.1
  10.5 0.1 eq.67
  10.6 0.8 %multiply_reduce_fusion = f32[4,12,6,216]{3,2,1,0:T(8,128)S(1)} fusion(f32[4,4,6,216]{3,1,2,0:T(4,128)S(1)} %mul.91, f32[4,4,12,216]{3,1,2,0:T(4,128)S(1)} %fusion.1), kind=kLoop, calls=%fused_computation | loop fusion | flops 435456 | bytes 497664 | tf_op jit(solution)/shard_map/reduce_sum | solution.py:134
  11.4 0.3 fusion
  11.8 0.1 copy.46
  11.9 0.1 copy.52
  12.0 0.1 copy.53
  12.1 0.3 copy.51
  12.4 0.1 reshape_squeeze.7
  12.5 0.1 fusion.18
  12.7 2.3 %collective-permute-done.south_ref = bf16[4,24,1152]{2,1,0:T(8,128)(2,1)S(1)} collective-permute-done((bf16[4,24,1152]{2,1,0:T(8,128)(2,1)S(1)}, bf16[4,24,1152]{2,1,0:T(8,128)(2,1)S(1)}, u32[]{:S(2)}, u32[]{:S(2)}) %collective-permute-start) | collective-permute-done | bytes 221216 | tf_op jit(solution)/shard_map/ppermute | solution.py:19
  15.0 0.1 convert_add_fusion
  15.1 0.1 slice_convert_fusion.1
  15.3 0.1 copy.57
  15.4 2.8 %collective-permute-done.1.north_ref = bf16[3,24,1152]{2,1,0:T(8,128)(2,1)S(1)} collective-permute-done((bf16[3,24,1152]{2,1,0:T(8,128)(2,1)S(1)}, bf16[3,24,1152]{2,1,0:T(8,128)(2,1)S(1)}, u32[]{:S(2)}, u32[]{:S(2)}) %collective-permute-start.1) | collective-permute-done | bytes 165920 | tf_op jit(solution)/shard_map/ppermute | solution.py:25
  18.3 0.2 fusion.2
  18.5 10.5 %collective-permute-start.2 = (bf16[15,4,1152]{2,1,0:T(4,128)(2,1)S(1)}, bf16[15,4,1152]{2,1,0:T(4,128)(2,1)S(1)}, u32[]{:S(2)}, u32[]{:S(2)}) collective-permute-start(bf16[15,4,1152]{2,1,0:T(4,128)(2,1)S(1)} %fusion.2), channel_id=1, source_target_pairs={{0,1},{1,2},{2,3},{3,4},{4,5},{5,6},{6,7},{7,8},{8,9},{9,10},{10,1... | collective-permute-start | bytes 414728 | tf_op jit(solution)/shard_map/ppermute | solution.py:19
  29.1 1.9 %collective-permute-start.3 = (bf16[15,3,1152]{2,1,0:T(4,128)(2,1)S(1)}, bf16[15,3,1152]{2,1,0:T(4,128)(2,1)S(1)}, u32[]{:S(2)}, u32[]{:S(2)}) collective-permute-start(bf16[15,3,1152]{2,1,0:T(4,128)(2,1)S(1)} %pad_maximum_fusion.1), channel_id=1, source_target_pairs={{1,0},{2,1},{3,2},{4,3},{5,4},{6,5},{7,6},{8,7},{9,8},{10,9},{11,1... | collective-permute-start | bytes 311048 | tf_op jit(solution)/shard_map/ppermute | solution.py:25
  31.0 0.1 multiply_reduce_fusion.1
  31.1 0.2 convolution_bitcast_fusion.1
  31.3 0.5 %collective-permute-done.2.west_ref = bf16[15,4,1152]{2,1,0:T(4,128)(2,1)S(1)} collective-permute-done((bf16[15,4,1152]{2,1,0:T(4,128)(2,1)S(1)}, bf16[15,4,1152]{2,1,0:T(4,128)(2,1)S(1)}, u32[]{:S(2)}, u32[]{:S(2)}) %collective-permute-start.2) | collective-permute-done | bytes 138272 | tf_op jit(solution)/shard_map/ppermute | solution.py:19
  31.9 0.1 convert_add_fusion.1
  32.0 0.1 slice_convert_fusion.2
  32.1 0.1 mul.97
  32.2 0.1 copy.55
  32.3 0.1 fusion.20
  32.4 0.1 multiply_reduce_fusion.2
  32.6 0.3 convolution_bitcast_fusion.2
  32.8 0.8 %add_divide_fusion.w_ref = f32[9,24,45]{2,1,0:T(8,128)} fusion(f32[1,24,45]{2,1,0:T(8,128)S(1)} %convolution_bitcast_fusion.1, f32[9,24,45]{2,1,0:T(8,128)S(1)} %bitcast.71, f32[9,1,45]{2,1,0:T(1,128)S(1)} %broadcast_in_dim.34, f32[9,24]{1,0:T(8,128)S(1)} %copy-done.10), kind=kLoop, calls=%fused_computation.21 | loop fusion | flops 29160 | bytes 84564 | tf_op jit(solution)/shard_map/div | solution.py:225
  33.6 3.9 %collective-permute-done.3.east_ref = bf16[15,3,1152]{2,1,0:T(4,128)(2,1)S(1)} collective-permute-done((bf16[15,3,1152]{2,1,0:T(4,128)(2,1)S(1)}, bf16[15,3,1152]{2,1,0:T(4,128)(2,1)S(1)}, u32[]{:S(2)}, u32[]{:S(2)}) %collective-permute-start.3) | collective-permute-done | bytes 103712 | tf_op jit(solution)/shard_map/ppermute | solution.py:25
  37.5 0.6 %copy-done.6 = bf16[15,3,1152]{2,1,0:T(4,128)(2,1)} copy-done((bf16[15,3,1152]{2,1,0:T(4,128)(2,1)}, bf16[15,3,1152]{2,1,0:T(4,128)(2,1)S(1)}, u32[]{:S(2)}) %copy-start.6) | copy-done | bytes 103704
  38.2 9.1 %shard_map.55 = bf16[9,24,1152]{2,1,0:T(8,128)(2,1)} custom-call(f32[9,24,45]{2,1,0:T(8,128)} %add_divide_fusion.w_ref, bf16[4,24,1152]{2,1,0:T(8,128)(2,1)} %copy-done.2, bf16[9,24,1152]{2,1,0:T(8,128)(2,1)} %t_ref.1, bf16[3,24,1152]{2,1,0:T(8,128)(2,1)} %copy-done.1, bf16[15,4,1152]{2,1,0:T(4,128)(2,1)} %copy-done.4, bf16[15,3,1152]{2,1,0:T(4,128)(2,1)} %copy-done.6), custom_call_target="tpu_custom_call" | custom-call | tf_op jit(solution)/shard_map/pallas_call | solution.py:163
  (45 shorter events, 0.5 us)
Async XLA Ops:
  0.0 9.2 %copy-start.3 = (f32[2,9,24,4,6]{2,3,4,1,0:T(4,128)S(1)}, f32[2,9,24,4,6]{2,3,4,1,0:T(4,128)}, u32[]{:S(2)}) copy-start(f32[2,9,24,4,6]{2,3,4,1,0:T(4,128)} %param.6) | copy-start | bytes 124420
  1.7 7.6 %copy-start.7 = (s32[2,9,24,4]{2,3,1,0:T(4,128)S(1)}, s32[2,9,24,4]{2,3,1,0:T(4,128)}, u32[]{:S(2)}) copy-start(s32[2,9,24,4]{2,3,1,0:T(4,128)} %param.7) | copy-start | bytes 20740
  2.8 12.2 %collective-permute-start = (bf16[4,24,1152]{2,1,0:T(8,128)(2,1)S(1)}, bf16[4,24,1152]{2,1,0:T(8,128)(2,1)S(1)}, u32[]{:S(2)}, u32[]{:S(2)}) collective-permute-start(bf16[4,24,1152]{2,1,0:T(8,128)(2,1)S(1)} %pad_maximum_fusion), channel_id=1, source_target_pairs={{0,32},{32,64},{64,96},{96,128},{128,160},{160,192},{192,224},{224... | collective-permute-start | bytes 663560 | tf_op jit(solution)/shard_map/ppermute | solution.py:19
  7.3 11.0 %collective-permute-start.1 = (bf16[3,24,1152]{2,1,0:T(8,128)(2,1)S(1)}, bf16[3,24,1152]{2,1,0:T(8,128)(2,1)S(1)}, u32[]{:S(2)}, u32[]{:S(2)}) collective-permute-start(bf16[3,24,1152]{2,1,0:T(8,128)(2,1)S(1)} %get-tuple-element.5), channel_id=1, source_target_pairs={{32,0},{64,32},{96,64},{128,96},{160,128},{192,160},{224,192},{256... | collective-permute-start | bytes 497672 | tf_op jit(solution)/shard_map/ppermute | solution.py:25
  10.2 1.2 %copy-start.5 = (f32[4,12,6,45]{3,2,1,0:T(8,128)S(1)}, f32[4,12,6,45]{3,2,1,0:T(8,128)}, u32[]{:S(2)}) copy-start(f32[4,12,6,45]{3,2,1,0:T(8,128)} %constant.47) | copy-start | bytes 155524
  11.4 6.8 %copy-start = (bf16[9,24,1152]{2,1,0:T(8,128)(2,1)S(1)}, bf16[9,24,1152]{2,1,0:T(8,128)(2,1)}, u32[]{:S(2)}) copy-start(bf16[9,24,1152]{2,1,0:T(8,128)(2,1)} %t_ref.1) | copy-start | bytes 1492996
  15.0 3.4 %copy-start.2 = (bf16[4,24,1152]{2,1,0:T(8,128)(2,1)}, bf16[4,24,1152]{2,1,0:T(8,128)(2,1)S(1)}, u32[]{:S(2)}) copy-start(bf16[4,24,1152]{2,1,0:T(8,128)(2,1)S(1)} %collective-permute-done.south_ref) | copy-start | bytes 663556
  15.4 15.7 %copy-start.8 = (f32[12,6,45]{2,1,0:T(8,128)S(1)}, f32[12,6,45]{2,1,0:T(8,128)}, u32[]{:S(2)}) copy-start(f32[12,6,45]{2,1,0:T(8,128)} %constant.51) | copy-start | bytes 38884
  18.3 10.8 %copy-start.1 = (bf16[3,24,1152]{2,1,0:T(8,128)(2,1)}, bf16[3,24,1152]{2,1,0:T(8,128)(2,1)S(1)}, u32[]{:S(2)}) copy-start(bf16[3,24,1152]{2,1,0:T(8,128)(2,1)S(1)} %collective-permute-done.1.north_ref) | copy-start | bytes 497668
  18.4 14.1 %copy-start.9 = (f32[12,6,45]{2,0,1:T(8,128)S(1)}, f32[12,6,45]{2,0,1:T(8,128)}, u32[]{:S(2)}) copy-start(f32[12,6,45]{2,0,1:T(8,128)} %constant.49) | copy-start | bytes 38884
  18.5 14.4 %copy-start.10 = (f32[9,24]{1,0:T(8,128)S(1)}, f32[9,24]{1,0:T(8,128)}, u32[]{:S(2)}) copy-start(f32[9,24]{1,0:T(8,128)} %param.8) | copy-start | bytes 2596
  18.5 13.4 %collective-permute-start.2 = (bf16[15,4,1152]{2,1,0:T(4,128)(2,1)S(1)}, bf16[15,4,1152]{2,1,0:T(4,128)(2,1)S(1)}, u32[]{:S(2)}, u32[]{:S(2)}) collective-permute-start(bf16[15,4,1152]{2,1,0:T(4,128)(2,1)S(1)} %fusion.2), channel_id=1, source_target_pairs={{0,1},{1,2},{2,3},{3,4},{4,5},{5,6},{6,7},{7,8},{8,9},{9,10},{10,1... | collective-permute-start | bytes 414728 | tf_op jit(solution)/shard_map/ppermute | solution.py:19
  29.1 8.5 %collective-permute-start.3 = (bf16[15,3,1152]{2,1,0:T(4,128)(2,1)S(1)}, bf16[15,3,1152]{2,1,0:T(4,128)(2,1)S(1)}, u32[]{:S(2)}, u32[]{:S(2)}) collective-permute-start(bf16[15,3,1152]{2,1,0:T(4,128)(2,1)S(1)} %pad_maximum_fusion.1), channel_id=1, source_target_pairs={{1,0},{2,1},{3,2},{4,3},{5,4},{6,5},{7,6},{8,7},{9,8},{10,9},{11,1... | collective-permute-start | bytes 311048 | tf_op jit(solution)/shard_map/ppermute | solution.py:25
  31.9 5.7 %copy-start.4 = (bf16[15,4,1152]{2,1,0:T(4,128)(2,1)}, bf16[15,4,1152]{2,1,0:T(4,128)(2,1)S(1)}, u32[]{:S(2)}) copy-start(bf16[15,4,1152]{2,1,0:T(4,128)(2,1)S(1)} %collective-permute-done.2.west_ref) | copy-start | bytes 414724
  37.5 0.7 %copy-start.6 = (bf16[15,3,1152]{2,1,0:T(4,128)(2,1)}, bf16[15,3,1152]{2,1,0:T(4,128)(2,1)S(1)}, u32[]{:S(2)}) copy-start(bf16[15,3,1152]{2,1,0:T(4,128)(2,1)S(1)} %collective-permute-done.3.east_ref) | copy-start | bytes 311044
